TPU v7x, 512 devices: a whole 4x8x8 slice. The times are simulated.
512 devices in a mesh: gx: 8 (over z), gy: 8 (over y), gz: 8 (over x, core).
Axes of the slice: x: 4, y: 8, z: 8, core: 2. Of those that a mesh axis runs over, the one named last changes fastest.
Arguments:
- reference_image: bfloat16 [128, 128, 1024], P('gx', 'gy', 'gz'), may hold values from -60 to 60
- deformed_image: bfloat16 [128, 128, 1024], P('gx', 'gy', 'gz'), may hold values from -60 to 60
- roi_mask: int32 [128, 128, 1024], P('gx', 'gy', 'gz'), may hold values 0 or 1
- displacement: float32 [3, 32768, 8], P(None, ('gx', 'gy', 'gz')), may hold values from -12 to 12
- node_map: int32 [32768], P(('gx', 'gy', 'gz')), may hold values from 0 to 4095, as said below
Outputs:
- displacement_out: float32 [3, 32768, 8], P(None, ('gx', 'gy', 'gz'))
Inputs may be any that keep to these rules, and one draw needn't show every extreme that they name: Within each slab (devices with one gx index) node_map is a permutation of 0 to 4095. Every device lists exactly 2 blocks of one tile and at most one block of each other tile.
All inputs are finite; a program needn't handle non-finite values. No bound on the sum of `roi_mask` on one device may be relied on, other than what follows from the above.
Results may differ from a plain program's by a relative error of at most 0.00083.
Values may be sent and summed in bfloat16 or wider, within the bound.
No kernel may reach another device: no remote copies, remote signals or barrier semaphores. Data moves between devices by JAX's collectives and lax.ppermute only.
A program may use at most 64 MiB of HBM per device.

v0:
```python
import jax
import jax.numpy as jnp
from jax import lax
from jax.sharding import PartitionSpec as P

ELEM = 4
ITERS = 2
CAP = 2


binomial = (0.0625, 0.25, 0.375, 0.25, 0.0625)
lame_lambda = 1.0
shear_modulus = 0.5
elastic_weight = 2.0
diagonal_shift = 6.0
highest = lax.Precision.HIGHEST


def with_halo(block, sides, width):
    for axis, dim in sides:
        count = lax.axis_size(axis)
        forward = [(i, i + 1) for i in range(count - 1)]
        backward = [(target, source) for source, target in forward]
        low = lax.ppermute(
            lax.slice_in_dim(block, block.shape[dim] - width, None, axis=dim), axis, forward
        )
        high = lax.ppermute(lax.slice_in_dim(block, 0, width, axis=dim), axis, backward)
        block = jnp.concatenate([low, block, high], axis=dim)
    return block


def smooth_axis(volume, dimension):
    length = volume.shape[dimension] - 4
    summed = binomial[0] * lax.slice_in_dim(volume, 0, length, axis=dimension)
    for offset in range(1, 5):
        summed = summed + binomial[offset] * lax.slice_in_dim(
            volume, offset, offset + length, axis=dimension
        )
    return summed


def derive_fields(first_padded, second_padded):
    first_smooth = first_padded
    second_smooth = second_padded
    for dimension in range(3):
        first_smooth = smooth_axis(first_smooth, dimension)
        second_smooth = smooth_axis(second_smooth, dimension)
    average = (first_smooth + second_smooth) * 0.5
    contrast = (second_smooth - first_smooth)[1:-1, 1:-1, 1:-1].astype(jnp.bfloat16)
    slopes = []
    for dimension in range(3):
        length = average.shape[dimension] - 2
        forward_part = lax.slice_in_dim(average, 2, length + 2, axis=dimension)
        backward_part = lax.slice_in_dim(average, 0, length, axis=dimension)
        gradient = (forward_part - backward_part) * 0.5
        for cropped_dim in range(3):
            if cropped_dim != dimension:
                gradient = lax.slice_in_dim(
                    gradient, 1, gradient.shape[cropped_dim] - 1, axis=cropped_dim
                )
        slopes.append(gradient.astype(jnp.bfloat16))
    return jnp.stack([contrast] + slopes)


def interp_axis(volume, dimension, cells_edge):
    length = volume.shape[dimension]
    before = lax.slice_in_dim(volume, 0, length - 1, axis=dimension)
    after = lax.slice_in_dim(volume, 1, length, axis=dimension)
    shape_one = [1] * (volume.ndim + 1)
    shape_one[dimension + 1] = cells_edge
    fraction = (jnp.arange(cells_edge, dtype=jnp.float32) / cells_edge).reshape(shape_one)
    merged = (
        jnp.expand_dims(before, dimension + 1) * (1.0 - fraction)
        + jnp.expand_dims(after, dimension + 1) * fraction
    )
    new_shape = list(volume.shape)
    new_shape[dimension] = (length - 1) * cells_edge
    return merged.reshape(new_shape)


def collect_axis(volume, dimension, cells_edge, squared):
    elements = volume.shape[dimension] // cells_edge
    split_shape = (
        list(volume.shape[:dimension])
        + [elements, cells_edge]
        + list(volume.shape[dimension + 1 :])
    )
    pieces = volume.reshape(split_shape)
    shape_one = [1] * len(split_shape)
    shape_one[dimension + 1] = cells_edge
    fraction = (jnp.arange(cells_edge, dtype=jnp.float32) / cells_edge).reshape(shape_one)
    weight_low = 1.0 - fraction
    weight_high = fraction
    if squared:
        weight_low = weight_low * weight_low
        weight_high = weight_high * weight_high
    low_side = jnp.sum(pieces * weight_low, axis=dimension + 1)
    high_side = jnp.sum(pieces * weight_high, axis=dimension + 1)
    return lax.slice_in_dim(low_side, 1, elements, axis=dimension) + lax.slice_in_dim(
        high_side, 0, elements - 1, axis=dimension
    )


def pair_op(volume, dimension, factor):
    length = volume.shape[dimension]
    return lax.slice_in_dim(volume, 1, length, axis=dimension) + factor * lax.slice_in_dim(
        volume, 0, length - 1, axis=dimension
    )


def cross_pairs(volume, chosen, factor, offset):
    for dimension in range(3):
        volume = pair_op(volume, dimension + offset, factor if dimension == chosen else 1.0)
    return volume


def elastic_force(padded):
    gradients = [cross_pairs(padded, chosen, -1.0, 1) * (1.0 / (4.0 * ELEM)) for chosen in range(3)]
    deform = [
        [gradients[source][target] + (1.0 if target == source else 0.0) for source in range(3)]
        for target in range(3)
    ]
    strain = [
        [
            0.5
            * (
                deform[0][target] * deform[0][source]
                + deform[1][target] * deform[1][source]
                + deform[2][target] * deform[2][source]
            )
            - (0.5 if target == source else 0.0)
            for source in range(3)
        ]
        for target in range(3)
    ]
    trace_strain = strain[0][0] + strain[1][1] + strain[2][2]
    stress = [
        [
            2.0 * shear_modulus * strain[target][source]
            + (lame_lambda * trace_strain if target == source else 0.0)
            for source in range(3)
        ]
        for target in range(3)
    ]
    nominal = [
        [
            deform[target][0] * stress[0][source]
            + deform[target][1] * stress[1][source]
            + deform[target][2] * stress[2][source]
            for source in range(3)
        ]
        for target in range(3)
    ]
    coefficient = ELEM * ELEM / 4.0
    forces = []
    for target in range(3):
        summed = cross_pairs(nominal[target][0], 0, -1.0, 0)
        for source in range(1, 3):
            summed = summed + cross_pairs(nominal[target][source], source, -1.0, 0)
        forces.append(-coefficient * summed)
    return jnp.stack(forces)


def axis_table(nodes_len, cells_edge, squared):
    voxels = (nodes_len - 1) * cells_edge
    column = jnp.arange(voxels, dtype=jnp.int32)
    element = column // cells_edge
    fraction = (column % cells_edge).astype(jnp.float32) / cells_edge
    weight_low = 1.0 - fraction
    weight_high = fraction
    if squared:
        weight_low = weight_low * weight_low
        weight_high = weight_high * weight_high
    node_row = jnp.arange(nodes_len, dtype=jnp.int32)[:, None]
    return jnp.where(node_row == element[None, :], weight_low[None, :], 0.0) + jnp.where(
        node_row == element[None, :] + 1, weight_high[None, :], 0.0
    )


def spread(padded, weights_table):
    shape_all = padded.shape
    stretched = jnp.dot(padded.reshape(-1, shape_all[3]), weights_table, precision=highest)
    stretched = stretched.reshape(shape_all[0], shape_all[1], shape_all[2], weights_table.shape[1])
    stretched = interp_axis(stretched, 1, ELEM)
    return interp_axis(stretched, 2, ELEM)


def collect(volume, table_back, squared):
    shape_all = volume.shape
    reduced = jnp.dot(volume.reshape(-1, shape_all[3]), table_back, precision=highest)
    reduced = reduced.reshape(shape_all[0], shape_all[1], shape_all[2], table_back.shape[1])
    reduced = collect_axis(reduced, 2, ELEM, squared)
    return collect_axis(reduced, 1, ELEM, squared)


def per_device(reference_image, deformed_image, roi_mask, displacement, node_map):
    mask_half = roi_mask.astype(jnp.bfloat16)
    stacked = jnp.stack([reference_image, deformed_image])
    padded_images = with_halo(stacked, (("gx", 1), ("gy", 2), ("gz", 3)), 5)
    derived = derive_fields(
        padded_images[0].astype(jnp.float32), padded_images[1].astype(jnp.float32)
    )
    region = with_halo(mask_half, (("gx", 0), ("gy", 1), ("gz", 2)), 2).astype(jnp.float32)
    contrast = derived[0].astype(jnp.float32)
    slopes = derived[1:].astype(jnp.float32)
    masked_slopes = slopes * region[None]
    nodes_shape = (
        3,
        reference_image.shape[0] // ELEM,
        reference_image.shape[1] // ELEM,
        reference_image.shape[2] // ELEM,
    )
    weights_table = axis_table(nodes_shape[3] + 2, ELEM, False)
    table_back = weights_table[1:-1].T
    table_square = axis_table(nodes_shape[3] + 2, ELEM, True)[1:-1].T
    curvature = collect(masked_slopes * slopes, table_square, True) + diagonal_shift
    members = lax.axis_size(("gy", "gz"))
    blocks = node_map.shape[0]
    block_nodes = displacement.shape[2]
    owner_tile = node_map // blocks
    tile_block = node_map % blocks
    position = jnp.arange(blocks, dtype=jnp.int32)
    earlier = (owner_tile[:, None] == owner_tile[None, :]) & (position[None, :] < position[:, None])
    ranking = jnp.sum(earlier.astype(jnp.int32), axis=1)
    target_slot = owner_tile * CAP + ranking
    packing = (target_slot[:, None] == jnp.arange(members * CAP, dtype=jnp.int32)[None, :]).astype(
        jnp.float32
    )
    labels = jnp.dot((tile_block + 1).astype(jnp.float32), packing, precision=highest).reshape(
        1, members * CAP
    )
    current = displacement
    for iteration in range(ITERS):
        send_channels = current.shape[0]
        send_outgoing = jnp.einsum("cjn,jp->cpn", current, packing, precision=highest).reshape(
            send_channels, -1
        )
        send_incoming = lax.all_to_all(
            send_outgoing, ("gy", "gz"), split_axis=1, concat_axis=1, tiled=True
        )
        received_labels = lax.all_to_all(
            labels, ("gy", "gz"), split_axis=1, concat_axis=1, tiled=True
        )
        send_placing = (
            received_labels.reshape(-1)[:, None] == (position + 1).astype(jnp.float32)[None, :]
        ).astype(jnp.float32)
        send_tile_values = jnp.einsum(
            "cpn,pk->ckn",
            send_incoming.reshape(send_channels, members * CAP, -1),
            send_placing,
            precision=highest,
        )
        padded = with_halo(
            send_tile_values.reshape(nodes_shape), (("gx", 1), ("gy", 2), ("gz", 3)), 1
        )
        moved = spread(padded, weights_table)
        residual = contrast + slopes[0] * moved[0] + slopes[1] * moved[1] + slopes[2] * moved[2]
        image_part = collect(masked_slopes * residual[None], table_back, False)
        force_total = image_part + elastic_weight * elastic_force(padded)
        sums = jnp.concatenate([force_total, curvature]).reshape(6, blocks, block_nodes)
        channels = sums.shape[0]
        outgoing = jnp.einsum("ckn,pk->cpn", sums, send_placing, precision=highest).reshape(
            channels, -1
        )
        incoming = lax.all_to_all(outgoing, ("gy", "gz"), split_axis=1, concat_axis=1, tiled=True)
        returned = jnp.einsum(
            "cpn,jp->cjn", incoming.reshape(channels, members * CAP, -1), packing, precision=highest
        )
        current = current - returned[:3] / returned[3:]
    return current


def solution(mesh):
    in_specs = (
        P("gx", "gy", "gz"),
        P("gx", "gy", "gz"),
        P("gx", "gy", "gz"),
        P(None, ("gx", "gy", "gz"), None),
        P(("gx", "gy", "gz")),
    )
    out_specs = P(None, ("gx", "gy", "gz"), None)
    return jax.shard_map(
        per_device, mesh=mesh, in_specs=in_specs, out_specs=out_specs, check_vma=False
    )
```

profile of v0, /device:TPU:1, one launch (start us, length us, event | category | flops | bytes accessed | tf_op | source)
XLA Modules:
  0.0 223.1 jit_solution(1348251170482457069)
XLA Ops:
  0.0 0.7 and_select_fusion.3
  0.8 0.7 multiply_add_fusion.32
  1.5 0.8 convolution_bitcast_fusion.8
  2.4 0.8 all_to_all.31
  3.1 11.6 %all-to-all-start = ((f32[1,64,2]{2,0,1:T(1,128)}), f32[1,64,2]{2,0,1:T(1,128)S(1)}, u32[]{:S(2)}, u32[]{:S(2)}) async-start(f32[1,64,2]{2,0,1:T(1,128)} %bitcast.2), calls=%async_computation | async-start | bytes 65536 | tf_op jit(solution)/shard_map/all_to_all | solution.py:241
  14.8 0.8 pad_maximum_fusion.12
  15.5 4.0 %collective-permute-start = (bf16[2,5,16,128]{3,2,1,0:T(8,128)(2,1)S(1)}, bf16[2,5,16,128]{3,2,1,0:T(8,128)(2,1)S(1)}, u32[]{:S(2)}, u32[]{:S(2)}) collective-permute-start(bf16[2,5,16,128]{3,2,1,0:T(8,128)(2,1)S(1)} %get-tuple-element.88), channel_id=1, source_target_pairs={{0,64},{64,128},{128,192},{192,256},{256,320},{320,384},{384,448},... | collective-permute-start | bytes 122888 | tf_op jit(solution)/shard_map/ppermute | solution.py:24
  19.6 0.9 convert_element_type.84
  20.5 4.0 %collective-permute-start.6 = (bf16[2,16,128]{2,1,0:T(8,128)(2,1)S(1)}, bf16[2,16,128]{2,1,0:T(8,128)(2,1)S(1)}, u32[]{:S(2)}, u32[]{:S(2)}) collective-permute-start(bf16[2,16,128]{2,1,0:T(8,128)(2,1)S(1)} %get-tuple-element.102), channel_id=1, source_target_pairs={{0,64},{64,128},{128,192},{192,256},{256,320},{320,384},{384,448},... | collective-permute-start | bytes 24584 | tf_op jit(solution)/shard_map/ppermute | solution.py:24
  24.5 1.3 collective-permute-start.7
  25.9 0.6 fusion.159
  26.5 0.9 convolution_bitcast_fusion.7
  27.4 0.6 iota_compare_fusion
  28.0 0.6 iota_compare_fusion.1
  28.6 0.6 select_add_fusion
  29.6 3.3 %collective-permute-start.8 = (bf16[20,2,128]{2,1,0:T(2,128)(2,1)S(1)}, bf16[20,2,128]{2,1,0:T(2,128)(2,1)S(1)}, u32[]{:S(2)}, u32[]{:S(2)}) collective-permute-start(bf16[20,2,128]{2,1,0:T(2,128)(2,1)S(1)} %get-tuple-element.92), channel_id=1, source_target_pairs={{0,8},{8,16},{16,24},{24,32},{32,40},{40,48},{48,56},{1,9},{9,17},... | collective-permute-start | bytes 30728 | tf_op jit(solution)/shard_map/ppermute | solution.py:24
  32.9 1.3 collective-permute-start.9
  34.4 0.7 copy.112
  35.1 14.2 %all-to-all-start.1 = ((f32[3,64,16]{2,0,1:T(4,128)}), f32[3,64,16]{2,0,1:T(4,128)S(1)}, u32[]{:S(2)}, u32[]{:S(2)}) async-start(f32[3,64,16]{2,0,1:T(4,128)} %copy.112), calls=%async_computation.1 | async-start | bytes 262144 | tf_op jit(solution)/shard_map/all_to_all | solution.py:238
  49.3 0.6 broadcast.553
  49.9 0.7 reduce.3
  50.9 9.6 %all-to-all-done.1 = f32[3,64,16]{2,0,1:T(4,128)S(1)} async-done(((f32[3,64,16]{2,0,1:T(4,128)}), f32[3,64,16]{2,0,1:T(4,128)S(1)}, u32[]{:S(2)}, u32[]{:S(2)}) %all-to-all-start.1) | async-done | bytes 12320 | tf_op jit(solution)/shard_map/all_to_all | solution.py:238
  61.1 5.2 %collective-permute-start.12 = (f32[3,1,4,32]{3,2,1,0:T(4,128)S(1)}, f32[3,1,4,32]{3,2,1,0:T(4,128)S(1)}, u32[]{:S(2)}, u32[]{:S(2)}) collective-permute-start(f32[3,1,4,32]{3,2,1,0:T(4,128)S(1)} %get-tuple-element.115), channel_id=1, source_target_pairs={{0,64},{64,128},{128,192},{192,256},{256,320},{320,384},{384,448},... | collective-permute-start | bytes 4616 | tf_op jit(solution)/shard_map/ppermute | solution.py:24
  66.5 2.7 %collective-permute-start.10 = (bf16[20,20,2]{2,1,0:T(8,128)(2,1)S(1)}, bf16[20,20,2]{2,1,0:T(8,128)(2,1)S(1)}, u32[]{:S(2)}, u32[]{:S(2)}) collective-permute-start(bf16[20,20,2]{2,1,0:T(8,128)(2,1)S(1)} %get-tuple-element.90), channel_id=1, source_target_pairs={{0,1},{1,2},{2,3},{3,4},{4,5},{5,6},{6,7},{8,9},{9,10},{10,11},{11... | collective-permute-start | bytes 4808 | tf_op jit(solution)/shard_map/ppermute | solution.py:24
  69.1 1.9 collective-permute-start.11
  71.1 1.3 collective-permute-start.13
  72.4 3.3 %collective-permute-done.13 = f32[3,1,4,32]{3,2,1,0:T(4,128)S(1)} collective-permute-done((f32[3,1,4,32]{3,2,1,0:T(4,128)S(1)}, f32[3,1,4,32]{3,2,1,0:T(4,128)S(1)}, u32[]{:S(2)}, u32[]{:S(2)}) %collective-permute-start.13) | collective-permute-done | bytes 1568 | tf_op jit(solution)/shard_map/ppermute | solution.py:27
  75.7 2.6 %collective-permute-start.14 = (f32[3,6,1,32]{3,2,1,0:T(1,128)S(1)}, f32[3,6,1,32]{3,2,1,0:T(1,128)S(1)}, u32[]{:S(2)}, u32[]{:S(2)}) collective-permute-start(f32[3,6,1,32]{3,2,1,0:T(1,128)S(1)} %get-tuple-element.110), channel_id=1, source_target_pairs={{0,8},{8,16},{16,24},{24,32},{32,40},{40,48},{48,56},{1,9},{9,17},... | collective-permute-start | bytes 6920 | tf_op jit(solution)/shard_map/ppermute | solution.py:24
  78.3 1.3 collective-permute-start.15
  79.6 0.6 fusion.164
  80.4 1.3 collective-permute-start.1
  82.8 5.9 %collective-permute-start.16 = (f32[3,6,6,1]{3,2,1,0:T(8,128)S(1)}, f32[3,6,6,1]{3,2,1,0:T(8,128)S(1)}, u32[]{:S(2)}, u32[]{:S(2)}) collective-permute-start(f32[3,6,6,1]{3,2,1,0:T(8,128)S(1)} %get-tuple-element.100), channel_id=1, source_target_pairs={{0,1},{1,2},{2,3},{3,4},{4,5},{5,6},{6,7},{8,9},{9,10},{10,11},{11... | collective-permute-start | bytes 1304 | tf_op jit(solution)/shard_map/ppermute | solution.py:24
  88.8 1.9 collective-permute-start.17
  91.1 3.3 %collective-permute-done.17 = f32[3,6,6,1]{3,2,1,0:T(8,128)S(1)} collective-permute-done((f32[3,6,6,1]{3,2,1,0:T(8,128)S(1)}, f32[3,6,6,1]{3,2,1,0:T(8,128)S(1)}, u32[]{:S(2)}, u32[]{:S(2)}) %collective-permute-start.17) | collective-permute-done | bytes 464 | tf_op jit(solution)/shard_map/ppermute | solution.py:27
  96.7 0.7 fusion.136
  97.5 3.1 %collective-permute-start.2 = (bf16[2,26,5,128]{3,2,1,0:T(8,128)(2,1)S(1)}, bf16[2,26,5,128]{3,2,1,0:T(8,128)(2,1)S(1)}, u32[]{:S(2)}, u32[]{:S(2)}) collective-permute-start(bf16[2,26,5,128]{3,2,1,0:T(8,128)(2,1)S(1)} %get-tuple-element.78), channel_id=1, source_target_pairs={{0,8},{8,16},{16,24},{24,32},{32,40},{40,48},{48,56},{1,9},{9,17},... | collective-permute-start | bytes 199688 | tf_op jit(solution)/shard_map/ppermute | solution.py:24
  100.7 1.3 collective-permute-start.3
  102.3 3.8 %collective-permute-done.3 = bf16[2,26,5,128]{3,2,1,0:T(8,128)(2,1)S(1)} collective-permute-done((bf16[2,26,5,128]{3,2,1,0:T(8,128)(2,1)S(1)}, bf16[2,26,5,128]{3,2,1,0:T(8,128)(2,1)S(1)}, u32[]{:S(2)}, u32[]{:S(2)}) %collective-permute-start.3) | collective-permute-done | bytes 66592 | tf_op jit(solution)/shard_map/ppermute | solution.py:27
  106.3 1.1 fusion.189
  107.4 4.1 %collective-permute-start.4 = (bf16[2,26,26,5]{3,2,1,0:T(8,128)(2,1)}, bf16[2,26,26,5]{3,2,1,0:T(8,128)(2,1)}, u32[]{:S(2)}, u32[]{:S(2)}) collective-permute-start(bf16[2,26,26,5]{3,2,1,0:T(8,128)(2,1)} %get-tuple-element.64), channel_id=1, source_target_pairs={{0,1},{1,2},{2,3},{3,4},{4,5},{5,6},{6,7},{8,9},{9,10},{10,11},{11... | collective-permute-start | bytes 40568 | tf_op jit(solution)/shard_map/ppermute | solution.py:24
  111.5 2.1 collective-permute-start.5
  113.7 0.7 fusion.130
  114.8 2.1 collective-permute-done.4
  116.9 4.4 %collective-permute-done.5 = bf16[2,26,26,5]{3,2,1,0:T(8,128)(2,1)} collective-permute-done((bf16[2,26,26,5]{3,2,1,0:T(8,128)(2,1)}, bf16[2,26,26,5]{3,2,1,0:T(8,128)(2,1)}, u32[]{:S(2)}, u32[]{:S(2)}) %collective-permute-start.5) | collective-permute-done | bytes 13552 | tf_op jit(solution)/shard_map/ppermute | solution.py:27
  121.3 1.9 pad_maximum_fusion
  124.4 1.2 add_multiply_fusion
  127.2 1.1 fusion.35
  128.5 1.4 multiply_reduce_fusion.5
  130.3 1.4 multiply_reduce_fusion.3
  132.9 18.6 %all_to_all.46 = f32[6,64,16]{2,0,1:T(8,128)S(1)} all-to-all(f32[6,64,16]{2,0,1:T(8,128)S(1)} %copy.121), channel_id=1, replica_groups=mesh['gx'=8,'gy'=8,'gz'=8] {'gy','gz'}, dimensions={1} | all-to-all | bytes 49152 | tf_op jit(solution)/shard_map/all_to_all | solution.py:265
  152.7 15.6 %all_to_all.47 = f32[3,64,16]{2,0,1:T(4,128)S(1)} all-to-all(f32[3,64,16]{2,0,1:T(4,128)S(1)} %copy.125), channel_id=1, replica_groups=mesh['gx'=8,'gy'=8,'gz'=8] {'gy','gz'}, dimensions={1} | all-to-all | bytes 24576 | tf_op jit(solution)/shard_map/all_to_all | solution.py:238
  169.0 5.2 %collective-permute-start.18 = (f32[3,1,4,32]{3,2,1,0:T(4,128)S(1)}, f32[3,1,4,32]{3,2,1,0:T(4,128)S(1)}, u32[]{:S(2)}, u32[]{:S(2)}) collective-permute-start(f32[3,1,4,32]{3,2,1,0:T(4,128)S(1)} %get-tuple-element.113), channel_id=1, source_target_pairs={{0,64},{64,128},{128,192},{192,256},{256,320},{320,384},{384,448},... | collective-permute-start | bytes 4616 | tf_op jit(solution)/shard_map/ppermute | solution.py:24
  174.1 1.3 collective-permute-start.19
  175.5 3.3 %collective-permute-done.19 = f32[3,1,4,32]{3,2,1,0:T(4,128)S(1)} collective-permute-done((f32[3,1,4,32]{3,2,1,0:T(4,128)S(1)}, f32[3,1,4,32]{3,2,1,0:T(4,128)S(1)}, u32[]{:S(2)}, u32[]{:S(2)}) %collective-permute-start.19) | collective-permute-done | bytes 1568 | tf_op jit(solution)/shard_map/ppermute | solution.py:27
  178.8 2.3 %collective-permute-start.20 = (f32[3,6,1,32]{3,2,1,0:T(1,128)S(1)}, f32[3,6,1,32]{3,2,1,0:T(1,128)S(1)}, u32[]{:S(2)}, u32[]{:S(2)}) collective-permute-start(f32[3,6,1,32]{3,2,1,0:T(1,128)S(1)} %get-tuple-element.108), channel_id=1, source_target_pairs={{0,8},{8,16},{16,24},{24,32},{32,40},{40,48},{48,56},{1,9},{9,17},... | collective-permute-start | bytes 6920 | tf_op jit(solution)/shard_map/ppermute | solution.py:24
  181.1 1.3 collective-permute-start.21
  182.4 3.1 %collective-permute-done.21 = f32[3,6,1,32]{3,2,1,0:T(1,128)S(1)} collective-permute-done((f32[3,6,1,32]{3,2,1,0:T(1,128)S(1)}, f32[3,6,1,32]{3,2,1,0:T(1,128)S(1)}, u32[]{:S(2)}, u32[]{:S(2)}) %collective-permute-start.21) | collective-permute-done | bytes 2336 | tf_op jit(solution)/shard_map/ppermute | solution.py:27
  185.7 5.2 %collective-permute-start.22 = (f32[3,6,6,1]{3,2,1,0:T(8,128)S(1)}, f32[3,6,6,1]{3,2,1,0:T(8,128)S(1)}, u32[]{:S(2)}, u32[]{:S(2)}) collective-permute-start(f32[3,6,6,1]{3,2,1,0:T(8,128)S(1)} %get-tuple-element.96), channel_id=1, source_target_pairs={{0,1},{1,2},{2,3},{3,4},{4,5},{5,6},{6,7},{8,9},{9,10},{10,11},{11... | collective-permute-start | bytes 1304 | tf_op jit(solution)/shard_map/ppermute | solution.py:24
  190.9 1.9 collective-permute-start.23
  192.8 3.7 %collective-permute-done.23 = f32[3,6,6,1]{3,2,1,0:T(8,128)S(1)} collective-permute-done((f32[3,6,6,1]{3,2,1,0:T(8,128)S(1)}, f32[3,6,6,1]{3,2,1,0:T(8,128)S(1)}, u32[]{:S(2)}, u32[]{:S(2)}) %collective-permute-start.23) | collective-permute-done | bytes 464 | tf_op jit(solution)/shard_map/ppermute | solution.py:27
  199.4 1.2 fusion.37
  200.9 1.4 multiply_reduce_fusion.1
  203.6 18.3 %all_to_all.48 = f32[6,64,16]{2,0,1:T(8,128)S(1)} all-to-all(f32[6,64,16]{2,0,1:T(8,128)S(1)} %copy.133), channel_id=1, replica_groups=mesh['gx'=8,'gy'=8,'gz'=8] {'gy','gz'}, dimensions={1} | all-to-all | bytes 49152 | tf_op jit(solution)/shard_map/all_to_all | solution.py:265
  222.5 0.6 fusion.103
  (302 shorter events, 16.9 us)
Async XLA Ops:
  1.5 32.7 %copy-start.42 = (s32[64]{0:T(128)}, s32[64]{0:T(128)S(1)}, u32[]{:S(2)}) copy-start(s32[64]{0:T(128)S(1)} %multiply_add_fusion.32) | copy-start | bytes 772
  3.1 32.0 %all-to-all-start = ((f32[1,64,2]{2,0,1:T(1,128)}), f32[1,64,2]{2,0,1:T(1,128)S(1)}, u32[]{:S(2)}, u32[]{:S(2)}) async-start(f32[1,64,2]{2,0,1:T(1,128)} %bitcast.2), calls=%async_computation | async-start | bytes 65536 | tf_op jit(solution)/shard_map/all_to_all | solution.py:241
  15.5 81.8 %collective-permute-start = (bf16[2,5,16,128]{3,2,1,0:T(8,128)(2,1)S(1)}, bf16[2,5,16,128]{3,2,1,0:T(8,128)(2,1)S(1)}, u32[]{:S(2)}, u32[]{:S(2)}) collective-permute-start(bf16[2,5,16,128]{3,2,1,0:T(8,128)(2,1)S(1)} %get-tuple-element.88), channel_id=1, source_target_pairs={{0,64},{64,128},{128,192},{192,256},{256,320},{320,384},{384,448},... | collective-permute-start | bytes 122888 | tf_op jit(solution)/shard_map/ppermute | solution.py:24
  20.5 8.7 %collective-permute-start.6 = (bf16[2,16,128]{2,1,0:T(8,128)(2,1)S(1)}, bf16[2,16,128]{2,1,0:T(8,128)(2,1)S(1)}, u32[]{:S(2)}, u32[]{:S(2)}) collective-permute-start(bf16[2,16,128]{2,1,0:T(8,128)(2,1)S(1)} %get-tuple-element.102), channel_id=1, source_target_pairs={{0,64},{64,128},{128,192},{192,256},{256,320},{320,384},{384,448},... | collective-permute-start | bytes 24584 | tf_op jit(solution)/shard_map/ppermute | solution.py:24
  24.5 5.0 %collective-permute-start.7 = (bf16[2,16,128]{2,1,0:T(8,128)(2,1)S(1)}, bf16[2,16,128]{2,1,0:T(8,128)(2,1)S(1)}, u32[]{:S(2)}, u32[]{:S(2)}) collective-permute-start(bf16[2,16,128]{2,1,0:T(8,128)(2,1)S(1)} %get-tuple-element.103), channel_id=1, source_target_pairs={{64,0},{128,64},{192,128},{256,192},{320,256},{384,320},{448,384},... | collective-permute-start | bytes 24584 | tf_op jit(solution)/shard_map/ppermute | solution.py:27
  25.8 68.8 %copy-start.17 = (s32[132]{0:T(256)}, s32[132]{0:T(256)S(1)}, u32[]{:S(2)}) copy-start(s32[132]{0:T(256)S(1)} %get-tuple-element.118) | copy-start | bytes 1588
  25.8 68.8 %copy-start.19 = (s32[132]{0:T(256)}, s32[132]{0:T(256)S(1)}, u32[]{:S(2)}) copy-start(s32[132]{0:T(256)S(1)} %get-tuple-element.119) | copy-start | bytes 1588
  25.8 68.8 %copy-start.21 = (f32[132]{0:T(256)}, f32[132]{0:T(256)S(1)}, u32[]{:S(2)}) copy-start(f32[132]{0:T(256)S(1)} %get-tuple-element.120) | copy-start | bytes 1588
  25.8 68.8 %copy-start.23 = (f32[132]{0:T(256)}, f32[132]{0:T(256)S(1)}, u32[]{:S(2)}) copy-start(f32[132]{0:T(256)S(1)} %get-tuple-element.121) | copy-start | bytes 1588
  29.2 66.7 %copy-start.25 = (f32[4]{0:T(128)}, f32[4]{0:T(128)S(1)}, u32[]{:S(2)}) copy-start(f32[4]{0:T(128)S(1)} %get-tuple-element.122) | copy-start | bytes 52
  29.2 66.7 %copy-start.27 = (f32[4]{0:T(128)}, f32[4]{0:T(128)S(1)}, u32[]{:S(2)}) copy-start(f32[4]{0:T(128)S(1)} %get-tuple-element.123) | copy-start | bytes 52
  29.6 21.2 %collective-permute-start.8 = (bf16[20,2,128]{2,1,0:T(2,128)(2,1)S(1)}, bf16[20,2,128]{2,1,0:T(2,128)(2,1)S(1)}, u32[]{:S(2)}, u32[]{:S(2)}) collective-permute-start(bf16[20,2,128]{2,1,0:T(2,128)(2,1)S(1)} %get-tuple-element.92), channel_id=1, source_target_pairs={{0,8},{8,16},{16,24},{24,32},{32,40},{40,48},{48,56},{1,9},{9,17},... | collective-permute-start | bytes 30728 | tf_op jit(solution)/shard_map/ppermute | solution.py:24
  32.9 17.9 %collective-permute-start.9 = (bf16[20,2,128]{2,1,0:T(2,128)(2,1)S(1)}, bf16[20,2,128]{2,1,0:T(2,128)(2,1)S(1)}, u32[]{:S(2)}, u32[]{:S(2)}) collective-permute-start(bf16[20,2,128]{2,1,0:T(2,128)(2,1)S(1)} %get-tuple-element.93), channel_id=1, source_target_pairs={{8,0},{16,8},{24,16},{32,24},{40,32},{48,40},{56,48},{9,1},{17,9},... | collective-permute-start | bytes 30728 | tf_op jit(solution)/shard_map/ppermute | solution.py:27
  34.2 32.3 %copy-start.44 = (f32[64]{0:T(128)}, f32[64]{0:T(128)S(1)}, u32[]{:S(2)}) copy-start(f32[64]{0:T(128)S(1)} %add_convert_fusion) | copy-start | bytes 772
  35.1 25.3 %all-to-all-start.1 = ((f32[3,64,16]{2,0,1:T(4,128)}), f32[3,64,16]{2,0,1:T(4,128)S(1)}, u32[]{:S(2)}, u32[]{:S(2)}) async-start(f32[3,64,16]{2,0,1:T(4,128)} %copy.112), calls=%async_computation.1 | async-start | bytes 262144 | tf_op jit(solution)/shard_map/all_to_all | solution.py:238
  50.8 15.7 %copy-start.38 = (f32[128]{0:T(128)}, f32[128]{0:T(128)S(1)}, u32[]{:S(2)}) copy-start(f32[128]{0:T(128)S(1)} %eq.137) | copy-start | bytes 1540
  61.1 11.2 %collective-permute-start.12 = (f32[3,1,4,32]{3,2,1,0:T(4,128)S(1)}, f32[3,1,4,32]{3,2,1,0:T(4,128)S(1)}, u32[]{:S(2)}, u32[]{:S(2)}) collective-permute-start(f32[3,1,4,32]{3,2,1,0:T(4,128)S(1)} %get-tuple-element.115), channel_id=1, source_target_pairs={{0,64},{64,128},{128,192},{192,256},{256,320},{320,384},{384,448},... | collective-permute-start | bytes 4616 | tf_op jit(solution)/shard_map/ppermute | solution.py:24
  66.5 13.9 %collective-permute-start.10 = (bf16[20,20,2]{2,1,0:T(8,128)(2,1)S(1)}, bf16[20,20,2]{2,1,0:T(8,128)(2,1)S(1)}, u32[]{:S(2)}, u32[]{:S(2)}) collective-permute-start(bf16[20,20,2]{2,1,0:T(8,128)(2,1)S(1)} %get-tuple-element.90), channel_id=1, source_target_pairs={{0,1},{1,2},{2,3},{3,4},{4,5},{5,6},{6,7},{8,9},{9,10},{10,11},{11... | collective-permute-start | bytes 4808 | tf_op jit(solution)/shard_map/ppermute | solution.py:24
  69.1 13.1 %collective-permute-start.11 = (bf16[20,20,2]{2,1,0:T(8,128)(2,1)S(1)}, bf16[20,20,2]{2,1,0:T(8,128)(2,1)S(1)}, u32[]{:S(2)}, u32[]{:S(2)}) collective-permute-start(bf16[20,20,2]{2,1,0:T(8,128)(2,1)S(1)} %get-tuple-element.91), channel_id=1, source_target_pairs={{1,0},{2,1},{3,2},{4,3},{5,4},{6,5},{7,6},{9,8},{10,9},{11,10},{12... | collective-permute-start | bytes 4808 | tf_op jit(solution)/shard_map/ppermute | solution.py:27
  71.1 4.7 %collective-permute-start.13 = (f32[3,1,4,32]{3,2,1,0:T(4,128)S(1)}, f32[3,1,4,32]{3,2,1,0:T(4,128)S(1)}, u32[]{:S(2)}, u32[]{:S(2)}) collective-permute-start(f32[3,1,4,32]{3,2,1,0:T(4,128)S(1)} %get-tuple-element.114), channel_id=1, source_target_pairs={{64,0},{128,64},{192,128},{256,192},{320,256},{384,320},{448,384},... | collective-permute-start | bytes 4616 | tf_op jit(solution)/shard_map/ppermute | solution.py:27
  75.7 7.0 %collective-permute-start.14 = (f32[3,6,1,32]{3,2,1,0:T(1,128)S(1)}, f32[3,6,1,32]{3,2,1,0:T(1,128)S(1)}, u32[]{:S(2)}, u32[]{:S(2)}) collective-permute-start(f32[3,6,1,32]{3,2,1,0:T(1,128)S(1)} %get-tuple-element.110), channel_id=1, source_target_pairs={{0,8},{8,16},{16,24},{24,32},{32,40},{40,48},{48,56},{1,9},{9,17},... | collective-permute-start | bytes 6920 | tf_op jit(solution)/shard_map/ppermute | solution.py:24
  78.3 4.4 %collective-permute-start.15 = (f32[3,6,1,32]{3,2,1,0:T(1,128)S(1)}, f32[3,6,1,32]{3,2,1,0:T(1,128)S(1)}, u32[]{:S(2)}, u32[]{:S(2)}) collective-permute-start(f32[3,6,1,32]{3,2,1,0:T(1,128)S(1)} %get-tuple-element.111), channel_id=1, source_target_pairs={{8,0},{16,8},{24,16},{32,24},{40,32},{48,40},{56,48},{9,1},{17,9},... | collective-permute-start | bytes 6920 | tf_op jit(solution)/shard_map/ppermute | solution.py:27
  80.2 15.5 %copy-start.32 = (f32[20]{0:T(128)}, f32[20]{0:T(128)S(1)}, u32[]{:S(2)}) copy-start(f32[20]{0:T(128)S(1)} %mul.966) | copy-start | bytes 244
  80.3 15.4 %copy-start.34 = (f32[20]{0:T(128)}, f32[20]{0:T(128)S(1)}, u32[]{:S(2)}) copy-start(f32[20]{0:T(128)S(1)} %mul.972) | copy-start | bytes 244
  80.4 17.0 %collective-permute-start.1 = (bf16[2,5,16,128]{3,2,1,0:T(8,128)(2,1)S(1)}, bf16[2,5,16,128]{3,2,1,0:T(8,128)(2,1)S(1)}, u32[]{:S(2)}, u32[]{:S(2)}) collective-permute-start(bf16[2,5,16,128]{3,2,1,0:T(8,128)(2,1)S(1)} %get-tuple-element.89), channel_id=1, source_target_pairs={{64,0},{128,64},{192,128},{256,192},{320,256},{384,320},{448,384},... | collective-permute-start | bytes 122888 | tf_op jit(solution)/shard_map/ppermute | solution.py:27
  82.8 8.2 %collective-permute-start.16 = (f32[3,6,6,1]{3,2,1,0:T(8,128)S(1)}, f32[3,6,6,1]{3,2,1,0:T(8,128)S(1)}, u32[]{:S(2)}, u32[]{:S(2)}) collective-permute-start(f32[3,6,6,1]{3,2,1,0:T(8,128)S(1)} %get-tuple-element.100), channel_id=1, source_target_pairs={{0,1},{1,2},{2,3},{3,4},{4,5},{5,6},{6,7},{8,9},{9,10},{10,11},{11... | collective-permute-start | bytes 1304 | tf_op jit(solution)/shard_map/ppermute | solution.py:24
  88.8 5.7 %collective-permute-start.17 = (f32[3,6,6,1]{3,2,1,0:T(8,128)S(1)}, f32[3,6,6,1]{3,2,1,0:T(8,128)S(1)}, u32[]{:S(2)}, u32[]{:S(2)}) collective-permute-start(f32[3,6,6,1]{3,2,1,0:T(8,128)S(1)} %get-tuple-element.101), channel_id=1, source_target_pairs={{1,0},{2,1},{3,2},{4,3},{5,4},{6,5},{7,6},{9,8},{10,9},{11,10},{12... | collective-permute-start | bytes 1304 | tf_op jit(solution)/shard_map/ppermute | solution.py:27
  91.1 39.1 %copy-start.2 = (f32[20,5,4,132]{3,0,2,1:T(8,128)}, f32[20,5,4,132]{3,0,2,1:T(8,128)S(1)}, u32[]{:S(2)}) copy-start(f32[20,5,4,132]{3,0,2,1:T(8,128)S(1)} %copy.110) | copy-start | bytes 633604
  97.4 10.0 %copy-start.4 = (bf16[2,5,16,128]{3,2,1,0:T(8,128)(2,1)}, bf16[2,5,16,128]{3,2,1,0:T(8,128)(2,1)S(1)}, u32[]{:S(2)}) copy-start(bf16[2,5,16,128]{3,2,1,0:T(8,128)(2,1)S(1)} %collective-permute-done) | copy-start | bytes 122884
  97.4 10.0 %copy-start.6 = (bf16[2,5,16,128]{3,2,1,0:T(8,128)(2,1)}, bf16[2,5,16,128]{3,2,1,0:T(8,128)(2,1)S(1)}, u32[]{:S(2)}) copy-start(bf16[2,5,16,128]{3,2,1,0:T(8,128)(2,1)S(1)} %collective-permute-done.1) | copy-start | bytes 122884
  97.5 4.8 %collective-permute-start.2 = (bf16[2,26,5,128]{3,2,1,0:T(8,128)(2,1)S(1)}, bf16[2,26,5,128]{3,2,1,0:T(8,128)(2,1)S(1)}, u32[]{:S(2)}, u32[]{:S(2)}) collective-permute-start(bf16[2,26,5,128]{3,2,1,0:T(8,128)(2,1)S(1)} %get-tuple-element.78), channel_id=1, source_target_pairs={{0,8},{8,16},{16,24},{24,32},{32,40},{40,48},{48,56},{1,9},{9,17},... | collective-permute-start | bytes 199688 | tf_op jit(solution)/shard_map/ppermute | solution.py:24
  100.7 5.4 %collective-permute-start.3 = (bf16[2,26,5,128]{3,2,1,0:T(8,128)(2,1)S(1)}, bf16[2,26,5,128]{3,2,1,0:T(8,128)(2,1)S(1)}, u32[]{:S(2)}, u32[]{:S(2)}) collective-permute-start(bf16[2,26,5,128]{3,2,1,0:T(8,128)(2,1)S(1)} %get-tuple-element.79), channel_id=1, source_target_pairs={{8,0},{16,8},{24,16},{32,24},{40,32},{48,40},{56,48},{9,1},{17,9},... | collective-permute-start | bytes 199688 | tf_op jit(solution)/shard_map/ppermute | solution.py:27
  107.4 9.5 %collective-permute-start.4 = (bf16[2,26,26,5]{3,2,1,0:T(8,128)(2,1)}, bf16[2,26,26,5]{3,2,1,0:T(8,128)(2,1)}, u32[]{:S(2)}, u32[]{:S(2)}) collective-permute-start(bf16[2,26,26,5]{3,2,1,0:T(8,128)(2,1)} %get-tuple-element.64), channel_id=1, source_target_pairs={{0,1},{1,2},{2,3},{3,4},{4,5},{5,6},{6,7},{8,9},{9,10},{10,11},{11... | collective-permute-start | bytes 40568 | tf_op jit(solution)/shard_map/ppermute | solution.py:24
  111.5 9.8 %collective-permute-start.5 = (bf16[2,26,26,5]{3,2,1,0:T(8,128)(2,1)}, bf16[2,26,26,5]{3,2,1,0:T(8,128)(2,1)}, u32[]{:S(2)}, u32[]{:S(2)}) collective-permute-start(bf16[2,26,26,5]{3,2,1,0:T(8,128)(2,1)} %get-tuple-element.65), channel_id=1, source_target_pairs={{1,0},{2,1},{3,2},{4,3},{5,4},{6,5},{7,6},{9,8},{10,9},{11,10},{12... | collective-permute-start | bytes 40568 | tf_op jit(solution)/shard_map/ppermute | solution.py:27
  114.5 6.8 %copy-start.5 = (bf16[2,5,16,128]{3,2,1,0:T(8,128)(2,1)S(1)}, bf16[2,5,16,128]{3,2,1,0:T(8,128)(2,1)}, u32[]{:S(2)}) copy-start(bf16[2,5,16,128]{3,2,1,0:T(8,128)(2,1)} %copy-done.4) | copy-start | bytes 122884
  114.5 6.8 %copy-start.7 = (bf16[2,5,16,128]{3,2,1,0:T(8,128)(2,1)S(1)}, bf16[2,5,16,128]{3,2,1,0:T(8,128)(2,1)}, u32[]{:S(2)}) copy-start(bf16[2,5,16,128]{3,2,1,0:T(8,128)(2,1)} %copy-done.6) | copy-start | bytes 122884
  126.4 3.8 %copy-start.8 = (bf16[20,20,132]{2,0,1:T(8,128)(2,1)}, bf16[20,20,132]{2,0,1:T(8,128)(2,1)S(1)}, u32[]{:S(2)}) copy-start(bf16[20,20,132]{2,0,1:T(8,128)(2,1)S(1)} %copy.139) | copy-start | bytes 316804
  126.8 3.4 %copy-start.10 = (bf16[20,20,132]{2,0,1:T(8,128)(2,1)}, bf16[20,20,132]{2,0,1:T(8,128)(2,1)S(1)}, u32[]{:S(2)}) copy-start(bf16[20,20,132]{2,0,1:T(8,128)(2,1)S(1)} %copy.140) | copy-start | bytes 316804
  127.0 3.2 %copy-start.12 = (bf16[20,20,132]{2,0,1:T(8,128)(2,1)}, bf16[20,20,132]{2,0,1:T(8,128)(2,1)S(1)}, u32[]{:S(2)}) copy-start(bf16[20,20,132]{2,0,1:T(8,128)(2,1)S(1)} %copy.141) | copy-start | bytes 316804
  127.2 1.2 copy-start.14
  128.5 1.7 copy-start.30
  128.5 1.7 copy-start.31
  128.5 1.7 copy-start.36
  128.5 1.7 copy-start.37
  128.5 1.7 copy-start.40
  128.5 1.7 copy-start.41
  130.2 1.7 copy-start.15
  130.3 1.7 copy-start.16
  132.7 19.2 %copy-start.43 = (s32[64]{0:T(128)S(1)}, s32[64]{0:T(128)}, u32[]{:S(2)}) copy-start(s32[64]{0:T(128)} %copy-done.42) | copy-start | bytes 772
  132.7 19.4 %copy-start.29 = (f32[3,64,8]{1,2,0:T(8,128)S(1)}, f32[3,64,8]{1,2,0:T(8,128)}, u32[]{:S(2)}) copy-start(f32[3,64,8]{1,2,0:T(8,128)} %param.8) | copy-start | bytes 18436
  152.5 44.2 %copy-start.18 = (s32[132]{0:T(256)S(1)}, s32[132]{0:T(256)}, u32[]{:S(2)}) copy-start(s32[132]{0:T(256)} %copy-done.17) | copy-start | bytes 1588
  152.5 44.2 %copy-start.20 = (s32[132]{0:T(256)S(1)}, s32[132]{0:T(256)}, u32[]{:S(2)}) copy-start(s32[132]{0:T(256)} %copy-done.19) | copy-start | bytes 1588
  152.5 44.2 %copy-start.22 = (f32[132]{0:T(256)S(1)}, f32[132]{0:T(256)}, u32[]{:S(2)}) copy-start(f32[132]{0:T(256)} %copy-done.21) | copy-start | bytes 1588
  152.5 44.2 %copy-start.24 = (f32[132]{0:T(256)S(1)}, f32[132]{0:T(256)}, u32[]{:S(2)}) copy-start(f32[132]{0:T(256)} %copy-done.23) | copy-start | bytes 1588
  169.0 6.5 %collective-permute-start.18 = (f32[3,1,4,32]{3,2,1,0:T(4,128)S(1)}, f32[3,1,4,32]{3,2,1,0:T(4,128)S(1)}, u32[]{:S(2)}, u32[]{:S(2)}) collective-permute-start(f32[3,1,4,32]{3,2,1,0:T(4,128)S(1)} %get-tuple-element.113), channel_id=1, source_target_pairs={{0,64},{64,128},{128,192},{192,256},{256,320},{320,384},{384,448},... | collective-permute-start | bytes 4616 | tf_op jit(solution)/shard_map/ppermute | solution.py:24
  174.1 4.7 %collective-permute-start.19 = (f32[3,1,4,32]{3,2,1,0:T(4,128)S(1)}, f32[3,1,4,32]{3,2,1,0:T(4,128)S(1)}, u32[]{:S(2)}, u32[]{:S(2)}) collective-permute-start(f32[3,1,4,32]{3,2,1,0:T(4,128)S(1)} %get-tuple-element.112), channel_id=1, source_target_pairs={{64,0},{128,64},{192,128},{256,192},{320,256},{384,320},{448,384},... | collective-permute-start | bytes 4616 | tf_op jit(solution)/shard_map/ppermute | solution.py:27
  178.8 3.6 %collective-permute-start.20 = (f32[3,6,1,32]{3,2,1,0:T(1,128)S(1)}, f32[3,6,1,32]{3,2,1,0:T(1,128)S(1)}, u32[]{:S(2)}, u32[]{:S(2)}) collective-permute-start(f32[3,6,1,32]{3,2,1,0:T(1,128)S(1)} %get-tuple-element.108), channel_id=1, source_target_pairs={{0,8},{8,16},{16,24},{24,32},{32,40},{40,48},{48,56},{1,9},{9,17},... | collective-permute-start | bytes 6920 | tf_op jit(solution)/shard_map/ppermute | solution.py:24
  181.1 4.4 %collective-permute-start.21 = (f32[3,6,1,32]{3,2,1,0:T(1,128)S(1)}, f32[3,6,1,32]{3,2,1,0:T(1,128)S(1)}, u32[]{:S(2)}, u32[]{:S(2)}) collective-permute-start(f32[3,6,1,32]{3,2,1,0:T(1,128)S(1)} %get-tuple-element.109), channel_id=1, source_target_pairs={{8,0},{16,8},{24,16},{32,24},{40,32},{48,40},{56,48},{9,1},{17,9},... | collective-permute-start | bytes 6920 | tf_op jit(solution)/shard_map/ppermute | solution.py:27
  185.7 7.1 %collective-permute-start.22 = (f32[3,6,6,1]{3,2,1,0:T(8,128)S(1)}, f32[3,6,6,1]{3,2,1,0:T(8,128)S(1)}, u32[]{:S(2)}, u32[]{:S(2)}) collective-permute-start(f32[3,6,6,1]{3,2,1,0:T(8,128)S(1)} %get-tuple-element.96), channel_id=1, source_target_pairs={{0,1},{1,2},{2,3},{3,4},{4,5},{5,6},{6,7},{8,9},{9,10},{10,11},{11... | collective-permute-start | bytes 1304 | tf_op jit(solution)/shard_map/ppermute | solution.py:24
  190.9 5.7 %collective-permute-start.23 = (f32[3,6,6,1]{3,2,1,0:T(8,128)S(1)}, f32[3,6,6,1]{3,2,1,0:T(8,128)S(1)}, u32[]{:S(2)}, u32[]{:S(2)}) collective-permute-start(f32[3,6,6,1]{3,2,1,0:T(8,128)S(1)} %get-tuple-element.97), channel_id=1, source_target_pairs={{1,0},{2,1},{3,2},{4,3},{5,4},{6,5},{7,6},{9,8},{10,9},{11,10},{12... | collective-permute-start | bytes 1304 | tf_op jit(solution)/shard_map/ppermute | solution.py:27
  199.4 1.4 copy-start.3
  199.4 1.4 copy-start.9
  199.4 1.4 copy-start.11
  199.4 1.4 copy-start.13
  (9 other events, 7.9 us)
where the time goes:
time: 226 us; the launch traced here: 223 us
  starting transfers between devices  91.6 us (41%)
  blocking collectives  52.5 us (23%)
  waiting for transfers between devices  37.4 us (17%)
  other arithmetic  20.4 us (9%)
  local copies, waits for them, and re-layouts  11 us (5%)
  matrix products  8 us (4%)
    ppermute x12, starting transfers between devices, with_halo(): lax.ppermute(lax.slice_in_dim(block, block.shape[dim] - width, None, axis...  47.6 us
    all_to_all x2, blocking collectives, per_device(): lax.all_to_all(outgoing, ('gy', 'gz'), split_axis=1, concat_axis=1, tiled...  36.9 us
    ppermute x12, waiting for transfers between devices, with_halo(): lax.ppermute(lax.slice_in_dim(block, 0, width, axis=dim), axis, backward)  25.3 us
    ppermute x12, starting transfers between devices, with_halo(): lax.ppermute(lax.slice_in_dim(block, 0, width, axis=dim), axis, backward)  18.2 us
    all_to_all x1, blocking collectives, per_device(): lax.all_to_all(send_outgoing, ('gy', 'gz'), split_axis=1, concat_axis=1,...  15.6 us
    all_to_all x1, starting transfers between devices, per_device(): lax.all_to_all(send_outgoing, ('gy', 'gz'), split_axis=1, concat_axis=1,...  14.2 us
    all_to_all x1, starting transfers between devices, per_device(): lax.all_to_all(labels, ('gy', 'gz'), split_axis=1, concat_axis=1, tiled=T...  11.6 us
    all_to_all x1, waiting for transfers between devices, per_device(): lax.all_to_all(send_outgoing, ('gy', 'gz'), split_axis=1, concat_axis=1,...  9.59 us
  transfers between devices with their start and end apart: 26, of which 11 were waited for; matrix products, arithmetic and copies ran while one was open for 6% of the time, Pallas kernels for 0%

commit v1 on v0

--- a/solution.py
+++ b/solution.py
@@ -195,12 +195,12 @@
 
 def per_device(reference_image, deformed_image, roi_mask, displacement, node_map):
     mask_half = roi_mask.astype(jnp.bfloat16)
-    stacked = jnp.stack([reference_image, deformed_image])
+    stacked = jnp.stack([reference_image, deformed_image, mask_half])
     padded_images = with_halo(stacked, (("gx", 1), ("gy", 2), ("gz", 3)), 5)
     derived = derive_fields(
         padded_images[0].astype(jnp.float32), padded_images[1].astype(jnp.float32)
     )
-    region = with_halo(mask_half, (("gx", 0), ("gy", 1), ("gz", 2)), 2).astype(jnp.float32)
+    region = padded_images[2][3:-3, 3:-3, 3:-3].astype(jnp.float32)
     contrast = derived[0].astype(jnp.float32)
     slopes = derived[1:].astype(jnp.float32)
     masked_slopes = slopes * region[None]
@@ -226,48 +226,43 @@
     packing = (target_slot[:, None] == jnp.arange(members * CAP, dtype=jnp.int32)[None, :]).astype(
         jnp.float32
     )
-    labels = jnp.dot((tile_block + 1).astype(jnp.float32), packing, precision=highest).reshape(
-        1, members * CAP
-    )
-    current = displacement
+    labelled = jnp.concatenate(
+        [
+            displacement,
+            jnp.broadcast_to(
+                (tile_block + 1).astype(jnp.float32)[None, :, None], (1, blocks, block_nodes)
+            ),
+        ]
+    )
+    send_channels = labelled.shape[0]
+    send_outgoing = jnp.einsum("cjn,jp->cpn", labelled, packing, precision=highest).reshape(
+        send_channels, -1
+    )
+    send_incoming = lax.all_to_all(
+        send_outgoing, ("gy", "gz"), split_axis=1, concat_axis=1, tiled=True
+    ).reshape(send_channels, members * CAP, block_nodes)
+    received_labels = send_incoming[3, :, 0]
+    send_placing = (
+        received_labels[:, None] == (position + 1).astype(jnp.float32)[None, :]
+    ).astype(jnp.float32)
+    tile_values = jnp.einsum(
+        "cpn,pk->ckn", send_incoming[:3], send_placing, precision=highest
+    ).reshape(nodes_shape)
     for iteration in range(ITERS):
-        send_channels = current.shape[0]
-        send_outgoing = jnp.einsum("cjn,jp->cpn", current, packing, precision=highest).reshape(
-            send_channels, -1
-        )
-        send_incoming = lax.all_to_all(
-            send_outgoing, ("gy", "gz"), split_axis=1, concat_axis=1, tiled=True
-        )
-        received_labels = lax.all_to_all(
-            labels, ("gy", "gz"), split_axis=1, concat_axis=1, tiled=True
-        )
-        send_placing = (
-            received_labels.reshape(-1)[:, None] == (position + 1).astype(jnp.float32)[None, :]
-        ).astype(jnp.float32)
-        send_tile_values = jnp.einsum(
-            "cpn,pk->ckn",
-            send_incoming.reshape(send_channels, members * CAP, -1),
-            send_placing,
-            precision=highest,
-        )
-        padded = with_halo(
-            send_tile_values.reshape(nodes_shape), (("gx", 1), ("gy", 2), ("gz", 3)), 1
-        )
+        padded = with_halo(tile_values, (("gx", 1), ("gy", 2), ("gz", 3)), 1)
         moved = spread(padded, weights_table)
         residual = contrast + slopes[0] * moved[0] + slopes[1] * moved[1] + slopes[2] * moved[2]
         image_part = collect(masked_slopes * residual[None], table_back, False)
         force_total = image_part + elastic_weight * elastic_force(padded)
-        sums = jnp.concatenate([force_total, curvature]).reshape(6, blocks, block_nodes)
-        channels = sums.shape[0]
-        outgoing = jnp.einsum("ckn,pk->cpn", sums, send_placing, precision=highest).reshape(
-            channels, -1
-        )
-        incoming = lax.all_to_all(outgoing, ("gy", "gz"), split_axis=1, concat_axis=1, tiled=True)
-        returned = jnp.einsum(
-            "cpn,jp->cjn", incoming.reshape(channels, members * CAP, -1), packing, precision=highest
-        )
-        current = current - returned[:3] / returned[3:]
-    return current
+        tile_values = tile_values - force_total / curvature
+    final_blocks = tile_values.reshape(3, blocks, block_nodes)
+    outgoing = jnp.einsum("ckn,pk->cpn", final_blocks, send_placing, precision=highest).reshape(
+        3, -1
+    )
+    incoming = lax.all_to_all(outgoing, ("gy", "gz"), split_axis=1, concat_axis=1, tiled=True)
+    return jnp.einsum(
+        "cpn,jp->cjn", incoming.reshape(3, members * CAP, -1), packing, precision=highest
+    )
 
 
 def solution(mesh):

time: 226 us -> 159 us (0.70)
  starting transfers between devices: 91.6 us -> 64.5 us
  blocking collectives: 52.5 us -> 25.8 us
  waiting for transfers between devices: 37.4 us -> 14 us
  local copies, waits for them, and re-layouts: 11 us -> 20.3 us
  other arithmetic: 20.4 us -> 23.9 us
    ppermute x12 -> x9, waiting for transfers between devices: 25.3 us -> 5.72 us  [with_halo(): lax.ppermute(lax.slice_in_dim(block, 0, width, axis=dim), axis, backward)]
    all_to_all x1 -> x0, blocking collectives: 15.6 us -> none  [per_device(): lax.all_to_all(send_outgoing, ('gy', 'gz'), split_axis=1, concat_axis=1,...]
    ppermute x12 -> x9, starting transfers between devices: 47.6 us -> 34.5 us  [with_halo(): lax.ppermute(lax.slice_in_dim(block, block.shape[dim] - width, None, axis...]
    all_to_all x1 -> x0, starting transfers between devices: 11.6 us -> none  [per_device(): lax.all_to_all(labels, ('gy', 'gz'), split_axis=1, concat_axis=1, tiled=T...]
    all_to_all x2 -> x1, blocking collectives: 36.9 us -> 25.8 us  [per_device(): lax.all_to_all(outgoing, ('gy', 'gz'), split_axis=1, concat_axis=1, tiled...]
    all_to_all x1, waiting for transfers between devices: 9.59 us -> 3.2 us  [per_device(): lax.all_to_all(send_outgoing, ('gy', 'gz'), split_axis=1, concat_axis=1,...]
    all_to_all x1, starting transfers between devices: 14.2 us -> 11.6 us  [per_device(): lax.all_to_all(send_outgoing, ('gy', 'gz'), split_axis=1, concat_axis=1,...]
    ppermute x12 -> x9, waiting for transfers between devices: 2.52 us -> 5.04 us  [with_halo(): lax.ppermute(lax.slice_in_dim(block, block.shape[dim] - width, None, axis...]
  transfers between devices with their start and end apart: 26 -> 19, of which waited for: 11 -> 9; matrix products, arithmetic and copies ran while one was open for 6% -> 9% of each run, Pallas kernels for 0% -> 0%
where the time goes in v1:
time: 159 us; the launch traced here: 157 us
  starting transfers between devices  64.5 us (41%)
  blocking collectives  25.8 us (16%)
  other arithmetic  23.9 us (15%)
  local copies, waits for them, and re-layouts  20.3 us (13%)
  waiting for transfers between devices  14 us (9%)
  matrix products  6.69 us (4%)
  between operations  1.8 us (1%)
    ppermute x9, starting transfers between devices, with_halo(): lax.ppermute(lax.slice_in_dim(block, block.shape[dim] - width, None, axis...  34.5 us
    all_to_all x1, blocking collectives, per_device(): lax.all_to_all(outgoing, ('gy', 'gz'), split_axis=1, concat_axis=1, tiled...  25.8 us
    ppermute x9, starting transfers between devices, with_halo(): lax.ppermute(lax.slice_in_dim(block, 0, width, axis=dim), axis, backward)  18.4 us
    all_to_all x1, starting transfers between devices, per_device(): lax.all_to_all(send_outgoing, ('gy', 'gz'), split_axis=1, concat_axis=1,...  11.6 us
    ppermute x9, waiting for transfers between devices, with_halo(): lax.ppermute(lax.slice_in_dim(block, 0, width, axis=dim), axis, backward)  5.72 us
    ppermute x9, waiting for transfers between devices, with_halo(): lax.ppermute(lax.slice_in_dim(block, block.shape[dim] - width, None, axis...  5.04 us
    dot_general x3, matrix products, collect(): jnp.dot(volume.reshape(-1, shape_all[3]), table_back, precision=highest)  3.93 us
    all_to_all x1, waiting for transfers between devices, per_device(): lax.all_to_all(send_outgoing, ('gy', 'gz'), split_axis=1, concat_axis=1,...  3.2 us
  transfers between devices with their start and end apart: 19, of which 9 were waited for; matrix products, arithmetic and copies ran while one was open for 9% of the time, Pallas kernels for 0%

profile of v1, /device:TPU:1, one launch (start us, length us, event | category | flops | bytes accessed | tf_op | source)
XLA Modules:
  0.0 157.0 jit_solution(11241195298574607670)
XLA Ops:
  0.0 0.7 fusion.144
  0.9 0.9 convolution_bitcast_fusion
  2.1 0.7 copy.91
  2.8 11.6 %all-to-all-start = ((f32[4,64,16]{2,0,1:T(4,128)}), f32[4,64,16]{2,0,1:T(4,128)S(1)}, u32[]{:S(2)}, u32[]{:S(2)}) async-start(f32[4,64,16]{2,0,1:T(4,128)} %copy.91), calls=%async_computation | async-start | bytes 262144 | tf_op jit(solution)/shard_map/all_to_all | solution.py:241
  14.5 1.3 collective-permute-start.1
  15.8 4.6 %collective-permute-start = (bf16[3,5,16,128]{3,2,1,0:T(8,128)(2,1)S(1)}, bf16[3,5,16,128]{3,2,1,0:T(8,128)(2,1)S(1)}, u32[]{:S(2)}, u32[]{:S(2)}) collective-permute-start(bf16[3,5,16,128]{3,2,1,0:T(8,128)(2,1)S(1)} %get-tuple-element.87), channel_id=1, source_target_pairs={{0,64},{64,128},{128,192},{192,256},{256,320},{320,384},{384,448},... | collective-permute-start | bytes 184328 | tf_op jit(solution)/shard_map/ppermute | solution.py:24
  20.5 0.6 iota_compare_fusion
  21.1 0.6 iota_compare_fusion.1
  21.7 0.6 select_add_fusion
  22.4 3.2 %all-to-all-done = f32[4,64,16]{2,0,1:T(4,128)S(1)} async-done(((f32[4,64,16]{2,0,1:T(4,128)}), f32[4,64,16]{2,0,1:T(4,128)S(1)}, u32[]{:S(2)}, u32[]{:S(2)}) %all-to-all-start) | async-done | bytes 16416 | tf_op jit(solution)/shard_map/all_to_all | solution.py:241
  26.5 4.0 %collective-permute-start.6 = (f32[3,1,4,32]{3,2,1,0:T(4,128)S(1)}, f32[3,1,4,32]{3,2,1,0:T(4,128)S(1)}, u32[]{:S(2)}, u32[]{:S(2)}) collective-permute-start(f32[3,1,4,32]{3,2,1,0:T(4,128)S(1)} %get-tuple-element.112), channel_id=1, source_target_pairs={{0,64},{64,128},{128,192},{192,256},{256,320},{320,384},{384,448},... | collective-permute-start | bytes 4616 | tf_op jit(solution)/shard_map/ppermute | solution.py:24
  30.5 0.6 fusion.145
  31.1 1.3 collective-permute-start.7
  32.4 3.7 %collective-permute-done.7 = f32[3,1,4,32]{3,2,1,0:T(4,128)S(1)} collective-permute-done((f32[3,1,4,32]{3,2,1,0:T(4,128)S(1)}, f32[3,1,4,32]{3,2,1,0:T(4,128)S(1)}, u32[]{:S(2)}, u32[]{:S(2)}) %collective-permute-start.7) | collective-permute-done | bytes 1568 | tf_op jit(solution)/shard_map/ppermute | solution.py:27
  36.1 1.3 collective-permute-start.9
  37.4 4.0 %collective-permute-start.8 = (f32[3,6,1,32]{3,2,1,0:T(1,128)S(1)}, f32[3,6,1,32]{3,2,1,0:T(1,128)S(1)}, u32[]{:S(2)}, u32[]{:S(2)}) collective-permute-start(f32[3,6,1,32]{3,2,1,0:T(1,128)S(1)} %get-tuple-element.107), channel_id=1, source_target_pairs={{0,8},{8,16},{16,24},{24,32},{32,40},{40,48},{48,56},{1,9},{9,17},... | collective-permute-start | bytes 6920 | tf_op jit(solution)/shard_map/ppermute | solution.py:24
  41.5 0.7 collective-permute-done.8
  42.3 4.6 %collective-permute-start.11 = (f32[3,6,6,1]{3,2,1,0:T(8,128)S(1)}, f32[3,6,6,1]{3,2,1,0:T(8,128)S(1)}, u32[]{:S(2)}, u32[]{:S(2)}) collective-permute-start(f32[3,6,6,1]{3,2,1,0:T(8,128)S(1)} %get-tuple-element.100), channel_id=1, source_target_pairs={{1,0},{2,1},{3,2},{4,3},{5,4},{6,5},{7,6},{9,8},{10,9},{11,10},{12... | collective-permute-start | bytes 1304 | tf_op jit(solution)/shard_map/ppermute | solution.py:27
  46.9 2.0 %collective-permute-start.10 = (f32[3,6,6,1]{3,2,1,0:T(8,128)S(1)}, f32[3,6,6,1]{3,2,1,0:T(8,128)S(1)}, u32[]{:S(2)}, u32[]{:S(2)}) collective-permute-start(f32[3,6,6,1]{3,2,1,0:T(8,128)S(1)} %get-tuple-element.99), channel_id=1, source_target_pairs={{0,1},{1,2},{2,3},{3,4},{4,5},{5,6},{6,7},{8,9},{9,10},{10,11},{11... | collective-permute-start | bytes 1304 | tf_op jit(solution)/shard_map/ppermute | solution.py:24
  49.7 0.6 collective-permute-done.10
  53.1 0.7 fusion.118
  53.8 0.7 fusion.124
  54.6 1.3 collective-permute-start.3
  55.9 4.5 %collective-permute-start.2 = (bf16[3,26,5,128]{3,2,1,0:T(8,128)(2,1)S(1)}, bf16[3,26,5,128]{3,2,1,0:T(8,128)(2,1)S(1)}, u32[]{:S(2)}, u32[]{:S(2)}) collective-permute-start(bf16[3,26,5,128]{3,2,1,0:T(8,128)(2,1)S(1)} %get-tuple-element.69), channel_id=1, source_target_pairs={{0,8},{8,16},{16,24},{24,32},{32,40},{40,48},{48,56},{1,9},{9,17},... | collective-permute-start | bytes 299528 | tf_op jit(solution)/shard_map/ppermute | solution.py:24
  60.4 0.6 slice_add_fusion.57
  61.0 2.0 %collective-permute-done.3 = bf16[3,26,5,128]{3,2,1,0:T(8,128)(2,1)S(1)} collective-permute-done((bf16[3,26,5,128]{3,2,1,0:T(8,128)(2,1)S(1)}, bf16[3,26,5,128]{3,2,1,0:T(8,128)(2,1)S(1)}, u32[]{:S(2)}, u32[]{:S(2)}) %collective-permute-start.3) | collective-permute-done | bytes 99872 | tf_op jit(solution)/shard_map/ppermute | solution.py:27
  63.1 1.0 collective-permute-done.2
  64.6 0.8 copy.97
  65.5 2.6 %collective-permute-start.5 = (bf16[3,26,26,5]{2,1,3,0:T(8,128)(2,1)S(1)}, bf16[3,26,26,5]{2,1,3,0:T(8,128)(2,1)S(1)}, u32[]{:S(2)}, u32[]{:S(2)}) collective-permute-start(bf16[3,26,26,5]{2,1,3,0:T(8,128)(2,1)S(1)} %copy.97), channel_id=1, source_target_pairs={{1,0},{2,1},{3,2},{4,3},{5,4},{6,5},{7,6},{9,8},{10,9},{11,10},{12... | collective-permute-start | bytes 60848 | tf_op jit(solution)/shard_map/ppermute | solution.py:27
  68.1 0.8 copy.96
  68.9 3.2 %collective-permute-start.4 = (bf16[3,26,26,5]{2,1,3,0:T(8,128)(2,1)S(1)}, bf16[3,26,26,5]{2,1,3,0:T(8,128)(2,1)}, u32[]{:S(2)}, u32[]{:S(2)}) collective-permute-start(bf16[3,26,26,5]{2,1,3,0:T(8,128)(2,1)S(1)} %copy.96), channel_id=1, source_target_pairs={{0,1},{1,2},{2,3},{3,4},{4,5},{5,6},{6,7},{8,9},{9,10},{10,11},{11... | collective-permute-start | bytes 60848 | tf_op jit(solution)/shard_map/ppermute | solution.py:24
  72.1 1.5 fusion.130
  73.6 0.9 squeeze.83
  74.5 0.9 squeeze.81
  75.4 0.9 squeeze.79
  76.3 0.7 copy.99
  77.0 1.6 %copy.98 = bf16[3,26,26,5]{3,2,1,0:T(8,128)(2,1)S(1)} copy(bf16[3,26,26,5]{2,1,3,0:T(8,128)(2,1)} %collective-permute-done.4) | data formatting | bytes 40560 | tf_op jit(solution)/shard_map/ppermute | solution.py:24
  78.6 2.3 %pad_maximum_fusion = bf16[3,26,26,138]{3,2,1,0:T(8,128)(2,1)S(1)} fusion(bf16[3,26,26,5]{3,2,1,0:T(8,128)(2,1)S(1)} %copy.99, bf16[3,26,5,128]{3,2,1,0:T(8,128)(2,1)S(1)} %collective-permute-done.3, bf16[3,5,16,128]{3,2,1,0:T(8,128)(2,1)S(1)} %collective-permute-done.1, bf16[1,16,16,128]{3,2,1,0:T(8,128)(2,1)S(1)} %convert_bitcast_fusion, ...), kind=kLoop, calls=%fused_computation.9 | loop fusion | flops 5037552 | bytes 1119456 | tf_op jit(solution)/shard_map/concatenate | solution.py:28
  82.0 2.2 %add_multiply_fusion = (f32[22,22,134]{2,1,0:T(8,128)S(1)}, f32[22,22,134]{2,1,0:T(8,128)}, f32[22,22,134]{2,1,0:T(8,128)}) fusion(f32[22,22,138]{2,1,0:T(8,128)S(1)} %fusion.20, f32[22,22,138]{2,1,0:T(8,128)S(1)} %fusion.28), kind=kLoop, calls=%fused_computation.83 | loop fusion | flops 1297120 | bytes 3372512 | tf_op jit(solution)/shard_map/mul | solution.py:48
  84.5 1.0 fusion.165
  86.5 0.8 stack.61
  87.3 1.4 fusion.42
  88.7 0.8 stack.60
  89.8 0.8 copy-done.1
  91.0 1.1 fusion.33
  93.1 1.3 multiply_reduce_fusion.5
  94.7 1.3 multiply_reduce_fusion.3
  96.3 1.3 collective-permute-start.13
  97.6 4.6 %collective-permute-start.12 = (f32[3,1,4,32]{3,2,1,0:T(4,128)S(1)}, f32[3,1,4,32]{3,2,1,0:T(4,128)S(1)}, u32[]{:S(2)}, u32[]{:S(2)}) collective-permute-start(f32[3,1,4,32]{3,2,1,0:T(4,128)S(1)} %get-tuple-element.109), channel_id=1, source_target_pairs={{0,64},{64,128},{128,192},{192,256},{256,320},{320,384},{384,448},... | collective-permute-start | bytes 4616 | tf_op jit(solution)/shard_map/ppermute | solution.py:24
  102.3 0.7 collective-permute-done.12
  103.0 1.3 collective-permute-start.15
  104.3 4.7 %collective-permute-start.14 = (f32[3,6,1,32]{3,2,1,0:T(1,128)S(1)}, f32[3,6,1,32]{3,2,1,0:T(1,128)S(1)}, u32[]{:S(2)}, u32[]{:S(2)}) collective-permute-start(f32[3,6,1,32]{3,2,1,0:T(1,128)S(1)} %get-tuple-element.105), channel_id=1, source_target_pairs={{0,8},{8,16},{16,24},{24,32},{32,40},{40,48},{48,56},{1,9},{9,17},... | collective-permute-start | bytes 6920 | tf_op jit(solution)/shard_map/ppermute | solution.py:24
  109.1 0.8 collective-permute-done.14
  110.0 3.5 %collective-permute-start.17 = (f32[3,6,6,1]{3,2,1,0:T(8,128)S(1)}, f32[3,6,6,1]{3,2,1,0:T(8,128)S(1)}, u32[]{:S(2)}, u32[]{:S(2)}) collective-permute-start(f32[3,6,6,1]{3,2,1,0:T(8,128)S(1)} %get-tuple-element.96), channel_id=1, source_target_pairs={{1,0},{2,1},{3,2},{4,3},{5,4},{6,5},{7,6},{9,8},{10,9},{11,10},{12... | collective-permute-start | bytes 1304 | tf_op jit(solution)/shard_map/ppermute | solution.py:27
  113.4 2.8 %collective-permute-start.16 = (f32[3,6,6,1]{3,2,1,0:T(8,128)S(1)}, f32[3,6,6,1]{3,2,1,0:T(8,128)S(1)}, u32[]{:S(2)}, u32[]{:S(2)}) collective-permute-start(f32[3,6,6,1]{3,2,1,0:T(8,128)S(1)} %get-tuple-element.95), channel_id=1, source_target_pairs={{0,1},{1,2},{2,3},{3,4},{4,5},{5,6},{6,7},{8,9},{9,10},{10,11},{11... | collective-permute-start | bytes 1304 | tf_op jit(solution)/shard_map/ppermute | solution.py:24
  116.3 1.2 collective-permute-done.16
  120.5 1.0 fusion.162
  121.8 1.1 squeeze.90
  122.9 2.0 %fusion.35 = f32[20,20,132]{2,1,0:T(8,128)} fusion(bf16[20,20,132]{2,1,0:T(8,128)(2,1)} %get-tuple-element.30, f32[20,20,132]{2,1,0:T(8,128)S(1)} %squeeze.92, f32[20,20,132]{2,1,0:T(8,128)S(1)} %squeeze.91, f32[20,20,132]{2,1,0:T(8,128)S(1)} %squeeze.90, f32[3,20,20,132]{3,2,1,0:T(8,128)S(1)} %maximum_convert_fusion), kind=kLoop, calls=%fused_computation.87 | loop fusion | flops 369600 | bytes 1584000 | tf_op jit(solution)/shard_map/add | solution.py:254
  124.9 1.1 mul.1097
  126.1 1.5 multiply_multiply_fusion
  127.6 1.3 multiply_reduce_fusion.1
  130.1 25.8 %all_to_all.18 = f32[3,64,16]{2,0,1:T(4,128)S(1)} all-to-all(f32[3,64,16]{2,0,1:T(4,128)S(1)} %copy.116), channel_id=1, replica_groups=mesh['gx'=8,'gy'=8,'gz'=8] {'gy','gz'}, dimensions={1} | all-to-all | bytes 24576 | tf_op jit(solution)/shard_map/all_to_all | solution.py:262
  156.1 0.9 convolution_bitcast_fusion.1
  (267 shorter events, 14.3 us)
Async XLA Ops:
  0.0 14.5 %copy-start.13 = (s32[16,16,128]{2,1,0:T(8,128)S(1)}, s32[16,16,128]{2,1,0:T(8,128)}, u32[]{:S(2)}) copy-start(s32[16,16,128]{2,1,0:T(8,128)} %param.7) | copy-start | bytes 393220
  0.0 14.5 %copy-start.9 = (bf16[16,16,128]{2,1,0:T(8,128)(2,1)S(1)}, bf16[16,16,128]{2,1,0:T(8,128)(2,1)}, u32[]{:S(2)}) copy-start(bf16[16,16,128]{2,1,0:T(8,128)(2,1)} %param.6) | copy-start | bytes 196612
  0.0 14.5 %copy-start.10 = (bf16[16,16,128]{2,1,0:T(8,128)(2,1)S(1)}, bf16[16,16,128]{2,1,0:T(8,128)(2,1)}, u32[]{:S(2)}) copy-start(bf16[16,16,128]{2,1,0:T(8,128)(2,1)} %param.5) | copy-start | bytes 196612
  0.9 0.9 copy-start.43
  2.8 22.7 %all-to-all-start = ((f32[4,64,16]{2,0,1:T(4,128)}), f32[4,64,16]{2,0,1:T(4,128)S(1)}, u32[]{:S(2)}, u32[]{:S(2)}) async-start(f32[4,64,16]{2,0,1:T(4,128)} %copy.91), calls=%async_computation | async-start | bytes 262144 | tf_op jit(solution)/shard_map/all_to_all | solution.py:241
  14.5 39.9 %collective-permute-start.1 = (bf16[3,5,16,128]{3,2,1,0:T(8,128)(2,1)S(1)}, bf16[3,5,16,128]{3,2,1,0:T(8,128)(2,1)S(1)}, u32[]{:S(2)}, u32[]{:S(2)}) collective-permute-start(bf16[3,5,16,128]{3,2,1,0:T(8,128)(2,1)S(1)} %get-tuple-element.88), channel_id=1, source_target_pairs={{64,0},{128,64},{192,128},{256,192},{320,256},{384,320},{448,384},... | collective-permute-start | bytes 184328 | tf_op jit(solution)/shard_map/ppermute | solution.py:27
  15.8 38.6 %collective-permute-start = (bf16[3,5,16,128]{3,2,1,0:T(8,128)(2,1)S(1)}, bf16[3,5,16,128]{3,2,1,0:T(8,128)(2,1)S(1)}, u32[]{:S(2)}, u32[]{:S(2)}) collective-permute-start(bf16[3,5,16,128]{3,2,1,0:T(8,128)(2,1)S(1)} %get-tuple-element.87), channel_id=1, source_target_pairs={{0,64},{64,128},{128,192},{192,256},{256,320},{320,384},{384,448},... | collective-permute-start | bytes 184328 | tf_op jit(solution)/shard_map/ppermute | solution.py:24
  20.5 30.0 %copy-start.29 = (f32[132]{0:T(256)}, f32[132]{0:T(256)S(1)}, u32[]{:S(2)}) copy-start(f32[132]{0:T(256)S(1)} %get-tuple-element.119) | copy-start | bytes 1588
  20.5 30.0 %copy-start.31 = (f32[132]{0:T(256)}, f32[132]{0:T(256)S(1)}, u32[]{:S(2)}) copy-start(f32[132]{0:T(256)S(1)} %get-tuple-element.120) | copy-start | bytes 1588
  20.5 30.0 %copy-start.19 = (s32[132]{0:T(256)}, s32[132]{0:T(256)S(1)}, u32[]{:S(2)}) copy-start(s32[132]{0:T(256)S(1)} %get-tuple-element.117) | copy-start | bytes 1588
  20.5 30.0 %copy-start.21 = (s32[132]{0:T(256)}, s32[132]{0:T(256)S(1)}, u32[]{:S(2)}) copy-start(s32[132]{0:T(256)S(1)} %get-tuple-element.118) | copy-start | bytes 1588
  22.4 19.8 %copy-start.45 = (f32[64]{0:T(128)}, f32[64]{0:T(128)S(1)}, u32[]{:S(2)}) copy-start(f32[64]{0:T(128)S(1)} %add_convert_fusion) | copy-start | bytes 772
  25.8 25.0 %copy-start.41 = (f32[128]{0:T(128)}, f32[128]{0:T(128)S(1)}, u32[]{:S(2)}) copy-start(f32[128]{0:T(128)S(1)} %slice_reduce_fusion) | copy-start | bytes 1540
  26.5 5.9 %collective-permute-start.6 = (f32[3,1,4,32]{3,2,1,0:T(4,128)S(1)}, f32[3,1,4,32]{3,2,1,0:T(4,128)S(1)}, u32[]{:S(2)}, u32[]{:S(2)}) collective-permute-start(f32[3,1,4,32]{3,2,1,0:T(4,128)S(1)} %get-tuple-element.112), channel_id=1, source_target_pairs={{0,64},{64,128},{128,192},{192,256},{256,320},{320,384},{384,448},... | collective-permute-start | bytes 4616 | tf_op jit(solution)/shard_map/ppermute | solution.py:24
  31.1 5.0 %collective-permute-start.7 = (f32[3,1,4,32]{3,2,1,0:T(4,128)S(1)}, f32[3,1,4,32]{3,2,1,0:T(4,128)S(1)}, u32[]{:S(2)}, u32[]{:S(2)}) collective-permute-start(f32[3,1,4,32]{3,2,1,0:T(4,128)S(1)} %get-tuple-element.111), channel_id=1, source_target_pairs={{64,0},{128,64},{192,128},{256,192},{320,256},{384,320},{448,384},... | collective-permute-start | bytes 4616 | tf_op jit(solution)/shard_map/ppermute | solution.py:27
  36.1 5.3 %collective-permute-start.9 = (f32[3,6,1,32]{3,2,1,0:T(1,128)S(1)}, f32[3,6,1,32]{3,2,1,0:T(1,128)S(1)}, u32[]{:S(2)}, u32[]{:S(2)}) collective-permute-start(f32[3,6,1,32]{3,2,1,0:T(1,128)S(1)} %get-tuple-element.108), channel_id=1, source_target_pairs={{8,0},{16,8},{24,16},{32,24},{40,32},{48,40},{56,48},{9,1},{17,9},... | collective-permute-start | bytes 6920 | tf_op jit(solution)/shard_map/ppermute | solution.py:27
  37.4 4.8 %collective-permute-start.8 = (f32[3,6,1,32]{3,2,1,0:T(1,128)S(1)}, f32[3,6,1,32]{3,2,1,0:T(1,128)S(1)}, u32[]{:S(2)}, u32[]{:S(2)}) collective-permute-start(f32[3,6,1,32]{3,2,1,0:T(1,128)S(1)} %get-tuple-element.107), channel_id=1, source_target_pairs={{0,8},{8,16},{16,24},{24,32},{32,40},{40,48},{48,56},{1,9},{9,17},... | collective-permute-start | bytes 6920 | tf_op jit(solution)/shard_map/ppermute | solution.py:24
  41.4 11.0 %copy-start.23 = (f32[4]{0:T(128)}, f32[4]{0:T(128)S(1)}, u32[]{:S(2)}) copy-start(f32[4]{0:T(128)S(1)} %get-tuple-element.121) | copy-start | bytes 52
  41.4 11.0 %copy-start.26 = (f32[4]{0:T(128)}, f32[4]{0:T(128)S(1)}, u32[]{:S(2)}) copy-start(f32[4]{0:T(128)S(1)} %get-tuple-element.122) | copy-start | bytes 52
  42.3 7.4 %collective-permute-start.11 = (f32[3,6,6,1]{3,2,1,0:T(8,128)S(1)}, f32[3,6,6,1]{3,2,1,0:T(8,128)S(1)}, u32[]{:S(2)}, u32[]{:S(2)}) collective-permute-start(f32[3,6,6,1]{3,2,1,0:T(8,128)S(1)} %get-tuple-element.100), channel_id=1, source_target_pairs={{1,0},{2,1},{3,2},{4,3},{5,4},{6,5},{7,6},{9,8},{10,9},{11,10},{12... | collective-permute-start | bytes 1304 | tf_op jit(solution)/shard_map/ppermute | solution.py:27
  46.9 3.4 %collective-permute-start.10 = (f32[3,6,6,1]{3,2,1,0:T(8,128)S(1)}, f32[3,6,6,1]{3,2,1,0:T(8,128)S(1)}, u32[]{:S(2)}, u32[]{:S(2)}) collective-permute-start(f32[3,6,6,1]{3,2,1,0:T(8,128)S(1)} %get-tuple-element.99), channel_id=1, source_target_pairs={{0,1},{1,2},{2,3},{3,4},{4,5},{5,6},{6,7},{8,9},{9,10},{10,11},{11... | collective-permute-start | bytes 1304 | tf_op jit(solution)/shard_map/ppermute | solution.py:24
  49.6 2.4 %copy-start.33 = (f32[20]{0:T(128)}, f32[20]{0:T(128)S(1)}, u32[]{:S(2)}) copy-start(f32[20]{0:T(128)S(1)} %mul.978) | copy-start | bytes 244
  49.7 2.3 %copy-start.35 = (f32[20]{0:T(128)}, f32[20]{0:T(128)S(1)}, u32[]{:S(2)}) copy-start(f32[20]{0:T(128)S(1)} %mul.972) | copy-start | bytes 244
  54.6 8.5 %collective-permute-start.3 = (bf16[3,26,5,128]{3,2,1,0:T(8,128)(2,1)S(1)}, bf16[3,26,5,128]{3,2,1,0:T(8,128)(2,1)S(1)}, u32[]{:S(2)}, u32[]{:S(2)}) collective-permute-start(bf16[3,26,5,128]{3,2,1,0:T(8,128)(2,1)S(1)} %get-tuple-element.70), channel_id=1, source_target_pairs={{8,0},{16,8},{24,16},{32,24},{40,32},{48,40},{56,48},{9,1},{17,9},... | collective-permute-start | bytes 299528 | tf_op jit(solution)/shard_map/ppermute | solution.py:27
  55.9 8.2 %collective-permute-start.2 = (bf16[3,26,5,128]{3,2,1,0:T(8,128)(2,1)S(1)}, bf16[3,26,5,128]{3,2,1,0:T(8,128)(2,1)S(1)}, u32[]{:S(2)}, u32[]{:S(2)}) collective-permute-start(bf16[3,26,5,128]{3,2,1,0:T(8,128)(2,1)S(1)} %get-tuple-element.69), channel_id=1, source_target_pairs={{0,8},{8,16},{16,24},{24,32},{32,40},{40,48},{48,56},{1,9},{9,17},... | collective-permute-start | bytes 299528 | tf_op jit(solution)/shard_map/ppermute | solution.py:24
  65.5 10.9 %collective-permute-start.5 = (bf16[3,26,26,5]{2,1,3,0:T(8,128)(2,1)S(1)}, bf16[3,26,26,5]{2,1,3,0:T(8,128)(2,1)S(1)}, u32[]{:S(2)}, u32[]{:S(2)}) collective-permute-start(bf16[3,26,26,5]{2,1,3,0:T(8,128)(2,1)S(1)} %copy.97), channel_id=1, source_target_pairs={{1,0},{2,1},{3,2},{4,3},{5,4},{6,5},{7,6},{9,8},{10,9},{11,10},{12... | collective-permute-start | bytes 60848 | tf_op jit(solution)/shard_map/ppermute | solution.py:27
  68.9 8.1 %collective-permute-start.4 = (bf16[3,26,26,5]{2,1,3,0:T(8,128)(2,1)S(1)}, bf16[3,26,26,5]{2,1,3,0:T(8,128)(2,1)}, u32[]{:S(2)}, u32[]{:S(2)}) collective-permute-start(bf16[3,26,26,5]{2,1,3,0:T(8,128)(2,1)S(1)} %copy.96), channel_id=1, source_target_pairs={{0,1},{1,2},{2,3},{3,4},{4,5},{5,6},{6,7},{8,9},{9,10},{10,11},{11... | collective-permute-start | bytes 60848 | tf_op jit(solution)/shard_map/ppermute | solution.py:24
  86.0 1.2 copy-start.5
  86.1 6.0 %copy-start.6 = (bf16[1,20,5,4,132]{4,3,2,1,0:T(4,128)(2,1)}, bf16[1,20,5,4,132]{4,3,2,1,0:T(4,128)(2,1)S(1)}, u32[]{:S(2)}) copy-start(bf16[1,20,5,4,132]{4,3,2,1,0:T(4,128)(2,1)S(1)} %stack.62) | copy-start | bytes 316804
  88.6 1.1 copy-start
  89.4 1.1 copy-start.1
  89.4 1.2 copy-start.2
  89.4 1.4 copy-start.3
  89.4 1.5 copy-start.4
  91.0 1.2 copy-start.7
  91.0 1.2 copy-start.8
  92.2 0.8 copy-start.11
  92.2 0.8 copy-start.24
  92.2 0.8 copy-start.27
  93.0 1.6 %copy-start.14 = (pred[34,132]{1,0:T(8,128)(4,1)S(1)}, pred[34,132]{1,0:T(8,128)(4,1)}, u32[]{:S(2)}) copy-start(pred[34,132]{1,0:T(8,128)(4,1)} %iota_compare_fusion) | copy-start | bytes 13468
  93.0 1.6 %copy-start.15 = (pred[34,132]{1,0:T(8,128)(4,1)S(1)}, pred[34,132]{1,0:T(8,128)(4,1)}, u32[]{:S(2)}) copy-start(pred[34,132]{1,0:T(8,128)(4,1)} %iota_compare_fusion.1) | copy-start | bytes 13468
  93.0 1.6 %copy-start.37 = (f32[132]{0:T(256)S(1)}, f32[132]{0:T(256)}, u32[]{:S(2)}) copy-start(f32[132]{0:T(256)} %get-tuple-element.124) | copy-start | bytes 1588
  93.0 1.6 %copy-start.38 = (f32[132]{0:T(256)S(1)}, f32[132]{0:T(256)}, u32[]{:S(2)}) copy-start(f32[132]{0:T(256)} %get-tuple-element.125) | copy-start | bytes 1588
  93.0 1.6 %copy-start.39 = (f32[4]{0:T(128)S(1)}, f32[4]{0:T(128)}, u32[]{:S(2)}) copy-start(f32[4]{0:T(128)} %get-tuple-element.126) | copy-start | bytes 52
  93.0 1.6 %copy-start.40 = (f32[4]{0:T(128)S(1)}, f32[4]{0:T(128)}, u32[]{:S(2)}) copy-start(f32[4]{0:T(128)} %get-tuple-element.127) | copy-start | bytes 52
  94.6 1.6 %copy-start.16 = (f32[1,4,4,32]{3,2,1,0:T(4,128)S(1)}, f32[1,4,4,32]{3,2,1,0:T(4,128)}, u32[]{:S(2)}) copy-start(f32[1,4,4,32]{3,2,1,0:T(4,128)} %fusion.118) | copy-start | bytes 6148
  94.7 1.6 %copy-start.17 = (f32[1,4,4,32]{3,2,1,0:T(4,128)S(1)}, f32[1,4,4,32]{3,2,1,0:T(4,128)}, u32[]{:S(2)}) copy-start(f32[1,4,4,32]{3,2,1,0:T(4,128)} %fusion.124) | copy-start | bytes 6148
  94.7 1.6 %copy-start.18 = (f32[1,4,4,32]{3,2,1,0:T(4,128)S(1)}, f32[1,4,4,32]{3,2,1,0:T(4,128)}, u32[]{:S(2)}) copy-start(f32[1,4,4,32]{3,2,1,0:T(4,128)} %fusion.130) | copy-start | bytes 6148
  96.0 21.6 %copy-start.20 = (s32[132]{0:T(256)S(1)}, s32[132]{0:T(256)}, u32[]{:S(2)}) copy-start(s32[132]{0:T(256)} %copy-done.19) | copy-start | bytes 1588
  96.0 21.6 %copy-start.22 = (s32[132]{0:T(256)S(1)}, s32[132]{0:T(256)}, u32[]{:S(2)}) copy-start(s32[132]{0:T(256)} %copy-done.21) | copy-start | bytes 1588
  96.0 21.6 %copy-start.30 = (f32[132]{0:T(256)S(1)}, f32[132]{0:T(256)}, u32[]{:S(2)}) copy-start(f32[132]{0:T(256)} %copy-done.29) | copy-start | bytes 1588
  96.0 21.6 %copy-start.32 = (f32[132]{0:T(256)S(1)}, f32[132]{0:T(256)}, u32[]{:S(2)}) copy-start(f32[132]{0:T(256)} %copy-done.31) | copy-start | bytes 1588
  96.3 5.9 %collective-permute-start.13 = (f32[3,1,4,32]{3,2,1,0:T(4,128)S(1)}, f32[3,1,4,32]{3,2,1,0:T(4,128)S(1)}, u32[]{:S(2)}, u32[]{:S(2)}) collective-permute-start(f32[3,1,4,32]{3,2,1,0:T(4,128)S(1)} %get-tuple-element.110), channel_id=1, source_target_pairs={{64,0},{128,64},{192,128},{256,192},{320,256},{384,320},{448,384},... | collective-permute-start | bytes 4616 | tf_op jit(solution)/shard_map/ppermute | solution.py:27
  97.6 5.4 %collective-permute-start.12 = (f32[3,1,4,32]{3,2,1,0:T(4,128)S(1)}, f32[3,1,4,32]{3,2,1,0:T(4,128)S(1)}, u32[]{:S(2)}, u32[]{:S(2)}) collective-permute-start(f32[3,1,4,32]{3,2,1,0:T(4,128)S(1)} %get-tuple-element.109), channel_id=1, source_target_pairs={{0,64},{64,128},{128,192},{192,256},{256,320},{320,384},{384,448},... | collective-permute-start | bytes 4616 | tf_op jit(solution)/shard_map/ppermute | solution.py:24
  103.0 6.0 %collective-permute-start.15 = (f32[3,6,1,32]{3,2,1,0:T(1,128)S(1)}, f32[3,6,1,32]{3,2,1,0:T(1,128)S(1)}, u32[]{:S(2)}, u32[]{:S(2)}) collective-permute-start(f32[3,6,1,32]{3,2,1,0:T(1,128)S(1)} %get-tuple-element.106), channel_id=1, source_target_pairs={{8,0},{16,8},{24,16},{32,24},{40,32},{48,40},{56,48},{9,1},{17,9},... | collective-permute-start | bytes 6920 | tf_op jit(solution)/shard_map/ppermute | solution.py:27
  104.3 5.5 %collective-permute-start.14 = (f32[3,6,1,32]{3,2,1,0:T(1,128)S(1)}, f32[3,6,1,32]{3,2,1,0:T(1,128)S(1)}, u32[]{:S(2)}, u32[]{:S(2)}) collective-permute-start(f32[3,6,1,32]{3,2,1,0:T(1,128)S(1)} %get-tuple-element.105), channel_id=1, source_target_pairs={{0,8},{8,16},{16,24},{24,32},{32,40},{40,48},{48,56},{1,9},{9,17},... | collective-permute-start | bytes 6920 | tf_op jit(solution)/shard_map/ppermute | solution.py:24
  110.0 6.3 %collective-permute-start.17 = (f32[3,6,6,1]{3,2,1,0:T(8,128)S(1)}, f32[3,6,6,1]{3,2,1,0:T(8,128)S(1)}, u32[]{:S(2)}, u32[]{:S(2)}) collective-permute-start(f32[3,6,6,1]{3,2,1,0:T(8,128)S(1)} %get-tuple-element.96), channel_id=1, source_target_pairs={{1,0},{2,1},{3,2},{4,3},{5,4},{6,5},{7,6},{9,8},{10,9},{11,10},{12... | collective-permute-start | bytes 1304 | tf_op jit(solution)/shard_map/ppermute | solution.py:27
  113.4 4.0 %collective-permute-start.16 = (f32[3,6,6,1]{3,2,1,0:T(8,128)S(1)}, f32[3,6,6,1]{3,2,1,0:T(8,128)S(1)}, u32[]{:S(2)}, u32[]{:S(2)}) collective-permute-start(f32[3,6,6,1]{3,2,1,0:T(8,128)S(1)} %get-tuple-element.95), channel_id=1, source_target_pairs={{0,1},{1,2},{2,3},{3,4},{4,5},{5,6},{6,7},{8,9},{9,10},{10,11},{11... | collective-permute-start | bytes 1304 | tf_op jit(solution)/shard_map/ppermute | solution.py:24
  119.5 0.6 copy-start.25
  119.5 0.6 copy-start.28
  126.1 1.5 copy-start.12
  127.6 2.0 %copy-start.42 = (f32[128]{0:T(128)S(1)}, f32[128]{0:T(128)}, u32[]{:S(2)}) copy-start(f32[128]{0:T(128)} %copy-done.41) | copy-start | bytes 1540
  127.6 2.0 %copy-start.46 = (f32[64]{0:T(128)S(1)}, f32[64]{0:T(128)}, u32[]{:S(2)}) copy-start(f32[64]{0:T(128)} %copy-done.45) | copy-start | bytes 772
  129.0 27.2 %copy-start.44 = (s32[64]{0:T(128)S(1)}, s32[64]{0:T(128)}, u32[]{:S(2)}) copy-start(s32[64]{0:T(128)} %copy-done.43) | copy-start | bytes 772
  (2 other events, 1.2 us)

commit v2 on v1

--- a/solution.py
+++ b/solution.py
@@ -27,6 +27,35 @@
         high = lax.ppermute(lax.slice_in_dim(block, 0, width, axis=dim), axis, backward)
         block = jnp.concatenate([low, block, high], axis=dim)
     return block
+
+
+def with_halo_pair(first, second, sides, widths):
+    for axis, first_dim, second_dim in sides:
+        count = lax.axis_size(axis)
+        forward = [(i, i + 1) for i in range(count - 1)]
+        backward = [(target, source) for source, target in forward]
+        parts = []
+        for block, dim, width in ((first, first_dim, widths[0]), (second, second_dim, widths[1])):
+            parts.append(
+                (
+                    lax.slice_in_dim(block, block.shape[dim] - width, None, axis=dim),
+                    lax.slice_in_dim(block, 0, width, axis=dim),
+                )
+            )
+        low_flat = jnp.concatenate([p[0].reshape(-1) for p in parts])
+        high_flat = jnp.concatenate([p[1].reshape(-1) for p in parts])
+        low_flat = lax.ppermute(low_flat, axis, forward)
+        high_flat = lax.ppermute(high_flat, axis, backward)
+        split = parts[0][0].size
+        pieces = []
+        for index, (block, dim) in enumerate(((first, first_dim), (second, second_dim))):
+            shape = parts[index][0].shape
+            begin, end = (0, split) if index == 0 else (split, low_flat.shape[0])
+            low = low_flat[begin:end].reshape(shape)
+            high = high_flat[begin:end].reshape(shape)
+            pieces.append(jnp.concatenate([low, block, high], axis=dim))
+        first, second = pieces
+    return first, second
 
 
 def smooth_axis(volume, dimension):
@@ -194,16 +223,13 @@
 
 
 def per_device(reference_image, deformed_image, roi_mask, displacement, node_map):
-    mask_half = roi_mask.astype(jnp.bfloat16)
-    stacked = jnp.stack([reference_image, deformed_image, mask_half])
-    padded_images = with_halo(stacked, (("gx", 1), ("gy", 2), ("gz", 3)), 5)
-    derived = derive_fields(
-        padded_images[0].astype(jnp.float32), padded_images[1].astype(jnp.float32)
-    )
-    region = padded_images[2][3:-3, 3:-3, 3:-3].astype(jnp.float32)
-    contrast = derived[0].astype(jnp.float32)
-    slopes = derived[1:].astype(jnp.float32)
-    masked_slopes = slopes * region[None]
+    stacked = jnp.stack(
+        [
+            reference_image.astype(jnp.float32),
+            deformed_image.astype(jnp.float32),
+            roi_mask.astype(jnp.float32),
+        ]
+    )
     nodes_shape = (
         3,
         reference_image.shape[0] // ELEM,
@@ -213,7 +239,6 @@
     weights_table = axis_table(nodes_shape[3] + 2, ELEM, False)
     table_back = weights_table[1:-1].T
     table_square = axis_table(nodes_shape[3] + 2, ELEM, True)[1:-1].T
-    curvature = collect(masked_slopes * slopes, table_square, True) + diagonal_shift
     members = lax.axis_size(("gy", "gz"))
     blocks = node_map.shape[0]
     block_nodes = displacement.shape[2]
@@ -248,8 +273,20 @@
     tile_values = jnp.einsum(
         "cpn,pk->ckn", send_incoming[:3], send_placing, precision=highest
     ).reshape(nodes_shape)
+    padded_images, first_padded = with_halo_pair(
+        stacked, tile_values, (("gx", 1, 1), ("gy", 2, 2), ("gz", 3, 3)), (5, 1)
+    )
+    derived = derive_fields(padded_images[0], padded_images[1])
+    region = padded_images[2][3:-3, 3:-3, 3:-3]
+    contrast = derived[0].astype(jnp.float32)
+    slopes = derived[1:].astype(jnp.float32)
+    masked_slopes = slopes * region[None]
+    curvature = collect(masked_slopes * slopes, table_square, True) + diagonal_shift
     for iteration in range(ITERS):
-        padded = with_halo(tile_values, (("gx", 1), ("gy", 2), ("gz", 3)), 1)
+        if iteration == 0:
+            padded = first_padded
+        else:
+            padded = with_halo(tile_values, (("gx", 1), ("gy", 2), ("gz", 3)), 1)
         moved = spread(padded, weights_table)
         residual = contrast + slopes[0] * moved[0] + slopes[1] * moved[1] + slopes[2] * moved[2]
         image_part = collect(masked_slopes * residual[None], table_back, False)

time: 159 us -> 148 us (0.931)
  starting transfers between devices: 64.5 us -> 42.6 us
  waiting for transfers between devices: 14 us -> 31.7 us
  blocking collectives: 25.8 us -> 17.3 us
  local copies, waits for them, and re-layouts: 20.3 us -> 24.8 us
  other arithmetic: 23.9 us -> 21.4 us
    ppermute x9 -> x3, starting transfers between devices: 34.5 us -> 10.8 us  [with_halo(): lax.ppermute(lax.slice_in_dim(block, block.shape[dim] - width, None, axis...]
    ppermute x0 -> x6, starting transfers between devices: none -> 15.7 us  [the longest x3 11 us: with_halo_pair(): low_flat = lax.ppermute(low_flat, axis, forward)]
    ppermute x9 -> x3, starting transfers between devices: 18.4 us -> 4.5 us  [with_halo(): lax.ppermute(lax.slice_in_dim(block, 0, width, axis=dim), axis, backward)]
    ppermute x0 -> x6, waiting for transfers between devices: none -> 12.3 us  [the longest x3 10.2 us: with_halo_pair(): high_flat = lax.ppermute(high_flat, axis, backward)]
    all_to_all x1, blocking collectives: 25.8 us -> 17.3 us  [per_device(): lax.all_to_all(outgoing, ('gy', 'gz'), split_axis=1, concat_axis=1, tiled...]
    ppermute x9 -> x3, waiting for transfers between devices: 5.72 us -> 11.7 us  [with_halo(): lax.ppermute(lax.slice_in_dim(block, 0, width, axis=dim), axis, backward)]
    ppermute x9 -> x3, waiting for transfers between devices: 5.04 us -> 0.01 us  [with_halo(): lax.ppermute(lax.slice_in_dim(block, block.shape[dim] - width, None, axis...]
    concatenate x0 -> x11, other arithmetic: none -> 4.58 us  [the longest x5 3.59 us: with_halo_pair(): pieces.append(jnp.concatenate([low, block, high], axis=dim))]
  transfers between devices with their start and end apart: 19 -> 13, of which waited for: 9 -> 9; matrix products, arithmetic and copies ran while one was open for 9% -> 5% of each run, Pallas kernels for 0% -> 0%
where the time goes in v2:
time: 148 us; the launch traced here: 147 us
  starting transfers between devices  42.6 us (29%)
  waiting for transfers between devices  31.7 us (21%)
  local copies, waits for them, and re-layouts  24.8 us (17%)
  other arithmetic  21.4 us (14%)
  blocking collectives  17.3 us (12%)
  matrix products  6.91 us (5%)
  between operations  2.12 us (1%)
    all_to_all x1, blocking collectives, per_device(): lax.all_to_all(outgoing, ('gy', 'gz'), split_axis=1, concat_axis=1, tiled...  17.3 us
    ppermute x3, waiting for transfers between devices, with_halo(): lax.ppermute(lax.slice_in_dim(block, 0, width, axis=dim), axis, backward)  11.7 us
    all_to_all x1, starting transfers between devices, per_device(): lax.all_to_all(send_outgoing, ('gy', 'gz'), split_axis=1, concat_axis=1,...  11.6 us
    ppermute x3, starting transfers between devices, with_halo_pair(): low_flat = lax.ppermute(low_flat, axis, forward)  11 us
    ppermute x3, starting transfers between devices, with_halo(): lax.ppermute(lax.slice_in_dim(block, block.shape[dim] - width, None, axis...  10.8 us
    ppermute x3, waiting for transfers between devices, with_halo_pair(): high_flat = lax.ppermute(high_flat, axis, backward)  10.2 us
    all_to_all x1, waiting for transfers between devices, per_device(): lax.all_to_all(send_outgoing, ('gy', 'gz'), split_axis=1, concat_axis=1,...  7.67 us
    unnamed x130, local copies, waits for them, and re-layouts  5.31 us
  transfers between devices with their start and end apart: 13, of which 9 were waited for; matrix products, arithmetic and copies ran while one was open for 5% of the time, Pallas kernels for 0%

profile of v2, /device:TPU:1, one launch (start us, length us, event | category | flops | bytes accessed | tf_op | source)
XLA Modules:
  0.0 146.8 jit_solution(13817398875157925125)
XLA Ops:
  0.0 0.7 fusion.146
  0.9 0.9 convolution_bitcast_fusion
  2.1 0.7 copy.85
  2.8 11.6 %all-to-all-start = ((f32[4,64,16]{2,0,1:T(4,128)}), f32[4,64,16]{2,0,1:T(4,128)S(1)}, u32[]{:S(2)}, u32[]{:S(2)}) async-start(f32[4,64,16]{2,0,1:T(4,128)} %copy.85), calls=%async_computation | async-start | bytes 262144 | tf_op jit(solution)/shard_map/all_to_all | solution.py:266
  14.5 0.6 fusion.149
  15.1 0.6 fusion.147
  15.7 0.9 convert_bitcast_fusion
  16.6 0.6 iota_compare_fusion
  17.3 0.6 select_add_fusion
  17.9 7.7 %all-to-all-done = f32[4,64,16]{2,0,1:T(4,128)S(1)} async-done(((f32[4,64,16]{2,0,1:T(4,128)}), f32[4,64,16]{2,0,1:T(4,128)S(1)}, u32[]{:S(2)}, u32[]{:S(2)}) %all-to-all-start) | async-done | bytes 16416 | tf_op jit(solution)/shard_map/all_to_all | solution.py:266
  26.6 4.0 %collective-permute-start = (f32[31104]{0:T(1024)S(1)}, f32[31104]{0:T(1024)S(1)}, u32[]{:S(2)}, u32[]{:S(2)}) collective-permute-start(f32[31104]{0:T(1024)S(1)} %pad_maximum_fusion.6), channel_id=1, source_target_pairs={{0,64},{64,128},{128,192},{192,256},{256,320},{320,384},{384,448},... | collective-permute-start | bytes 373256 | tf_op jit(solution)/shard_map/ppermute | solution.py:47
  30.7 1.3 collective-permute-start.1
  32.0 1.0 collective-permute-done
  33.1 4.8 %collective-permute-done.1 = f32[31104]{0:T(1024)S(1)} collective-permute-done((f32[31104]{0:T(1024)S(1)}, f32[31104]{0:T(1024)S(1)}, u32[]{:S(2)}, u32[]{:S(2)}) %collective-permute-start.1) | collective-permute-done | bytes 124448 | tf_op jit(solution)/shard_map/ppermute | solution.py:48
  38.0 0.6 copy-done.10
  38.8 2.3 %collective-permute-start.2 = (f32[50496]{0:T(1024)S(1)}, f32[50496]{0:T(1024)S(1)}, u32[]{:S(2)}, u32[]{:S(2)}) collective-permute-start(f32[50496]{0:T(1024)S(1)} %pad_maximum_fusion.4), channel_id=1, source_target_pairs={{0,8},{8,16},{16,24},{24,32},{32,40},{40,48},{48,56},{1,9},{9,17},... | collective-permute-start | bytes 605960 | tf_op jit(solution)/shard_map/ppermute | solution.py:47
  41.3 1.3 collective-permute-start.3
  42.6 0.6 iota_compare_fusion.1
  43.2 1.1 collective-permute-done.2
  44.3 3.9 %collective-permute-done.3 = f32[50496]{0:T(1024)S(1)} collective-permute-done((f32[50496]{0:T(1024)S(1)}, f32[50496]{0:T(1024)S(1)}, u32[]{:S(2)}, u32[]{:S(2)}) %collective-permute-start.3) | collective-permute-done | bytes 202016 | tf_op jit(solution)/shard_map/ppermute | solution.py:48
  48.3 0.6 copy-done.26
  48.9 0.7 copy-done
  50.4 1.2 reshape.390
  51.5 0.7 slice.1127
  52.3 0.7 slice.1128
  53.1 0.8 pad_maximum_fusion.11
  54.2 0.9 pad_maximum_fusion.15
  55.1 4.6 %collective-permute-start.4 = (f32[10248]{0:T(1024)S(1)}, f32[10248]{0:T(1024)S(1)}, u32[]{:S(2)}, u32[]{:S(2)}) collective-permute-start(f32[10248]{0:T(1024)S(1)} %pad_maximum_fusion.15), channel_id=1, source_target_pairs={{0,1},{1,2},{2,3},{3,4},{4,5},{5,6},{6,7},{8,9},{9,10},{10,11},{11... | collective-permute-start | bytes 122984 | tf_op jit(solution)/shard_map/ppermute | solution.py:47
  59.7 0.6 reshape.395
  60.5 2.1 %collective-permute-start.5 = (f32[10248]{0:T(1024)S(1)}, f32[10248]{0:T(1024)S(1)}, u32[]{:S(2)}, u32[]{:S(2)}) collective-permute-start(f32[10248]{0:T(1024)S(1)} %pad_maximum_fusion.16), channel_id=1, source_target_pairs={{1,0},{2,1},{3,2},{4,3},{5,4},{6,5},{7,6},{9,8},{10,9},{11,10},{12... | collective-permute-start | bytes 122984 | tf_op jit(solution)/shard_map/ppermute | solution.py:48
  62.6 0.6 mul.963
  63.2 0.7 mul.969
  64.3 1.6 %collective-permute-done.5 = f32[10248]{0:T(1024)S(1)} collective-permute-done((f32[10248]{0:T(1024)S(1)}, f32[10248]{0:T(1024)S(1)}, u32[]{:S(2)}, u32[]{:S(2)}) %collective-permute-start.5) | collective-permute-done | bytes 41024 | tf_op jit(solution)/shard_map/ppermute | solution.py:48
  65.8 0.6 copy-done.34
  66.4 0.6 slice.1133
  67.1 1.1 reshape.397
  68.2 2.4 %pad_maximum_fusion = f32[3,26,26,138]{3,2,1,0:T(8,128)S(1)} fusion(f32[3,26,26,5]{3,2,1,0:T(8,128)S(1)} %reshape.397, f32[3,26,5,128]{3,2,1,0:T(8,128)} %copy-done, f32[3,5,16,128]{3,2,1,0:T(8,128)S(1)} %bitcast.442, f32[1,16,16,128]{3,2,1,0:T(8,128)S(1)} %convert_bitcast_fusion, f32[1,16,16,128]{3,2,1,0:T(8,128)S(1)} %get-tuple-element.112, ...), kind=kLoop, calls=%fused_computation | loop fusion | flops 2238912 | bytes 2238912 | tf_op jit(solution)/shard_map/concatenate | solution.py:56
  71.5 2.2 %add_multiply_fusion = (f32[22,22,134]{2,1,0:T(8,128)S(1)}, f32[22,22,134]{2,1,0:T(8,128)}, f32[22,22,134]{2,1,0:T(8,128)}) fusion(f32[22,22,138]{2,1,0:T(8,128)S(1)} %fusion.22, f32[22,22,138]{2,1,0:T(8,128)S(1)} %fusion.30), kind=kLoop, calls=%fused_computation.87 | loop fusion | flops 1297120 | bytes 3372512 | tf_op jit(solution)/shard_map/mul | solution.py:77
  73.7 1.1 fusion.168
  74.8 0.9 fusion.169
  76.0 0.8 slice.1181
  77.0 0.8 slice.1182
  78.5 1.4 fusion.44
  79.9 1.4 fusion.42
  82.3 1.4 multiply_reduce_fusion.3
  85.6 0.9 squeeze.79
  86.6 0.9 squeeze.81
  87.5 0.9 squeeze.83
  88.9 0.7 copy-done.3
  89.8 1.1 fusion.35
  91.1 1.4 multiply_reduce_fusion.5
  94.0 4.0 %collective-permute-start.6 = (f32[3,1,4,32]{3,2,1,0:T(4,128)S(1)}, f32[3,1,4,32]{3,2,1,0:T(4,128)S(1)}, u32[]{:S(2)}, u32[]{:S(2)}) collective-permute-start(f32[3,1,4,32]{3,2,1,0:T(4,128)S(1)} %get-tuple-element.106), channel_id=1, source_target_pairs={{0,64},{64,128},{128,192},{192,256},{256,320},{320,384},{384,448},... | collective-permute-start | bytes 4616 | tf_op jit(solution)/shard_map/ppermute | solution.py:24
  98.0 1.3 collective-permute-start.7
  99.3 4.9 %collective-permute-done.7 = f32[3,1,4,32]{3,2,1,0:T(4,128)S(1)} collective-permute-done((f32[3,1,4,32]{3,2,1,0:T(4,128)S(1)}, f32[3,1,4,32]{3,2,1,0:T(4,128)S(1)}, u32[]{:S(2)}, u32[]{:S(2)}) %collective-permute-start.7) | collective-permute-done | bytes 1568 | tf_op jit(solution)/shard_map/ppermute | solution.py:27
  104.3 1.9 %collective-permute-start.8 = (f32[3,6,1,32]{3,2,1,0:T(1,128)S(1)}, f32[3,6,1,32]{3,2,1,0:T(1,128)S(1)}, u32[]{:S(2)}, u32[]{:S(2)}) collective-permute-start(f32[3,6,1,32]{3,2,1,0:T(1,128)S(1)} %get-tuple-element.104), channel_id=1, source_target_pairs={{0,8},{8,16},{16,24},{24,32},{32,40},{40,48},{48,56},{1,9},{9,17},... | collective-permute-start | bytes 6920 | tf_op jit(solution)/shard_map/ppermute | solution.py:24
  106.2 1.3 collective-permute-start.9
  107.5 3.1 %collective-permute-done.9 = f32[3,6,1,32]{3,2,1,0:T(1,128)S(1)} collective-permute-done((f32[3,6,1,32]{3,2,1,0:T(1,128)S(1)}, f32[3,6,1,32]{3,2,1,0:T(1,128)S(1)}, u32[]{:S(2)}, u32[]{:S(2)}) %collective-permute-start.9) | collective-permute-done | bytes 2336 | tf_op jit(solution)/shard_map/ppermute | solution.py:27
  110.7 4.9 %collective-permute-start.10 = (f32[3,6,6,1]{3,2,1,0:T(8,128)S(1)}, f32[3,6,6,1]{3,2,1,0:T(8,128)S(1)}, u32[]{:S(2)}, u32[]{:S(2)}) collective-permute-start(f32[3,6,6,1]{3,2,1,0:T(8,128)S(1)} %get-tuple-element.96), channel_id=1, source_target_pairs={{0,1},{1,2},{2,3},{3,4},{4,5},{5,6},{6,7},{8,9},{9,10},{10,11},{11... | collective-permute-start | bytes 1304 | tf_op jit(solution)/shard_map/ppermute | solution.py:24
  115.6 1.9 %collective-permute-start.11 = (f32[3,6,6,1]{3,2,1,0:T(8,128)S(1)}, f32[3,6,6,1]{3,2,1,0:T(8,128)S(1)}, u32[]{:S(2)}, u32[]{:S(2)}) collective-permute-start(f32[3,6,6,1]{3,2,1,0:T(8,128)S(1)} %get-tuple-element.97), channel_id=1, source_target_pairs={{1,0},{2,1},{3,2},{4,3},{5,4},{6,5},{7,6},{9,8},{10,9},{11,10},{12... | collective-permute-start | bytes 1304 | tf_op jit(solution)/shard_map/ppermute | solution.py:27
  117.6 3.7 %collective-permute-done.11 = f32[3,6,6,1]{3,2,1,0:T(8,128)S(1)} collective-permute-done((f32[3,6,6,1]{3,2,1,0:T(8,128)S(1)}, f32[3,6,6,1]{3,2,1,0:T(8,128)S(1)}, u32[]{:S(2)}, u32[]{:S(2)}) %collective-permute-start.11) | collective-permute-done | bytes 464 | tf_op jit(solution)/shard_map/ppermute | solution.py:27
  123.6 1.2 fusion.37
  125.1 1.4 multiply_reduce_fusion.1
  128.5 17.3 %all_to_all.18 = f32[3,64,16]{2,0,1:T(4,128)S(1)} all-to-all(f32[3,64,16]{2,0,1:T(4,128)S(1)} %copy.103), channel_id=1, replica_groups=mesh['gx'=8,'gy'=8,'gz'=8] {'gy','gz'}, dimensions={1} | all-to-all | bytes 24576 | tf_op jit(solution)/shard_map/all_to_all | solution.py:299
  145.9 0.9 convolution_bitcast_fusion.1
  (311 shorter events, 14.7 us)
Async XLA Ops:
  0.0 17.2 %copy-start.30 = (bf16[16,16,128]{2,1,0:T(8,128)(2,1)S(1)}, bf16[16,16,128]{2,1,0:T(8,128)(2,1)}, u32[]{:S(2)}) copy-start(bf16[16,16,128]{2,1,0:T(8,128)(2,1)} %param.5) | copy-start | bytes 196612
  0.0 17.2 %copy-start.29 = (bf16[16,16,128]{2,1,0:T(8,128)(2,1)S(1)}, bf16[16,16,128]{2,1,0:T(8,128)(2,1)}, u32[]{:S(2)}) copy-start(bf16[16,16,128]{2,1,0:T(8,128)(2,1)} %param.6) | copy-start | bytes 196612
  0.9 0.9 copy-start.60
  2.8 22.7 %all-to-all-start = ((f32[4,64,16]{2,0,1:T(4,128)}), f32[4,64,16]{2,0,1:T(4,128)S(1)}, u32[]{:S(2)}, u32[]{:S(2)}) async-start(f32[4,64,16]{2,0,1:T(4,128)} %copy.85), calls=%async_computation | async-start | bytes 262144 | tf_op jit(solution)/shard_map/all_to_all | solution.py:266
  14.5 11.1 %copy-start.35 = (s32[132]{0:T(256)}, s32[132]{0:T(256)S(1)}, u32[]{:S(2)}) copy-start(s32[132]{0:T(256)S(1)} %get-tuple-element.115) | copy-start | bytes 1588
  15.7 9.9 %copy-start.37 = (f32[132]{0:T(256)}, f32[132]{0:T(256)S(1)}, u32[]{:S(2)}) copy-start(f32[132]{0:T(256)S(1)} %get-tuple-element.116) | copy-start | bytes 1588
  15.7 9.9 %copy-start.40 = (f32[132]{0:T(256)}, f32[132]{0:T(256)S(1)}, u32[]{:S(2)}) copy-start(f32[132]{0:T(256)S(1)} %get-tuple-element.117) | copy-start | bytes 1588
  17.9 20.7 %copy-start.62 = (f32[64]{0:T(128)}, f32[64]{0:T(128)S(1)}, u32[]{:S(2)}) copy-start(f32[64]{0:T(128)S(1)} %add_convert_fusion) | copy-start | bytes 772
  25.8 4.9 %copy-start.56 = (f32[128]{0:T(128)}, f32[128]{0:T(128)S(1)}, u32[]{:S(2)}) copy-start(f32[128]{0:T(128)S(1)} %slice_reduce_fusion.2) | copy-start | bytes 1540
  26.6 6.4 %collective-permute-start = (f32[31104]{0:T(1024)S(1)}, f32[31104]{0:T(1024)S(1)}, u32[]{:S(2)}, u32[]{:S(2)}) collective-permute-start(f32[31104]{0:T(1024)S(1)} %pad_maximum_fusion.6), channel_id=1, source_target_pairs={{0,64},{64,128},{128,192},{192,256},{256,320},{320,384},{384,448},... | collective-permute-start | bytes 373256 | tf_op jit(solution)/shard_map/ppermute | solution.py:47
  30.7 7.1 %collective-permute-start.1 = (f32[31104]{0:T(1024)S(1)}, f32[31104]{0:T(1024)S(1)}, u32[]{:S(2)}, u32[]{:S(2)}) collective-permute-start(f32[31104]{0:T(1024)S(1)} %pad_maximum_fusion.7), channel_id=1, source_target_pairs={{64,0},{128,64},{192,128},{256,192},{320,256},{384,320},{448,384},... | collective-permute-start | bytes 373256 | tf_op jit(solution)/shard_map/ppermute | solution.py:48
  38.8 5.5 %collective-permute-start.2 = (f32[50496]{0:T(1024)S(1)}, f32[50496]{0:T(1024)S(1)}, u32[]{:S(2)}, u32[]{:S(2)}) collective-permute-start(f32[50496]{0:T(1024)S(1)} %pad_maximum_fusion.4), channel_id=1, source_target_pairs={{0,8},{8,16},{16,24},{24,32},{32,40},{40,48},{48,56},{1,9},{9,17},... | collective-permute-start | bytes 605960 | tf_op jit(solution)/shard_map/ppermute | solution.py:47
  41.3 7.0 %collective-permute-start.3 = (f32[50496]{0:T(1024)S(1)}, f32[50496]{0:T(1024)S(1)}, u32[]{:S(2)}, u32[]{:S(2)}) collective-permute-start(f32[50496]{0:T(1024)S(1)} %pad_maximum_fusion.5), channel_id=1, source_target_pairs={{8,0},{16,8},{24,16},{32,24},{40,32},{48,40},{56,48},{9,1},{17,9},... | collective-permute-start | bytes 605960 | tf_op jit(solution)/shard_map/ppermute | solution.py:48
  44.3 4.0 %copy-start.25 = (f32[50496]{0:T(1024)}, f32[50496]{0:T(1024)S(1)}, u32[]{:S(2)}) copy-start(f32[50496]{0:T(1024)S(1)} %collective-permute-done.2) | copy-start | bytes 605956
  48.9 0.8 copy-start
  53.1 6.6 %copy-start.27 = (f32[3,6,1,32]{3,2,1,0:T(1,128)}, f32[3,6,1,32]{3,2,1,0:T(1,128)S(1)}, u32[]{:S(2)}) copy-start(f32[3,6,1,32]{3,2,1,0:T(1,128)S(1)} %reshape.392) | copy-start | bytes 6916
  55.1 8.9 %collective-permute-start.4 = (f32[10248]{0:T(1024)S(1)}, f32[10248]{0:T(1024)S(1)}, u32[]{:S(2)}, u32[]{:S(2)}) collective-permute-start(f32[10248]{0:T(1024)S(1)} %pad_maximum_fusion.15), channel_id=1, source_target_pairs={{0,1},{1,2},{2,3},{3,4},{4,5},{5,6},{6,7},{8,9},{9,10},{10,11},{11... | collective-permute-start | bytes 122984 | tf_op jit(solution)/shard_map/ppermute | solution.py:47
  60.5 5.4 %collective-permute-start.5 = (f32[10248]{0:T(1024)S(1)}, f32[10248]{0:T(1024)S(1)}, u32[]{:S(2)}, u32[]{:S(2)}) collective-permute-start(f32[10248]{0:T(1024)S(1)} %pad_maximum_fusion.16), channel_id=1, source_target_pairs={{1,0},{2,1},{3,2},{4,3},{5,4},{6,5},{7,6},{9,8},{10,9},{11,10},{12... | collective-permute-start | bytes 122984 | tf_op jit(solution)/shard_map/ppermute | solution.py:48
  62.6 3.2 %copy-start.43 = (f32[4]{0:T(128)}, f32[4]{0:T(128)S(1)}, u32[]{:S(2)}) copy-start(f32[4]{0:T(128)S(1)} %get-tuple-element.118) | copy-start | bytes 52
  62.6 3.2 %copy-start.45 = (f32[4]{0:T(128)}, f32[4]{0:T(128)S(1)}, u32[]{:S(2)}) copy-start(f32[4]{0:T(128)S(1)} %get-tuple-element.119) | copy-start | bytes 52
  63.9 1.9 %copy-start.33 = (f32[10248]{0:T(1024)}, f32[10248]{0:T(1024)S(1)}, u32[]{:S(2)}) copy-start(f32[10248]{0:T(1024)S(1)} %collective-permute-done.4) | copy-start | bytes 122980
  75.7 2.3 %copy-start.11 = (f32[3,6,4,32]{3,2,1,0:T(4,128)S(1)}, f32[3,6,4,32]{3,2,1,0:T(4,128)}, u32[]{:S(2)}) copy-start(f32[3,6,4,32]{3,2,1,0:T(4,128)} %copy-done.10) | copy-start | bytes 27652
  75.7 2.3 %copy-start.28 = (f32[3,6,1,32]{3,2,1,0:T(1,128)S(1)}, f32[3,6,1,32]{3,2,1,0:T(1,128)}, u32[]{:S(2)}) copy-start(f32[3,6,1,32]{3,2,1,0:T(1,128)} %copy-done.27) | copy-start | bytes 6916
  75.9 2.3 %copy-start.36 = (s32[132]{0:T(256)S(1)}, s32[132]{0:T(256)}, u32[]{:S(2)}) copy-start(s32[132]{0:T(256)} %copy-done.35) | copy-start | bytes 1588
  75.9 2.3 %copy-start.38 = (f32[132]{0:T(256)S(1)}, f32[132]{0:T(256)}, u32[]{:S(2)}) copy-start(f32[132]{0:T(256)} %copy-done.37) | copy-start | bytes 1588
  75.9 2.3 %copy-start.41 = (f32[132]{0:T(256)S(1)}, f32[132]{0:T(256)}, u32[]{:S(2)}) copy-start(f32[132]{0:T(256)} %copy-done.40) | copy-start | bytes 1588
  75.9 2.6 %copy-start.6 = (f32[20,22,134]{2,1,0:T(8,128)S(1)}, f32[20,22,134]{2,1,0:T(8,128)}, u32[]{:S(2)}) copy-start(f32[20,22,134]{2,1,0:T(8,128)} %get-tuple-element.62) | copy-start | bytes 707524
  79.9 2.1 %copy-start.12 = (bf16[20,20,132]{2,0,1:T(8,128)(2,1)}, bf16[20,20,132]{2,0,1:T(8,128)(2,1)S(1)}, u32[]{:S(2)}) copy-start(bf16[20,20,132]{2,0,1:T(8,128)(2,1)S(1)} %copy.109) | copy-start | bytes 316804
  81.4 0.7 copy-start.15
  81.6 0.7 copy-start.49
  81.7 2.0 %copy-start.18 = (bf16[20,20,132]{2,0,1:T(8,128)(2,1)}, bf16[20,20,132]{2,0,1:T(8,128)(2,1)S(1)}, u32[]{:S(2)}) copy-start(bf16[20,20,132]{2,0,1:T(8,128)(2,1)S(1)} %copy.111) | copy-start | bytes 316804
  82.0 1.7 %copy-start.7 = (f32[20,20,132]{2,0,1:T(8,128)}, f32[20,20,132]{2,0,1:T(8,128)S(1)}, u32[]{:S(2)}) copy-start(f32[20,20,132]{2,0,1:T(8,128)S(1)} %copy.112) | copy-start | bytes 633604
  83.9 10.0 %copy-start.21 = (f32[3,5,4,32]{3,2,1,0:T(4,128)}, f32[3,5,4,32]{3,2,1,0:T(4,128)S(1)}, u32[]{:S(2)}) copy-start(f32[3,5,4,32]{3,2,1,0:T(4,128)S(1)} %get-tuple-element.13) | copy-start | bytes 23044
  83.9 10.0 %copy-start.23 = (f32[3,5,4,32]{3,2,1,0:T(4,128)}, f32[3,5,4,32]{3,2,1,0:T(4,128)S(1)}, u32[]{:S(2)}) copy-start(f32[3,5,4,32]{3,2,1,0:T(4,128)S(1)} %get-tuple-element.14) | copy-start | bytes 23044
  87.5 1.2 copy-start.1
  87.5 1.4 copy-start.2
  88.4 1.1 copy-start.3
  88.4 1.2 copy-start.4
  88.4 1.4 copy-start.5
  89.8 1.2 copy-start.8
  89.8 1.3 copy-start.13
  89.8 1.3 copy-start.16
  89.8 1.3 copy-start.19
  89.8 1.3 copy-start.31
  93.3 28.2 %copy-start.39 = (f32[132]{0:T(256)S(1)}, f32[132]{0:T(256)}, u32[]{:S(2)}) copy-start(f32[132]{0:T(256)} %copy-done.37) | copy-start | bytes 1588
  93.3 28.2 %copy-start.42 = (f32[132]{0:T(256)S(1)}, f32[132]{0:T(256)}, u32[]{:S(2)}) copy-start(f32[132]{0:T(256)} %copy-done.40) | copy-start | bytes 1588
  94.0 5.3 %collective-permute-start.6 = (f32[3,1,4,32]{3,2,1,0:T(4,128)S(1)}, f32[3,1,4,32]{3,2,1,0:T(4,128)S(1)}, u32[]{:S(2)}, u32[]{:S(2)}) collective-permute-start(f32[3,1,4,32]{3,2,1,0:T(4,128)S(1)} %get-tuple-element.106), channel_id=1, source_target_pairs={{0,64},{64,128},{128,192},{192,256},{256,320},{320,384},{384,448},... | collective-permute-start | bytes 4616 | tf_op jit(solution)/shard_map/ppermute | solution.py:24
  98.0 23.9 %copy-start.51 = (f32[20]{0:T(128)S(1)}, f32[20]{0:T(128)}, u32[]{:S(2)}) copy-start(f32[20]{0:T(128)} %mul.963) | copy-start | bytes 244
  98.0 23.9 %copy-start.53 = (f32[20]{0:T(128)S(1)}, f32[20]{0:T(128)}, u32[]{:S(2)}) copy-start(f32[20]{0:T(128)} %mul.969) | copy-start | bytes 244
  98.0 6.2 %collective-permute-start.7 = (f32[3,1,4,32]{3,2,1,0:T(4,128)S(1)}, f32[3,1,4,32]{3,2,1,0:T(4,128)S(1)}, u32[]{:S(2)}, u32[]{:S(2)}) collective-permute-start(f32[3,1,4,32]{3,2,1,0:T(4,128)S(1)} %get-tuple-element.107), channel_id=1, source_target_pairs={{64,0},{128,64},{192,128},{256,192},{320,256},{384,320},{448,384},... | collective-permute-start | bytes 4616 | tf_op jit(solution)/shard_map/ppermute | solution.py:27
  104.3 3.2 %collective-permute-start.8 = (f32[3,6,1,32]{3,2,1,0:T(1,128)S(1)}, f32[3,6,1,32]{3,2,1,0:T(1,128)S(1)}, u32[]{:S(2)}, u32[]{:S(2)}) collective-permute-start(f32[3,6,1,32]{3,2,1,0:T(1,128)S(1)} %get-tuple-element.104), channel_id=1, source_target_pairs={{0,8},{8,16},{16,24},{24,32},{32,40},{40,48},{48,56},{1,9},{9,17},... | collective-permute-start | bytes 6920 | tf_op jit(solution)/shard_map/ppermute | solution.py:24
  106.2 4.4 %collective-permute-start.9 = (f32[3,6,1,32]{3,2,1,0:T(1,128)S(1)}, f32[3,6,1,32]{3,2,1,0:T(1,128)S(1)}, u32[]{:S(2)}, u32[]{:S(2)}) collective-permute-start(f32[3,6,1,32]{3,2,1,0:T(1,128)S(1)} %get-tuple-element.105), channel_id=1, source_target_pairs={{8,0},{16,8},{24,16},{32,24},{40,32},{48,40},{56,48},{9,1},{17,9},... | collective-permute-start | bytes 6920 | tf_op jit(solution)/shard_map/ppermute | solution.py:27
  110.7 6.9 %collective-permute-start.10 = (f32[3,6,6,1]{3,2,1,0:T(8,128)S(1)}, f32[3,6,6,1]{3,2,1,0:T(8,128)S(1)}, u32[]{:S(2)}, u32[]{:S(2)}) collective-permute-start(f32[3,6,6,1]{3,2,1,0:T(8,128)S(1)} %get-tuple-element.96), channel_id=1, source_target_pairs={{0,1},{1,2},{2,3},{3,4},{4,5},{5,6},{6,7},{8,9},{9,10},{10,11},{11... | collective-permute-start | bytes 1304 | tf_op jit(solution)/shard_map/ppermute | solution.py:24
  115.6 5.7 %collective-permute-start.11 = (f32[3,6,6,1]{3,2,1,0:T(8,128)S(1)}, f32[3,6,6,1]{3,2,1,0:T(8,128)S(1)}, u32[]{:S(2)}, u32[]{:S(2)}) collective-permute-start(f32[3,6,6,1]{3,2,1,0:T(8,128)S(1)} %get-tuple-element.97), channel_id=1, source_target_pairs={{1,0},{2,1},{3,2},{4,3},{5,4},{6,5},{7,6},{9,8},{10,9},{11,10},{12... | collective-permute-start | bytes 1304 | tf_op jit(solution)/shard_map/ppermute | solution.py:27
  123.6 1.4 copy-start.9
  123.6 1.4 copy-start.14
  123.6 1.4 copy-start.17
  123.6 1.4 copy-start.20
  123.6 1.4 copy-start.32
  126.7 1.0 copy-start.22
  126.7 1.0 copy-start.24
  126.9 1.0 copy-start.57
  126.9 1.0 copy-start.63
  127.3 18.7 %copy-start.61 = (s32[64]{0:T(128)S(1)}, s32[64]{0:T(128)}, u32[]{:S(2)}) copy-start(s32[64]{0:T(128)} %copy-done.60) | copy-start | bytes 772
  (13 other events, 8.7 us)

commit v3 on v2

--- a/solution.py
+++ b/solution.py
@@ -222,60 +222,108 @@
     return collect_axis(reduced, 1, ELEM, squared)
 
 
+NEIGHBOURS = [(0, 0)] + [(ry, rz) for ry in (-1, 0, 1) for rz in (-1, 0, 1) if (ry, rz) != (0, 0)]
+HALO_CAP = 10
+
+
 def per_device(reference_image, deformed_image, roi_mask, displacement, node_map):
-    stacked = jnp.stack(
-        [
-            reference_image.astype(jnp.float32),
-            deformed_image.astype(jnp.float32),
-            roi_mask.astype(jnp.float32),
-        ]
-    )
+    stacked = jnp.stack([reference_image, deformed_image, roi_mask.astype(jnp.bfloat16)])
+    stacked = with_halo(stacked, (("gy", 2), ("gz", 3)), 5).astype(jnp.float32)
     nodes_shape = (
         3,
         reference_image.shape[0] // ELEM,
         reference_image.shape[1] // ELEM,
         reference_image.shape[2] // ELEM,
     )
-    weights_table = axis_table(nodes_shape[3] + 2, ELEM, False)
+    _, ex, ey, ez = nodes_shape
+    weights_table = axis_table(ez + 2, ELEM, False)
     table_back = weights_table[1:-1].T
-    table_square = axis_table(nodes_shape[3] + 2, ELEM, True)[1:-1].T
-    members = lax.axis_size(("gy", "gz"))
+    table_square = axis_table(ez + 2, ELEM, True)[1:-1].T
+    size_y = lax.axis_size("gy")
+    size_z = lax.axis_size("gz")
+    members = size_y * size_z
     blocks = node_map.shape[0]
     block_nodes = displacement.shape[2]
+    zchunks = ez // block_nodes
     owner_tile = node_map // blocks
     tile_block = node_map % blocks
-    position = jnp.arange(blocks, dtype=jnp.int32)
-    earlier = (owner_tile[:, None] == owner_tile[None, :]) & (position[None, :] < position[:, None])
+    tile_y = owner_tile // size_z
+    tile_z = owner_tile % size_z
+    block_y = (tile_block // zchunks) % ey
+    block_zc = tile_block % zchunks
+    dests, valids, labels = [], [], []
+    for index, (ry, rz) in enumerate(NEIGHBOURS):
+        dest_y = tile_y - ry
+        dest_z = tile_z - rz
+        valid = (dest_y >= 0) & (dest_y < size_y) & (dest_z >= 0) & (dest_z < size_z)
+        if ry == -1:
+            valid = valid & (block_y == ey - 1)
+        elif ry == 1:
+            valid = valid & (block_y == 0)
+        if rz == -1:
+            valid = valid & (block_zc == zchunks - 1)
+        elif rz == 1:
+            valid = valid & (block_zc == 0)
+        dests.append(dest_y * size_z + dest_z)
+        valids.append(valid)
+        labels.append(index * blocks + tile_block + 1)
+    cand_dest = jnp.concatenate(dests)
+    cand_valid = jnp.concatenate(valids)
+    cand_label = jnp.concatenate(labels).astype(jnp.float32)
+    count = cand_dest.shape[0]
+    order = jnp.arange(count, dtype=jnp.int32)
+    earlier = (
+        (cand_dest[:, None] == cand_dest[None, :])
+        & cand_valid[None, :]
+        & (order[None, :] < order[:, None])
+    )
     ranking = jnp.sum(earlier.astype(jnp.int32), axis=1)
-    target_slot = owner_tile * CAP + ranking
-    packing = (target_slot[:, None] == jnp.arange(members * CAP, dtype=jnp.int32)[None, :]).astype(
-        jnp.float32
-    )
-    labelled = jnp.concatenate(
-        [
-            displacement,
-            jnp.broadcast_to(
-                (tile_block + 1).astype(jnp.float32)[None, :, None], (1, blocks, block_nodes)
-            ),
+    target_slot = jnp.where(cand_valid, cand_dest * HALO_CAP + ranking, -1)
+    packing = (
+        target_slot[:, None] == jnp.arange(members * HALO_CAP, dtype=jnp.int32)[None, :]
+    ).astype(jnp.float32)
+    cand_data = jnp.concatenate(
+        [
+            jnp.concatenate([displacement] * len(NEIGHBOURS), axis=1),
+            jnp.broadcast_to(cand_label[None, :, None], (1, count, block_nodes)),
         ]
     )
-    send_channels = labelled.shape[0]
-    send_outgoing = jnp.einsum("cjn,jp->cpn", labelled, packing, precision=highest).reshape(
+    send_channels = cand_data.shape[0]
+    send_outgoing = jnp.einsum("cjn,jp->cpn", cand_data, packing, precision=highest).reshape(
         send_channels, -1
     )
     send_incoming = lax.all_to_all(
         send_outgoing, ("gy", "gz"), split_axis=1, concat_axis=1, tiled=True
-    ).reshape(send_channels, members * CAP, block_nodes)
+    ).reshape(send_channels, members * HALO_CAP, block_nodes)
     received_labels = send_incoming[3, :, 0]
-    send_placing = (
-        received_labels[:, None] == (position + 1).astype(jnp.float32)[None, :]
+    placing = (
+        received_labels[:, None] == jnp.arange(1, count + 1, dtype=jnp.float32)[None, :]
     ).astype(jnp.float32)
-    tile_values = jnp.einsum(
-        "cpn,pk->ckn", send_incoming[:3], send_placing, precision=highest
-    ).reshape(nodes_shape)
-    padded_images, first_padded = with_halo_pair(
-        stacked, tile_values, (("gx", 1, 1), ("gy", 2, 2), ("gz", 3, 3)), (5, 1)
-    )
+    around = jnp.einsum("cpn,pk->ckn", send_incoming[:3], placing, precision=highest).reshape(
+        3, len(NEIGHBOURS), ex, ey, ez
+    )
+
+    def near(ry, rz):
+        return around[:, NEIGHBOURS.index((ry, rz))]
+
+    tile_values = near(0, 0)
+    middle = jnp.concatenate(
+        [near(0, -1)[..., ez - 1 :], tile_values, near(0, 1)[..., :1]], axis=3
+    )
+    low_row = jnp.concatenate(
+        [
+            near(-1, -1)[:, :, ey - 1 :, ez - 1 :],
+            near(-1, 0)[:, :, ey - 1 :, :],
+            near(-1, 1)[:, :, ey - 1 :, :1],
+        ],
+        axis=3,
+    )
+    high_row = jnp.concatenate(
+        [near(1, -1)[:, :, :1, ez - 1 :], near(1, 0)[:, :, :1, :], near(1, 1)[:, :, :1, :1]],
+        axis=3,
+    )
+    extended = jnp.concatenate([low_row, middle, high_row], axis=2)
+    padded_images, first_padded = with_halo_pair(stacked, extended, (("gx", 1, 1),), (5, 1))
     derived = derive_fields(padded_images[0], padded_images[1])
     region = padded_images[2][3:-3, 3:-3, 3:-3]
     contrast = derived[0].astype(jnp.float32)
@@ -293,12 +341,21 @@
         force_total = image_part + elastic_weight * elastic_force(padded)
         tile_values = tile_values - force_total / curvature
     final_blocks = tile_values.reshape(3, blocks, block_nodes)
-    outgoing = jnp.einsum("ckn,pk->cpn", final_blocks, send_placing, precision=highest).reshape(
+    own_labels = received_labels.reshape(members, HALO_CAP)[:, :CAP].reshape(-1)
+    position = jnp.arange(blocks, dtype=jnp.int32)
+    back_placing = (own_labels[:, None] == (position + 1).astype(jnp.float32)[None, :]).astype(
+        jnp.float32
+    )
+    outgoing = jnp.einsum("ckn,pk->cpn", final_blocks, back_placing, precision=highest).reshape(
         3, -1
     )
     incoming = lax.all_to_all(outgoing, ("gy", "gz"), split_axis=1, concat_axis=1, tiled=True)
+    own_slot = owner_tile * CAP + ranking[:blocks]
+    back_packing = (
+        own_slot[:, None] == jnp.arange(members * CAP, dtype=jnp.int32)[None, :]
+    ).astype(jnp.float32)
     return jnp.einsum(
-        "cpn,jp->cjn", incoming.reshape(3, members * CAP, -1), packing, precision=highest
+        "cpn,jp->cjn", incoming.reshape(3, members * CAP, -1), back_packing, precision=highest
     )
 
 

time: 148 us -> 152 us (1.027)
  blocking collectives: 17.3 us -> 0 us
  starting transfers between devices: 42.6 us -> 57.8 us
  other arithmetic: 21.4 us -> 26.5 us
    all_to_all x1 -> x0, blocking collectives: 17.3 us -> none  [per_device(): lax.all_to_all(outgoing, ('gy', 'gz'), split_axis=1, concat_axis=1, tiled...]
    ppermute x3 -> x5, starting transfers between devices: 10.8 us -> 22 us  [with_halo(): lax.ppermute(lax.slice_in_dim(block, block.shape[dim] - width, None, axis...]
    all_to_all x0 -> x1, waiting for transfers between devices: none -> 10.4 us  [per_device(): lax.all_to_all(outgoing, ('gy', 'gz'), split_axis=1, concat_axis=1, tiled...]
    all_to_all x0 -> x1, starting transfers between devices: none -> 9.25 us  [per_device(): lax.all_to_all(outgoing, ('gy', 'gz'), split_axis=1, concat_axis=1, tiled...]
    all_to_all x1, waiting for transfers between devices: 7.67 us -> 0.01 us  [per_device(): lax.all_to_all(send_outgoing, ('gy', 'gz'), split_axis=1, concat_axis=1,...]
    add x42 -> x43, other arithmetic: 0.26 us -> 7.28 us  [pair_op(): lax.slice_in_dim(volume, 1, length, axis=dimension)]
    ppermute x3 -> x1, starting transfers between devices: 11 us -> 4 us  [with_halo_pair(): low_flat = lax.ppermute(low_flat, axis, forward)]
    ppermute x3 -> x1, waiting for transfers between devices: 10.2 us -> 4.37 us  [with_halo_pair(): high_flat = lax.ppermute(high_flat, axis, backward)]
  transfers between devices with their start and end apart: 13 -> 14, of which waited for: 9 -> 8; matrix products, arithmetic and copies ran while one was open for 5% -> 8% of each run, Pallas kernels for 0% -> 0%
where the time goes in v3:
time: 152 us; the launch traced here: 151 us
  starting transfers between devices  57.8 us (38%)
  waiting for transfers between devices  32.8 us (22%)
  other arithmetic  26.5 us (17%)
  local copies, waits for them, and re-layouts  23.9 us (16%)
  matrix products  8.03 us (5%)
  between operations  1.94 us (1%)
    ppermute x5, starting transfers between devices, with_halo(): lax.ppermute(lax.slice_in_dim(block, block.shape[dim] - width, None, axis...  22 us
    ppermute x5, waiting for transfers between devices, with_halo(): lax.ppermute(lax.slice_in_dim(block, 0, width, axis=dim), axis, backward)  15.8 us
    all_to_all x1, starting transfers between devices, per_device(): lax.all_to_all(send_outgoing, ('gy', 'gz'), split_axis=1, concat_axis=1,...  13.3 us
    all_to_all x1, waiting for transfers between devices, per_device(): lax.all_to_all(outgoing, ('gy', 'gz'), split_axis=1, concat_axis=1, tiled...  10.4 us
    all_to_all x1, starting transfers between devices, per_device(): lax.all_to_all(outgoing, ('gy', 'gz'), split_axis=1, concat_axis=1, tiled...  9.25 us
    ppermute x5, starting transfers between devices, with_halo(): lax.ppermute(lax.slice_in_dim(block, 0, width, axis=dim), axis, backward)  7.72 us
    add x43, other arithmetic, pair_op(): lax.slice_in_dim(volume, 1, length, axis=dimension)  7.28 us
    ppermute x1, waiting for transfers between devices, with_halo_pair(): high_flat = lax.ppermute(high_flat, axis, backward)  4.37 us
  transfers between devices with their start and end apart: 14, of which 8 were waited for; matrix products, arithmetic and copies ran while one was open for 8% of the time, Pallas kernels for 0%

profile of v3, /device:TPU:1, one launch (start us, length us, event | category | flops | bytes accessed | tf_op | source)
XLA Modules:
  0.0 151.0 jit_solution(7082936421173629391)
XLA Ops:
  0.0 0.9 convert_bitcast_fusion
  0.9 0.9 pad_maximum_fusion.5
  1.9 4.0 %collective-permute-start = (bf16[3,16,5,128]{3,2,1,0:T(8,128)(2,1)S(1)}, bf16[3,16,5,128]{3,2,1,0:T(8,128)(2,1)S(1)}, u32[]{:S(2)}, u32[]{:S(2)}) collective-permute-start(bf16[3,16,5,128]{3,2,1,0:T(8,128)(2,1)S(1)} %get-tuple-element.101), channel_id=1, source_target_pairs={{0,8},{8,16},{16,24},{24,32},{32,40},{40,48},{48,56},{1,9},{9,17},... | collective-permute-start | bytes 184328 | tf_op jit(solution)/shard_map/ppermute | solution.py:24
  5.9 1.3 collective-permute-start.1
  7.2 0.7 broadcast_add_fusion.1
  7.9 1.2 and_and_fusion
  10.3 1.1 concatenate.77
  11.5 0.7 fusion.7
  12.9 0.7 copy.127
  13.7 13.3 %all-to-all-start = ((f32[4,64,80]{2,0,1:T(4,128)}), f32[4,64,80]{2,0,1:T(4,128)S(1)}, u32[]{:S(2)}, u32[]{:S(2)}) async-start(f32[4,64,80]{2,0,1:T(4,128)} %copy.127), calls=%async_computation | async-start | bytes 262144 | tf_op jit(solution)/shard_map/all_to_all | solution.py:295
  27.6 0.6 iota_compare_fusion.6
  28.3 0.6 select_add_fusion
  28.9 0.6 fusion.180
  29.9 3.5 %collective-permute-start.2 = (bf16[3,16,26,5]{3,2,1,0:T(8,128)(2,1)S(1)}, bf16[3,16,26,5]{3,2,1,0:T(8,128)(2,1)S(1)}, u32[]{:S(2)}, u32[]{:S(2)}) collective-permute-start(bf16[3,16,26,5]{3,2,1,0:T(8,128)(2,1)S(1)} %get-tuple-element.74), channel_id=1, source_target_pairs={{0,1},{1,2},{2,3},{3,4},{4,5},{5,6},{6,7},{8,9},{9,10},{10,11},{11... | collective-permute-start | bytes 37448 | tf_op jit(solution)/shard_map/ppermute | solution.py:24
  33.4 1.9 %collective-permute-start.3 = (bf16[3,16,26,5]{3,2,1,0:T(8,128)(2,1)S(1)}, bf16[3,16,26,5]{3,2,1,0:T(8,128)(2,1)S(1)}, u32[]{:S(2)}, u32[]{:S(2)}) collective-permute-start(bf16[3,16,26,5]{3,2,1,0:T(8,128)(2,1)S(1)} %get-tuple-element.75), channel_id=1, source_target_pairs={{1,0},{2,1},{3,2},{4,3},{5,4},{6,5},{7,6},{9,8},{10,9},{11,10},{12... | collective-permute-start | bytes 37448 | tf_op jit(solution)/shard_map/ppermute | solution.py:27
  35.4 0.6 mul.999
  36.0 0.6 mul.993
  36.6 1.5 %collective-permute-done.2 = bf16[3,16,26,5]{3,2,1,0:T(8,128)(2,1)S(1)} collective-permute-done((bf16[3,16,26,5]{3,2,1,0:T(8,128)(2,1)S(1)}, bf16[3,16,26,5]{3,2,1,0:T(8,128)(2,1)S(1)}, u32[]{:S(2)}, u32[]{:S(2)}) %collective-permute-start.2) | collective-permute-done | bytes 12512 | tf_op jit(solution)/shard_map/ppermute | solution.py:24
  38.2 4.4 %collective-permute-done.3 = bf16[3,16,26,5]{3,2,1,0:T(8,128)(2,1)S(1)} collective-permute-done((bf16[3,16,26,5]{3,2,1,0:T(8,128)(2,1)S(1)}, bf16[3,16,26,5]{3,2,1,0:T(8,128)(2,1)S(1)}, u32[]{:S(2)}, u32[]{:S(2)}) %collective-permute-start.3) | collective-permute-done | bytes 12512 | tf_op jit(solution)/shard_map/ppermute | solution.py:27
  42.5 0.7 maximum_convert_fusion
  45.1 0.8 fusion.8
  47.2 4.0 %collective-permute-start.4 = (f32[54432]{0:T(1024)S(1)}, f32[54432]{0:T(1024)S(1)}, u32[]{:S(2)}, u32[]{:S(2)}) collective-permute-start(f32[54432]{0:T(1024)S(1)} %pad_maximum_fusion.3), channel_id=1, source_target_pairs={{0,64},{64,128},{128,192},{192,256},{256,320},{320,384},{384,448},... | collective-permute-start | bytes 653192 | tf_op jit(solution)/shard_map/ppermute | solution.py:47
  51.3 1.5 collective-permute-start.5
  52.7 0.6 iota_compare_fusion.5
  53.4 0.7 collective-permute-done.4
  54.2 4.4 %collective-permute-done.5 = f32[54432]{0:T(1024)S(1)} collective-permute-done((f32[54432]{0:T(1024)S(1)}, f32[54432]{0:T(1024)S(1)}, u32[]{:S(2)}, u32[]{:S(2)}) %collective-permute-start.5) | collective-permute-done | bytes 217760 | tf_op jit(solution)/shard_map/ppermute | solution.py:48
  58.7 0.9 fusion.193
  59.6 0.8 multiply_add_fusion.7
  60.5 1.1 fusion.58
  63.1 0.6 fusion.33
  63.7 2.0 %add_multiply_fusion = (f32[22,22,134]{2,1,0:T(8,128)S(1)}, f32[22,22,134]{2,1,0:T(8,128)S(1)}, f32[22,22,134]{2,1,0:T(8,128)}) fusion(f32[22,22,138]{2,1,0:T(8,128)S(1)} %get-tuple-element.146, f32[22,22,138]{2,1,0:T(8,128)S(1)} %get-tuple-element.147), kind=kLoop, calls=%fused_computation.96 | loop fusion | flops 1297120 | bytes 3372512 | tf_op jit(solution)/shard_map/mul | solution.py:77
  65.7 1.0 fusion.206
  68.0 0.6 slice_add_fusion.56
  68.6 0.6 slice_add_fusion.53
  69.3 0.6 fusion.163
  69.9 0.6 slice_add_fusion.49
  70.5 0.6 slice_add_fusion.52
  71.1 0.6 slice_add_fusion.48
  72.3 0.6 fusion.157
  74.7 1.1 fusion.205
  75.8 1.9 %squeeze.115 = f32[20,20,132]{2,1,0:T(8,128)} reshape(f32[1,20,5,4,132]{4,3,2,1,0:T(4,128)} %get-tuple-element.61) | data formatting | bytes 422400 | tf_op jit(solution)/shard_map/squeeze | solution.py:339
  77.7 1.9 %squeeze.119 = f32[20,20,132]{2,1,0:T(8,128)} reshape(f32[1,20,5,4,132]{4,3,2,1,0:T(4,128)} %get-tuple-element.62) | data formatting | bytes 422400 | tf_op jit(solution)/shard_map/squeeze | solution.py:339
  79.7 1.9 %squeeze.117 = f32[20,20,132]{2,1,0:T(8,128)} reshape(f32[1,20,5,4,132]{4,3,2,1,0:T(4,128)} %get-tuple-element.63) | data formatting | bytes 422400 | tf_op jit(solution)/shard_map/squeeze | solution.py:339
  81.9 0.7 copy-done.4
  84.0 1.4 multiply_reduce_fusion.3
  86.9 1.1 fusion.46
  88.2 1.4 multiply_reduce_fusion.5
  90.3 0.8 fusion.104
  91.0 4.0 %collective-permute-start.6 = (f32[3,1,4,32]{3,2,1,0:T(4,128)S(1)}, f32[3,1,4,32]{3,2,1,0:T(4,128)S(1)}, u32[]{:S(2)}, u32[]{:S(2)}) collective-permute-start(f32[3,1,4,32]{3,2,1,0:T(4,128)S(1)} %get-tuple-element.119), channel_id=1, source_target_pairs={{0,64},{64,128},{128,192},{192,256},{256,320},{320,384},{384,448},... | collective-permute-start | bytes 4616 | tf_op jit(solution)/shard_map/ppermute | solution.py:24
  95.1 1.3 collective-permute-start.7
  96.4 4.9 %collective-permute-done.7 = f32[3,1,4,32]{3,2,1,0:T(4,128)S(1)} collective-permute-done((f32[3,1,4,32]{3,2,1,0:T(4,128)S(1)}, f32[3,1,4,32]{3,2,1,0:T(4,128)S(1)}, u32[]{:S(2)}, u32[]{:S(2)}) %collective-permute-start.7) | collective-permute-done | bytes 1568 | tf_op jit(solution)/shard_map/ppermute | solution.py:27
  101.3 3.1 %collective-permute-start.8 = (f32[3,6,1,32]{3,2,1,0:T(1,128)S(1)}, f32[3,6,1,32]{3,2,1,0:T(1,128)S(1)}, u32[]{:S(2)}, u32[]{:S(2)}) collective-permute-start(f32[3,6,1,32]{3,2,1,0:T(1,128)S(1)} %get-tuple-element.117), channel_id=1, source_target_pairs={{0,8},{8,16},{16,24},{24,32},{32,40},{40,48},{48,56},{1,9},{9,17},... | collective-permute-start | bytes 6920 | tf_op jit(solution)/shard_map/ppermute | solution.py:24
  104.4 1.3 collective-permute-start.9
  105.7 3.1 %collective-permute-done.9 = f32[3,6,1,32]{3,2,1,0:T(1,128)S(1)} collective-permute-done((f32[3,6,1,32]{3,2,1,0:T(1,128)S(1)}, f32[3,6,1,32]{3,2,1,0:T(1,128)S(1)}, u32[]{:S(2)}, u32[]{:S(2)}) %collective-permute-start.9) | collective-permute-done | bytes 2336 | tf_op jit(solution)/shard_map/ppermute | solution.py:27
  108.9 7.3 %collective-permute-start.10 = (f32[3,6,6,1]{3,2,1,0:T(8,128)S(1)}, f32[3,6,6,1]{3,2,1,0:T(8,128)S(1)}, u32[]{:S(2)}, u32[]{:S(2)}) collective-permute-start(f32[3,6,6,1]{3,2,1,0:T(8,128)S(1)} %get-tuple-element.111), channel_id=1, source_target_pairs={{0,1},{1,2},{2,3},{3,4},{4,5},{5,6},{6,7},{8,9},{9,10},{10,11},{11... | collective-permute-start | bytes 1304 | tf_op jit(solution)/shard_map/ppermute | solution.py:24
  116.3 1.9 %collective-permute-start.11 = (f32[3,6,6,1]{3,2,1,0:T(8,128)S(1)}, f32[3,6,6,1]{3,2,1,0:T(8,128)S(1)}, u32[]{:S(2)}, u32[]{:S(2)}) collective-permute-start(f32[3,6,6,1]{3,2,1,0:T(8,128)S(1)} %get-tuple-element.112), channel_id=1, source_target_pairs={{1,0},{2,1},{3,2},{4,3},{5,4},{6,5},{7,6},{9,8},{10,9},{11,10},{12... | collective-permute-start | bytes 1304 | tf_op jit(solution)/shard_map/ppermute | solution.py:27
  118.5 3.4 %collective-permute-done.11 = f32[3,6,6,1]{3,2,1,0:T(8,128)S(1)} collective-permute-done((f32[3,6,6,1]{3,2,1,0:T(8,128)S(1)}, f32[3,6,6,1]{3,2,1,0:T(8,128)S(1)}, u32[]{:S(2)}, u32[]{:S(2)}) %collective-permute-start.11) | collective-permute-done | bytes 464 | tf_op jit(solution)/shard_map/ppermute | solution.py:27
  124.8 1.2 fusion.48
  126.3 1.4 multiply_reduce_fusion.1
  128.8 0.7 copy.156
  129.6 9.2 %all-to-all-start.1 = ((f32[3,64,16]{2,0,1:T(4,128)}), f32[3,64,16]{2,0,1:T(4,128)S(1)}, u32[]{:S(2)}, u32[]{:S(2)}) async-start(f32[3,64,16]{2,0,1:T(4,128)} %copy.156), calls=%async_computation.1 | async-start | bytes 262144 | tf_op jit(solution)/shard_map/all_to_all | solution.py:352
  138.8 0.7 slice_add_fusion.57
  139.5 10.4 %all-to-all-done.1 = f32[3,64,16]{2,0,1:T(4,128)S(1)} async-done(((f32[3,64,16]{2,0,1:T(4,128)}), f32[3,64,16]{2,0,1:T(4,128)S(1)}, u32[]{:S(2)}, u32[]{:S(2)}) %all-to-all-start.1) | async-done | bytes 12320 | tf_op jit(solution)/shard_map/all_to_all | solution.py:352
  150.1 0.9 convolution_bitcast_fusion
  (303 shorter events, 19.5 us)
Async XLA Ops:
  1.9 27.6 %collective-permute-start = (bf16[3,16,5,128]{3,2,1,0:T(8,128)(2,1)S(1)}, bf16[3,16,5,128]{3,2,1,0:T(8,128)(2,1)S(1)}, u32[]{:S(2)}, u32[]{:S(2)}) collective-permute-start(bf16[3,16,5,128]{3,2,1,0:T(8,128)(2,1)S(1)} %get-tuple-element.101), channel_id=1, source_target_pairs={{0,8},{8,16},{16,24},{24,32},{32,40},{40,48},{48,56},{1,9},{9,17},... | collective-permute-start | bytes 184328 | tf_op jit(solution)/shard_map/ppermute | solution.py:24
  5.9 23.6 %collective-permute-start.1 = (bf16[3,16,5,128]{3,2,1,0:T(8,128)(2,1)S(1)}, bf16[3,16,5,128]{3,2,1,0:T(8,128)(2,1)S(1)}, u32[]{:S(2)}, u32[]{:S(2)}) collective-permute-start(bf16[3,16,5,128]{3,2,1,0:T(8,128)(2,1)S(1)} %get-tuple-element.102), channel_id=1, source_target_pairs={{8,0},{16,8},{24,16},{32,24},{40,32},{48,40},{56,48},{9,1},{17,9},... | collective-permute-start | bytes 184328 | tf_op jit(solution)/shard_map/ppermute | solution.py:27
  12.1 17.4 %copy-start.7 = (bf16[16,16,128]{2,1,0:T(8,128)(2,1)S(1)}, bf16[16,16,128]{2,1,0:T(8,128)(2,1)}, u32[]{:S(2)}) copy-start(bf16[16,16,128]{2,1,0:T(8,128)(2,1)} %param.6) | copy-start | bytes 196612
  12.1 17.4 %copy-start.8 = (bf16[16,16,128]{2,1,0:T(8,128)(2,1)S(1)}, bf16[16,16,128]{2,1,0:T(8,128)(2,1)}, u32[]{:S(2)}) copy-start(bf16[16,16,128]{2,1,0:T(8,128)(2,1)} %param.5) | copy-start | bytes 196612
  13.7 30.2 %all-to-all-start = ((f32[4,64,80]{2,0,1:T(4,128)}), f32[4,64,80]{2,0,1:T(4,128)S(1)}, u32[]{:S(2)}, u32[]{:S(2)}) async-start(f32[4,64,80]{2,0,1:T(4,128)} %copy.127), calls=%async_computation | async-start | bytes 262144 | tf_op jit(solution)/shard_map/all_to_all | solution.py:295
  27.6 32.8 %copy-start.52 = (f32[132]{0:T(256)}, f32[132]{0:T(256)S(1)}, u32[]{:S(2)}) copy-start(f32[132]{0:T(256)S(1)} %get-tuple-element.150) | copy-start | bytes 1588
  27.6 32.8 %copy-start.54 = (f32[132]{0:T(256)}, f32[132]{0:T(256)S(1)}, u32[]{:S(2)}) copy-start(f32[132]{0:T(256)S(1)} %get-tuple-element.151) | copy-start | bytes 1588
  27.6 32.8 %copy-start.35 = (s32[132]{0:T(256)}, s32[132]{0:T(256)S(1)}, u32[]{:S(2)}) copy-start(s32[132]{0:T(256)S(1)} %get-tuple-element.148) | copy-start | bytes 1588
  27.6 32.8 %copy-start.37 = (s32[132]{0:T(256)}, s32[132]{0:T(256)S(1)}, u32[]{:S(2)}) copy-start(s32[132]{0:T(256)S(1)} %get-tuple-element.149) | copy-start | bytes 1588
  29.9 8.3 %collective-permute-start.2 = (bf16[3,16,26,5]{3,2,1,0:T(8,128)(2,1)S(1)}, bf16[3,16,26,5]{3,2,1,0:T(8,128)(2,1)S(1)}, u32[]{:S(2)}, u32[]{:S(2)}) collective-permute-start(bf16[3,16,26,5]{3,2,1,0:T(8,128)(2,1)S(1)} %get-tuple-element.74), channel_id=1, source_target_pairs={{0,1},{1,2},{2,3},{3,4},{4,5},{5,6},{6,7},{8,9},{9,10},{10,11},{11... | collective-permute-start | bytes 37448 | tf_op jit(solution)/shard_map/ppermute | solution.py:24
  33.4 9.1 %collective-permute-start.3 = (bf16[3,16,26,5]{3,2,1,0:T(8,128)(2,1)S(1)}, bf16[3,16,26,5]{3,2,1,0:T(8,128)(2,1)S(1)}, u32[]{:S(2)}, u32[]{:S(2)}) collective-permute-start(bf16[3,16,26,5]{3,2,1,0:T(8,128)(2,1)S(1)} %get-tuple-element.75), channel_id=1, source_target_pairs={{1,0},{2,1},{3,2},{4,3},{5,4},{6,5},{7,6},{9,8},{10,9},{11,10},{12... | collective-permute-start | bytes 37448 | tf_op jit(solution)/shard_map/ppermute | solution.py:27
  35.4 7.9 %copy-start.42 = (f32[4]{0:T(128)}, f32[4]{0:T(128)S(1)}, u32[]{:S(2)}) copy-start(f32[4]{0:T(128)S(1)} %get-tuple-element.152) | copy-start | bytes 52
  35.4 7.9 %copy-start.46 = (f32[4]{0:T(128)}, f32[4]{0:T(128)S(1)}, u32[]{:S(2)}) copy-start(f32[4]{0:T(128)S(1)} %get-tuple-element.153) | copy-start | bytes 52
  45.1 1.6 %copy-start.40 = (f32[640]{0:T(1024)}, f32[640]{0:T(1024)S(1)}, u32[]{:S(2)}) copy-start(f32[640]{0:T(1024)S(1)} %slice_reduce_fusion) | copy-start | bytes 7684
  46.5 15.1 %copy-start.6 = (f32[3,9,4,4,32]{4,3,2,1,0:T(4,128)}, f32[3,9,4,4,32]{4,3,2,1,0:T(4,128)S(1)}, u32[]{:S(2)}) copy-start(f32[3,9,4,4,32]{4,3,2,1,0:T(4,128)S(1)} %reshape.489) | copy-start | bytes 165892
  47.2 6.9 %collective-permute-start.4 = (f32[54432]{0:T(1024)S(1)}, f32[54432]{0:T(1024)S(1)}, u32[]{:S(2)}, u32[]{:S(2)}) collective-permute-start(f32[54432]{0:T(1024)S(1)} %pad_maximum_fusion.3), channel_id=1, source_target_pairs={{0,64},{64,128},{128,192},{192,256},{256,320},{320,384},{384,448},... | collective-permute-start | bytes 653192 | tf_op jit(solution)/shard_map/ppermute | solution.py:47
  51.3 7.3 %collective-permute-start.5 = (f32[54432]{0:T(1024)S(1)}, f32[54432]{0:T(1024)S(1)}, u32[]{:S(2)}, u32[]{:S(2)}) collective-permute-start(f32[54432]{0:T(1024)S(1)} %pad_maximum_fusion.4), channel_id=1, source_target_pairs={{64,0},{128,64},{192,128},{256,192},{320,256},{384,320},{448,384},... | collective-permute-start | bytes 653192 | tf_op jit(solution)/shard_map/ppermute | solution.py:48
  68.0 5.7 %copy-start.56 = (f32[20]{0:T(128)S(1)}, f32[20]{0:T(128)}, u32[]{:S(2)}) copy-start(f32[20]{0:T(128)} %mul.999) | copy-start | bytes 244
  68.0 5.7 %copy-start.58 = (f32[20]{0:T(128)S(1)}, f32[20]{0:T(128)}, u32[]{:S(2)}) copy-start(f32[20]{0:T(128)} %mul.993) | copy-start | bytes 244
  81.6 1.2 copy-start.5
  81.9 6.2 %copy-start.11 = (f32[20,20,132]{2,0,1:T(8,128)}, f32[20,20,132]{2,0,1:T(8,128)S(1)}, u32[]{:S(2)}) copy-start(f32[20,20,132]{2,0,1:T(8,128)S(1)} %copy.165) | copy-start | bytes 633604
  83.2 4.9 %copy-start.14 = (bf16[20,20,132]{2,0,1:T(8,128)(2,1)}, bf16[20,20,132]{2,0,1:T(8,128)(2,1)S(1)}, u32[]{:S(2)}) copy-start(bf16[20,20,132]{2,0,1:T(8,128)(2,1)S(1)} %copy.162) | copy-start | bytes 316804
  83.6 4.5 %copy-start.16 = (bf16[20,20,132]{2,0,1:T(8,128)(2,1)}, bf16[20,20,132]{2,0,1:T(8,128)(2,1)S(1)}, u32[]{:S(2)}) copy-start(bf16[20,20,132]{2,0,1:T(8,128)(2,1)S(1)} %copy.163) | copy-start | bytes 316804
  83.8 4.3 %copy-start.18 = (bf16[20,20,132]{2,0,1:T(8,128)(2,1)}, bf16[20,20,132]{2,0,1:T(8,128)(2,1)S(1)}, u32[]{:S(2)}) copy-start(bf16[20,20,132]{2,0,1:T(8,128)(2,1)S(1)} %copy.164) | copy-start | bytes 316804
  85.4 1.0 copy-start
  85.4 1.2 copy-start.1
  85.4 1.3 copy-start.2
  85.4 1.5 copy-start.3
  85.6 4.6 %copy-start.20 = (f32[3,5,4,32]{3,2,1,0:T(4,128)}, f32[3,5,4,32]{3,2,1,0:T(4,128)S(1)}, u32[]{:S(2)}) copy-start(f32[3,5,4,32]{3,2,1,0:T(4,128)S(1)} %get-tuple-element.13) | copy-start | bytes 23044
  85.6 4.6 %copy-start.22 = (f32[3,5,4,32]{3,2,1,0:T(4,128)}, f32[3,5,4,32]{3,2,1,0:T(4,128)S(1)}, u32[]{:S(2)}) copy-start(f32[3,5,4,32]{3,2,1,0:T(4,128)S(1)} %get-tuple-element.14) | copy-start | bytes 23044
  86.9 1.3 copy-start.33
  86.9 1.3 copy-start.44
  86.9 1.3 copy-start.48
  88.2 1.7 %copy-start.24 = (f32[4,4,33]{2,1,0:T(4,128)S(1)}, f32[4,4,33]{2,1,0:T(4,128)}, u32[]{:S(2)}) copy-start(f32[4,4,33]{2,1,0:T(4,128)} %slice_add_fusion.56) | copy-start | bytes 6340
  88.2 1.7 %copy-start.25 = (f32[4,4,33]{2,1,0:T(4,128)S(1)}, f32[4,4,33]{2,1,0:T(4,128)}, u32[]{:S(2)}) copy-start(f32[4,4,33]{2,1,0:T(4,128)} %slice_add_fusion.53) | copy-start | bytes 6340
  88.2 1.7 %copy-start.26 = (f32[4,4,33]{2,1,0:T(4,128)S(1)}, f32[4,4,33]{2,1,0:T(4,128)}, u32[]{:S(2)}) copy-start(f32[4,4,33]{2,1,0:T(4,128)} %fusion.163) | copy-start | bytes 6340
  88.2 1.8 %copy-start.27 = (f32[4,4,33]{2,1,0:T(4,128)S(1)}, f32[4,4,33]{2,1,0:T(4,128)}, u32[]{:S(2)}) copy-start(f32[4,4,33]{2,1,0:T(4,128)} %slice_add_fusion.49) | copy-start | bytes 6340
  88.2 1.8 %copy-start.28 = (f32[4,4,33]{2,1,0:T(4,128)S(1)}, f32[4,4,33]{2,1,0:T(4,128)}, u32[]{:S(2)}) copy-start(f32[4,4,33]{2,1,0:T(4,128)} %slice_add_fusion.52) | copy-start | bytes 6340
  88.2 1.8 %copy-start.31 = (f32[4,4,33]{2,1,0:T(4,128)S(1)}, f32[4,4,33]{2,1,0:T(4,128)}, u32[]{:S(2)}) copy-start(f32[4,4,33]{2,1,0:T(4,128)} %fusion.157) | copy-start | bytes 6340
  88.2 1.9 %copy-start.29 = (f32[4,4,33]{2,1,0:T(4,128)S(1)}, f32[4,4,33]{2,1,0:T(4,128)}, u32[]{:S(2)}) copy-start(f32[4,4,33]{2,1,0:T(4,128)} %slice_add_fusion.48) | copy-start | bytes 6340
  88.2 1.9 %copy-start.30 = (f32[4,4,33]{2,1,0:T(4,128)S(1)}, f32[4,4,33]{2,1,0:T(4,128)}, u32[]{:S(2)}) copy-start(f32[4,4,33]{2,1,0:T(4,128)} %fusion.151) | copy-start | bytes 6340
  88.2 1.9 %copy-start.32 = (f32[4,4,33]{2,1,0:T(4,128)S(1)}, f32[4,4,33]{2,1,0:T(4,128)}, u32[]{:S(2)}) copy-start(f32[4,4,33]{2,1,0:T(4,128)} %slice_add_fusion.45) | copy-start | bytes 6340
  89.6 28.6 %copy-start.41 = (f32[640]{0:T(1024)S(1)}, f32[640]{0:T(1024)}, u32[]{:S(2)}) copy-start(f32[640]{0:T(1024)} %copy-done.40) | copy-start | bytes 7684
  89.6 32.5 %copy-start.36 = (s32[132]{0:T(256)S(1)}, s32[132]{0:T(256)}, u32[]{:S(2)}) copy-start(s32[132]{0:T(256)} %copy-done.35) | copy-start | bytes 1588
  89.7 32.5 %copy-start.38 = (s32[132]{0:T(256)S(1)}, s32[132]{0:T(256)}, u32[]{:S(2)}) copy-start(s32[132]{0:T(256)} %copy-done.37) | copy-start | bytes 1588
  89.7 32.5 %copy-start.53 = (f32[132]{0:T(256)S(1)}, f32[132]{0:T(256)}, u32[]{:S(2)}) copy-start(f32[132]{0:T(256)} %copy-done.52) | copy-start | bytes 1588
  89.7 32.5 %copy-start.55 = (f32[132]{0:T(256)S(1)}, f32[132]{0:T(256)}, u32[]{:S(2)}) copy-start(f32[132]{0:T(256)} %copy-done.54) | copy-start | bytes 1588
  91.0 5.3 %collective-permute-start.6 = (f32[3,1,4,32]{3,2,1,0:T(4,128)S(1)}, f32[3,1,4,32]{3,2,1,0:T(4,128)S(1)}, u32[]{:S(2)}, u32[]{:S(2)}) collective-permute-start(f32[3,1,4,32]{3,2,1,0:T(4,128)S(1)} %get-tuple-element.119), channel_id=1, source_target_pairs={{0,64},{64,128},{128,192},{192,256},{256,320},{320,384},{384,448},... | collective-permute-start | bytes 4616 | tf_op jit(solution)/shard_map/ppermute | solution.py:24
  95.1 6.2 %collective-permute-start.7 = (f32[3,1,4,32]{3,2,1,0:T(4,128)S(1)}, f32[3,1,4,32]{3,2,1,0:T(4,128)S(1)}, u32[]{:S(2)}, u32[]{:S(2)}) collective-permute-start(f32[3,1,4,32]{3,2,1,0:T(4,128)S(1)} %get-tuple-element.120), channel_id=1, source_target_pairs={{64,0},{128,64},{192,128},{256,192},{320,256},{384,320},{448,384},... | collective-permute-start | bytes 4616 | tf_op jit(solution)/shard_map/ppermute | solution.py:27
  101.3 4.4 %collective-permute-start.8 = (f32[3,6,1,32]{3,2,1,0:T(1,128)S(1)}, f32[3,6,1,32]{3,2,1,0:T(1,128)S(1)}, u32[]{:S(2)}, u32[]{:S(2)}) collective-permute-start(f32[3,6,1,32]{3,2,1,0:T(1,128)S(1)} %get-tuple-element.117), channel_id=1, source_target_pairs={{0,8},{8,16},{16,24},{24,32},{32,40},{40,48},{48,56},{1,9},{9,17},... | collective-permute-start | bytes 6920 | tf_op jit(solution)/shard_map/ppermute | solution.py:24
  104.4 4.4 %collective-permute-start.9 = (f32[3,6,1,32]{3,2,1,0:T(1,128)S(1)}, f32[3,6,1,32]{3,2,1,0:T(1,128)S(1)}, u32[]{:S(2)}, u32[]{:S(2)}) collective-permute-start(f32[3,6,1,32]{3,2,1,0:T(1,128)S(1)} %get-tuple-element.118), channel_id=1, source_target_pairs={{8,0},{16,8},{24,16},{32,24},{40,32},{48,40},{56,48},{9,1},{17,9},... | collective-permute-start | bytes 6920 | tf_op jit(solution)/shard_map/ppermute | solution.py:27
  108.9 9.6 %collective-permute-start.10 = (f32[3,6,6,1]{3,2,1,0:T(8,128)S(1)}, f32[3,6,6,1]{3,2,1,0:T(8,128)S(1)}, u32[]{:S(2)}, u32[]{:S(2)}) collective-permute-start(f32[3,6,6,1]{3,2,1,0:T(8,128)S(1)} %get-tuple-element.111), channel_id=1, source_target_pairs={{0,1},{1,2},{2,3},{3,4},{4,5},{5,6},{6,7},{8,9},{9,10},{10,11},{11... | collective-permute-start | bytes 1304 | tf_op jit(solution)/shard_map/ppermute | solution.py:24
  116.3 5.7 %collective-permute-start.11 = (f32[3,6,6,1]{3,2,1,0:T(8,128)S(1)}, f32[3,6,6,1]{3,2,1,0:T(8,128)S(1)}, u32[]{:S(2)}, u32[]{:S(2)}) collective-permute-start(f32[3,6,6,1]{3,2,1,0:T(8,128)S(1)} %get-tuple-element.112), channel_id=1, source_target_pairs={{1,0},{2,1},{3,2},{4,3},{5,4},{6,5},{7,6},{9,8},{10,9},{11,10},{12... | collective-permute-start | bytes 1304 | tf_op jit(solution)/shard_map/ppermute | solution.py:27
  124.7 1.5 copy-start.12
  124.8 1.5 copy-start.15
  124.8 1.5 copy-start.17
  124.8 1.5 copy-start.19
  124.8 1.5 copy-start.34
  124.8 1.5 copy-start.45
  124.8 1.5 copy-start.49
  126.3 1.9 %copy-start.21 = (f32[3,5,4,32]{3,2,1,0:T(4,128)S(1)}, f32[3,5,4,32]{3,2,1,0:T(4,128)}, u32[]{:S(2)}) copy-start(f32[3,5,4,32]{3,2,1,0:T(4,128)} %copy-done.20) | copy-start | bytes 23044
  126.3 1.9 %copy-start.23 = (f32[3,5,4,32]{3,2,1,0:T(4,128)S(1)}, f32[3,5,4,32]{3,2,1,0:T(4,128)}, u32[]{:S(2)}) copy-start(f32[3,5,4,32]{3,2,1,0:T(4,128)} %copy-done.22) | copy-start | bytes 23044
  127.7 11.1 %copy-start.64 = (s32[64]{0:T(128)S(1)}, s32[64]{0:T(128)}, u32[]{:S(2)}) copy-start(s32[64]{0:T(128)} %get-tuple-element.53) | copy-start | bytes 772
  129.6 20.4 %all-to-all-start.1 = ((f32[3,64,16]{2,0,1:T(4,128)}), f32[3,64,16]{2,0,1:T(4,128)S(1)}, u32[]{:S(2)}, u32[]{:S(2)}) async-start(f32[3,64,16]{2,0,1:T(4,128)} %copy.156), calls=%async_computation.1 | async-start | bytes 262144 | tf_op jit(solution)/shard_map/all_to_all | solution.py:352
  (15 other events, 11.5 us)

commit v4 on v3

--- a/solution.py
+++ b/solution.py
@@ -228,7 +228,7 @@
 
 def per_device(reference_image, deformed_image, roi_mask, displacement, node_map):
     stacked = jnp.stack([reference_image, deformed_image, roi_mask.astype(jnp.bfloat16)])
-    stacked = with_halo(stacked, (("gy", 2), ("gz", 3)), 5).astype(jnp.float32)
+    padded_images = with_halo(stacked, (("gy", 2), ("gz", 3), ("gx", 1)), 5).astype(jnp.float32)
     nodes_shape = (
         3,
         reference_image.shape[0] // ELEM,
@@ -323,7 +323,7 @@
         axis=3,
     )
     extended = jnp.concatenate([low_row, middle, high_row], axis=2)
-    padded_images, first_padded = with_halo_pair(stacked, extended, (("gx", 1, 1),), (5, 1))
+    first_padded = with_halo(extended, (("gx", 1),), 1)
     derived = derive_fields(padded_images[0], padded_images[1])
     region = padded_images[2][3:-3, 3:-3, 3:-3]
     contrast = derived[0].astype(jnp.float32)

time: 152 us -> 132 us (0.87)
  local copies, waits for them, and re-layouts: 23.9 us -> 11.8 us
  waiting for transfers between devices: 32.8 us -> 24.8 us
  starting transfers between devices: 57.8 us -> 61.9 us
  other arithmetic: 26.5 us -> 23.4 us
    ppermute x5 -> x7, starting transfers between devices: 22 us -> 31.4 us  [with_halo(): lax.ppermute(lax.slice_in_dim(block, block.shape[dim] - width, None, axis...]
    ppermute x5 -> x7, waiting for transfers between devices: 15.8 us -> 10.3 us  [with_halo(): lax.ppermute(lax.slice_in_dim(block, 0, width, axis=dim), axis, backward)]
    ppermute x2 -> x0, starting transfers between devices: 5.46 us -> none  [the longest x1 4 us: with_halo_pair(): low_flat = lax.ppermute(low_flat, axis, forward)]
    ppermute x2 -> x0, waiting for transfers between devices: 5.06 us -> none  [the longest x1 4.37 us: with_halo_pair(): high_flat = lax.ppermute(high_flat, axis, backward)]
    add x43, other arithmetic: 7.28 us -> 3.1 us  [pair_op(): lax.slice_in_dim(volume, 1, length, axis=dimension)]
    all_to_all x1, waiting for transfers between devices: 0.01 us -> 4.08 us  [per_device(): lax.all_to_all(send_outgoing, ('gy', 'gz'), split_axis=1, concat_axis=1,...]
    unnamed x130 -> x92, local copies, waits for them, and re-layouts: 4.06 us -> 0.78 us
    ppermute x5 -> x7, starting transfers between devices: 7.72 us -> 10.7 us  [with_halo(): lax.ppermute(lax.slice_in_dim(block, 0, width, axis=dim), axis, backward)]
  transfers between devices with their start and end apart: 14 -> 16, of which waited for: 8 -> 6; matrix products, arithmetic and copies ran while one was open for 8% -> 13% of each run, Pallas kernels for 0% -> 0%
where the time goes in v4:
time: 132 us; the launch traced here: 131 us
  starting transfers between devices  61.9 us (47%)
  waiting for transfers between devices  24.8 us (19%)
  other arithmetic  23.4 us (18%)
  local copies, waits for them, and re-layouts  11.8 us (9%)
  matrix products  7.36 us (6%)
  between operations  1.92 us (1%)
    ppermute x7, starting transfers between devices, with_halo(): lax.ppermute(lax.slice_in_dim(block, block.shape[dim] - width, None, axis...  31.4 us
    all_to_all x1, starting transfers between devices, per_device(): lax.all_to_all(send_outgoing, ('gy', 'gz'), split_axis=1, concat_axis=1,...  13.3 us
    ppermute x7, starting transfers between devices, with_halo(): lax.ppermute(lax.slice_in_dim(block, 0, width, axis=dim), axis, backward)  10.7 us
    all_to_all x1, waiting for transfers between devices, per_device(): lax.all_to_all(outgoing, ('gy', 'gz'), split_axis=1, concat_axis=1, tiled...  10.4 us
    ppermute x7, waiting for transfers between devices, with_halo(): lax.ppermute(lax.slice_in_dim(block, 0, width, axis=dim), axis, backward)  10.3 us
    all_to_all x1, starting transfers between devices, per_device(): lax.all_to_all(outgoing, ('gy', 'gz'), split_axis=1, concat_axis=1, tiled...  6.42 us
    dot_general x3, matrix products, collect(): jnp.dot(volume.reshape(-1, shape_all[3]), table_back, precision=highest)  4.15 us
    all_to_all x1, waiting for transfers between devices, per_device(): lax.all_to_all(send_outgoing, ('gy', 'gz'), split_axis=1, concat_axis=1,...  4.08 us
  transfers between devices with their start and end apart: 16, of which 6 were waited for; matrix products, arithmetic and copies ran while one was open for 13% of the time, Pallas kernels for 0%

profile of v4, /device:TPU:1, one launch (start us, length us, event | category | flops | bytes accessed | tf_op | source)
XLA Modules:
  0.0 131.1 jit_solution(14754586956724597123)
XLA Ops:
  0.0 0.9 convert_bitcast_fusion
  0.9 0.9 pad_maximum_fusion.9
  1.9 4.0 %collective-permute-start = (bf16[3,16,5,128]{3,2,1,0:T(8,128)(2,1)S(1)}, bf16[3,16,5,128]{3,2,1,0:T(8,128)(2,1)S(1)}, u32[]{:S(2)}, u32[]{:S(2)}) collective-permute-start(bf16[3,16,5,128]{3,2,1,0:T(8,128)(2,1)S(1)} %get-tuple-element.101), channel_id=1, source_target_pairs={{0,8},{8,16},{16,24},{24,32},{32,40},{40,48},{48,56},{1,9},{9,17},... | collective-permute-start | bytes 184328 | tf_op jit(solution)/shard_map/ppermute | solution.py:24
  5.9 1.3 collective-permute-start.1
  7.2 0.7 broadcast_add_fusion.1
  7.9 1.2 and_and_fusion
  9.4 0.3 convert_reduce_fusion
  9.8 0.6 copy-done.24
  10.3 1.1 concatenate.71
  11.5 0.7 fusion.7
  12.2 0.4 copy.110
  12.6 0.4 all_to_all.12
  12.9 0.7 copy.111
  13.7 13.3 %all-to-all-start = ((f32[4,64,80]{2,0,1:T(4,128)}), f32[4,64,80]{2,0,1:T(4,128)S(1)}, u32[]{:S(2)}, u32[]{:S(2)}) async-start(f32[4,64,80]{2,0,1:T(4,128)} %copy.111), calls=%async_computation | async-start | bytes 262144 | tf_op jit(solution)/shard_map/all_to_all | solution.py:295
  27.7 0.9 fusion.210
  28.6 3.5 %collective-permute-start.2 = (bf16[3,16,26,5]{3,2,1,0:T(8,128)(2,1)}, bf16[3,16,26,5]{3,2,1,0:T(8,128)(2,1)S(1)}, u32[]{:S(2)}, u32[]{:S(2)}) collective-permute-start(bf16[3,16,26,5]{3,2,1,0:T(8,128)(2,1)} %get-tuple-element.74), channel_id=1, source_target_pairs={{0,1},{1,2},{2,3},{3,4},{4,5},{5,6},{6,7},{8,9},{9,10},{10,11},{11... | collective-permute-start | bytes 37448 | tf_op jit(solution)/shard_map/ppermute | solution.py:24
  32.1 1.9 %collective-permute-start.3 = (bf16[3,16,26,5]{3,2,1,0:T(8,128)(2,1)S(1)}, bf16[3,16,26,5]{3,2,1,0:T(8,128)(2,1)S(1)}, u32[]{:S(2)}, u32[]{:S(2)}) collective-permute-start(bf16[3,16,26,5]{3,2,1,0:T(8,128)(2,1)S(1)} %get-tuple-element.75), channel_id=1, source_target_pairs={{1,0},{2,1},{3,2},{4,3},{5,4},{6,5},{7,6},{9,8},{10,9},{11,10},{12... | collective-permute-start | bytes 37448 | tf_op jit(solution)/shard_map/ppermute | solution.py:27
  34.1 4.1 %all-to-all-done = f32[4,64,80]{2,0,1:T(4,128)S(1)} async-done(((f32[4,64,80]{2,0,1:T(4,128)}), f32[4,64,80]{2,0,1:T(4,128)S(1)}, u32[]{:S(2)}, u32[]{:S(2)}) %all-to-all-start) | async-done | bytes 81952 | tf_op jit(solution)/shard_map/all_to_all | solution.py:295
  38.8 0.4 reshape.464
  39.3 0.8 fusion.8
  41.2 1.3 collective-permute-start.7
  42.5 4.6 %collective-permute-start.6 = (f32[3,1,6,34]{3,2,1,0:T(8,128)S(1)}, f32[3,1,6,34]{3,2,1,0:T(8,128)S(1)}, u32[]{:S(2)}, u32[]{:S(2)}) collective-permute-start(f32[3,1,6,34]{3,2,1,0:T(8,128)S(1)} %get-tuple-element.108), channel_id=1, source_target_pairs={{0,64},{64,128},{128,192},{192,256},{256,320},{320,384},{384,448},... | collective-permute-start | bytes 7352 | tf_op jit(solution)/shard_map/ppermute | solution.py:24
  47.2 1.2 pad_maximum_fusion.8
  48.3 4.7 %collective-permute-start.4 = (bf16[3,5,26,138]{3,2,1,0:T(8,128)(2,1)}, bf16[3,5,26,138]{3,2,1,0:T(8,128)(2,1)}, u32[]{:S(2)}, u32[]{:S(2)}) collective-permute-start(bf16[3,5,26,138]{3,2,1,0:T(8,128)(2,1)} %get-tuple-element.62), channel_id=1, source_target_pairs={{0,64},{64,128},{128,192},{192,256},{256,320},{320,384},{384,448},... | collective-permute-start | bytes 322928 | tf_op jit(solution)/shard_map/ppermute | solution.py:24
  53.0 1.5 %collective-permute-start.5 = (bf16[3,5,26,138]{3,2,1,0:T(8,128)(2,1)S(1)}, bf16[3,5,26,138]{3,2,1,0:T(8,128)(2,1)}, u32[]{:S(2)}, u32[]{:S(2)}) collective-permute-start(bf16[3,5,26,138]{3,2,1,0:T(8,128)(2,1)S(1)} %get-tuple-element.63), channel_id=1, source_target_pairs={{64,0},{128,64},{192,128},{256,192},{320,256},{384,320},{448,384},... | collective-permute-start | bytes 322928 | tf_op jit(solution)/shard_map/ppermute | solution.py:27
  55.1 0.4 fusion.58
  56.4 0.4 multiply_add_fusion.1
  57.0 0.7 fusion.161
  57.7 0.7 fusion.155
  58.4 0.7 fusion.149
  59.5 1.9 %collective-permute-done.5 = bf16[3,5,26,138]{3,2,1,0:T(8,128)(2,1)} collective-permute-done((bf16[3,5,26,138]{3,2,1,0:T(8,128)(2,1)S(1)}, bf16[3,5,26,138]{3,2,1,0:T(8,128)(2,1)}, u32[]{:S(2)}, u32[]{:S(2)}) %collective-permute-start.5) | collective-permute-done | bytes 107672 | tf_op jit(solution)/shard_map/ppermute | solution.py:27
  61.4 1.8 %maximum_convert_fusion = f32[3,26,26,138]{3,2,1,0:T(8,128)S(1)} fusion(bf16[3,5,26,138]{3,2,1,0:T(8,128)(2,1)} %collective-permute-done.5, bf16[3,16,26,5]{3,2,1,0:T(8,128)(2,1)S(1)} %collective-permute-done.3, bf16[3,16,5,128]{3,2,1,0:T(8,128)(2,1)S(1)} %collective-permute-done.1, bf16[1,16,16,128]{3,2,1,0:T(8,128)(2,1)S(1)} %convert_bitcast_fusion, ...), kind=kLoop, calls=%fused_computation.13 | loop fusion | flops 5037552 | bytes 1679184 | tf_op jit(solution)/shard_map/convert_element_type | solution.py:231
  63.3 0.4 fusion.25
  63.7 0.6 fusion.33
  64.3 1.2 add_multiply_fusion
  66.2 0.3 fusion.55
  67.2 1.4 %multiply_reduce_fusion.3 = (f32[3,20,5,32]{3,1,2,0:T(8,128)S(1)}, f32[3,20,5,32]{3,1,2,0:T(8,128)S(1)}) fusion(f32[4]{0:T(128)S(1)} %get-tuple-element.159, f32[4]{0:T(128)S(1)} %get-tuple-element.158, pred[34,132]{1,0:T(8,128)(4,1)S(1)} %iota_compare_fusion.5, pred[34,132]{1,0:T(8,128)(4,1)S(1)} %iota_compare_fusion.6, f32[132]{0:T(256)S(1)} %get-tuple-element.156, ...), kind=kOutput, calls=%fused_computation.27 | convolution fusion | flops 61764672 | bytes 1325056 | tf_op jit(solution)/shard_map/dot_general | solution.py:219
  68.6 0.8 multiply_reduce_fusion.9
  69.7 1.1 fusion.46
  71.0 1.4 %multiply_reduce_fusion.5 = (f32[3,20,5,32]{3,1,2,0:T(8,128)S(1)}, f32[3,20,5,32]{3,1,2,0:T(8,128)S(1)}) fusion(f32[4]{0:T(128)S(1)} %copy-done.31, f32[4]{0:T(128)S(1)} %copy-done.28, f32[34,132]{1,0:T(8,128)S(1)} %select_add_fusion, f32[20,5,4,132]{3,0,2,1:T(8,128)S(1)} %bitcast.484, f32[20,5,4,132]{3,0,2,1:T(8,128)S(1)} %bitcast.481, ...), kind=kOutput, calls=%fused_computation.29 | convolution fusion | flops 61752000 | bytes 1830912 | tf_op jit(solution)/shard_map/dot_general | solution.py:219
  72.7 0.8 fusion.104
  73.5 5.5 %collective-permute-start.8 = (f32[3,1,4,32]{3,2,1,0:T(4,128)S(1)}, f32[3,1,4,32]{3,2,1,0:T(4,128)S(1)}, u32[]{:S(2)}, u32[]{:S(2)}) collective-permute-start(f32[3,1,4,32]{3,2,1,0:T(4,128)S(1)} %get-tuple-element.119), channel_id=1, source_target_pairs={{0,64},{64,128},{128,192},{192,256},{256,320},{320,384},{384,448},... | collective-permute-start | bytes 4616 | tf_op jit(solution)/shard_map/ppermute | solution.py:24
  79.0 1.3 collective-permute-start.9
  80.3 3.1 %collective-permute-done.9 = f32[3,1,4,32]{3,2,1,0:T(4,128)S(1)} collective-permute-done((f32[3,1,4,32]{3,2,1,0:T(4,128)S(1)}, f32[3,1,4,32]{3,2,1,0:T(4,128)S(1)}, u32[]{:S(2)}, u32[]{:S(2)}) %collective-permute-start.9) | collective-permute-done | bytes 1568 | tf_op jit(solution)/shard_map/ppermute | solution.py:27
  83.4 2.3 %collective-permute-start.10 = (f32[3,6,1,32]{3,2,1,0:T(1,128)S(1)}, f32[3,6,1,32]{3,2,1,0:T(1,128)S(1)}, u32[]{:S(2)}, u32[]{:S(2)}) collective-permute-start(f32[3,6,1,32]{3,2,1,0:T(1,128)S(1)} %get-tuple-element.117), channel_id=1, source_target_pairs={{0,8},{8,16},{16,24},{24,32},{32,40},{40,48},{48,56},{1,9},{9,17},... | collective-permute-start | bytes 6920 | tf_op jit(solution)/shard_map/ppermute | solution.py:24
  85.8 1.3 collective-permute-start.11
  87.1 3.1 %collective-permute-done.11 = f32[3,6,1,32]{3,2,1,0:T(1,128)S(1)} collective-permute-done((f32[3,6,1,32]{3,2,1,0:T(1,128)S(1)}, f32[3,6,1,32]{3,2,1,0:T(1,128)S(1)}, u32[]{:S(2)}, u32[]{:S(2)}) %collective-permute-start.11) | collective-permute-done | bytes 2336 | tf_op jit(solution)/shard_map/ppermute | solution.py:27
  90.3 6.7 %collective-permute-start.12 = (f32[3,6,6,1]{3,2,1,0:T(8,128)S(1)}, f32[3,6,6,1]{3,2,1,0:T(8,128)S(1)}, u32[]{:S(2)}, u32[]{:S(2)}) collective-permute-start(f32[3,6,6,1]{3,2,1,0:T(8,128)S(1)} %get-tuple-element.111), channel_id=1, source_target_pairs={{0,1},{1,2},{2,3},{3,4},{4,5},{5,6},{6,7},{8,9},{9,10},{10,11},{11... | collective-permute-start | bytes 1304 | tf_op jit(solution)/shard_map/ppermute | solution.py:24
  97.0 2.1 %collective-permute-start.13 = (f32[3,6,6,1]{3,2,1,0:T(8,128)S(1)}, f32[3,6,6,1]{3,2,1,0:T(8,128)S(1)}, u32[]{:S(2)}, u32[]{:S(2)}) collective-permute-start(f32[3,6,6,1]{3,2,1,0:T(8,128)S(1)} %get-tuple-element.112), channel_id=1, source_target_pairs={{1,0},{2,1},{3,2},{4,3},{5,4},{6,5},{7,6},{9,8},{10,9},{11,10},{12... | collective-permute-start | bytes 1304 | tf_op jit(solution)/shard_map/ppermute | solution.py:27
  99.1 0.5 add_convert_fusion
  99.8 0.6 eq.188
  100.5 2.2 %collective-permute-done.13 = f32[3,6,6,1]{3,2,1,0:T(8,128)S(1)} collective-permute-done((f32[3,6,6,1]{3,2,1,0:T(8,128)S(1)}, f32[3,6,6,1]{3,2,1,0:T(8,128)S(1)}, u32[]{:S(2)}, u32[]{:S(2)}) %collective-permute-start.13) | collective-permute-done | bytes 464 | tf_op jit(solution)/shard_map/ppermute | solution.py:27
  103.8 0.6 slice_add_fusion.36
  104.4 0.6 fusion.133
  105.0 0.6 fusion.139
  105.6 0.6 slice_add_fusion.33
  106.6 0.4 multiply_add_fusion
  107.7 1.2 fusion.48
  109.2 1.4 %multiply_reduce_fusion.1 = (f32[3,20,5,32]{3,1,2,0:T(8,128)S(1)}, f32[3,20,5,32]{3,1,2,0:T(8,128)S(1)}) fusion(f32[4]{0:T(128)S(1)} %copy-done.32, f32[4]{0:T(128)S(1)} %copy-done.29, f32[34,132]{1,0:T(8,128)S(1)} %copy-done.16, f32[20,5,4,132]{3,0,2,1:T(8,128)S(1)} %bitcast.483, f32[20,5,4,132]{3,0,2,1:T(8,128)S(1)} %bitcast.482, ...), kind=kOutput, calls=%fused_computation.24 | convolution fusion | flops 61752000 | bytes 1830912 | tf_op jit(solution)/shard_map/dot_general | solution.py:219
  111.8 0.7 copy.136
  112.5 6.4 %all-to-all-start.1 = ((f32[3,64,16]{2,0,1:T(4,128)}), f32[3,64,16]{2,0,1:T(4,128)S(1)}, u32[]{:S(2)}, u32[]{:S(2)}) async-start(f32[3,64,16]{2,0,1:T(4,128)} %copy.136), calls=%async_computation.1 | async-start | bytes 262144 | tf_op jit(solution)/shard_map/all_to_all | solution.py:352
  119.0 0.7 slice_add_fusion.57
  119.6 10.4 %all-to-all-done.1 = f32[3,64,16]{2,0,1:T(4,128)S(1)} async-done(((f32[3,64,16]{2,0,1:T(4,128)}), f32[3,64,16]{2,0,1:T(4,128)S(1)}, u32[]{:S(2)}, u32[]{:S(2)}) %all-to-all-start.1) | async-done | bytes 12320 | tf_op jit(solution)/shard_map/all_to_all | solution.py:352
  130.2 0.9 convolution_bitcast_fusion
  (254 shorter events, 9.9 us)
Async XLA Ops:
  1.9 25.6 %collective-permute-start = (bf16[3,16,5,128]{3,2,1,0:T(8,128)(2,1)S(1)}, bf16[3,16,5,128]{3,2,1,0:T(8,128)(2,1)S(1)}, u32[]{:S(2)}, u32[]{:S(2)}) collective-permute-start(bf16[3,16,5,128]{3,2,1,0:T(8,128)(2,1)S(1)} %get-tuple-element.101), channel_id=1, source_target_pairs={{0,8},{8,16},{16,24},{24,32},{32,40},{40,48},{48,56},{1,9},{9,17},... | collective-permute-start | bytes 184328 | tf_op jit(solution)/shard_map/ppermute | solution.py:24
  5.9 21.5 %collective-permute-start.1 = (bf16[3,16,5,128]{3,2,1,0:T(8,128)(2,1)S(1)}, bf16[3,16,5,128]{3,2,1,0:T(8,128)(2,1)S(1)}, u32[]{:S(2)}, u32[]{:S(2)}) collective-permute-start(bf16[3,16,5,128]{3,2,1,0:T(8,128)(2,1)S(1)} %get-tuple-element.102), channel_id=1, source_target_pairs={{8,0},{16,8},{24,16},{32,24},{40,32},{48,40},{56,48},{9,1},{17,9},... | collective-permute-start | bytes 184328 | tf_op jit(solution)/shard_map/ppermute | solution.py:27
  9.7 0.6 copy-start.24
  12.1 15.3 %copy-start = (bf16[16,16,128]{2,1,0:T(8,128)(2,1)S(1)}, bf16[16,16,128]{2,1,0:T(8,128)(2,1)}, u32[]{:S(2)}) copy-start(bf16[16,16,128]{2,1,0:T(8,128)(2,1)} %param.6) | copy-start | bytes 196612
  12.2 15.3 %copy-start.1 = (bf16[16,16,128]{2,1,0:T(8,128)(2,1)S(1)}, bf16[16,16,128]{2,1,0:T(8,128)(2,1)}, u32[]{:S(2)}) copy-start(bf16[16,16,128]{2,1,0:T(8,128)(2,1)} %param.5) | copy-start | bytes 196612
  13.7 24.5 %all-to-all-start = ((f32[4,64,80]{2,0,1:T(4,128)}), f32[4,64,80]{2,0,1:T(4,128)S(1)}, u32[]{:S(2)}, u32[]{:S(2)}) async-start(f32[4,64,80]{2,0,1:T(4,128)} %copy.111), calls=%async_computation | async-start | bytes 262144 | tf_op jit(solution)/shard_map/all_to_all | solution.py:295
  27.1 29.3 %copy-start.27 = (f32[4]{0:T(128)}, f32[4]{0:T(128)S(1)}, u32[]{:S(2)}) copy-start(f32[4]{0:T(128)S(1)} %get-tuple-element.152) | copy-start | bytes 52
  27.1 29.3 %copy-start.30 = (f32[4]{0:T(128)}, f32[4]{0:T(128)S(1)}, u32[]{:S(2)}) copy-start(f32[4]{0:T(128)S(1)} %get-tuple-element.153) | copy-start | bytes 52
  27.1 28.0 %copy-start.33 = (f32[132]{0:T(256)}, f32[132]{0:T(256)S(1)}, u32[]{:S(2)}) copy-start(f32[132]{0:T(256)S(1)} %get-tuple-element.150) | copy-start | bytes 1588
  27.1 28.0 %copy-start.35 = (f32[132]{0:T(256)}, f32[132]{0:T(256)S(1)}, u32[]{:S(2)}) copy-start(f32[132]{0:T(256)S(1)} %get-tuple-element.151) | copy-start | bytes 1588
  27.1 28.0 %copy-start.20 = (s32[132]{0:T(256)}, s32[132]{0:T(256)S(1)}, u32[]{:S(2)}) copy-start(s32[132]{0:T(256)S(1)} %get-tuple-element.148) | copy-start | bytes 1588
  27.1 28.0 %copy-start.22 = (s32[132]{0:T(256)}, s32[132]{0:T(256)S(1)}, u32[]{:S(2)}) copy-start(s32[132]{0:T(256)S(1)} %get-tuple-element.149) | copy-start | bytes 1588
  27.2 28.9 %copy-start.37 = (f32[20]{0:T(128)}, f32[20]{0:T(128)S(1)}, u32[]{:S(2)}) copy-start(f32[20]{0:T(128)S(1)} %mul.999) | copy-start | bytes 244
  27.3 28.8 %copy-start.39 = (f32[20]{0:T(128)}, f32[20]{0:T(128)S(1)}, u32[]{:S(2)}) copy-start(f32[20]{0:T(128)S(1)} %mul.993) | copy-start | bytes 244
  27.4 43.5 %copy-start.15 = (f32[34,132]{1,0:T(8,128)}, f32[34,132]{1,0:T(8,128)S(1)}, u32[]{:S(2)}) copy-start(f32[34,132]{1,0:T(8,128)S(1)} %select_add_fusion) | copy-start | bytes 53860
  27.4 39.7 %copy-start.41 = (f32[4]{0:T(128)}, f32[4]{0:T(128)S(1)}, u32[]{:S(2)}) copy-start(f32[4]{0:T(128)S(1)} %get-tuple-element.158) | copy-start | bytes 52
  27.4 39.7 %copy-start.42 = (f32[4]{0:T(128)}, f32[4]{0:T(128)S(1)}, u32[]{:S(2)}) copy-start(f32[4]{0:T(128)S(1)} %get-tuple-element.159) | copy-start | bytes 52
  28.6 18.5 %collective-permute-start.2 = (bf16[3,16,26,5]{3,2,1,0:T(8,128)(2,1)}, bf16[3,16,26,5]{3,2,1,0:T(8,128)(2,1)S(1)}, u32[]{:S(2)}, u32[]{:S(2)}) collective-permute-start(bf16[3,16,26,5]{3,2,1,0:T(8,128)(2,1)} %get-tuple-element.74), channel_id=1, source_target_pairs={{0,1},{1,2},{2,3},{3,4},{4,5},{5,6},{6,7},{8,9},{9,10},{10,11},{11... | collective-permute-start | bytes 37448 | tf_op jit(solution)/shard_map/ppermute | solution.py:24
  32.1 15.0 %collective-permute-start.3 = (bf16[3,16,26,5]{3,2,1,0:T(8,128)(2,1)S(1)}, bf16[3,16,26,5]{3,2,1,0:T(8,128)(2,1)S(1)}, u32[]{:S(2)}, u32[]{:S(2)}) collective-permute-start(bf16[3,16,26,5]{3,2,1,0:T(8,128)(2,1)S(1)} %get-tuple-element.75), channel_id=1, source_target_pairs={{1,0},{2,1},{3,2},{4,3},{5,4},{6,5},{7,6},{9,8},{10,9},{11,10},{12... | collective-permute-start | bytes 37448 | tf_op jit(solution)/shard_map/ppermute | solution.py:27
  39.3 1.1 copy-start.25
  40.8 14.1 %copy-start.2 = (f32[3,9,4,4,32]{4,3,2,1,0:T(4,128)}, f32[3,9,4,4,32]{4,3,2,1,0:T(4,128)S(1)}, u32[]{:S(2)}) copy-start(f32[3,9,4,4,32]{4,3,2,1,0:T(4,128)S(1)} %reshape.465) | copy-start | bytes 165892
  41.2 13.3 %collective-permute-start.7 = (f32[3,1,6,34]{3,2,1,0:T(8,128)S(1)}, f32[3,1,6,34]{3,2,1,0:T(8,128)S(1)}, u32[]{:S(2)}, u32[]{:S(2)}) collective-permute-start(f32[3,1,6,34]{3,2,1,0:T(8,128)S(1)} %get-tuple-element.107), channel_id=1, source_target_pairs={{64,0},{128,64},{192,128},{256,192},{320,256},{384,320},{448,384},... | collective-permute-start | bytes 7352 | tf_op jit(solution)/shard_map/ppermute | solution.py:27
  42.5 12.0 %collective-permute-start.6 = (f32[3,1,6,34]{3,2,1,0:T(8,128)S(1)}, f32[3,1,6,34]{3,2,1,0:T(8,128)S(1)}, u32[]{:S(2)}, u32[]{:S(2)}) collective-permute-start(f32[3,1,6,34]{3,2,1,0:T(8,128)S(1)} %get-tuple-element.108), channel_id=1, source_target_pairs={{0,64},{64,128},{128,192},{192,256},{256,320},{320,384},{384,448},... | collective-permute-start | bytes 7352 | tf_op jit(solution)/shard_map/ppermute | solution.py:24
  48.3 11.2 %collective-permute-start.4 = (bf16[3,5,26,138]{3,2,1,0:T(8,128)(2,1)}, bf16[3,5,26,138]{3,2,1,0:T(8,128)(2,1)}, u32[]{:S(2)}, u32[]{:S(2)}) collective-permute-start(bf16[3,5,26,138]{3,2,1,0:T(8,128)(2,1)} %get-tuple-element.62), channel_id=1, source_target_pairs={{0,64},{64,128},{128,192},{192,256},{256,320},{320,384},{384,448},... | collective-permute-start | bytes 322928 | tf_op jit(solution)/shard_map/ppermute | solution.py:24
  53.0 8.4 %collective-permute-start.5 = (bf16[3,5,26,138]{3,2,1,0:T(8,128)(2,1)S(1)}, bf16[3,5,26,138]{3,2,1,0:T(8,128)(2,1)}, u32[]{:S(2)}, u32[]{:S(2)}) collective-permute-start(bf16[3,5,26,138]{3,2,1,0:T(8,128)(2,1)S(1)} %get-tuple-element.63), channel_id=1, source_target_pairs={{64,0},{128,64},{192,128},{256,192},{320,256},{384,320},{448,384},... | collective-permute-start | bytes 322928 | tf_op jit(solution)/shard_map/ppermute | solution.py:27
  66.2 4.8 %copy-start.3 = (f32[20,20,132]{2,0,1:T(8,128)}, f32[20,20,132]{2,0,1:T(8,128)S(1)}, u32[]{:S(2)}) copy-start(f32[20,20,132]{2,0,1:T(8,128)S(1)} %copy.145) | copy-start | bytes 633604
  66.6 4.4 %copy-start.5 = (bf16[20,20,132]{2,0,1:T(8,128)(2,1)}, bf16[20,20,132]{2,0,1:T(8,128)(2,1)S(1)}, u32[]{:S(2)}) copy-start(bf16[20,20,132]{2,0,1:T(8,128)(2,1)S(1)} %copy.142) | copy-start | bytes 316804
  67.0 4.0 %copy-start.7 = (bf16[20,20,132]{2,0,1:T(8,128)(2,1)}, bf16[20,20,132]{2,0,1:T(8,128)(2,1)S(1)}, u32[]{:S(2)}) copy-start(bf16[20,20,132]{2,0,1:T(8,128)(2,1)S(1)} %copy.143) | copy-start | bytes 316804
  67.2 3.8 %copy-start.9 = (bf16[20,20,132]{2,0,1:T(8,128)(2,1)}, bf16[20,20,132]{2,0,1:T(8,128)(2,1)S(1)}, u32[]{:S(2)}) copy-start(bf16[20,20,132]{2,0,1:T(8,128)(2,1)S(1)} %copy.144) | copy-start | bytes 316804
  69.7 1.3 copy-start.28
  69.7 1.3 copy-start.31
  71.0 1.7 %copy-start.17 = (f32[1,4,4,32]{3,2,1,0:T(4,128)S(1)}, f32[1,4,4,32]{3,2,1,0:T(4,128)}, u32[]{:S(2)}) copy-start(f32[1,4,4,32]{3,2,1,0:T(4,128)} %fusion.161) | copy-start | bytes 6148
  71.0 1.7 %copy-start.18 = (f32[1,4,4,32]{3,2,1,0:T(4,128)S(1)}, f32[1,4,4,32]{3,2,1,0:T(4,128)}, u32[]{:S(2)}) copy-start(f32[1,4,4,32]{3,2,1,0:T(4,128)} %fusion.155) | copy-start | bytes 6148
  71.0 1.7 %copy-start.19 = (f32[1,4,4,32]{3,2,1,0:T(4,128)S(1)}, f32[1,4,4,32]{3,2,1,0:T(4,128)}, u32[]{:S(2)}) copy-start(f32[1,4,4,32]{3,2,1,0:T(4,128)} %fusion.149) | copy-start | bytes 6148
  72.4 27.3 %copy-start.26 = (f32[640]{0:T(1024)S(1)}, f32[640]{0:T(1024)}, u32[]{:S(2)}) copy-start(f32[640]{0:T(1024)} %copy-done.25) | copy-start | bytes 7684
  72.4 30.4 %copy-start.21 = (s32[132]{0:T(256)S(1)}, s32[132]{0:T(256)}, u32[]{:S(2)}) copy-start(s32[132]{0:T(256)} %copy-done.20) | copy-start | bytes 1588
  72.5 30.4 %copy-start.23 = (s32[132]{0:T(256)S(1)}, s32[132]{0:T(256)}, u32[]{:S(2)}) copy-start(s32[132]{0:T(256)} %copy-done.22) | copy-start | bytes 1588
  72.5 30.4 %copy-start.34 = (f32[132]{0:T(256)S(1)}, f32[132]{0:T(256)}, u32[]{:S(2)}) copy-start(f32[132]{0:T(256)} %copy-done.33) | copy-start | bytes 1588
  72.5 30.4 %copy-start.36 = (f32[132]{0:T(256)S(1)}, f32[132]{0:T(256)}, u32[]{:S(2)}) copy-start(f32[132]{0:T(256)} %copy-done.35) | copy-start | bytes 1588
  73.5 6.8 %collective-permute-start.8 = (f32[3,1,4,32]{3,2,1,0:T(4,128)S(1)}, f32[3,1,4,32]{3,2,1,0:T(4,128)S(1)}, u32[]{:S(2)}, u32[]{:S(2)}) collective-permute-start(f32[3,1,4,32]{3,2,1,0:T(4,128)S(1)} %get-tuple-element.119), channel_id=1, source_target_pairs={{0,64},{64,128},{128,192},{192,256},{256,320},{320,384},{384,448},... | collective-permute-start | bytes 4616 | tf_op jit(solution)/shard_map/ppermute | solution.py:24
  79.0 4.4 %collective-permute-start.9 = (f32[3,1,4,32]{3,2,1,0:T(4,128)S(1)}, f32[3,1,4,32]{3,2,1,0:T(4,128)S(1)}, u32[]{:S(2)}, u32[]{:S(2)}) collective-permute-start(f32[3,1,4,32]{3,2,1,0:T(4,128)S(1)} %get-tuple-element.120), channel_id=1, source_target_pairs={{64,0},{128,64},{192,128},{256,192},{320,256},{384,320},{448,384},... | collective-permute-start | bytes 4616 | tf_op jit(solution)/shard_map/ppermute | solution.py:27
  83.4 3.7 %collective-permute-start.10 = (f32[3,6,1,32]{3,2,1,0:T(1,128)S(1)}, f32[3,6,1,32]{3,2,1,0:T(1,128)S(1)}, u32[]{:S(2)}, u32[]{:S(2)}) collective-permute-start(f32[3,6,1,32]{3,2,1,0:T(1,128)S(1)} %get-tuple-element.117), channel_id=1, source_target_pairs={{0,8},{8,16},{16,24},{24,32},{32,40},{40,48},{48,56},{1,9},{9,17},... | collective-permute-start | bytes 6920 | tf_op jit(solution)/shard_map/ppermute | solution.py:24
  85.8 4.4 %collective-permute-start.11 = (f32[3,6,1,32]{3,2,1,0:T(1,128)S(1)}, f32[3,6,1,32]{3,2,1,0:T(1,128)S(1)}, u32[]{:S(2)}, u32[]{:S(2)}) collective-permute-start(f32[3,6,1,32]{3,2,1,0:T(1,128)S(1)} %get-tuple-element.118), channel_id=1, source_target_pairs={{8,0},{16,8},{24,16},{32,24},{40,32},{48,40},{56,48},{9,1},{17,9},... | collective-permute-start | bytes 6920 | tf_op jit(solution)/shard_map/ppermute | solution.py:27
  90.3 10.2 %collective-permute-start.12 = (f32[3,6,6,1]{3,2,1,0:T(8,128)S(1)}, f32[3,6,6,1]{3,2,1,0:T(8,128)S(1)}, u32[]{:S(2)}, u32[]{:S(2)}) collective-permute-start(f32[3,6,6,1]{3,2,1,0:T(8,128)S(1)} %get-tuple-element.111), channel_id=1, source_target_pairs={{0,1},{1,2},{2,3},{3,4},{4,5},{5,6},{6,7},{8,9},{9,10},{10,11},{11... | collective-permute-start | bytes 1304 | tf_op jit(solution)/shard_map/ppermute | solution.py:24
  97.0 5.7 %collective-permute-start.13 = (f32[3,6,6,1]{3,2,1,0:T(8,128)S(1)}, f32[3,6,6,1]{3,2,1,0:T(8,128)S(1)}, u32[]{:S(2)}, u32[]{:S(2)}) collective-permute-start(f32[3,6,6,1]{3,2,1,0:T(8,128)S(1)} %get-tuple-element.112), channel_id=1, source_target_pairs={{1,0},{2,1},{3,2},{4,3},{5,4},{6,5},{7,6},{9,8},{10,9},{11,10},{12... | collective-permute-start | bytes 1304 | tf_op jit(solution)/shard_map/ppermute | solution.py:27
  103.5 2.8 %copy-start.38 = (f32[20]{0:T(128)S(1)}, f32[20]{0:T(128)}, u32[]{:S(2)}) copy-start(f32[20]{0:T(128)} %copy-done.37) | copy-start | bytes 244
  103.5 2.8 %copy-start.40 = (f32[20]{0:T(128)S(1)}, f32[20]{0:T(128)}, u32[]{:S(2)}) copy-start(f32[20]{0:T(128)} %copy-done.39) | copy-start | bytes 244
  107.6 1.5 %copy-start.4 = (f32[20,20,132]{2,0,1:T(8,128)S(1)}, f32[20,20,132]{2,0,1:T(8,128)}, u32[]{:S(2)}) copy-start(f32[20,20,132]{2,0,1:T(8,128)} %copy-done.3) | copy-start | bytes 633604
  107.6 1.5 %copy-start.6 = (bf16[20,20,132]{2,0,1:T(8,128)(2,1)S(1)}, bf16[20,20,132]{2,0,1:T(8,128)(2,1)}, u32[]{:S(2)}) copy-start(bf16[20,20,132]{2,0,1:T(8,128)(2,1)} %copy-done.5) | copy-start | bytes 316804
  107.6 1.5 %copy-start.8 = (bf16[20,20,132]{2,0,1:T(8,128)(2,1)S(1)}, bf16[20,20,132]{2,0,1:T(8,128)(2,1)}, u32[]{:S(2)}) copy-start(bf16[20,20,132]{2,0,1:T(8,128)(2,1)} %copy-done.7) | copy-start | bytes 316804
  107.6 1.5 %copy-start.10 = (bf16[20,20,132]{2,0,1:T(8,128)(2,1)S(1)}, bf16[20,20,132]{2,0,1:T(8,128)(2,1)}, u32[]{:S(2)}) copy-start(bf16[20,20,132]{2,0,1:T(8,128)(2,1)} %copy-done.9) | copy-start | bytes 316804
  107.7 1.5 %copy-start.16 = (f32[34,132]{1,0:T(8,128)S(1)}, f32[34,132]{1,0:T(8,128)}, u32[]{:S(2)}) copy-start(f32[34,132]{1,0:T(8,128)} %copy-done.15) | copy-start | bytes 53860
  107.7 1.5 %copy-start.29 = (f32[4]{0:T(128)S(1)}, f32[4]{0:T(128)}, u32[]{:S(2)}) copy-start(f32[4]{0:T(128)} %copy-done.27) | copy-start | bytes 52
  107.7 1.5 %copy-start.32 = (f32[4]{0:T(128)S(1)}, f32[4]{0:T(128)}, u32[]{:S(2)}) copy-start(f32[4]{0:T(128)} %copy-done.30) | copy-start | bytes 52
  109.1 1.8 %copy-start.13 = (f32[4,4,33]{2,1,0:T(4,128)S(1)}, f32[4,4,33]{2,1,0:T(4,128)}, u32[]{:S(2)}) copy-start(f32[4,4,33]{2,1,0:T(4,128)} %fusion.139) | copy-start | bytes 6340
  109.2 1.8 %copy-start.11 = (f32[4,4,33]{2,1,0:T(4,128)S(1)}, f32[4,4,33]{2,1,0:T(4,128)}, u32[]{:S(2)}) copy-start(f32[4,4,33]{2,1,0:T(4,128)} %slice_add_fusion.36) | copy-start | bytes 6340
  109.2 1.8 %copy-start.12 = (f32[4,4,33]{2,1,0:T(4,128)S(1)}, f32[4,4,33]{2,1,0:T(4,128)}, u32[]{:S(2)}) copy-start(f32[4,4,33]{2,1,0:T(4,128)} %fusion.133) | copy-start | bytes 6340
  109.2 1.8 %copy-start.14 = (f32[4,4,33]{2,1,0:T(4,128)S(1)}, f32[4,4,33]{2,1,0:T(4,128)}, u32[]{:S(2)}) copy-start(f32[4,4,33]{2,1,0:T(4,128)} %slice_add_fusion.33) | copy-start | bytes 6340
  110.6 0.7 copy-start.43
  110.6 0.7 copy-start.45
  110.6 8.3 %copy-start.44 = (s32[64]{0:T(128)S(1)}, s32[64]{0:T(128)}, u32[]{:S(2)}) copy-start(s32[64]{0:T(128)} %get-tuple-element.53) | copy-start | bytes 772
  112.5 17.5 %all-to-all-start.1 = ((f32[3,64,16]{2,0,1:T(4,128)}), f32[3,64,16]{2,0,1:T(4,128)S(1)}, u32[]{:S(2)}, u32[]{:S(2)}) async-start(f32[3,64,16]{2,0,1:T(4,128)} %copy.136), calls=%async_computation.1 | async-start | bytes 262144 | tf_op jit(solution)/shard_map/all_to_all | solution.py:352

commit v5 on v4

--- a/solution.py
+++ b/solution.py
@@ -228,7 +228,9 @@
 
 def per_device(reference_image, deformed_image, roi_mask, displacement, node_map):
     stacked = jnp.stack([reference_image, deformed_image, roi_mask.astype(jnp.bfloat16)])
-    padded_images = with_halo(stacked, (("gy", 2), ("gz", 3), ("gx", 1)), 5).astype(jnp.float32)
+    stacked = with_halo(stacked, (("gy", 2),), 5)
+    stacked = with_halo(stacked, (("gz", 3),), 5 + ELEM)
+    padded_images = with_halo(stacked, (("gx", 1),), 5).astype(jnp.float32)
     nodes_shape = (
         3,
         reference_image.shape[0] // ELEM,
@@ -238,7 +240,9 @@
     _, ex, ey, ez = nodes_shape
     weights_table = axis_table(ez + 2, ELEM, False)
     table_back = weights_table[1:-1].T
-    table_square = axis_table(ez + 2, ELEM, True)[1:-1].T
+    wide_table = axis_table(ez + 4, ELEM, False)
+    wide_back = wide_table[1:-1].T
+    wide_square = axis_table(ez + 4, ELEM, True)[1:-1].T
     size_y = lax.axis_size("gy")
     size_z = lax.axis_size("gz")
     members = size_y * size_z
@@ -306,20 +310,20 @@
     def near(ry, rz):
         return around[:, NEIGHBOURS.index((ry, rz))]
 
-    tile_values = near(0, 0)
+    centre = near(0, 0)
     middle = jnp.concatenate(
-        [near(0, -1)[..., ez - 1 :], tile_values, near(0, 1)[..., :1]], axis=3
+        [near(0, -1)[..., ez - 2 :], centre, near(0, 1)[..., :2]], axis=3
     )
     low_row = jnp.concatenate(
         [
-            near(-1, -1)[:, :, ey - 1 :, ez - 1 :],
+            near(-1, -1)[:, :, ey - 1 :, ez - 2 :],
             near(-1, 0)[:, :, ey - 1 :, :],
-            near(-1, 1)[:, :, ey - 1 :, :1],
+            near(-1, 1)[:, :, ey - 1 :, :2],
         ],
         axis=3,
     )
     high_row = jnp.concatenate(
-        [near(1, -1)[:, :, :1, ez - 1 :], near(1, 0)[:, :, :1, :], near(1, 1)[:, :, :1, :1]],
+        [near(1, -1)[:, :, :1, ez - 2 :], near(1, 0)[:, :, :1, :], near(1, 1)[:, :, :1, :2]],
         axis=3,
     )
     extended = jnp.concatenate([low_row, middle, high_row], axis=2)
@@ -329,17 +333,28 @@
     contrast = derived[0].astype(jnp.float32)
     slopes = derived[1:].astype(jnp.float32)
     masked_slopes = slopes * region[None]
-    curvature = collect(masked_slopes * slopes, table_square, True) + diagonal_shift
-    for iteration in range(ITERS):
-        if iteration == 0:
-            padded = first_padded
-        else:
-            padded = with_halo(tile_values, (("gx", 1), ("gy", 2), ("gz", 3)), 1)
-        moved = spread(padded, weights_table)
-        residual = contrast + slopes[0] * moved[0] + slopes[1] * moved[1] + slopes[2] * moved[2]
-        image_part = collect(masked_slopes * residual[None], table_back, False)
-        force_total = image_part + elastic_weight * elastic_force(padded)
-        tile_values = tile_values - force_total / curvature
+    wide_curvature = collect(masked_slopes * slopes, wide_square, True) + diagonal_shift
+    moved = spread(first_padded, wide_table)
+    residual = contrast + slopes[0] * moved[0] + slopes[1] * moved[1] + slopes[2] * moved[2]
+    image_part = collect(masked_slopes * residual[None], wide_back, False)
+    force_total = image_part + elastic_weight * elastic_force(first_padded)
+    wide_values = first_padded[:, 1:-1, 1:-1, 1:-1] - force_total / wide_curvature
+    column = jnp.arange(ez + 2, dtype=jnp.int32)
+    ghost = ((column == 0) & (lax.axis_index("gz") == 0)) | (
+        (column == ez + 1) & (lax.axis_index("gz") == size_z - 1)
+    )
+    wide_values = jnp.where(ghost, 0.0, wide_values)
+    tile_values = wide_values[..., 1:-1]
+    curvature = wide_curvature[..., 1:-1]
+    contrast = contrast[..., ELEM:-ELEM]
+    slopes = slopes[..., ELEM:-ELEM]
+    masked_slopes = masked_slopes[..., ELEM:-ELEM]
+    padded = with_halo(wide_values, (("gx", 1), ("gy", 2)), 1)
+    moved = spread(padded, weights_table)
+    residual = contrast + slopes[0] * moved[0] + slopes[1] * moved[1] + slopes[2] * moved[2]
+    image_part = collect(masked_slopes * residual[None], table_back, False)
+    force_total = image_part + elastic_weight * elastic_force(padded)
+    tile_values = tile_values - force_total / curvature
     final_blocks = tile_values.reshape(3, blocks, block_nodes)
     own_labels = received_labels.reshape(members, HALO_CAP)[:, :CAP].reshape(-1)
     position = jnp.arange(blocks, dtype=jnp.int32)

time: 132 us -> 132 us (level)
  waiting for transfers between devices: 24.8 us -> 18.5 us
  local copies, waits for them, and re-layouts: 11.8 us -> 17.7 us
    all_to_all x1, starting transfers between devices: 6.42 us -> 13.4 us  [per_device(): lax.all_to_all(outgoing, ('gy', 'gz'), split_axis=1, concat_axis=1, tiled...]
    ppermute x7 -> x6, starting transfers between devices: 31.4 us -> 25.6 us  [with_halo(): lax.ppermute(lax.slice_in_dim(block, block.shape[dim] - width, None, axis...]
    all_to_all x1, waiting for transfers between devices: 4.08 us -> 0.01 us  [per_device(): lax.all_to_all(send_outgoing, ('gy', 'gz'), split_axis=1, concat_axis=1,...]
    ppermute x7 -> x6, waiting for transfers between devices: 10.3 us -> 8.09 us  [with_halo(): lax.ppermute(lax.slice_in_dim(block, 0, width, axis=dim), axis, backward)]
    ppermute x7 -> x6, starting transfers between devices: 10.7 us -> 8.77 us  [with_halo(): lax.ppermute(lax.slice_in_dim(block, 0, width, axis=dim), axis, backward)]
    unnamed x92 -> x98, local copies, waits for them, and re-layouts: 0.78 us -> 2.65 us
    squeeze x2, local copies, waits for them, and re-layouts: 0.28 us -> 2.1 us  [per_device(): moved[1]]
    another operation x6, other arithmetic: 2.28 us -> 0.48 us  [elastic_force(): return jnp.stack(forces)]
  transfers between devices with their start and end apart: 16 -> 14, of which waited for: 6 -> 4; matrix products, arithmetic and copies ran while one was open for 13% -> 17% of each run, Pallas kernels for 0% -> 0%
where the time goes in v5:
time: 132 us; the launch traced here: 131 us
  starting transfers between devices  61.1 us (46%)
  other arithmetic  24.7 us (19%)
  waiting for transfers between devices  18.5 us (14%)
  local copies, waits for them, and re-layouts  17.7 us (13%)
  matrix products  7.29 us (6%)
  between operations  1.7 us (1%)
    ppermute x6, starting transfers between devices, with_halo(): lax.ppermute(lax.slice_in_dim(block, block.shape[dim] - width, None, axis...  25.6 us
    all_to_all x1, starting transfers between devices, per_device(): lax.all_to_all(outgoing, ('gy', 'gz'), split_axis=1, concat_axis=1, tiled...  13.4 us
    all_to_all x1, starting transfers between devices, per_device(): lax.all_to_all(send_outgoing, ('gy', 'gz'), split_axis=1, concat_axis=1,...  13.3 us
    all_to_all x1, waiting for transfers between devices, per_device(): lax.all_to_all(outgoing, ('gy', 'gz'), split_axis=1, concat_axis=1, tiled...  10.4 us
    ppermute x6, starting transfers between devices, with_halo(): lax.ppermute(lax.slice_in_dim(block, 0, width, axis=dim), axis, backward)  8.77 us
    ppermute x6, waiting for transfers between devices, with_halo(): lax.ppermute(lax.slice_in_dim(block, 0, width, axis=dim), axis, backward)  8.09 us
    dot_general x3, matrix products, collect(): jnp.dot(volume.reshape(-1, shape_all[3]), table_back, precision=highest)  4.06 us
    unnamed x98, local copies, waits for them, and re-layouts  2.65 us
  transfers between devices with their start and end apart: 14, of which 4 were waited for; matrix products, arithmetic and copies ran while one was open for 17% of the time, Pallas kernels for 0%

profile of v5, /device:TPU:1, one launch (start us, length us, event | category | flops | bytes accessed | tf_op | source)
XLA Modules:
  0.0 131.0 jit_solution(15082787187574991375)
XLA Ops:
  0.0 0.9 convert_bitcast_fusion
  0.9 0.9 pad_maximum_fusion.11
  1.9 4.0 %collective-permute-start = (bf16[3,16,5,128]{3,2,1,0:T(8,128)(2,1)S(1)}, bf16[3,16,5,128]{3,2,1,0:T(8,128)(2,1)S(1)}, u32[]{:S(2)}, u32[]{:S(2)}) collective-permute-start(bf16[3,16,5,128]{3,2,1,0:T(8,128)(2,1)S(1)} %get-tuple-element.103), channel_id=1, source_target_pairs={{0,8},{8,16},{16,24},{24,32},{32,40},{40,48},{48,56},{1,9},{9,17},... | collective-permute-start | bytes 184328 | tf_op jit(solution)/shard_map/ppermute | solution.py:24
  5.9 1.3 collective-permute-start.1
  7.2 0.7 broadcast_add_fusion.2
  7.9 1.2 and_and_fusion
  9.7 0.6 copy-done.20
  10.3 1.1 concatenate.67
  11.4 0.7 fusion.7
  12.9 0.7 copy.111
  13.6 13.3 %all-to-all-start = ((f32[4,64,80]{2,0,1:T(4,128)}), f32[4,64,80]{2,0,1:T(4,128)S(1)}, u32[]{:S(2)}, u32[]{:S(2)}) async-start(f32[4,64,80]{2,0,1:T(4,128)} %copy.111), calls=%async_computation | async-start | bytes 262144 | tf_op jit(solution)/shard_map/all_to_all | solution.py:299
  27.0 0.6 fusion.192
  27.6 0.6 fusion.187
  28.2 0.6 fusion.183
  28.8 0.6 and_select_fusion.1
  29.4 0.6 mul.1021
  30.1 0.6 mul.1015
  30.7 0.6 iota_compare_fusion.8
  31.3 0.6 iota_compare_fusion.7
  31.9 0.6 select_add_fusion.1
  32.5 0.5 and_or_fusion
  33.4 3.5 %collective-permute-start.2 = (bf16[3,16,26,9]{3,2,1,0:T(8,128)(2,1)S(1)}, bf16[3,16,26,9]{3,2,1,0:T(8,128)(2,1)S(1)}, u32[]{:S(2)}, u32[]{:S(2)}) collective-permute-start(bf16[3,16,26,9]{3,2,1,0:T(8,128)(2,1)S(1)} %get-tuple-element.76), channel_id=1, source_target_pairs={{0,1},{1,2},{2,3},{3,4},{4,5},{5,6},{6,7},{8,9},{9,10},{10,11},{11... | collective-permute-start | bytes 67400 | tf_op jit(solution)/shard_map/ppermute | solution.py:24
  37.0 1.9 %collective-permute-start.3 = (bf16[3,16,26,9]{3,2,1,0:T(8,128)(2,1)S(1)}, bf16[3,16,26,9]{3,2,1,0:T(8,128)(2,1)S(1)}, u32[]{:S(2)}, u32[]{:S(2)}) collective-permute-start(bf16[3,16,26,9]{3,2,1,0:T(8,128)(2,1)S(1)} %get-tuple-element.77), channel_id=1, source_target_pairs={{1,0},{2,1},{3,2},{4,3},{5,4},{6,5},{7,6},{9,8},{10,9},{11,10},{12... | collective-permute-start | bytes 67400 | tf_op jit(solution)/shard_map/ppermute | solution.py:27
  40.2 0.8 fusion.8
  42.0 4.0 %collective-permute-start.6 = (f32[3,1,6,36]{3,2,1,0:T(8,128)S(1)}, f32[3,1,6,36]{3,2,1,0:T(8,128)S(1)}, u32[]{:S(2)}, u32[]{:S(2)}) collective-permute-start(f32[3,1,6,36]{3,2,1,0:T(8,128)S(1)} %get-tuple-element.109), channel_id=1, source_target_pairs={{0,64},{64,128},{128,192},{192,256},{256,320},{320,384},{384,448},... | collective-permute-start | bytes 7784 | tf_op jit(solution)/shard_map/ppermute | solution.py:24
  46.0 1.3 collective-permute-start.7
  47.4 1.2 pad_maximum_fusion.10
  48.6 5.3 %collective-permute-start.4 = (bf16[3,5,26,146]{3,2,1,0:T(8,128)(2,1)}, bf16[3,5,26,146]{3,2,1,0:T(8,128)(2,1)}, u32[]{:S(2)}, u32[]{:S(2)}) collective-permute-start(bf16[3,5,26,146]{3,2,1,0:T(8,128)(2,1)} %get-tuple-element.64), channel_id=1, source_target_pairs={{0,64},{64,128},{128,192},{192,256},{256,320},{320,384},{384,448},... | collective-permute-start | bytes 341648 | tf_op jit(solution)/shard_map/ppermute | solution.py:24
  53.9 1.5 %collective-permute-start.5 = (bf16[3,5,26,146]{3,2,1,0:T(8,128)(2,1)}, bf16[3,5,26,146]{3,2,1,0:T(8,128)(2,1)}, u32[]{:S(2)}, u32[]{:S(2)}) collective-permute-start(bf16[3,5,26,146]{3,2,1,0:T(8,128)(2,1)} %get-tuple-element.65), channel_id=1, source_target_pairs={{64,0},{128,64},{192,128},{256,192},{320,256},{384,320},{448,384},... | collective-permute-start | bytes 341648 | tf_op jit(solution)/shard_map/ppermute | solution.py:27
  56.1 0.4 fusion.65
  57.5 0.4 copy-done.13
  58.8 1.0 squeeze.123
  60.1 3.5 %collective-permute-done.5 = bf16[3,5,26,146]{3,2,1,0:T(8,128)(2,1)} collective-permute-done((bf16[3,5,26,146]{3,2,1,0:T(8,128)(2,1)}, bf16[3,5,26,146]{3,2,1,0:T(8,128)(2,1)}, u32[]{:S(2)}, u32[]{:S(2)}) %collective-permute-start.5) | collective-permute-done | bytes 113912 | tf_op jit(solution)/shard_map/ppermute | solution.py:27
  63.6 1.8 %maximum_convert_fusion = f32[3,26,26,146]{3,2,1,0:T(8,128)S(1)} fusion(bf16[3,5,26,146]{3,2,1,0:T(8,128)(2,1)} %collective-permute-done.5, bf16[3,16,26,9]{3,2,1,0:T(8,128)(2,1)S(1)} %collective-permute-done.3, bf16[3,16,5,128]{3,2,1,0:T(8,128)(2,1)S(1)} %collective-permute-done.1, bf16[1,16,16,128]{3,2,1,0:T(8,128)(2,1)S(1)} %convert_bitcast_fusion, ...), kind=kLoop, calls=%fused_computation.13 | loop fusion | flops 5329584 | bytes 1776528 | tf_op jit(solution)/shard_map/convert_element_type | solution.py:233
  65.8 0.6 fusion.31
  66.4 1.2 add_multiply_fusion
  69.5 1.4 %multiply_reduce_fusion.3 = (f32[3,20,5,34]{3,1,2,0:T(8,128)S(1)}, f32[3,20,5,34]{3,1,2,0:T(8,128)S(1)}) fusion(f32[4]{0:T(128)S(1)} %copy-done.44, f32[4]{0:T(128)S(1)} %copy-done.43, pred[36,140]{1,0:T(8,128)(4,1)S(1)} %copy-done.24, pred[36,140]{1,0:T(8,128)(4,1)S(1)} %copy-done.23, f32[140]{0:T(256)S(1)} %copy-done.41, f32[140]{0:T(256)S(1)} %copy-done.42, ...), kind=kOutput, calls=%fused_computation.26 | convolution fusion | flops 69541080 | bytes 652832 | tf_op jit(solution)/shard_map/dot_general | solution.py:219
  71.3 0.6 copy-done
  71.9 1.2 fusion.50
  73.3 1.4 %multiply_reduce_fusion.5 = (f32[3,20,5,34]{3,1,2,0:T(8,128)S(1)}, f32[3,20,5,34]{3,1,2,0:T(8,128)S(1)}) fusion(f32[4]{0:T(128)S(1)} %copy-done.18, f32[4]{0:T(128)S(1)} %copy-done.14, f32[36,140]{1,0:T(8,128)S(1)} %copy-done.11, f32[20,5,4,140]{3,0,2,1:T(8,128)S(1)} %bitcast.519, f32[20,5,4,140]{3,0,2,1:T(8,128)S(1)} %bitcast.518, ...), kind=kOutput, calls=%fused_computation.28 | convolution fusion | flops 69526800 | bytes 885792 | tf_op jit(solution)/shard_map/dot_general | solution.py:219
  74.9 0.6 fusion.113
  75.6 5.4 %collective-permute-start.8 = (f32[3,1,4,34]{3,2,1,0:T(4,128)S(1)}, f32[3,1,4,34]{3,2,1,0:T(4,128)S(1)}, u32[]{:S(2)}, u32[]{:S(2)}) collective-permute-start(f32[3,1,4,34]{3,2,1,0:T(4,128)S(1)} %get-tuple-element.119), channel_id=1, source_target_pairs={{0,64},{64,128},{128,192},{192,256},{256,320},{320,384},{384,448},... | collective-permute-start | bytes 4904 | tf_op jit(solution)/shard_map/ppermute | solution.py:24
  81.0 1.3 collective-permute-start.9
  82.4 4.0 %collective-permute-done.9 = f32[3,1,4,34]{3,2,1,0:T(4,128)S(1)} collective-permute-done((f32[3,1,4,34]{3,2,1,0:T(4,128)S(1)}, f32[3,1,4,34]{3,2,1,0:T(4,128)S(1)}, u32[]{:S(2)}, u32[]{:S(2)}) %collective-permute-start.9) | collective-permute-done | bytes 1664 | tf_op jit(solution)/shard_map/ppermute | solution.py:27
  86.4 3.3 %collective-permute-start.10 = (f32[3,6,1,34]{3,2,1,0:T(1,128)S(1)}, f32[3,6,1,34]{3,2,1,0:T(1,128)S(1)}, u32[]{:S(2)}, u32[]{:S(2)}) collective-permute-start(f32[3,6,1,34]{3,2,1,0:T(1,128)S(1)} %get-tuple-element.117), channel_id=1, source_target_pairs={{0,8},{8,16},{16,24},{24,32},{32,40},{40,48},{48,56},{1,9},{9,17},... | collective-permute-start | bytes 7352 | tf_op jit(solution)/shard_map/ppermute | solution.py:24
  89.7 1.5 %collective-permute-start.11 = (f32[3,6,1,34]{3,2,1,0:T(1,128)S(1)}, f32[3,6,1,34]{3,2,1,0:T(1,128)S(1)}, u32[]{:S(2)}, u32[]{:S(2)}) collective-permute-start(f32[3,6,1,34]{3,2,1,0:T(1,128)S(1)} %get-tuple-element.118), channel_id=1, source_target_pairs={{8,0},{16,8},{24,16},{32,24},{40,32},{48,40},{56,48},{9,1},{17,9},... | collective-permute-start | bytes 7352 | tf_op jit(solution)/shard_map/ppermute | solution.py:27
  91.2 0.5 add_convert_fusion
  91.9 0.6 eq.222
  92.5 1.0 slice.1281
  93.5 0.6 collective-permute-done.11
  95.1 0.6 fusion.141
  95.7 0.6 fusion.147
  96.3 0.6 slice_add_fusion.33
  97.6 1.0 fusion.218
  98.9 1.1 squeeze.135
  100.1 0.6 fusion.44
  100.7 0.4 copy-done.2
  101.1 0.5 fusion.2
  102.2 1.3 multiply_reduce_fusion.1
  104.8 0.7 copy.136
  105.5 13.4 %all-to-all-start.1 = ((f32[3,64,16]{2,0,1:T(4,128)}), f32[3,64,16]{2,0,1:T(4,128)S(1)}, u32[]{:S(2)}, u32[]{:S(2)}) async-start(f32[3,64,16]{2,0,1:T(4,128)} %copy.136), calls=%async_computation.1 | async-start | bytes 262144 | tf_op jit(solution)/shard_map/all_to_all | solution.py:367
  118.9 0.7 slice_add_fusion.57
  119.6 10.4 %all-to-all-done.1 = f32[3,64,16]{2,0,1:T(4,128)S(1)} async-done(((f32[3,64,16]{2,0,1:T(4,128)}), f32[3,64,16]{2,0,1:T(4,128)S(1)}, u32[]{:S(2)}, u32[]{:S(2)}) %all-to-all-start.1) | async-done | bytes 12320 | tf_op jit(solution)/shard_map/all_to_all | solution.py:367
  130.2 0.9 convolution_bitcast_fusion
  (260 shorter events, 13.3 us)
Async XLA Ops:
  1.9 31.2 %collective-permute-start = (bf16[3,16,5,128]{3,2,1,0:T(8,128)(2,1)S(1)}, bf16[3,16,5,128]{3,2,1,0:T(8,128)(2,1)S(1)}, u32[]{:S(2)}, u32[]{:S(2)}) collective-permute-start(bf16[3,16,5,128]{3,2,1,0:T(8,128)(2,1)S(1)} %get-tuple-element.103), channel_id=1, source_target_pairs={{0,8},{8,16},{16,24},{24,32},{32,40},{40,48},{48,56},{1,9},{9,17},... | collective-permute-start | bytes 184328 | tf_op jit(solution)/shard_map/ppermute | solution.py:24
  5.9 27.1 %collective-permute-start.1 = (bf16[3,16,5,128]{3,2,1,0:T(8,128)(2,1)S(1)}, bf16[3,16,5,128]{3,2,1,0:T(8,128)(2,1)S(1)}, u32[]{:S(2)}, u32[]{:S(2)}) collective-permute-start(bf16[3,16,5,128]{3,2,1,0:T(8,128)(2,1)S(1)} %get-tuple-element.104), channel_id=1, source_target_pairs={{8,0},{16,8},{24,16},{32,24},{40,32},{48,40},{56,48},{9,1},{17,9},... | collective-permute-start | bytes 184328 | tf_op jit(solution)/shard_map/ppermute | solution.py:27
  9.7 0.6 copy-start.20
  12.1 20.9 %copy-start.3 = (bf16[16,16,128]{2,1,0:T(8,128)(2,1)S(1)}, bf16[16,16,128]{2,1,0:T(8,128)(2,1)}, u32[]{:S(2)}) copy-start(bf16[16,16,128]{2,1,0:T(8,128)(2,1)} %param.6) | copy-start | bytes 196612
  12.1 20.9 %copy-start.4 = (bf16[16,16,128]{2,1,0:T(8,128)(2,1)S(1)}, bf16[16,16,128]{2,1,0:T(8,128)(2,1)}, u32[]{:S(2)}) copy-start(bf16[16,16,128]{2,1,0:T(8,128)(2,1)} %param.5) | copy-start | bytes 196612
  13.6 25.3 %all-to-all-start = ((f32[4,64,80]{2,0,1:T(4,128)}), f32[4,64,80]{2,0,1:T(4,128)S(1)}, u32[]{:S(2)}, u32[]{:S(2)}) async-start(f32[4,64,80]{2,0,1:T(4,128)} %copy.111), calls=%async_computation | async-start | bytes 262144 | tf_op jit(solution)/shard_map/all_to_all | solution.py:299
  27.6 11.3 %copy-start.12 = (f32[4]{0:T(128)}, f32[4]{0:T(128)S(1)}, u32[]{:S(2)}) copy-start(f32[4]{0:T(128)S(1)} %get-tuple-element.152) | copy-start | bytes 52
  27.6 11.3 %copy-start.16 = (f32[4]{0:T(128)}, f32[4]{0:T(128)S(1)}, u32[]{:S(2)}) copy-start(f32[4]{0:T(128)S(1)} %get-tuple-element.153) | copy-start | bytes 52
  28.2 10.7 %copy-start.37 = (f32[140]{0:T(256)}, f32[140]{0:T(256)S(1)}, u32[]{:S(2)}) copy-start(f32[140]{0:T(256)S(1)} %get-tuple-element.150) | copy-start | bytes 1684
  28.2 10.7 %copy-start.39 = (f32[140]{0:T(256)}, f32[140]{0:T(256)S(1)}, u32[]{:S(2)}) copy-start(f32[140]{0:T(256)S(1)} %get-tuple-element.151) | copy-start | bytes 1684
  28.8 10.1 %copy-start.25 = (s32[140]{0:T(256)}, s32[140]{0:T(256)S(1)}, u32[]{:S(2)}) copy-start(s32[140]{0:T(256)S(1)} %get-tuple-element.148) | copy-start | bytes 1684
  28.8 10.2 %copy-start.27 = (s32[140]{0:T(256)}, s32[140]{0:T(256)S(1)}, u32[]{:S(2)}) copy-start(s32[140]{0:T(256)S(1)} %get-tuple-element.149) | copy-start | bytes 1684
  33.4 13.9 %collective-permute-start.2 = (bf16[3,16,26,9]{3,2,1,0:T(8,128)(2,1)S(1)}, bf16[3,16,26,9]{3,2,1,0:T(8,128)(2,1)S(1)}, u32[]{:S(2)}, u32[]{:S(2)}) collective-permute-start(bf16[3,16,26,9]{3,2,1,0:T(8,128)(2,1)S(1)} %get-tuple-element.76), channel_id=1, source_target_pairs={{0,1},{1,2},{2,3},{3,4},{4,5},{5,6},{6,7},{8,9},{9,10},{10,11},{11... | collective-permute-start | bytes 67400 | tf_op jit(solution)/shard_map/ppermute | solution.py:24
  37.0 10.4 %collective-permute-start.3 = (bf16[3,16,26,9]{3,2,1,0:T(8,128)(2,1)S(1)}, bf16[3,16,26,9]{3,2,1,0:T(8,128)(2,1)S(1)}, u32[]{:S(2)}, u32[]{:S(2)}) collective-permute-start(bf16[3,16,26,9]{3,2,1,0:T(8,128)(2,1)S(1)} %get-tuple-element.77), channel_id=1, source_target_pairs={{1,0},{2,1},{3,2},{4,3},{5,4},{6,5},{7,6},{9,8},{10,9},{11,10},{12... | collective-permute-start | bytes 67400 | tf_op jit(solution)/shard_map/ppermute | solution.py:27
  40.1 1.1 copy-start.21
  41.7 14.4 %copy-start.26 = (s32[140]{0:T(256)S(1)}, s32[140]{0:T(256)}, u32[]{:S(2)}) copy-start(s32[140]{0:T(256)} %copy-done.25) | copy-start | bytes 1684
  41.7 14.4 %copy-start.28 = (s32[140]{0:T(256)S(1)}, s32[140]{0:T(256)}, u32[]{:S(2)}) copy-start(s32[140]{0:T(256)} %copy-done.27) | copy-start | bytes 1684
  41.7 14.4 %copy-start.38 = (f32[140]{0:T(256)S(1)}, f32[140]{0:T(256)}, u32[]{:S(2)}) copy-start(f32[140]{0:T(256)} %copy-done.37) | copy-start | bytes 1684
  41.7 14.4 %copy-start.40 = (f32[140]{0:T(256)S(1)}, f32[140]{0:T(256)}, u32[]{:S(2)}) copy-start(f32[140]{0:T(256)} %copy-done.39) | copy-start | bytes 1684
  41.9 14.6 %copy-start.5 = (f32[3,4,4,2]{3,2,1,0:T(4,128)}, f32[3,4,4,2]{3,2,1,0:T(4,128)S(1)}, u32[]{:S(2)}) copy-start(f32[3,4,4,2]{3,2,1,0:T(4,128)S(1)} %slice.1119) | copy-start | bytes 1156
  42.0 13.4 %collective-permute-start.6 = (f32[3,1,6,36]{3,2,1,0:T(8,128)S(1)}, f32[3,1,6,36]{3,2,1,0:T(8,128)S(1)}, u32[]{:S(2)}, u32[]{:S(2)}) collective-permute-start(f32[3,1,6,36]{3,2,1,0:T(8,128)S(1)} %get-tuple-element.109), channel_id=1, source_target_pairs={{0,64},{64,128},{128,192},{192,256},{256,320},{320,384},{384,448},... | collective-permute-start | bytes 7784 | tf_op jit(solution)/shard_map/ppermute | solution.py:24
  46.0 9.4 %collective-permute-start.7 = (f32[3,1,6,36]{3,2,1,0:T(8,128)S(1)}, f32[3,1,6,36]{3,2,1,0:T(8,128)S(1)}, u32[]{:S(2)}, u32[]{:S(2)}) collective-permute-start(f32[3,1,6,36]{3,2,1,0:T(8,128)S(1)} %get-tuple-element.110), channel_id=1, source_target_pairs={{64,0},{128,64},{192,128},{256,192},{320,256},{384,320},{448,384},... | collective-permute-start | bytes 7784 | tf_op jit(solution)/shard_map/ppermute | solution.py:27
  48.6 11.4 %collective-permute-start.4 = (bf16[3,5,26,146]{3,2,1,0:T(8,128)(2,1)}, bf16[3,5,26,146]{3,2,1,0:T(8,128)(2,1)}, u32[]{:S(2)}, u32[]{:S(2)}) collective-permute-start(bf16[3,5,26,146]{3,2,1,0:T(8,128)(2,1)} %get-tuple-element.64), channel_id=1, source_target_pairs={{0,64},{64,128},{128,192},{192,256},{256,320},{320,384},{384,448},... | collective-permute-start | bytes 341648 | tf_op jit(solution)/shard_map/ppermute | solution.py:24
  53.9 9.6 %collective-permute-start.5 = (bf16[3,5,26,146]{3,2,1,0:T(8,128)(2,1)}, bf16[3,5,26,146]{3,2,1,0:T(8,128)(2,1)}, u32[]{:S(2)}, u32[]{:S(2)}) collective-permute-start(bf16[3,5,26,146]{3,2,1,0:T(8,128)(2,1)} %get-tuple-element.65), channel_id=1, source_target_pairs={{64,0},{128,64},{192,128},{256,192},{320,256},{384,320},{448,384},... | collective-permute-start | bytes 341648 | tf_op jit(solution)/shard_map/ppermute | solution.py:27
  56.7 0.7 copy-start.29
  56.7 0.7 copy-start.31
  57.3 0.6 copy-start.13
  57.3 0.6 copy-start.17
  68.7 0.7 copy-start.23
  68.7 0.7 copy-start.24
  68.7 0.7 copy-start.41
  68.8 0.7 copy-start.42
  68.8 0.7 copy-start.43
  68.8 0.7 copy-start.44
  70.8 1.0 copy-start
  71.9 1.3 %copy-start.11 = (f32[36,140]{1,0:T(8,128)S(1)}, f32[36,140]{1,0:T(8,128)}, u32[]{:S(2)}) copy-start(f32[36,140]{1,0:T(8,128)} %select_add_fusion.1) | copy-start | bytes 60484
  71.9 1.4 %copy-start.14 = (f32[4]{0:T(128)S(1)}, f32[4]{0:T(128)}, u32[]{:S(2)}) copy-start(f32[4]{0:T(128)} %copy-done.12) | copy-start | bytes 52
  71.9 1.4 %copy-start.18 = (f32[4]{0:T(128)S(1)}, f32[4]{0:T(128)}, u32[]{:S(2)}) copy-start(f32[4]{0:T(128)} %copy-done.16) | copy-start | bytes 52
  73.3 1.7 %copy-start.6 = (f32[3,4,4,2]{3,2,1,0:T(4,128)S(1)}, f32[3,4,4,2]{3,2,1,0:T(4,128)}, u32[]{:S(2)}) copy-start(f32[3,4,4,2]{3,2,1,0:T(4,128)} %copy-done.5) | copy-start | bytes 1156
  73.3 1.7 %copy-start.45 = (pred[34]{0:T(512)(128)(4,1)S(1)}, pred[34]{0:T(512)(128)(4,1)}, u32[]{:S(2)}) copy-start(pred[34]{0:T(512)(128)(4,1)} %and_or_fusion) | copy-start | bytes 106
  73.3 9.0 %copy-start.33 = (f32[132]{0:T(256)S(1)}, f32[132]{0:T(256)}, u32[]{:S(2)}) copy-start(f32[132]{0:T(256)} %get-tuple-element.162) | copy-start | bytes 1588
  73.3 9.0 %copy-start.34 = (f32[132]{0:T(256)S(1)}, f32[132]{0:T(256)}, u32[]{:S(2)}) copy-start(f32[132]{0:T(256)} %get-tuple-element.163) | copy-start | bytes 1588
  73.3 9.0 %copy-start.35 = (s32[132]{0:T(256)S(1)}, s32[132]{0:T(256)}, u32[]{:S(2)}) copy-start(s32[132]{0:T(256)} %get-tuple-element.160) | copy-start | bytes 1588
  73.3 9.0 %copy-start.36 = (s32[132]{0:T(256)S(1)}, s32[132]{0:T(256)}, u32[]{:S(2)}) copy-start(s32[132]{0:T(256)} %get-tuple-element.161) | copy-start | bytes 1588
  73.3 18.4 %copy-start.22 = (f32[640]{0:T(1024)S(1)}, f32[640]{0:T(1024)}, u32[]{:S(2)}) copy-start(f32[640]{0:T(1024)} %copy-done.21) | copy-start | bytes 7684
  75.6 6.8 %collective-permute-start.8 = (f32[3,1,4,34]{3,2,1,0:T(4,128)S(1)}, f32[3,1,4,34]{3,2,1,0:T(4,128)S(1)}, u32[]{:S(2)}, u32[]{:S(2)}) collective-permute-start(f32[3,1,4,34]{3,2,1,0:T(4,128)S(1)} %get-tuple-element.119), channel_id=1, source_target_pairs={{0,64},{64,128},{128,192},{192,256},{256,320},{320,384},{384,448},... | collective-permute-start | bytes 4904 | tf_op jit(solution)/shard_map/ppermute | solution.py:24
  81.0 5.4 %collective-permute-start.9 = (f32[3,1,4,34]{3,2,1,0:T(4,128)S(1)}, f32[3,1,4,34]{3,2,1,0:T(4,128)S(1)}, u32[]{:S(2)}, u32[]{:S(2)}) collective-permute-start(f32[3,1,4,34]{3,2,1,0:T(4,128)S(1)} %get-tuple-element.120), channel_id=1, source_target_pairs={{64,0},{128,64},{192,128},{256,192},{320,256},{384,320},{448,384},... | collective-permute-start | bytes 4904 | tf_op jit(solution)/shard_map/ppermute | solution.py:27
  86.4 7.1 %collective-permute-start.10 = (f32[3,6,1,34]{3,2,1,0:T(1,128)S(1)}, f32[3,6,1,34]{3,2,1,0:T(1,128)S(1)}, u32[]{:S(2)}, u32[]{:S(2)}) collective-permute-start(f32[3,6,1,34]{3,2,1,0:T(1,128)S(1)} %get-tuple-element.117), channel_id=1, source_target_pairs={{0,8},{8,16},{16,24},{24,32},{32,40},{40,48},{48,56},{1,9},{9,17},... | collective-permute-start | bytes 7352 | tf_op jit(solution)/shard_map/ppermute | solution.py:24
  89.7 4.4 %collective-permute-start.11 = (f32[3,6,1,34]{3,2,1,0:T(1,128)S(1)}, f32[3,6,1,34]{3,2,1,0:T(1,128)S(1)}, u32[]{:S(2)}, u32[]{:S(2)}) collective-permute-start(f32[3,6,1,34]{3,2,1,0:T(1,128)S(1)} %get-tuple-element.118), channel_id=1, source_target_pairs={{8,0},{16,8},{24,16},{32,24},{40,32},{48,40},{56,48},{9,1},{17,9},... | collective-permute-start | bytes 7352 | tf_op jit(solution)/shard_map/ppermute | solution.py:27
  94.8 2.2 %copy-start.30 = (f32[20]{0:T(128)S(1)}, f32[20]{0:T(128)}, u32[]{:S(2)}) copy-start(f32[20]{0:T(128)} %mul.1021) | copy-start | bytes 244
  94.8 2.2 %copy-start.32 = (f32[20]{0:T(128)S(1)}, f32[20]{0:T(128)}, u32[]{:S(2)}) copy-start(f32[20]{0:T(128)} %mul.1015) | copy-start | bytes 244
  98.6 1.4 %copy-start.1 = (f32[20,20,140]{2,1,0:T(8,128)S(1)}, f32[20,20,140]{2,1,0:T(8,128)}, u32[]{:S(2)}) copy-start(f32[20,20,140]{2,1,0:T(8,128)} %get-tuple-element.44) | copy-start | bytes 672004
  100.1 1.0 copy-start.2
  101.6 0.6 copy-start.15
  101.6 0.6 copy-start.19
  102.0 1.8 %copy-start.9 = (f32[4,4,33]{2,1,0:T(4,128)S(1)}, f32[4,4,33]{2,1,0:T(4,128)}, u32[]{:S(2)}) copy-start(f32[4,4,33]{2,1,0:T(4,128)} %fusion.147) | copy-start | bytes 6340
  102.0 1.9 %copy-start.8 = (f32[4,4,33]{2,1,0:T(4,128)S(1)}, f32[4,4,33]{2,1,0:T(4,128)}, u32[]{:S(2)}) copy-start(f32[4,4,33]{2,1,0:T(4,128)} %fusion.141) | copy-start | bytes 6340
  102.0 1.9 %copy-start.10 = (f32[4,4,33]{2,1,0:T(4,128)S(1)}, f32[4,4,33]{2,1,0:T(4,128)}, u32[]{:S(2)}) copy-start(f32[4,4,33]{2,1,0:T(4,128)} %slice_add_fusion.33) | copy-start | bytes 6340
  102.2 1.8 %copy-start.7 = (f32[3,4,4,34]{3,2,1,0:T(4,128)S(1)}, f32[3,4,4,34]{3,2,1,0:T(4,128)}, u32[]{:S(2)}) copy-start(f32[3,4,4,34]{3,2,1,0:T(4,128)} %get-tuple-element.30) | copy-start | bytes 19588
  102.2 2.1 %copy-start.46 = (f32[128]{0:T(128)S(1)}, f32[128]{0:T(128)}, u32[]{:S(2)}) copy-start(f32[128]{0:T(128)} %eq.222) | copy-start | bytes 1540
  102.2 2.1 %copy-start.48 = (f32[64]{0:T(128)S(1)}, f32[64]{0:T(128)}, u32[]{:S(2)}) copy-start(f32[64]{0:T(128)} %add_convert_fusion) | copy-start | bytes 772
  103.5 15.4 %copy-start.47 = (s32[64]{0:T(128)S(1)}, s32[64]{0:T(128)}, u32[]{:S(2)}) copy-start(s32[64]{0:T(128)} %get-tuple-element.55) | copy-start | bytes 772
  105.5 24.5 %all-to-all-start.1 = ((f32[3,64,16]{2,0,1:T(4,128)}), f32[3,64,16]{2,0,1:T(4,128)S(1)}, u32[]{:S(2)}, u32[]{:S(2)}) async-start(f32[3,64,16]{2,0,1:T(4,128)} %copy.136), calls=%async_computation.1 | async-start | bytes 262144 | tf_op jit(solution)/shard_map/all_to_all | solution.py:367

commit v6 on v5

--- a/solution.py
+++ b/solution.py
@@ -238,8 +238,6 @@
         reference_image.shape[2] // ELEM,
     )
     _, ex, ey, ez = nodes_shape
-    weights_table = axis_table(ez + 2, ELEM, False)
-    table_back = weights_table[1:-1].T
     wide_table = axis_table(ez + 4, ELEM, False)
     wide_back = wide_table[1:-1].T
     wide_square = axis_table(ez + 4, ELEM, True)[1:-1].T
@@ -344,17 +342,13 @@
         (column == ez + 1) & (lax.axis_index("gz") == size_z - 1)
     )
     wide_values = jnp.where(ghost, 0.0, wide_values)
-    tile_values = wide_values[..., 1:-1]
-    curvature = wide_curvature[..., 1:-1]
-    contrast = contrast[..., ELEM:-ELEM]
-    slopes = slopes[..., ELEM:-ELEM]
-    masked_slopes = masked_slopes[..., ELEM:-ELEM]
     padded = with_halo(wide_values, (("gx", 1), ("gy", 2)), 1)
-    moved = spread(padded, weights_table)
+    padded = jnp.pad(padded, ((0, 0), (0, 0), (0, 0), (1, 1)))
+    moved = spread(padded, wide_table)
     residual = contrast + slopes[0] * moved[0] + slopes[1] * moved[1] + slopes[2] * moved[2]
-    image_part = collect(masked_slopes * residual[None], table_back, False)
+    image_part = collect(masked_slopes * residual[None], wide_back, False)
     force_total = image_part + elastic_weight * elastic_force(padded)
-    tile_values = tile_values - force_total / curvature
+    tile_values = (wide_values - force_total / wide_curvature)[..., 1:-1]
     final_blocks = tile_values.reshape(3, blocks, block_nodes)
     own_labels = received_labels.reshape(members, HALO_CAP)[:, :CAP].reshape(-1)
     position = jnp.arange(blocks, dtype=jnp.int32)

time: 132 us -> 124 us (0.939)
  local copies, waits for them, and re-layouts: 17.7 us -> 12.4 us
  other arithmetic: 24.7 us -> 19.6 us
  waiting for transfers between devices: 18.5 us -> 21.5 us
    unnamed x98 -> x62, local copies, waits for them, and re-layouts: 2.65 us -> 0.37 us
    squeeze x2, local copies, waits for them, and re-layouts: 2.1 us -> 0.28 us  [per_device(): moved[1]]
    add x43, other arithmetic: 2.49 us -> 0.71 us  [pair_op(): lax.slice_in_dim(volume, 1, length, axis=dimension)]
    ppermute x6, waiting for transfers between devices: 8.09 us -> 9.66 us  [with_halo(): lax.ppermute(lax.slice_in_dim(block, 0, width, axis=dim), axis, backward)]
  transfers between devices with their start and end apart: 14 -> 14, of which waited for: 4 -> 5; matrix products, arithmetic and copies ran while one was open for 17% -> 15% of each run, Pallas kernels for 0% -> 0%
where the time goes in v6:
time: 124 us; the launch traced here: 123 us
  starting transfers between devices  60.6 us (49%)
  waiting for transfers between devices  21.5 us (17%)
  other arithmetic  19.6 us (16%)
  local copies, waits for them, and re-layouts  12.4 us (10%)
  matrix products  7.51 us (6%)
  between operations  1.7 us (1%)
    ppermute x6, starting transfers between devices, with_halo(): lax.ppermute(lax.slice_in_dim(block, block.shape[dim] - width, None, axis...  24.7 us
    all_to_all x1, starting transfers between devices, per_device(): lax.all_to_all(outgoing, ('gy', 'gz'), split_axis=1, concat_axis=1, tiled...  13.8 us
    all_to_all x1, starting transfers between devices, per_device(): lax.all_to_all(send_outgoing, ('gy', 'gz'), split_axis=1, concat_axis=1,...  13.3 us
    all_to_all x1, waiting for transfers between devices, per_device(): lax.all_to_all(outgoing, ('gy', 'gz'), split_axis=1, concat_axis=1, tiled...  11.1 us
    ppermute x6, waiting for transfers between devices, with_halo(): lax.ppermute(lax.slice_in_dim(block, 0, width, axis=dim), axis, backward)  9.66 us
    ppermute x6, starting transfers between devices, with_halo(): lax.ppermute(lax.slice_in_dim(block, 0, width, axis=dim), axis, backward)  8.77 us
    dot_general x3, matrix products, collect(): jnp.dot(volume.reshape(-1, shape_all[3]), table_back, precision=highest)  4.17 us
    unnamed x4, matrix products  2.57 us
  transfers between devices with their start and end apart: 14, of which 5 were waited for; matrix products, arithmetic and copies ran while one was open for 15% of the time, Pallas kernels for 0%

profile of v6, /device:TPU:1, one launch (start us, length us, event | category | flops | bytes accessed | tf_op | source)
XLA Modules:
  0.0 123.3 jit_solution(13425206772243382032)
XLA Ops:
  0.0 0.9 convert_bitcast_fusion
  0.9 0.9 pad_maximum_fusion.9
  1.9 4.0 %collective-permute-start = (bf16[3,16,5,128]{3,2,1,0:T(8,128)(2,1)S(1)}, bf16[3,16,5,128]{3,2,1,0:T(8,128)(2,1)S(1)}, u32[]{:S(2)}, u32[]{:S(2)}) collective-permute-start(bf16[3,16,5,128]{3,2,1,0:T(8,128)(2,1)S(1)} %get-tuple-element.103), channel_id=1, source_target_pairs={{0,8},{8,16},{16,24},{24,32},{32,40},{40,48},{48,56},{1,9},{9,17},... | collective-permute-start | bytes 184328 | tf_op jit(solution)/shard_map/ppermute | solution.py:24
  5.9 1.3 %collective-permute-start.1 = (bf16[3,16,5,128]{3,2,1,0:T(8,128)(2,1)S(1)}, bf16[3,16,5,128]{3,2,1,0:T(8,128)(2,1)S(1)}, u32[]{:S(2)}, u32[]{:S(2)}) collective-permute-start(bf16[3,16,5,128]{3,2,1,0:T(8,128)(2,1)S(1)} %get-tuple-element.104), channel_id=1, source_target_pairs={{8,0},{16,8},{24,16},{32,24},{40,32},{48,40},{56,48},{9,1},{17,9},... | collective-permute-start | bytes 184328 | tf_op jit(solution)/shard_map/ppermute | solution.py:27
  7.2 0.7 broadcast_add_fusion.1
  7.9 1.2 %and_and_fusion = (pred[64]{0:T(512)(128)(4,1)S(1)}, s32[64]{0:T(128)S(1)}, s32[64]{0:T(128)S(1)}, s32[64]{0:T(128)S(1)}, s32[64]{0:T(128)S(1)}, /*index=5*/s32[64]{0:T(128)}) fusion(s32[64]{0:T(128)S(1)} %get-tuple-element.49, s32[64]{0:T(128)} %param.9), kind=kLoop, calls=%fused_computation.423 | loop fusion | flops 4928 | bytes 1856 | tf_op jit(solution)/shard_map/and | solution.py:268
  9.3 0.3 convert_reduce_fusion
  9.8 1.1 concatenate.68
  10.9 0.7 fusion.7
  11.6 0.4 copy.110
  12.0 0.4 all_to_all.12
  12.4 0.7 copy.111
  13.1 13.3 %all-to-all-start = ((f32[4,64,80]{2,0,1:T(4,128)}), f32[4,64,80]{2,0,1:T(4,128)S(1)}, u32[]{:S(2)}, u32[]{:S(2)}) async-start(f32[4,64,80]{2,0,1:T(4,128)} %copy.111), calls=%async_computation | async-start | bytes 262144 | tf_op jit(solution)/shard_map/all_to_all | solution.py:297
  26.5 0.6 fusion.181
  27.1 0.6 fusion.176
  27.7 0.6 iota_compare_fusion.8
  28.3 0.6 mul.993
  29.0 0.6 mul.999
  29.6 0.6 and_or_fusion
  30.4 1.0 fusion.212
  31.3 3.5 %collective-permute-start.2 = (bf16[3,16,26,9]{3,2,1,0:T(8,128)(2,1)}, bf16[3,16,26,9]{3,2,1,0:T(8,128)(2,1)S(1)}, u32[]{:S(2)}, u32[]{:S(2)}) collective-permute-start(bf16[3,16,26,9]{3,2,1,0:T(8,128)(2,1)} %get-tuple-element.76), channel_id=1, source_target_pairs={{0,1},{1,2},{2,3},{3,4},{4,5},{5,6},{6,7},{8,9},{9,10},{10,11},{11... | collective-permute-start | bytes 67400 | tf_op jit(solution)/shard_map/ppermute | solution.py:24
  34.9 1.9 %collective-permute-start.3 = (bf16[3,16,26,9]{3,2,1,0:T(8,128)(2,1)S(1)}, bf16[3,16,26,9]{3,2,1,0:T(8,128)(2,1)S(1)}, u32[]{:S(2)}, u32[]{:S(2)}) collective-permute-start(bf16[3,16,26,9]{3,2,1,0:T(8,128)(2,1)S(1)} %get-tuple-element.77), channel_id=1, source_target_pairs={{1,0},{2,1},{3,2},{4,3},{5,4},{6,5},{7,6},{9,8},{10,9},{11,10},{12... | collective-permute-start | bytes 67400 | tf_op jit(solution)/shard_map/ppermute | solution.py:27
  36.8 0.8 all-to-all-done
  37.6 0.4 reshape.464
  38.2 0.3 slice.835
  38.5 0.3 copy.114
  38.8 0.8 fusion.8
  39.6 0.3 copy.115
  39.9 0.3 reshape.465
  40.6 4.0 %collective-permute-start.6 = (f32[3,1,6,36]{3,2,1,0:T(8,128)S(1)}, f32[3,1,6,36]{3,2,1,0:T(8,128)S(1)}, u32[]{:S(2)}, u32[]{:S(2)}) collective-permute-start(f32[3,1,6,36]{3,2,1,0:T(8,128)S(1)} %get-tuple-element.109), channel_id=1, source_target_pairs={{0,64},{64,128},{128,192},{192,256},{256,320},{320,384},{384,448},... | collective-permute-start | bytes 7784 | tf_op jit(solution)/shard_map/ppermute | solution.py:24
  44.6 1.3 %collective-permute-start.7 = (f32[3,1,6,36]{3,2,1,0:T(8,128)S(1)}, f32[3,1,6,36]{3,2,1,0:T(8,128)S(1)}, u32[]{:S(2)}, u32[]{:S(2)}) collective-permute-start(f32[3,1,6,36]{3,2,1,0:T(8,128)S(1)} %get-tuple-element.110), channel_id=1, source_target_pairs={{64,0},{128,64},{192,128},{256,192},{320,256},{384,320},{448,384},... | collective-permute-start | bytes 7784 | tf_op jit(solution)/shard_map/ppermute | solution.py:27
  45.9 1.1 pad_maximum_fusion.8
  47.1 5.3 %collective-permute-start.4 = (bf16[3,5,26,146]{3,2,1,0:T(8,128)(2,1)}, bf16[3,5,26,146]{3,2,1,0:T(8,128)(2,1)}, u32[]{:S(2)}, u32[]{:S(2)}) collective-permute-start(bf16[3,5,26,146]{3,2,1,0:T(8,128)(2,1)} %get-tuple-element.64), channel_id=1, source_target_pairs={{0,64},{64,128},{128,192},{192,256},{256,320},{320,384},{384,448},... | collective-permute-start | bytes 341648 | tf_op jit(solution)/shard_map/ppermute | solution.py:24
  52.4 1.5 %collective-permute-start.5 = (bf16[3,5,26,146]{3,2,1,0:T(8,128)(2,1)S(1)}, bf16[3,5,26,146]{3,2,1,0:T(8,128)(2,1)}, u32[]{:S(2)}, u32[]{:S(2)}) collective-permute-start(bf16[3,5,26,146]{3,2,1,0:T(8,128)(2,1)S(1)} %get-tuple-element.65), channel_id=1, source_target_pairs={{64,0},{128,64},{192,128},{256,192},{320,256},{384,320},{448,384},... | collective-permute-start | bytes 341648 | tf_op jit(solution)/shard_map/ppermute | solution.py:27
  55.1 0.4 fusion.58
  55.8 0.4 multiply_add_fusion.1
  57.1 3.8 %collective-permute-done.5 = bf16[3,5,26,146]{3,2,1,0:T(8,128)(2,1)} collective-permute-done((bf16[3,5,26,146]{3,2,1,0:T(8,128)(2,1)S(1)}, bf16[3,5,26,146]{3,2,1,0:T(8,128)(2,1)}, u32[]{:S(2)}, u32[]{:S(2)}) %collective-permute-start.5) | collective-permute-done | bytes 113912 | tf_op jit(solution)/shard_map/ppermute | solution.py:27
  60.9 1.8 %maximum_convert_fusion = f32[3,26,26,146]{3,2,1,0:T(8,128)S(1)} fusion(bf16[3,5,26,146]{3,2,1,0:T(8,128)(2,1)} %collective-permute-done.5, bf16[3,16,26,9]{3,2,1,0:T(8,128)(2,1)S(1)} %collective-permute-done.3, bf16[3,16,5,128]{3,2,1,0:T(8,128)(2,1)S(1)} %collective-permute-done.1, bf16[1,16,16,128]{3,2,1,0:T(8,128)(2,1)S(1)} %convert_bitcast_fusion, ...), kind=kLoop, calls=%fused_computation.13 | loop fusion | flops 5329584 | bytes 1776528 | tf_op jit(solution)/shard_map/convert_element_type | solution.py:233
  62.7 0.4 fusion.25
  63.1 0.6 fusion.33
  63.7 1.2 add_multiply_fusion
  65.3 0.3 fusion.55
  65.7 0.3 fusion.53
  66.7 0.2 copy-done.10
  67.0 1.4 %multiply_reduce_fusion.3 = (f32[3,20,5,34]{3,1,2,0:T(8,128)S(1)}, f32[3,20,5,34]{3,1,2,0:T(8,128)S(1)}) fusion(f32[4]{0:T(128)S(1)} %copy-done.27, f32[4]{0:T(128)S(1)} %copy-done.26, pred[36,140]{1,0:T(8,128)(4,1)S(1)} %iota_compare_fusion.7, pred[36,140]{1,0:T(8,128)(4,1)S(1)} %copy-done.10, f32[140]{0:T(256)S(1)} %copy-done.23, f32[140]{0:T(256)S(1)} %copy-done.24, ...), kind=kOutput, calls=%fused_computation.27 | convolution fusion | flops 69541080 | bytes 652832 | tf_op jit(solution)/shard_map/dot_general | solution.py:219
  68.6 0.2 maximum_convert_fusion.1
  68.8 1.1 fusion.46
  70.1 1.4 %multiply_reduce_fusion.5 = (f32[3,20,5,34]{3,1,2,0:T(8,128)S(1)}, f32[3,20,5,34]{3,1,2,0:T(8,128)S(1)}) fusion(f32[4]{0:T(128)S(1)} %get-tuple-element.153, f32[4]{0:T(128)S(1)} %get-tuple-element.152, f32[36,140]{1,0:T(8,128)S(1)} %select_add_fusion, f32[20,5,4,140]{3,0,2,1:T(8,128)S(1)} %bitcast.486, f32[20,5,4,140]{3,0,2,1:T(8,128)S(1)} %bitcast.483, ...), kind=kOutput, calls=%fused_computation.29 | convolution fusion | flops 69526800 | bytes 885792 | tf_op jit(solution)/shard_map/dot_general | solution.py:219
  71.8 5.5 %collective-permute-start.8 = (f32[3,1,4,34]{3,2,1,0:T(4,128)S(1)}, f32[3,1,4,34]{3,2,1,0:T(4,128)S(1)}, u32[]{:S(2)}, u32[]{:S(2)}) collective-permute-start(f32[3,1,4,34]{3,2,1,0:T(4,128)S(1)} %get-tuple-element.119), channel_id=1, source_target_pairs={{0,64},{64,128},{128,192},{192,256},{256,320},{320,384},{384,448},... | collective-permute-start | bytes 4904 | tf_op jit(solution)/shard_map/ppermute | solution.py:24
  77.3 1.3 %collective-permute-start.9 = (f32[3,1,4,34]{3,2,1,0:T(4,128)S(1)}, f32[3,1,4,34]{3,2,1,0:T(4,128)S(1)}, u32[]{:S(2)}, u32[]{:S(2)}) collective-permute-start(f32[3,1,4,34]{3,2,1,0:T(4,128)S(1)} %get-tuple-element.120), channel_id=1, source_target_pairs={{64,0},{128,64},{192,128},{256,192},{320,256},{384,320},{448,384},... | collective-permute-start | bytes 4904 | tf_op jit(solution)/shard_map/ppermute | solution.py:27
  78.6 4.0 %collective-permute-done.9 = f32[3,1,4,34]{3,2,1,0:T(4,128)S(1)} collective-permute-done((f32[3,1,4,34]{3,2,1,0:T(4,128)S(1)}, f32[3,1,4,34]{3,2,1,0:T(4,128)S(1)}, u32[]{:S(2)}, u32[]{:S(2)}) %collective-permute-start.9) | collective-permute-done | bytes 1664 | tf_op jit(solution)/shard_map/ppermute | solution.py:27
  82.6 2.3 %collective-permute-start.10 = (f32[3,6,1,34]{3,2,1,0:T(1,128)S(1)}, f32[3,6,1,34]{3,2,1,0:T(1,128)S(1)}, u32[]{:S(2)}, u32[]{:S(2)}) collective-permute-start(f32[3,6,1,34]{3,2,1,0:T(1,128)S(1)} %get-tuple-element.117), channel_id=1, source_target_pairs={{0,8},{8,16},{16,24},{24,32},{32,40},{40,48},{48,56},{1,9},{9,17},... | collective-permute-start | bytes 7352 | tf_op jit(solution)/shard_map/ppermute | solution.py:24
  85.0 1.5 %collective-permute-start.11 = (f32[3,6,1,34]{3,2,1,0:T(1,128)S(1)}, f32[3,6,1,34]{3,2,1,0:T(1,128)S(1)}, u32[]{:S(2)}, u32[]{:S(2)}) collective-permute-start(f32[3,6,1,34]{3,2,1,0:T(1,128)S(1)} %get-tuple-element.118), channel_id=1, source_target_pairs={{8,0},{16,8},{24,16},{32,24},{40,32},{48,40},{56,48},{9,1},{17,9},... | collective-permute-start | bytes 7352 | tf_op jit(solution)/shard_map/ppermute | solution.py:27
  86.5 0.6 add_convert_fusion
  87.2 0.7 eq.206
  87.9 1.9 %collective-permute-done.11 = f32[3,6,1,34]{3,2,1,0:T(1,128)S(1)} collective-permute-done((f32[3,6,1,34]{3,2,1,0:T(1,128)S(1)}, f32[3,6,1,34]{3,2,1,0:T(1,128)S(1)}, u32[]{:S(2)}, u32[]{:S(2)}) %collective-permute-start.11) | collective-permute-done | bytes 2480 | tf_op jit(solution)/shard_map/ppermute | solution.py:27
  90.7 0.4 fusion.91
  91.5 0.4 multiply_add_fusion
  92.6 1.2 %fusion.48 = f32[20,20,140]{2,1,0:T(8,128)S(1)} fusion(bf16[20,20,140]{2,1,0:T(8,128)(2,1)} %get-tuple-element.44, f32[20,20,140]{2,1,0:T(8,128)S(1)} %squeeze.128, f32[20,20,140]{2,1,0:T(8,128)S(1)} %squeeze.127, f32[20,20,140]{2,1,0:T(8,128)S(1)} %squeeze.126, f32[3,20,20,140]{3,2,1,0:T(8,128)S(1)} %maximum_convert_fusion.1), kind=kLoop, calls=%fused_computation.99 | loop fusion | flops 392000 | bytes 1680000 | tf_op jit(solution)/shard_map/add | solution.py:348
  94.0 1.4 %multiply_reduce_fusion.1 = (f32[3,20,5,34]{3,1,2,0:T(8,128)S(1)}, f32[3,20,5,34]{3,1,2,0:T(8,128)S(1)}) fusion(f32[4]{0:T(128)S(1)} %get-tuple-element.153, f32[4]{0:T(128)S(1)} %get-tuple-element.152, f32[36,140]{1,0:T(8,128)S(1)} %select_add_fusion, f32[20,5,4,140]{3,0,2,1:T(8,128)S(1)} %bitcast.485, f32[20,5,4,140]{3,0,2,1:T(8,128)S(1)} %bitcast.484, ...), kind=kOutput, calls=%fused_computation.24 | convolution fusion | flops 69526800 | bytes 885792 | tf_op jit(solution)/shard_map/dot_general | solution.py:219
  96.7 0.7 copy.136
  97.4 13.8 %all-to-all-start.1 = ((f32[3,64,16]{2,0,1:T(4,128)}), f32[3,64,16]{2,0,1:T(4,128)S(1)}, u32[]{:S(2)}, u32[]{:S(2)}) async-start(f32[3,64,16]{2,0,1:T(4,128)} %copy.136), calls=%async_computation.1 | async-start | bytes 262144 | tf_op jit(solution)/shard_map/all_to_all | solution.py:361
  111.2 11.1 %all-to-all-done.1 = f32[3,64,16]{2,0,1:T(4,128)S(1)} async-done(((f32[3,64,16]{2,0,1:T(4,128)}), f32[3,64,16]{2,0,1:T(4,128)S(1)}, u32[]{:S(2)}, u32[]{:S(2)}) %all-to-all-start.1) | async-done | bytes 12320 | tf_op jit(solution)/shard_map/all_to_all | solution.py:361
  122.5 0.9 convolution_bitcast_fusion
  (221 shorter events, 8.2 us)
Async XLA Ops:
  1.9 28.3 %collective-permute-start = (bf16[3,16,5,128]{3,2,1,0:T(8,128)(2,1)S(1)}, bf16[3,16,5,128]{3,2,1,0:T(8,128)(2,1)S(1)}, u32[]{:S(2)}, u32[]{:S(2)}) collective-permute-start(bf16[3,16,5,128]{3,2,1,0:T(8,128)(2,1)S(1)} %get-tuple-element.103), channel_id=1, source_target_pairs={{0,8},{8,16},{16,24},{24,32},{32,40},{40,48},{48,56},{1,9},{9,17},... | collective-permute-start | bytes 184328 | tf_op jit(solution)/shard_map/ppermute | solution.py:24
  5.9 24.3 %collective-permute-start.1 = (bf16[3,16,5,128]{3,2,1,0:T(8,128)(2,1)S(1)}, bf16[3,16,5,128]{3,2,1,0:T(8,128)(2,1)S(1)}, u32[]{:S(2)}, u32[]{:S(2)}) collective-permute-start(bf16[3,16,5,128]{3,2,1,0:T(8,128)(2,1)S(1)} %get-tuple-element.104), channel_id=1, source_target_pairs={{8,0},{16,8},{24,16},{32,24},{40,32},{48,40},{56,48},{9,1},{17,9},... | collective-permute-start | bytes 184328 | tf_op jit(solution)/shard_map/ppermute | solution.py:27
  11.6 18.6 %copy-start = (bf16[16,16,128]{2,1,0:T(8,128)(2,1)S(1)}, bf16[16,16,128]{2,1,0:T(8,128)(2,1)}, u32[]{:S(2)}) copy-start(bf16[16,16,128]{2,1,0:T(8,128)(2,1)} %param.6) | copy-start | bytes 196612
  11.6 18.6 %copy-start.1 = (bf16[16,16,128]{2,1,0:T(8,128)(2,1)S(1)}, bf16[16,16,128]{2,1,0:T(8,128)(2,1)}, u32[]{:S(2)}) copy-start(bf16[16,16,128]{2,1,0:T(8,128)(2,1)} %param.5) | copy-start | bytes 196612
  13.1 24.5 %all-to-all-start = ((f32[4,64,80]{2,0,1:T(4,128)}), f32[4,64,80]{2,0,1:T(4,128)S(1)}, u32[]{:S(2)}, u32[]{:S(2)}) async-start(f32[4,64,80]{2,0,1:T(4,128)} %copy.111), calls=%async_computation | async-start | bytes 262144 | tf_op jit(solution)/shard_map/all_to_all | solution.py:297
  26.5 28.6 %copy-start.11 = (s32[140]{0:T(256)}, s32[140]{0:T(256)S(1)}, u32[]{:S(2)}) copy-start(s32[140]{0:T(256)S(1)} %get-tuple-element.149) | copy-start | bytes 1684
  27.7 9.9 %copy-start.17 = (f32[140]{0:T(256)}, f32[140]{0:T(256)S(1)}, u32[]{:S(2)}) copy-start(f32[140]{0:T(256)S(1)} %get-tuple-element.150) | copy-start | bytes 1684
  27.7 10.3 %copy-start.20 = (f32[140]{0:T(256)}, f32[140]{0:T(256)S(1)}, u32[]{:S(2)}) copy-start(f32[140]{0:T(256)S(1)} %get-tuple-element.151) | copy-start | bytes 1684
  31.3 14.6 %collective-permute-start.2 = (bf16[3,16,26,9]{3,2,1,0:T(8,128)(2,1)}, bf16[3,16,26,9]{3,2,1,0:T(8,128)(2,1)S(1)}, u32[]{:S(2)}, u32[]{:S(2)}) collective-permute-start(bf16[3,16,26,9]{3,2,1,0:T(8,128)(2,1)} %get-tuple-element.76), channel_id=1, source_target_pairs={{0,1},{1,2},{2,3},{3,4},{4,5},{5,6},{6,7},{8,9},{9,10},{10,11},{11... | collective-permute-start | bytes 67400 | tf_op jit(solution)/shard_map/ppermute | solution.py:24
  34.9 11.1 %collective-permute-start.3 = (bf16[3,16,26,9]{3,2,1,0:T(8,128)(2,1)S(1)}, bf16[3,16,26,9]{3,2,1,0:T(8,128)(2,1)S(1)}, u32[]{:S(2)}, u32[]{:S(2)}) collective-permute-start(bf16[3,16,26,9]{3,2,1,0:T(8,128)(2,1)S(1)} %get-tuple-element.77), channel_id=1, source_target_pairs={{1,0},{2,1},{3,2},{4,3},{5,4},{6,5},{7,6},{9,8},{10,9},{11,10},{12... | collective-permute-start | bytes 67400 | tf_op jit(solution)/shard_map/ppermute | solution.py:27
  40.6 13.3 %collective-permute-start.6 = (f32[3,1,6,36]{3,2,1,0:T(8,128)S(1)}, f32[3,1,6,36]{3,2,1,0:T(8,128)S(1)}, u32[]{:S(2)}, u32[]{:S(2)}) collective-permute-start(f32[3,1,6,36]{3,2,1,0:T(8,128)S(1)} %get-tuple-element.109), channel_id=1, source_target_pairs={{0,64},{64,128},{128,192},{192,256},{256,320},{320,384},{384,448},... | collective-permute-start | bytes 7784 | tf_op jit(solution)/shard_map/ppermute | solution.py:24
  44.6 9.3 %collective-permute-start.7 = (f32[3,1,6,36]{3,2,1,0:T(8,128)S(1)}, f32[3,1,6,36]{3,2,1,0:T(8,128)S(1)}, u32[]{:S(2)}, u32[]{:S(2)}) collective-permute-start(f32[3,1,6,36]{3,2,1,0:T(8,128)S(1)} %get-tuple-element.110), channel_id=1, source_target_pairs={{64,0},{128,64},{192,128},{256,192},{320,256},{384,320},{448,384},... | collective-permute-start | bytes 7784 | tf_op jit(solution)/shard_map/ppermute | solution.py:27
  47.1 10.0 %collective-permute-start.4 = (bf16[3,5,26,146]{3,2,1,0:T(8,128)(2,1)}, bf16[3,5,26,146]{3,2,1,0:T(8,128)(2,1)}, u32[]{:S(2)}, u32[]{:S(2)}) collective-permute-start(bf16[3,5,26,146]{3,2,1,0:T(8,128)(2,1)} %get-tuple-element.64), channel_id=1, source_target_pairs={{0,64},{64,128},{128,192},{192,256},{256,320},{320,384},{384,448},... | collective-permute-start | bytes 341648 | tf_op jit(solution)/shard_map/ppermute | solution.py:24
  52.4 8.5 %collective-permute-start.5 = (bf16[3,5,26,146]{3,2,1,0:T(8,128)(2,1)S(1)}, bf16[3,5,26,146]{3,2,1,0:T(8,128)(2,1)}, u32[]{:S(2)}, u32[]{:S(2)}) collective-permute-start(bf16[3,5,26,146]{3,2,1,0:T(8,128)(2,1)S(1)} %get-tuple-element.65), channel_id=1, source_target_pairs={{64,0},{128,64},{192,128},{256,192},{320,256},{384,320},{448,384},... | collective-permute-start | bytes 341648 | tf_op jit(solution)/shard_map/ppermute | solution.py:27
  54.2 0.8 copy-start.18
  54.3 0.8 copy-start.21
  54.8 0.7 copy-start.13
  54.9 0.7 copy-start.15
  65.7 4.3 %copy-start.4 = (bf16[20,20,140]{2,0,1:T(8,128)(2,1)}, bf16[20,20,140]{2,0,1:T(8,128)(2,1)S(1)}, u32[]{:S(2)}) copy-start(bf16[20,20,140]{2,0,1:T(8,128)(2,1)S(1)} %copy.142) | copy-start | bytes 336004
  66.1 3.9 %copy-start.6 = (bf16[20,20,140]{2,0,1:T(8,128)(2,1)}, bf16[20,20,140]{2,0,1:T(8,128)(2,1)S(1)}, u32[]{:S(2)}) copy-start(bf16[20,20,140]{2,0,1:T(8,128)(2,1)S(1)} %copy.143) | copy-start | bytes 336004
  66.2 0.7 copy-start.10
  66.3 0.7 copy-start.23
  66.3 0.7 copy-start.24
  66.3 0.7 copy-start.26
  66.3 0.7 copy-start.27
  66.3 3.7 %copy-start.8 = (bf16[20,20,140]{2,0,1:T(8,128)(2,1)}, bf16[20,20,140]{2,0,1:T(8,128)(2,1)S(1)}, u32[]{:S(2)}) copy-start(bf16[20,20,140]{2,0,1:T(8,128)(2,1)S(1)} %copy.144) | copy-start | bytes 336004
  66.7 3.4 %copy-start.2 = (f32[20,20,140]{2,0,1:T(8,128)}, f32[20,20,140]{2,0,1:T(8,128)S(1)}, u32[]{:S(2)}) copy-start(f32[20,20,140]{2,0,1:T(8,128)S(1)} %copy.145) | copy-start | bytes 672004
  70.1 1.6 %copy-start.25 = (pred[34]{0:T(512)(128)(4,1)S(1)}, pred[34]{0:T(512)(128)(4,1)}, u32[]{:S(2)}) copy-start(pred[34]{0:T(512)(128)(4,1)} %and_or_fusion) | copy-start | bytes 106
  71.8 6.8 %collective-permute-start.8 = (f32[3,1,4,34]{3,2,1,0:T(4,128)S(1)}, f32[3,1,4,34]{3,2,1,0:T(4,128)S(1)}, u32[]{:S(2)}, u32[]{:S(2)}) collective-permute-start(f32[3,1,4,34]{3,2,1,0:T(4,128)S(1)} %get-tuple-element.119), channel_id=1, source_target_pairs={{0,64},{64,128},{128,192},{192,256},{256,320},{320,384},{384,448},... | collective-permute-start | bytes 4904 | tf_op jit(solution)/shard_map/ppermute | solution.py:24
  77.3 5.3 %collective-permute-start.9 = (f32[3,1,4,34]{3,2,1,0:T(4,128)S(1)}, f32[3,1,4,34]{3,2,1,0:T(4,128)S(1)}, u32[]{:S(2)}, u32[]{:S(2)}) collective-permute-start(f32[3,1,4,34]{3,2,1,0:T(4,128)S(1)} %get-tuple-element.120), channel_id=1, source_target_pairs={{64,0},{128,64},{192,128},{256,192},{320,256},{384,320},{448,384},... | collective-permute-start | bytes 4904 | tf_op jit(solution)/shard_map/ppermute | solution.py:27
  82.6 5.3 %collective-permute-start.10 = (f32[3,6,1,34]{3,2,1,0:T(1,128)S(1)}, f32[3,6,1,34]{3,2,1,0:T(1,128)S(1)}, u32[]{:S(2)}, u32[]{:S(2)}) collective-permute-start(f32[3,6,1,34]{3,2,1,0:T(1,128)S(1)} %get-tuple-element.117), channel_id=1, source_target_pairs={{0,8},{8,16},{16,24},{24,32},{32,40},{40,48},{48,56},{1,9},{9,17},... | collective-permute-start | bytes 7352 | tf_op jit(solution)/shard_map/ppermute | solution.py:24
  85.0 4.8 %collective-permute-start.11 = (f32[3,6,1,34]{3,2,1,0:T(1,128)S(1)}, f32[3,6,1,34]{3,2,1,0:T(1,128)S(1)}, u32[]{:S(2)}, u32[]{:S(2)}) collective-permute-start(f32[3,6,1,34]{3,2,1,0:T(1,128)S(1)} %get-tuple-element.118), channel_id=1, source_target_pairs={{8,0},{16,8},{24,16},{32,24},{40,32},{48,40},{56,48},{9,1},{17,9},... | collective-permute-start | bytes 7352 | tf_op jit(solution)/shard_map/ppermute | solution.py:27
  90.0 0.8 copy-start.12
  90.0 0.8 copy-start.19
  90.0 0.8 copy-start.22
  90.5 0.7 copy-start.14
  90.5 0.7 copy-start.16
  92.5 1.4 %copy-start.3 = (f32[20,20,140]{2,0,1:T(8,128)S(1)}, f32[20,20,140]{2,0,1:T(8,128)}, u32[]{:S(2)}) copy-start(f32[20,20,140]{2,0,1:T(8,128)} %copy-done.2) | copy-start | bytes 672004
  92.5 1.4 %copy-start.5 = (bf16[20,20,140]{2,0,1:T(8,128)(2,1)S(1)}, bf16[20,20,140]{2,0,1:T(8,128)(2,1)}, u32[]{:S(2)}) copy-start(bf16[20,20,140]{2,0,1:T(8,128)(2,1)} %copy-done.4) | copy-start | bytes 336004
  92.5 1.4 %copy-start.7 = (bf16[20,20,140]{2,0,1:T(8,128)(2,1)S(1)}, bf16[20,20,140]{2,0,1:T(8,128)(2,1)}, u32[]{:S(2)}) copy-start(bf16[20,20,140]{2,0,1:T(8,128)(2,1)} %copy-done.6) | copy-start | bytes 336004
  92.6 1.4 %copy-start.9 = (bf16[20,20,140]{2,0,1:T(8,128)(2,1)S(1)}, bf16[20,20,140]{2,0,1:T(8,128)(2,1)}, u32[]{:S(2)}) copy-start(bf16[20,20,140]{2,0,1:T(8,128)(2,1)} %copy-done.8) | copy-start | bytes 336004
  95.4 0.8 copy-start.28
  95.4 0.8 copy-start.30
  95.4 15.8 %copy-start.29 = (s32[64]{0:T(128)S(1)}, s32[64]{0:T(128)}, u32[]{:S(2)}) copy-start(s32[64]{0:T(128)} %get-tuple-element.55) | copy-start | bytes 772
  97.4 24.9 %all-to-all-start.1 = ((f32[3,64,16]{2,0,1:T(4,128)}), f32[3,64,16]{2,0,1:T(4,128)S(1)}, u32[]{:S(2)}, u32[]{:S(2)}) async-start(f32[3,64,16]{2,0,1:T(4,128)} %copy.136), calls=%async_computation.1 | async-start | bytes 262144 | tf_op jit(solution)/shard_map/all_to_all | solution.py:361

commit v7 on v6

--- a/solution.py
+++ b/solution.py
@@ -42,8 +42,8 @@
                     lax.slice_in_dim(block, 0, width, axis=dim),
                 )
             )
-        low_flat = jnp.concatenate([p[0].reshape(-1) for p in parts])
-        high_flat = jnp.concatenate([p[1].reshape(-1) for p in parts])
+        low_flat = jnp.concatenate([p[0].reshape(-1).astype(jnp.float32) for p in parts])
+        high_flat = jnp.concatenate([p[1].reshape(-1).astype(jnp.float32) for p in parts])
         low_flat = lax.ppermute(low_flat, axis, forward)
         high_flat = lax.ppermute(high_flat, axis, backward)
         split = parts[0][0].size
@@ -51,8 +51,8 @@
         for index, (block, dim) in enumerate(((first, first_dim), (second, second_dim))):
             shape = parts[index][0].shape
             begin, end = (0, split) if index == 0 else (split, low_flat.shape[0])
-            low = low_flat[begin:end].reshape(shape)
-            high = high_flat[begin:end].reshape(shape)
+            low = low_flat[begin:end].reshape(shape).astype(block.dtype)
+            high = high_flat[begin:end].reshape(shape).astype(block.dtype)
             pieces.append(jnp.concatenate([low, block, high], axis=dim))
         first, second = pieces
     return first, second
@@ -230,7 +230,6 @@
     stacked = jnp.stack([reference_image, deformed_image, roi_mask.astype(jnp.bfloat16)])
     stacked = with_halo(stacked, (("gy", 2),), 5)
     stacked = with_halo(stacked, (("gz", 3),), 5 + ELEM)
-    padded_images = with_halo(stacked, (("gx", 1),), 5).astype(jnp.float32)
     nodes_shape = (
         3,
         reference_image.shape[0] // ELEM,
@@ -325,7 +324,8 @@
         axis=3,
     )
     extended = jnp.concatenate([low_row, middle, high_row], axis=2)
-    first_padded = with_halo(extended, (("gx", 1),), 1)
+    padded_images, first_padded = with_halo_pair(stacked, extended, (("gx", 1, 1),), (5, 1))
+    padded_images = padded_images.astype(jnp.float32)
     derived = derive_fields(padded_images[0], padded_images[1])
     region = padded_images[2][3:-3, 3:-3, 3:-3]
     contrast = derived[0].astype(jnp.float32)

time: 124 us -> 143 us (1.15)
  the two profiles are of different devices: /device:TPU:1 before, /device:TPU:193 now
where the time goes in v7:
time: 143 us; the launch traced here: 142 us
  starting transfers between devices  56.8 us (40%)
  other arithmetic  26.6 us (19%)
  waiting for transfers between devices  24.3 us (17%)
  local copies, waits for them, and re-layouts  24.2 us (17%)
  matrix products  8.15 us (6%)
  between operations  1.93 us (1%)
    all_to_all x1, starting transfers between devices, per_device(): lax.all_to_all(outgoing, ('gy', 'gz'), split_axis=1, concat_axis=1, tiled...  14.9 us
    ppermute x4, starting transfers between devices, with_halo(): lax.ppermute(lax.slice_in_dim(block, block.shape[dim] - width, None, axis...  14.9 us
    all_to_all x1, starting transfers between devices, per_device(): lax.all_to_all(send_outgoing, ('gy', 'gz'), split_axis=1, concat_axis=1,...  13.3 us
    ppermute x4, waiting for transfers between devices, with_halo(): lax.ppermute(lax.slice_in_dim(block, 0, width, axis=dim), axis, backward)  10.8 us
    all_to_all x1, waiting for transfers between devices, per_device(): lax.all_to_all(outgoing, ('gy', 'gz'), split_axis=1, concat_axis=1, tiled...  10.4 us
    add x43, other arithmetic, pair_op(): lax.slice_in_dim(volume, 1, length, axis=dimension)  7.3 us
    ppermute x4, starting transfers between devices, with_halo(): lax.ppermute(lax.slice_in_dim(block, 0, width, axis=dim), axis, backward)  6.43 us
    ppermute x1, starting transfers between devices, with_halo_pair(): low_flat = lax.ppermute(low_flat, axis, forward)  5.38 us
  transfers between devices with their start and end apart: 12, of which 6 were waited for; matrix products, arithmetic and copies ran while one was open for 9% of the time, Pallas kernels for 0%

profile of v7, /device:TPU:193, one launch (start us, length us, event | category | flops | bytes accessed | tf_op | source)
XLA Modules:
  0.0 141.9 jit_solution(15337012057001447427)
XLA Ops:
  0.0 0.9 convert_bitcast_fusion
  0.9 0.9 pad_maximum_fusion.10
  1.9 3.2 %collective-permute-start = (bf16[3,16,5,128]{3,2,1,0:T(8,128)(2,1)S(1)}, bf16[3,16,5,128]{3,2,1,0:T(8,128)(2,1)S(1)}, u32[]{:S(2)}, u32[]{:S(2)}) collective-permute-start(bf16[3,16,5,128]{3,2,1,0:T(8,128)(2,1)S(1)} %get-tuple-element.103), channel_id=1, source_target_pairs={{0,8},{8,16},{16,24},{24,32},{32,40},{40,48},{48,56},{1,9},{9,17},... | collective-permute-start | bytes 184328 | tf_op jit(solution)/shard_map/ppermute | solution.py:24
  5.1 1.3 collective-permute-start.1
  6.4 0.7 broadcast_add_fusion.1
  7.1 1.2 and_and_fusion
  8.9 0.6 copy-done.36
  9.5 1.1 concatenate.74
  10.6 0.7 fusion.7
  12.1 0.7 copy.127
  12.8 13.3 %all-to-all-start = ((f32[4,64,80]{2,0,1:T(4,128)}), f32[4,64,80]{2,0,1:T(4,128)S(1)}, u32[]{:S(2)}, u32[]{:S(2)}) async-start(f32[4,64,80]{2,0,1:T(4,128)} %copy.127), calls=%async_computation | async-start | bytes 262144 | tf_op jit(solution)/shard_map/all_to_all | solution.py:296
  26.2 0.6 fusion.177
  26.9 0.6 iota_compare_fusion.8
  27.5 0.6 iota_compare_fusion.7
  28.1 0.6 fusion.182
  29.0 3.5 %collective-permute-start.2 = (bf16[3,16,26,9]{3,2,1,0:T(8,128)(2,1)S(1)}, bf16[3,16,26,9]{3,2,1,0:T(8,128)(2,1)S(1)}, u32[]{:S(2)}, u32[]{:S(2)}) collective-permute-start(bf16[3,16,26,9]{3,2,1,0:T(8,128)(2,1)S(1)} %get-tuple-element.76), channel_id=1, source_target_pairs={{0,1},{1,2},{2,3},{3,4},{4,5},{5,6},{6,7},{8,9},{9,10},{10,11},{11... | collective-permute-start | bytes 67400 | tf_op jit(solution)/shard_map/ppermute | solution.py:24
  32.6 1.9 %collective-permute-start.3 = (bf16[3,16,26,9]{3,2,1,0:T(8,128)(2,1)S(1)}, bf16[3,16,26,9]{3,2,1,0:T(8,128)(2,1)S(1)}, u32[]{:S(2)}, u32[]{:S(2)}) collective-permute-start(bf16[3,16,26,9]{3,2,1,0:T(8,128)(2,1)S(1)} %get-tuple-element.77), channel_id=1, source_target_pairs={{1,0},{2,1},{3,2},{4,3},{5,4},{6,5},{7,6},{9,8},{10,9},{11,10},{12... | collective-permute-start | bytes 67400 | tf_op jit(solution)/shard_map/ppermute | solution.py:27
  34.6 2.8 %collective-permute-done.2 = bf16[3,16,26,9]{3,2,1,0:T(8,128)(2,1)S(1)} collective-permute-done((bf16[3,16,26,9]{3,2,1,0:T(8,128)(2,1)S(1)}, bf16[3,16,26,9]{3,2,1,0:T(8,128)(2,1)S(1)}, u32[]{:S(2)}, u32[]{:S(2)}) %collective-permute-start.2) | collective-permute-done | bytes 22496 | tf_op jit(solution)/shard_map/ppermute | solution.py:24
  37.3 4.4 %collective-permute-done.3 = bf16[3,16,26,9]{3,2,1,0:T(8,128)(2,1)S(1)} collective-permute-done((bf16[3,16,26,9]{3,2,1,0:T(8,128)(2,1)S(1)}, bf16[3,16,26,9]{3,2,1,0:T(8,128)(2,1)S(1)}, u32[]{:S(2)}, u32[]{:S(2)}) %collective-permute-start.3) | collective-permute-done | bytes 22496 | tf_op jit(solution)/shard_map/ppermute | solution.py:27
  44.1 0.8 fusion.8
  46.2 1.9 %collective-permute-start.5 = (f32[57588]{0:T(1024)S(1)}, f32[57588]{0:T(1024)S(1)}, u32[]{:S(2)}, u32[]{:S(2)}) collective-permute-start(f32[57588]{0:T(1024)S(1)} %pad_maximum_fusion.9), channel_id=1, source_target_pairs={{64,0},{128,64},{192,128},{256,192},{320,256},{384,320},{448,384},... | collective-permute-start | bytes 691064 | tf_op jit(solution)/shard_map/ppermute | solution.py:48
  48.2 5.4 %collective-permute-start.4 = (f32[57588]{0:T(1024)S(1)}, f32[57588]{0:T(1024)S(1)}, u32[]{:S(2)}, u32[]{:S(2)}) collective-permute-start(f32[57588]{0:T(1024)S(1)} %pad_maximum_fusion.8), channel_id=1, source_target_pairs={{0,64},{64,128},{128,192},{192,256},{256,320},{320,384},{384,448},... | collective-permute-start | bytes 691064 | tf_op jit(solution)/shard_map/ppermute | solution.py:47
  54.1 0.6 mul.999
  54.7 0.6 mul.993
  55.3 0.6 select_add_fusion
  56.5 0.9 fusion.195
  57.4 0.8 multiply_add_fusion.7
  58.3 1.1 fusion.59
  60.2 0.8 maximum_convert_fusion
  61.4 0.6 fusion.33
  62.0 2.0 %add_multiply_fusion = (f32[22,22,142]{2,1,0:T(8,128)S(1)}, f32[22,22,142]{2,1,0:T(8,128)S(1)}, f32[22,22,142]{2,1,0:T(8,128)}) fusion(f32[22,22,146]{2,1,0:T(8,128)S(1)} %get-tuple-element.146, f32[22,22,146]{2,1,0:T(8,128)S(1)} %get-tuple-element.147), kind=kLoop, calls=%fused_computation.95 | loop fusion | flops 1374560 | bytes 3573856 | tf_op jit(solution)/shard_map/mul | solution.py:77
  64.0 1.0 fusion.208
  65.3 0.6 copy-done.15
  66.3 0.6 slice_add_fusion.56
  66.9 0.6 slice_add_fusion.53
  67.5 0.6 fusion.165
  68.2 0.6 slice_add_fusion.49
  68.8 0.6 slice_add_fusion.52
  69.4 0.6 slice_add_fusion.48
  70.0 0.6 fusion.153
  70.6 0.6 fusion.159
  71.2 0.6 slice_add_fusion.45
  73.0 1.1 fusion.207
  74.1 1.9 %squeeze.115 = f32[20,20,140]{2,1,0:T(8,128)} reshape(f32[1,20,5,4,140]{4,3,2,1,0:T(4,128)} %get-tuple-element.61) | data formatting | bytes 448000 | tf_op jit(solution)/shard_map/squeeze | solution.py:336
  76.0 1.9 %squeeze.119 = f32[20,20,140]{2,1,0:T(8,128)} reshape(f32[1,20,5,4,140]{4,3,2,1,0:T(4,128)} %get-tuple-element.62) | data formatting | bytes 448000 | tf_op jit(solution)/shard_map/squeeze | solution.py:336
  78.0 1.9 %squeeze.117 = f32[20,20,140]{2,1,0:T(8,128)} reshape(f32[1,20,5,4,140]{4,3,2,1,0:T(4,128)} %get-tuple-element.63) | data formatting | bytes 448000 | tf_op jit(solution)/shard_map/squeeze | solution.py:336
  80.2 0.7 copy-done.4
  82.3 1.4 multiply_reduce_fusion.3
  84.1 0.6 copy-done
  85.2 1.1 fusion.46
  86.6 1.4 multiply_reduce_fusion.5
  89.0 5.0 %collective-permute-start.6 = (f32[3,1,4,34]{3,2,1,0:T(4,128)S(1)}, f32[3,1,4,34]{3,2,1,0:T(4,128)S(1)}, u32[]{:S(2)}, u32[]{:S(2)}) collective-permute-start(f32[3,1,4,34]{3,2,1,0:T(4,128)S(1)} %get-tuple-element.119), channel_id=1, source_target_pairs={{0,64},{64,128},{128,192},{192,256},{256,320},{320,384},{384,448},... | collective-permute-start | bytes 4904 | tf_op jit(solution)/shard_map/ppermute | solution.py:24
  94.0 1.9 %collective-permute-start.7 = (f32[3,1,4,34]{3,2,1,0:T(4,128)S(1)}, f32[3,1,4,34]{3,2,1,0:T(4,128)S(1)}, u32[]{:S(2)}, u32[]{:S(2)}) collective-permute-start(f32[3,1,4,34]{3,2,1,0:T(4,128)S(1)} %get-tuple-element.120), channel_id=1, source_target_pairs={{64,0},{128,64},{192,128},{256,192},{320,256},{384,320},{448,384},... | collective-permute-start | bytes 4904 | tf_op jit(solution)/shard_map/ppermute | solution.py:27
  95.9 3.6 %collective-permute-done.7 = f32[3,1,4,34]{3,2,1,0:T(4,128)S(1)} collective-permute-done((f32[3,1,4,34]{3,2,1,0:T(4,128)S(1)}, f32[3,1,4,34]{3,2,1,0:T(4,128)S(1)}, u32[]{:S(2)}, u32[]{:S(2)}) %collective-permute-start.7) | collective-permute-done | bytes 1664 | tf_op jit(solution)/shard_map/ppermute | solution.py:27
  99.6 3.1 %collective-permute-start.8 = (f32[3,6,1,34]{3,2,1,0:T(1,128)S(1)}, f32[3,6,1,34]{3,2,1,0:T(1,128)S(1)}, u32[]{:S(2)}, u32[]{:S(2)}) collective-permute-start(f32[3,6,1,34]{3,2,1,0:T(1,128)S(1)} %get-tuple-element.117), channel_id=1, source_target_pairs={{0,8},{8,16},{16,24},{24,32},{32,40},{40,48},{48,56},{1,9},{9,17},... | collective-permute-start | bytes 7352 | tf_op jit(solution)/shard_map/ppermute | solution.py:24
  102.7 1.3 collective-permute-start.9
  104.3 2.8 %collective-permute-done.9 = f32[3,6,1,34]{3,2,1,0:T(1,128)S(1)} collective-permute-done((f32[3,6,1,34]{3,2,1,0:T(1,128)S(1)}, f32[3,6,1,34]{3,2,1,0:T(1,128)S(1)}, u32[]{:S(2)}, u32[]{:S(2)}) %collective-permute-start.9) | collective-permute-done | bytes 2480 | tf_op jit(solution)/shard_map/ppermute | solution.py:27
  110.0 1.2 fusion.48
  111.5 1.4 multiply_reduce_fusion.1
  114.2 0.7 copy.156
  114.9 14.9 %all-to-all-start.1 = ((f32[3,64,16]{2,0,1:T(4,128)}), f32[3,64,16]{2,0,1:T(4,128)S(1)}, u32[]{:S(2)}, u32[]{:S(2)}) async-start(f32[3,64,16]{2,0,1:T(4,128)} %copy.156), calls=%async_computation.1 | async-start | bytes 262144 | tf_op jit(solution)/shard_map/all_to_all | solution.py:361
  129.8 0.7 slice_add_fusion.57
  130.5 10.4 %all-to-all-done.1 = f32[3,64,16]{2,0,1:T(4,128)S(1)} async-done(((f32[3,64,16]{2,0,1:T(4,128)}), f32[3,64,16]{2,0,1:T(4,128)S(1)}, u32[]{:S(2)}, u32[]{:S(2)}) %all-to-all-start.1) | async-done | bytes 12320 | tf_op jit(solution)/shard_map/all_to_all | solution.py:361
  141.1 0.9 convolution_bitcast_fusion
  (303 shorter events, 17.4 us)
Async XLA Ops:
  1.9 26.8 %collective-permute-start = (bf16[3,16,5,128]{3,2,1,0:T(8,128)(2,1)S(1)}, bf16[3,16,5,128]{3,2,1,0:T(8,128)(2,1)S(1)}, u32[]{:S(2)}, u32[]{:S(2)}) collective-permute-start(bf16[3,16,5,128]{3,2,1,0:T(8,128)(2,1)S(1)} %get-tuple-element.103), channel_id=1, source_target_pairs={{0,8},{8,16},{16,24},{24,32},{32,40},{40,48},{48,56},{1,9},{9,17},... | collective-permute-start | bytes 184328 | tf_op jit(solution)/shard_map/ppermute | solution.py:24
  5.1 23.6 %collective-permute-start.1 = (bf16[3,16,5,128]{3,2,1,0:T(8,128)(2,1)S(1)}, bf16[3,16,5,128]{3,2,1,0:T(8,128)(2,1)S(1)}, u32[]{:S(2)}, u32[]{:S(2)}) collective-permute-start(bf16[3,16,5,128]{3,2,1,0:T(8,128)(2,1)S(1)} %get-tuple-element.104), channel_id=1, source_target_pairs={{8,0},{16,8},{24,16},{32,24},{40,32},{48,40},{56,48},{9,1},{17,9},... | collective-permute-start | bytes 184328 | tf_op jit(solution)/shard_map/ppermute | solution.py:27
  11.3 17.3 %copy-start.6 = (bf16[16,16,128]{2,1,0:T(8,128)(2,1)S(1)}, bf16[16,16,128]{2,1,0:T(8,128)(2,1)}, u32[]{:S(2)}) copy-start(bf16[16,16,128]{2,1,0:T(8,128)(2,1)} %param.6) | copy-start | bytes 196612
  11.3 17.3 %copy-start.7 = (bf16[16,16,128]{2,1,0:T(8,128)(2,1)S(1)}, bf16[16,16,128]{2,1,0:T(8,128)(2,1)}, u32[]{:S(2)}) copy-start(bf16[16,16,128]{2,1,0:T(8,128)(2,1)} %param.5) | copy-start | bytes 196612
  12.8 30.0 %all-to-all-start = ((f32[4,64,80]{2,0,1:T(4,128)}), f32[4,64,80]{2,0,1:T(4,128)S(1)}, u32[]{:S(2)}, u32[]{:S(2)}) async-start(f32[4,64,80]{2,0,1:T(4,128)} %copy.127), calls=%async_computation | async-start | bytes 262144 | tf_op jit(solution)/shard_map/all_to_all | solution.py:296
  26.8 31.4 %copy-start.57 = (f32[140]{0:T(256)}, f32[140]{0:T(256)S(1)}, u32[]{:S(2)}) copy-start(f32[140]{0:T(256)S(1)} %get-tuple-element.150) | copy-start | bytes 1684
  26.8 31.4 %copy-start.59 = (f32[140]{0:T(256)}, f32[140]{0:T(256)S(1)}, u32[]{:S(2)}) copy-start(f32[140]{0:T(256)S(1)} %get-tuple-element.151) | copy-start | bytes 1684
  26.8 31.4 %copy-start.49 = (s32[140]{0:T(256)}, s32[140]{0:T(256)S(1)}, u32[]{:S(2)}) copy-start(s32[140]{0:T(256)S(1)} %get-tuple-element.148) | copy-start | bytes 1684
  26.8 31.4 %copy-start.51 = (s32[140]{0:T(256)}, s32[140]{0:T(256)S(1)}, u32[]{:S(2)}) copy-start(s32[140]{0:T(256)S(1)} %get-tuple-element.149) | copy-start | bytes 1684
  29.0 8.3 %collective-permute-start.2 = (bf16[3,16,26,9]{3,2,1,0:T(8,128)(2,1)S(1)}, bf16[3,16,26,9]{3,2,1,0:T(8,128)(2,1)S(1)}, u32[]{:S(2)}, u32[]{:S(2)}) collective-permute-start(bf16[3,16,26,9]{3,2,1,0:T(8,128)(2,1)S(1)} %get-tuple-element.76), channel_id=1, source_target_pairs={{0,1},{1,2},{2,3},{3,4},{4,5},{5,6},{6,7},{8,9},{9,10},{10,11},{11... | collective-permute-start | bytes 67400 | tf_op jit(solution)/shard_map/ppermute | solution.py:24
  32.6 9.1 %collective-permute-start.3 = (bf16[3,16,26,9]{3,2,1,0:T(8,128)(2,1)S(1)}, bf16[3,16,26,9]{3,2,1,0:T(8,128)(2,1)S(1)}, u32[]{:S(2)}, u32[]{:S(2)}) collective-permute-start(bf16[3,16,26,9]{3,2,1,0:T(8,128)(2,1)S(1)} %get-tuple-element.77), channel_id=1, source_target_pairs={{1,0},{2,1},{3,2},{4,3},{5,4},{6,5},{7,6},{9,8},{10,9},{11,10},{12... | collective-permute-start | bytes 67400 | tf_op jit(solution)/shard_map/ppermute | solution.py:27
  34.5 19.5 %copy-start.39 = (f32[4]{0:T(128)}, f32[4]{0:T(128)S(1)}, u32[]{:S(2)}) copy-start(f32[4]{0:T(128)S(1)} %get-tuple-element.152) | copy-start | bytes 52
  34.5 20.1 %copy-start.43 = (f32[4]{0:T(128)}, f32[4]{0:T(128)S(1)}, u32[]{:S(2)}) copy-start(f32[4]{0:T(128)S(1)} %get-tuple-element.153) | copy-start | bytes 52
  44.1 1.6 %copy-start.37 = (f32[640]{0:T(1024)}, f32[640]{0:T(1024)S(1)}, u32[]{:S(2)}) copy-start(f32[640]{0:T(1024)S(1)} %slice_reduce_fusion) | copy-start | bytes 7684
  45.5 14.3 %copy-start.8 = (f32[3,4,4,32]{3,2,1,0:T(4,128)}, f32[3,4,4,32]{3,2,1,0:T(4,128)S(1)}, u32[]{:S(2)}) copy-start(f32[3,4,4,32]{3,2,1,0:T(4,128)S(1)} %get-tuple-element.95) | copy-start | bytes 18436
  45.5 14.3 %copy-start.10 = (f32[3,4,4,32]{3,2,1,0:T(4,128)}, f32[3,4,4,32]{3,2,1,0:T(4,128)S(1)}, u32[]{:S(2)}) copy-start(f32[3,4,4,32]{3,2,1,0:T(4,128)S(1)} %get-tuple-element.96) | copy-start | bytes 18436
  45.8 14.3 %copy-start.12 = (f32[3,4,4,2]{3,2,1,0:T(4,128)}, f32[3,4,4,2]{3,2,1,0:T(4,128)S(1)}, u32[]{:S(2)}) copy-start(f32[3,4,4,2]{3,2,1,0:T(4,128)S(1)} %slice.1110) | copy-start | bytes 1156
  46.2 9.7 %collective-permute-start.5 = (f32[57588]{0:T(1024)S(1)}, f32[57588]{0:T(1024)S(1)}, u32[]{:S(2)}, u32[]{:S(2)}) collective-permute-start(f32[57588]{0:T(1024)S(1)} %pad_maximum_fusion.9), channel_id=1, source_target_pairs={{64,0},{128,64},{192,128},{256,192},{320,256},{384,320},{448,384},... | collective-permute-start | bytes 691064 | tf_op jit(solution)/shard_map/ppermute | solution.py:48
  48.2 8.2 %collective-permute-start.4 = (f32[57588]{0:T(1024)S(1)}, f32[57588]{0:T(1024)S(1)}, u32[]{:S(2)}, u32[]{:S(2)}) collective-permute-start(f32[57588]{0:T(1024)S(1)} %pad_maximum_fusion.8), channel_id=1, source_target_pairs={{0,64},{64,128},{128,192},{192,256},{256,320},{320,384},{384,448},... | collective-permute-start | bytes 691064 | tf_op jit(solution)/shard_map/ppermute | solution.py:47
  66.2 5.7 %copy-start.53 = (f32[20]{0:T(128)S(1)}, f32[20]{0:T(128)}, u32[]{:S(2)}) copy-start(f32[20]{0:T(128)} %mul.999) | copy-start | bytes 244
  66.3 5.7 %copy-start.55 = (f32[20]{0:T(128)S(1)}, f32[20]{0:T(128)}, u32[]{:S(2)}) copy-start(f32[20]{0:T(128)} %mul.993) | copy-start | bytes 244
  79.9 1.2 copy-start.5
  80.2 6.1 %copy-start.16 = (f32[20,20,140]{2,0,1:T(8,128)}, f32[20,20,140]{2,0,1:T(8,128)S(1)}, u32[]{:S(2)}) copy-start(f32[20,20,140]{2,0,1:T(8,128)S(1)} %copy.165) | copy-start | bytes 672004
  81.5 4.9 %copy-start.19 = (bf16[20,20,140]{2,0,1:T(8,128)(2,1)}, bf16[20,20,140]{2,0,1:T(8,128)(2,1)S(1)}, u32[]{:S(2)}) copy-start(bf16[20,20,140]{2,0,1:T(8,128)(2,1)S(1)} %copy.162) | copy-start | bytes 336004
  81.9 4.5 %copy-start.21 = (bf16[20,20,140]{2,0,1:T(8,128)(2,1)}, bf16[20,20,140]{2,0,1:T(8,128)(2,1)S(1)}, u32[]{:S(2)}) copy-start(bf16[20,20,140]{2,0,1:T(8,128)(2,1)S(1)} %copy.163) | copy-start | bytes 336004
  82.1 4.3 %copy-start.23 = (bf16[20,20,140]{2,0,1:T(8,128)(2,1)}, bf16[20,20,140]{2,0,1:T(8,128)(2,1)S(1)}, u32[]{:S(2)}) copy-start(bf16[20,20,140]{2,0,1:T(8,128)(2,1)S(1)} %copy.164) | copy-start | bytes 336004
  83.7 1.0 copy-start
  83.7 1.2 copy-start.1
  83.7 1.3 copy-start.2
  83.7 1.5 %copy-start.3 = (f32[20,20,140]{2,1,0:T(8,128)S(1)}, f32[20,20,140]{2,1,0:T(8,128)}, u32[]{:S(2)}) copy-start(f32[20,20,140]{2,1,0:T(8,128)} %squeeze.117) | copy-start | bytes 672004
  85.1 1.3 copy-start.34
  85.2 1.3 copy-start.41
  85.2 1.3 copy-start.45
  86.4 2.0 %copy-start.25 = (f32[4,4,35]{2,1,0:T(4,128)S(1)}, f32[4,4,35]{2,1,0:T(4,128)}, u32[]{:S(2)}) copy-start(f32[4,4,35]{2,1,0:T(4,128)} %slice_add_fusion.56) | copy-start | bytes 6724
  86.4 2.0 %copy-start.26 = (f32[4,4,35]{2,1,0:T(4,128)S(1)}, f32[4,4,35]{2,1,0:T(4,128)}, u32[]{:S(2)}) copy-start(f32[4,4,35]{2,1,0:T(4,128)} %slice_add_fusion.53) | copy-start | bytes 6724
  86.5 2.0 %copy-start.27 = (f32[4,4,35]{2,1,0:T(4,128)S(1)}, f32[4,4,35]{2,1,0:T(4,128)}, u32[]{:S(2)}) copy-start(f32[4,4,35]{2,1,0:T(4,128)} %fusion.165) | copy-start | bytes 6724
  86.5 2.1 %copy-start.28 = (f32[4,4,35]{2,1,0:T(4,128)S(1)}, f32[4,4,35]{2,1,0:T(4,128)}, u32[]{:S(2)}) copy-start(f32[4,4,35]{2,1,0:T(4,128)} %slice_add_fusion.49) | copy-start | bytes 6724
  86.5 2.1 %copy-start.29 = (f32[4,4,35]{2,1,0:T(4,128)S(1)}, f32[4,4,35]{2,1,0:T(4,128)}, u32[]{:S(2)}) copy-start(f32[4,4,35]{2,1,0:T(4,128)} %slice_add_fusion.52) | copy-start | bytes 6724
  86.5 2.1 %copy-start.32 = (f32[4,4,35]{2,1,0:T(4,128)S(1)}, f32[4,4,35]{2,1,0:T(4,128)}, u32[]{:S(2)}) copy-start(f32[4,4,35]{2,1,0:T(4,128)} %fusion.159) | copy-start | bytes 6724
  86.5 2.2 %copy-start.30 = (f32[4,4,35]{2,1,0:T(4,128)S(1)}, f32[4,4,35]{2,1,0:T(4,128)}, u32[]{:S(2)}) copy-start(f32[4,4,35]{2,1,0:T(4,128)} %slice_add_fusion.48) | copy-start | bytes 6724
  86.5 2.2 %copy-start.31 = (f32[4,4,35]{2,1,0:T(4,128)S(1)}, f32[4,4,35]{2,1,0:T(4,128)}, u32[]{:S(2)}) copy-start(f32[4,4,35]{2,1,0:T(4,128)} %fusion.153) | copy-start | bytes 6724
  86.5 2.2 %copy-start.33 = (f32[4,4,35]{2,1,0:T(4,128)S(1)}, f32[4,4,35]{2,1,0:T(4,128)}, u32[]{:S(2)}) copy-start(f32[4,4,35]{2,1,0:T(4,128)} %slice_add_fusion.45) | copy-start | bytes 6724
  86.5 2.3 %copy-start.9 = (f32[3,4,4,32]{3,2,1,0:T(4,128)S(1)}, f32[3,4,4,32]{3,2,1,0:T(4,128)}, u32[]{:S(2)}) copy-start(f32[3,4,4,32]{3,2,1,0:T(4,128)} %copy-done.8) | copy-start | bytes 18436
  86.5 2.3 %copy-start.11 = (f32[3,4,4,32]{3,2,1,0:T(4,128)S(1)}, f32[3,4,4,32]{3,2,1,0:T(4,128)}, u32[]{:S(2)}) copy-start(f32[3,4,4,32]{3,2,1,0:T(4,128)} %copy-done.10) | copy-start | bytes 18436
  86.5 2.3 %copy-start.13 = (f32[3,4,4,2]{3,2,1,0:T(4,128)S(1)}, f32[3,4,4,2]{3,2,1,0:T(4,128)}, u32[]{:S(2)}) copy-start(f32[3,4,4,2]{3,2,1,0:T(4,128)} %copy-done.12) | copy-start | bytes 1156
  86.6 2.3 %copy-start.65 = (pred[34]{0:T(512)(128)(4,1)S(1)}, pred[34]{0:T(512)(128)(4,1)}, u32[]{:S(2)}) copy-start(pred[34]{0:T(512)(128)(4,1)} %and_or_fusion) | copy-start | bytes 106
  86.6 17.5 %copy-start.38 = (f32[640]{0:T(1024)S(1)}, f32[640]{0:T(1024)}, u32[]{:S(2)}) copy-start(f32[640]{0:T(1024)} %copy-done.37) | copy-start | bytes 7684
  88.0 19.4 %copy-start.50 = (s32[140]{0:T(256)S(1)}, s32[140]{0:T(256)}, u32[]{:S(2)}) copy-start(s32[140]{0:T(256)} %copy-done.49) | copy-start | bytes 1684
  88.0 19.4 %copy-start.52 = (s32[140]{0:T(256)S(1)}, s32[140]{0:T(256)}, u32[]{:S(2)}) copy-start(s32[140]{0:T(256)} %copy-done.51) | copy-start | bytes 1684
  88.2 19.2 %copy-start.58 = (f32[140]{0:T(256)S(1)}, f32[140]{0:T(256)}, u32[]{:S(2)}) copy-start(f32[140]{0:T(256)} %copy-done.57) | copy-start | bytes 1684
  88.2 19.2 %copy-start.60 = (f32[140]{0:T(256)S(1)}, f32[140]{0:T(256)}, u32[]{:S(2)}) copy-start(f32[140]{0:T(256)} %copy-done.59) | copy-start | bytes 1684
  89.0 7.0 %collective-permute-start.6 = (f32[3,1,4,34]{3,2,1,0:T(4,128)S(1)}, f32[3,1,4,34]{3,2,1,0:T(4,128)S(1)}, u32[]{:S(2)}, u32[]{:S(2)}) collective-permute-start(f32[3,1,4,34]{3,2,1,0:T(4,128)S(1)} %get-tuple-element.119), channel_id=1, source_target_pairs={{0,64},{64,128},{128,192},{192,256},{256,320},{320,384},{384,448},... | collective-permute-start | bytes 4904 | tf_op jit(solution)/shard_map/ppermute | solution.py:24
  94.0 5.6 %collective-permute-start.7 = (f32[3,1,4,34]{3,2,1,0:T(4,128)S(1)}, f32[3,1,4,34]{3,2,1,0:T(4,128)S(1)}, u32[]{:S(2)}, u32[]{:S(2)}) collective-permute-start(f32[3,1,4,34]{3,2,1,0:T(4,128)S(1)} %get-tuple-element.120), channel_id=1, source_target_pairs={{64,0},{128,64},{192,128},{256,192},{320,256},{384,320},{448,384},... | collective-permute-start | bytes 4904 | tf_op jit(solution)/shard_map/ppermute | solution.py:27
  99.6 4.7 %collective-permute-start.8 = (f32[3,6,1,34]{3,2,1,0:T(1,128)S(1)}, f32[3,6,1,34]{3,2,1,0:T(1,128)S(1)}, u32[]{:S(2)}, u32[]{:S(2)}) collective-permute-start(f32[3,6,1,34]{3,2,1,0:T(1,128)S(1)} %get-tuple-element.117), channel_id=1, source_target_pairs={{0,8},{8,16},{16,24},{24,32},{32,40},{40,48},{48,56},{1,9},{9,17},... | collective-permute-start | bytes 7352 | tf_op jit(solution)/shard_map/ppermute | solution.py:24
  102.7 4.4 %collective-permute-start.9 = (f32[3,6,1,34]{3,2,1,0:T(1,128)S(1)}, f32[3,6,1,34]{3,2,1,0:T(1,128)S(1)}, u32[]{:S(2)}, u32[]{:S(2)}) collective-permute-start(f32[3,6,1,34]{3,2,1,0:T(1,128)S(1)} %get-tuple-element.118), channel_id=1, source_target_pairs={{8,0},{16,8},{24,16},{32,24},{40,32},{48,40},{56,48},{9,1},{17,9},... | collective-permute-start | bytes 7352 | tf_op jit(solution)/shard_map/ppermute | solution.py:27
  110.0 1.5 %copy-start.17 = (f32[20,20,140]{2,0,1:T(8,128)S(1)}, f32[20,20,140]{2,0,1:T(8,128)}, u32[]{:S(2)}) copy-start(f32[20,20,140]{2,0,1:T(8,128)} %copy-done.16) | copy-start | bytes 672004
  110.0 1.5 %copy-start.20 = (bf16[20,20,140]{2,0,1:T(8,128)(2,1)S(1)}, bf16[20,20,140]{2,0,1:T(8,128)(2,1)}, u32[]{:S(2)}) copy-start(bf16[20,20,140]{2,0,1:T(8,128)(2,1)} %copy-done.19) | copy-start | bytes 336004
  110.0 1.5 %copy-start.22 = (bf16[20,20,140]{2,0,1:T(8,128)(2,1)S(1)}, bf16[20,20,140]{2,0,1:T(8,128)(2,1)}, u32[]{:S(2)}) copy-start(bf16[20,20,140]{2,0,1:T(8,128)(2,1)} %copy-done.21) | copy-start | bytes 336004
  110.0 1.5 %copy-start.24 = (bf16[20,20,140]{2,0,1:T(8,128)(2,1)S(1)}, bf16[20,20,140]{2,0,1:T(8,128)(2,1)}, u32[]{:S(2)}) copy-start(bf16[20,20,140]{2,0,1:T(8,128)(2,1)} %copy-done.23) | copy-start | bytes 336004
  110.0 1.5 %copy-start.35 = (f32[36,140]{1,0:T(8,128)S(1)}, f32[36,140]{1,0:T(8,128)}, u32[]{:S(2)}) copy-start(f32[36,140]{1,0:T(8,128)} %select_add_fusion) | copy-start | bytes 60484
  110.0 1.5 %copy-start.42 = (f32[4]{0:T(128)S(1)}, f32[4]{0:T(128)}, u32[]{:S(2)}) copy-start(f32[4]{0:T(128)} %copy-done.39) | copy-start | bytes 52
  110.0 1.5 %copy-start.46 = (f32[4]{0:T(128)S(1)}, f32[4]{0:T(128)}, u32[]{:S(2)}) copy-start(f32[4]{0:T(128)} %copy-done.43) | copy-start | bytes 52
  112.9 16.9 %copy-start.66 = (s32[64]{0:T(128)S(1)}, s32[64]{0:T(128)}, u32[]{:S(2)}) copy-start(s32[64]{0:T(128)} %get-tuple-element.55) | copy-start | bytes 772
  114.9 26.0 %all-to-all-start.1 = ((f32[3,64,16]{2,0,1:T(4,128)}), f32[3,64,16]{2,0,1:T(4,128)S(1)}, u32[]{:S(2)}, u32[]{:S(2)}) async-start(f32[3,64,16]{2,0,1:T(4,128)} %copy.156), calls=%async_computation.1 | async-start | bytes 262144 | tf_op jit(solution)/shard_map/all_to_all | solution.py:361
  (15 other events, 11.4 us)

commit v8 on v6

--- a/solution.py
+++ b/solution.py
@@ -222,6 +222,26 @@
     return collect_axis(reduced, 1, ELEM, squared)
 
 
+def plane_tables(nodes_x, nodes_y, squared):
+    low_x = axis_table(nodes_x, ELEM, squared)
+    low_y = axis_table(nodes_y, ELEM, squared)
+    return jnp.kron(low_x.T, low_y.T), jnp.kron(low_x[1:-1], low_y[1:-1])
+
+
+def spread_plane(padded, plane, line):
+    channels, nx, ny, nz = padded.shape
+    along = jnp.einsum(
+        "cij,jz->ciz", padded.reshape(channels, nx * ny, nz), line, precision=highest
+    )
+    return jnp.einsum("vi,ciz->cvz", plane, along, precision=highest)
+
+
+def collect_plane(volume, plane_back, line_back, nodes_x, nodes_y):
+    along = jnp.einsum("cvz,zk->cvk", volume, line_back, precision=highest)
+    summed = jnp.einsum("av,cvk->cak", plane_back, along, precision=highest)
+    return summed.reshape(volume.shape[0], nodes_x, nodes_y, line_back.shape[1])
+
+
 NEIGHBOURS = [(0, 0)] + [(ry, rz) for ry in (-1, 0, 1) for rz in (-1, 0, 1) if (ry, rz) != (0, 0)]
 HALO_CAP = 10
 
@@ -327,14 +347,20 @@
     extended = jnp.concatenate([low_row, middle, high_row], axis=2)
     first_padded = with_halo(extended, (("gx", 1),), 1)
     derived = derive_fields(padded_images[0], padded_images[1])
-    region = padded_images[2][3:-3, 3:-3, 3:-3]
+    voxels_x, voxels_y, voxels_z = derived.shape[1:]
+    derived = derived.reshape(derived.shape[0], voxels_x * voxels_y, voxels_z)
+    region = padded_images[2][3:-3, 3:-3, 3:-3].reshape(voxels_x * voxels_y, voxels_z)
     contrast = derived[0].astype(jnp.float32)
     slopes = derived[1:].astype(jnp.float32)
     masked_slopes = slopes * region[None]
-    wide_curvature = collect(masked_slopes * slopes, wide_square, True) + diagonal_shift
-    moved = spread(first_padded, wide_table)
+    plane, plane_back = plane_tables(ex + 2, ey + 2, False)
+    _, plane_square = plane_tables(ex + 2, ey + 2, True)
+    wide_curvature = (
+        collect_plane(masked_slopes * slopes, plane_square, wide_square, ex, ey) + diagonal_shift
+    )
+    moved = spread_plane(first_padded, plane, wide_table)
     residual = contrast + slopes[0] * moved[0] + slopes[1] * moved[1] + slopes[2] * moved[2]
-    image_part = collect(masked_slopes * residual[None], wide_back, False)
+    image_part = collect_plane(masked_slopes * residual[None], plane_back, wide_back, ex, ey)
     force_total = image_part + elastic_weight * elastic_force(first_padded)
     wide_values = first_padded[:, 1:-1, 1:-1, 1:-1] - force_total / wide_curvature
     column = jnp.arange(ez + 2, dtype=jnp.int32)
@@ -344,9 +370,9 @@
     wide_values = jnp.where(ghost, 0.0, wide_values)
     padded = with_halo(wide_values, (("gx", 1), ("gy", 2)), 1)
     padded = jnp.pad(padded, ((0, 0), (0, 0), (0, 0), (1, 1)))
-    moved = spread(padded, wide_table)
+    moved = spread_plane(padded, plane, wide_table)
     residual = contrast + slopes[0] * moved[0] + slopes[1] * moved[1] + slopes[2] * moved[2]
-    image_part = collect(masked_slopes * residual[None], wide_back, False)
+    image_part = collect_plane(masked_slopes * residual[None], plane_back, wide_back, ex, ey)
     force_total = image_part + elastic_weight * elastic_force(padded)
     tile_values = (wide_values - force_total / wide_curvature)[..., 1:-1]
     final_blocks = tile_values.reshape(3, blocks, block_nodes)

time: 124 us -> 125 us (level)
  the two profiles are of different devices: /device:TPU:1 before, /device:TPU:193 now
where the time goes in v8:
time: 125 us; the launch traced here: 124 us
  starting transfers between devices  63.9 us (51%)
  local copies, waits for them, and re-layouts  19 us (15%)
  other arithmetic  17.3 us (14%)
  waiting for transfers between devices  13.4 us (11%)
  matrix products  8.82 us (7%)
  between operations  1.67 us (1%)
    ppermute x6, starting transfers between devices, with_halo(): lax.ppermute(lax.slice_in_dim(block, block.shape[dim] - width, None, axis...  26.6 us
    all_to_all x1, starting transfers between devices, per_device(): lax.all_to_all(outgoing, ('gy', 'gz'), split_axis=1, concat_axis=1, tiled...  15.3 us
    ppermute x6, starting transfers between devices, with_halo(): lax.ppermute(lax.slice_in_dim(block, 0, width, axis=dim), axis, backward)  11.3 us
    all_to_all x1, starting transfers between devices, per_device(): lax.all_to_all(send_outgoing, ('gy', 'gz'), split_axis=1, concat_axis=1,...  10.8 us
    all_to_all x1, waiting for transfers between devices, per_device(): lax.all_to_all(outgoing, ('gy', 'gz'), split_axis=1, concat_axis=1, tiled...  10.4 us
    another operation x6, local copies, waits for them, and re-layouts, derive_fields(): return jnp.stack([contrast] + slopes)  4.78 us
    another operation x3, other arithmetic  3.26 us
    mul x2, local copies, waits for them, and re-layouts, per_device(): masked_slopes = slopes * region[None]  2.75 us
  transfers between devices with their start and end apart: 14, of which 5 were waited for; matrix products, arithmetic and copies ran while one was open for 10% of the time, Pallas kernels for 0%

profile of v8, /device:TPU:193, one launch (start us, length us, event | category | flops | bytes accessed | tf_op | source)
XLA Modules:
  0.0 124.1 jit_solution(2746707855983988782)
XLA Ops:
  0.0 0.7 broadcast_add_fusion.2
  0.7 1.2 and_and_fusion
  2.1 0.3 convert_reduce_fusion
  2.5 0.5 copy-done.28
  3.0 1.1 concatenate.67
  4.2 0.7 fusion.4
  4.8 0.4 copy.61
  5.2 0.4 all_to_all.12
  5.6 0.7 copy.62
  6.4 10.8 %all-to-all-start = ((f32[4,64,80]{2,0,1:T(4,128)}), f32[4,64,80]{2,0,1:T(4,128)S(1)}, u32[]{:S(2)}, u32[]{:S(2)}) async-start(f32[4,64,80]{2,0,1:T(4,128)} %copy.62), calls=%async_computation | async-start | bytes 262144 | tf_op jit(solution)/shard_map/all_to_all | solution.py:317
  17.3 1.3 %collective-permute-start.1 = (bf16[3,16,5,128]{3,2,1,0:T(8,128)(2,1)S(1)}, bf16[3,16,5,128]{3,2,1,0:T(8,128)(2,1)S(1)}, u32[]{:S(2)}, u32[]{:S(2)}) collective-permute-start(bf16[3,16,5,128]{3,2,1,0:T(8,128)(2,1)S(1)} %get-tuple-element.78), channel_id=1, source_target_pairs={{8,0},{16,8},{24,16},{32,24},{40,32},{48,40},{56,48},{9,1},{17,9},... | collective-permute-start | bytes 184328 | tf_op jit(solution)/shard_map/ppermute | solution.py:27
  18.6 4.0 %collective-permute-start = (bf16[3,16,5,128]{3,2,1,0:T(8,128)(2,1)S(1)}, bf16[3,16,5,128]{3,2,1,0:T(8,128)(2,1)S(1)}, u32[]{:S(2)}, u32[]{:S(2)}) collective-permute-start(bf16[3,16,5,128]{3,2,1,0:T(8,128)(2,1)S(1)} %get-tuple-element.77), channel_id=1, source_target_pairs={{0,8},{8,16},{16,24},{24,32},{32,40},{40,48},{48,56},{1,9},{9,17},... | collective-permute-start | bytes 184328 | tf_op jit(solution)/shard_map/ppermute | solution.py:24
  22.6 0.6 fusion.169
  23.4 0.7 reshape.574
  24.5 0.7 reshape.572
  25.2 0.6 iota_compare_fusion.7
  25.9 0.6 select_add_fusion
  26.5 0.5 and_or_fusion
  27.1 0.9 fusion.199
  28.1 2.9 %collective-permute-start.3 = (bf16[3,16,26,9]{3,2,1,0:T(8,128)(2,1)}, bf16[3,16,26,9]{3,2,1,0:T(8,128)(2,1)S(1)}, u32[]{:S(2)}, u32[]{:S(2)}) collective-permute-start(bf16[3,16,26,9]{3,2,1,0:T(8,128)(2,1)} %get-tuple-element.51), channel_id=1, source_target_pairs={{1,0},{2,1},{3,2},{4,3},{5,4},{6,5},{7,6},{9,8},{10,9},{11,10},{12... | collective-permute-start | bytes 67400 | tf_op jit(solution)/shard_map/ppermute | solution.py:27
  31.0 3.1 %collective-permute-start.2 = (bf16[3,16,26,9]{3,2,1,0:T(8,128)(2,1)S(1)}, bf16[3,16,26,9]{3,2,1,0:T(8,128)(2,1)S(1)}, u32[]{:S(2)}, u32[]{:S(2)}) collective-permute-start(bf16[3,16,26,9]{3,2,1,0:T(8,128)(2,1)S(1)} %get-tuple-element.50), channel_id=1, source_target_pairs={{0,1},{1,2},{2,3},{3,4},{4,5},{5,6},{6,7},{8,9},{9,10},{10,11},{11... | collective-permute-start | bytes 67400 | tf_op jit(solution)/shard_map/ppermute | solution.py:24
  34.1 0.4 reshape.554
  35.3 0.8 fusion.5
  36.1 0.3 copy.66
  37.2 1.9 %collective-permute-start.7 = (f32[3,1,6,36]{3,2,1,0:T(8,128)S(1)}, f32[3,1,6,36]{3,2,1,0:T(8,128)S(1)}, u32[]{:S(2)}, u32[]{:S(2)}) collective-permute-start(f32[3,1,6,36]{3,2,1,0:T(8,128)S(1)} %get-tuple-element.80), channel_id=1, source_target_pairs={{64,0},{128,64},{192,128},{256,192},{320,256},{384,320},{448,384},... | collective-permute-start | bytes 7784 | tf_op jit(solution)/shard_map/ppermute | solution.py:27
  39.1 5.2 %collective-permute-start.6 = (f32[3,1,6,36]{3,2,1,0:T(8,128)S(1)}, f32[3,1,6,36]{3,2,1,0:T(8,128)S(1)}, u32[]{:S(2)}, u32[]{:S(2)}) collective-permute-start(f32[3,1,6,36]{3,2,1,0:T(8,128)S(1)} %get-tuple-element.79), channel_id=1, source_target_pairs={{0,64},{64,128},{128,192},{192,256},{256,320},{320,384},{384,448},... | collective-permute-start | bytes 7784 | tf_op jit(solution)/shard_map/ppermute | solution.py:24
  44.4 0.5 pad_maximum_fusion.8
  44.8 1.9 %collective-permute-start.5 = (bf16[3,5,26,146]{3,2,1,0:T(8,128)(2,1)S(1)}, bf16[3,5,26,146]{3,2,1,0:T(8,128)(2,1)S(1)}, u32[]{:S(2)}, u32[]{:S(2)}) collective-permute-start(bf16[3,5,26,146]{3,2,1,0:T(8,128)(2,1)S(1)} %get-tuple-element.43), channel_id=1, source_target_pairs={{64,0},{128,64},{192,128},{256,192},{320,256},{384,320},{448,384},... | collective-permute-start | bytes 341648 | tf_op jit(solution)/shard_map/ppermute | solution.py:27
  46.8 4.8 %collective-permute-start.4 = (bf16[3,5,26,146]{3,2,1,0:T(8,128)(2,1)S(1)}, bf16[3,5,26,146]{3,2,1,0:T(8,128)(2,1)S(1)}, u32[]{:S(2)}, u32[]{:S(2)}) collective-permute-start(bf16[3,5,26,146]{3,2,1,0:T(8,128)(2,1)S(1)} %get-tuple-element.42), channel_id=1, source_target_pairs={{0,64},{64,128},{128,192},{192,256},{256,320},{320,384},{384,448},... | collective-permute-start | bytes 341648 | tf_op jit(solution)/shard_map/ppermute | solution.py:24
  53.1 0.9 convolution_bitcast_fusion.1
  54.2 0.7 fusion.147
  54.9 0.9 collective-permute-done.5
  55.8 1.0 collective-permute-done.4
  56.8 0.8 maximum_convert_fusion
  57.7 0.4 fusion.20
  58.0 0.6 fusion.31
  58.6 2.2 %add_multiply_fusion = (f32[22,22,142]{2,1,0:T(8,128)S(1)}, f32[22,22,142]{2,1,0:T(8,128)}, f32[22,22,142]{2,1,0:T(8,128)}) fusion(f32[22,22,146]{2,1,0:T(8,128)S(1)} %get-tuple-element.118, f32[22,22,146]{2,1,0:T(8,128)S(1)} %get-tuple-element.119), kind=kLoop, calls=%fused_computation.84 | loop fusion | flops 1374560 | bytes 3573856 | tf_op jit(solution)/shard_map/mul | solution.py:77
  61.1 1.0 fusion.196
  62.3 0.8 mul.818
  63.1 2.0 %copy.71 = f32[400,140]{0,1:T(8,128)} copy(f32[400,140]{1,0:T(8,128)} %mul.818) | data formatting | bytes 448000 | tf_op jit(solution)/shard_map/mul | solution.py:355
  65.1 0.8 fusion.45
  65.9 1.8 %stack.55 = bf16[1,400,140]{2,1,0:T(8,128)(2,1)} reshape(bf16[20,20,140]{2,1,0:T(8,128)(2,1)} %fusion.45) | data formatting | bytes 224000 | tf_op jit(solution)/shard_map/stack | solution.py:91
  67.7 1.7 %copy.70 = bf16[1,400,140]{1,2,0:T(8,128)(2,1)} copy(bf16[1,400,140]{2,1,0:T(8,128)(2,1)} %stack.55) | data formatting | bytes 224000 | tf_op jit(solution)/shard_map/stack | solution.py:91
  69.4 1.0 fusion.47
  70.4 1.0 stack.54
  71.5 1.4 %fusion.49 = bf16[20,20,140]{2,1,0:T(8,128)(2,1)S(1)} fusion(f32[20,22,142]{2,1,0:T(8,128)} %get-tuple-element.45, f32[20,22,142]{2,1,0:T(8,128)S(1)} %copy-done.2), kind=kLoop, calls=%fused_computation.95 | loop fusion | flops 168000 | bytes 560000 | tf_op jit(solution)/shard_map/convert.4
  73.2 0.3 fusion.63
  74.0 0.9 fusion.9
  74.9 0.5 convolution_add_fusion
  75.6 0.8 fusion.8
  76.5 0.5 fusion.202
  77.2 1.9 %collective-permute-start.9 = (f32[3,1,4,34]{3,2,1,0:T(4,128)S(1)}, f32[3,1,4,34]{3,2,1,0:T(4,128)S(1)}, u32[]{:S(2)}, u32[]{:S(2)}) collective-permute-start(f32[3,1,4,34]{3,2,1,0:T(4,128)S(1)} %get-tuple-element.90), channel_id=1, source_target_pairs={{64,0},{128,64},{192,128},{256,192},{320,256},{384,320},{448,384},... | collective-permute-start | bytes 4904 | tf_op jit(solution)/shard_map/ppermute | solution.py:27
  79.1 5.3 %collective-permute-start.8 = (f32[3,1,4,34]{3,2,1,0:T(4,128)S(1)}, f32[3,1,4,34]{3,2,1,0:T(4,128)S(1)}, u32[]{:S(2)}, u32[]{:S(2)}) collective-permute-start(f32[3,1,4,34]{3,2,1,0:T(4,128)S(1)} %get-tuple-element.89), channel_id=1, source_target_pairs={{0,64},{64,128},{128,192},{192,256},{256,320},{320,384},{384,448},... | collective-permute-start | bytes 4904 | tf_op jit(solution)/shard_map/ppermute | solution.py:24
  84.4 0.7 collective-permute-done.8
  85.2 1.3 %collective-permute-start.11 = (f32[3,6,1,34]{3,2,1,0:T(1,128)S(1)}, f32[3,6,1,34]{3,2,1,0:T(1,128)S(1)}, u32[]{:S(2)}, u32[]{:S(2)}) collective-permute-start(f32[3,6,1,34]{3,2,1,0:T(1,128)S(1)} %get-tuple-element.88), channel_id=1, source_target_pairs={{8,0},{16,8},{24,16},{32,24},{40,32},{48,40},{56,48},{9,1},{17,9},... | collective-permute-start | bytes 7352 | tf_op jit(solution)/shard_map/ppermute | solution.py:27
  86.5 4.2 %collective-permute-start.10 = (f32[3,6,1,34]{3,2,1,0:T(1,128)S(1)}, f32[3,6,1,34]{3,2,1,0:T(1,128)S(1)}, u32[]{:S(2)}, u32[]{:S(2)}) collective-permute-start(f32[3,6,1,34]{3,2,1,0:T(1,128)S(1)} %get-tuple-element.87), channel_id=1, source_target_pairs={{0,8},{8,16},{16,24},{24,32},{32,40},{40,48},{48,56},{1,9},{9,17},... | collective-permute-start | bytes 7352 | tf_op jit(solution)/shard_map/ppermute | solution.py:24
  91.7 0.9 convolution_bitcast_fusion
  92.9 0.8 fusion.10
  93.7 0.5 fusion.203
  95.9 0.7 copy.78
  96.7 15.3 %all-to-all-start.1 = ((f32[3,64,16]{2,0,1:T(4,128)}), f32[3,64,16]{2,0,1:T(4,128)S(1)}, u32[]{:S(2)}, u32[]{:S(2)}) async-start(f32[3,64,16]{2,0,1:T(4,128)} %copy.78), calls=%async_computation.1 | async-start | bytes 262144 | tf_op jit(solution)/shard_map/all_to_all | solution.py:387
  112.0 0.7 slice_add_fusion.52
  112.7 10.4 %all-to-all-done.1 = f32[3,64,16]{2,0,1:T(4,128)S(1)} async-done(((f32[3,64,16]{2,0,1:T(4,128)}), f32[3,64,16]{2,0,1:T(4,128)S(1)}, u32[]{:S(2)}, u32[]{:S(2)}) %all-to-all-start.1) | async-done | bytes 12320 | tf_op jit(solution)/shard_map/all_to_all | solution.py:387
  123.3 0.9 convolution_bitcast_fusion.2
  (222 shorter events, 8.4 us)
Async XLA Ops:
  0.0 17.2 %copy-start.17 = (s32[16,16,128]{2,1,0:T(8,128)S(1)}, s32[16,16,128]{2,1,0:T(8,128)}, u32[]{:S(2)}) copy-start(s32[16,16,128]{2,1,0:T(8,128)} %param.7) | copy-start | bytes 393220
  0.0 17.2 %copy-start.3 = (bf16[16,16,128]{2,1,0:T(8,128)(2,1)S(1)}, bf16[16,16,128]{2,1,0:T(8,128)(2,1)}, u32[]{:S(2)}) copy-start(bf16[16,16,128]{2,1,0:T(8,128)(2,1)} %param.6) | copy-start | bytes 196612
  0.0 17.2 %copy-start.4 = (bf16[16,16,128]{2,1,0:T(8,128)(2,1)S(1)}, bf16[16,16,128]{2,1,0:T(8,128)(2,1)}, u32[]{:S(2)}) copy-start(bf16[16,16,128]{2,1,0:T(8,128)(2,1)} %param.5) | copy-start | bytes 196612
  2.4 0.6 copy-start.28
  6.4 27.7 %all-to-all-start = ((f32[4,64,80]{2,0,1:T(4,128)}), f32[4,64,80]{2,0,1:T(4,128)S(1)}, u32[]{:S(2)}, u32[]{:S(2)}) async-start(f32[4,64,80]{2,0,1:T(4,128)} %copy.62), calls=%async_computation | async-start | bytes 262144 | tf_op jit(solution)/shard_map/all_to_all | solution.py:317
  17.3 9.7 %collective-permute-start.1 = (bf16[3,16,5,128]{3,2,1,0:T(8,128)(2,1)S(1)}, bf16[3,16,5,128]{3,2,1,0:T(8,128)(2,1)S(1)}, u32[]{:S(2)}, u32[]{:S(2)}) collective-permute-start(bf16[3,16,5,128]{3,2,1,0:T(8,128)(2,1)S(1)} %get-tuple-element.78), channel_id=1, source_target_pairs={{8,0},{16,8},{24,16},{32,24},{40,32},{48,40},{56,48},{9,1},{17,9},... | collective-permute-start | bytes 184328 | tf_op jit(solution)/shard_map/ppermute | solution.py:27
  18.6 8.4 %collective-permute-start = (bf16[3,16,5,128]{3,2,1,0:T(8,128)(2,1)S(1)}, bf16[3,16,5,128]{3,2,1,0:T(8,128)(2,1)S(1)}, u32[]{:S(2)}, u32[]{:S(2)}) collective-permute-start(bf16[3,16,5,128]{3,2,1,0:T(8,128)(2,1)S(1)} %get-tuple-element.77), channel_id=1, source_target_pairs={{0,8},{8,16},{16,24},{24,32},{32,40},{40,48},{48,56},{1,9},{9,17},... | collective-permute-start | bytes 184328 | tf_op jit(solution)/shard_map/ppermute | solution.py:24
  22.6 29.1 %copy-start.20 = (s32[140]{0:T(256)}, s32[140]{0:T(256)S(1)}, u32[]{:S(2)}) copy-start(s32[140]{0:T(256)S(1)} %broadcast_add_fusion) | copy-start | bytes 1684
  22.6 29.1 %copy-start.22 = (s32[140]{0:T(256)}, s32[140]{0:T(256)S(1)}, u32[]{:S(2)}) copy-start(s32[140]{0:T(256)S(1)} %and_select_fusion.3) | copy-start | bytes 1684
  23.3 28.5 %copy-start.24 = (f32[140]{0:T(256)}, f32[140]{0:T(256)S(1)}, u32[]{:S(2)}) copy-start(f32[140]{0:T(256)S(1)} %get-tuple-element.130) | copy-start | bytes 1684
  23.3 28.5 %copy-start.26 = (f32[140]{0:T(256)}, f32[140]{0:T(256)S(1)}, u32[]{:S(2)}) copy-start(f32[140]{0:T(256)S(1)} %get-tuple-element.131) | copy-start | bytes 1684
  24.4 28.7 %copy-start.11 = (f32[400,36,1]{0,1,2:T(8,128)}, f32[400,36,1]{0,1,2:T(8,128)S(1)}, u32[]{:S(2)}) copy-start(f32[400,36,1]{0,1,2:T(8,128)S(1)} %reshape.570) | copy-start | bytes 172804
  28.1 16.3 %collective-permute-start.3 = (bf16[3,16,26,9]{3,2,1,0:T(8,128)(2,1)}, bf16[3,16,26,9]{3,2,1,0:T(8,128)(2,1)S(1)}, u32[]{:S(2)}, u32[]{:S(2)}) collective-permute-start(bf16[3,16,26,9]{3,2,1,0:T(8,128)(2,1)} %get-tuple-element.51), channel_id=1, source_target_pairs={{1,0},{2,1},{3,2},{4,3},{5,4},{6,5},{7,6},{9,8},{10,9},{11,10},{12... | collective-permute-start | bytes 67400 | tf_op jit(solution)/shard_map/ppermute | solution.py:27
  31.0 13.3 %collective-permute-start.2 = (bf16[3,16,26,9]{3,2,1,0:T(8,128)(2,1)S(1)}, bf16[3,16,26,9]{3,2,1,0:T(8,128)(2,1)S(1)}, u32[]{:S(2)}, u32[]{:S(2)}) collective-permute-start(bf16[3,16,26,9]{3,2,1,0:T(8,128)(2,1)S(1)} %get-tuple-element.50), channel_id=1, source_target_pairs={{0,1},{1,2},{2,3},{3,4},{4,5},{5,6},{6,7},{8,9},{9,10},{10,11},{11... | collective-permute-start | bytes 67400 | tf_op jit(solution)/shard_map/ppermute | solution.py:24
  34.7 1.8 %copy-start.29 = (f32[640]{0:T(1024)}, f32[640]{0:T(1024)S(1)}, u32[]{:S(2)}) copy-start(f32[640]{0:T(1024)S(1)} %slice_reduce_fusion) | copy-start | bytes 7684
  36.8 15.7 %copy-start.5 = (f32[3,4,4,32]{3,2,1,0:T(4,128)}, f32[3,4,4,32]{3,2,1,0:T(4,128)S(1)}, u32[]{:S(2)}) copy-start(f32[3,4,4,32]{3,2,1,0:T(4,128)S(1)} %get-tuple-element.70) | copy-start | bytes 18436
  36.8 15.7 %copy-start.7 = (f32[3,4,4,32]{3,2,1,0:T(4,128)}, f32[3,4,4,32]{3,2,1,0:T(4,128)S(1)}, u32[]{:S(2)}) copy-start(f32[3,4,4,32]{3,2,1,0:T(4,128)S(1)} %get-tuple-element.71) | copy-start | bytes 18436
  36.8 15.7 %copy-start.9 = (f32[3,4,4,2]{3,2,1,0:T(4,128)}, f32[3,4,4,2]{3,2,1,0:T(4,128)S(1)}, u32[]{:S(2)}) copy-start(f32[3,4,4,2]{3,2,1,0:T(4,128)S(1)} %slice.1023) | copy-start | bytes 1156
  37.2 14.3 %collective-permute-start.7 = (f32[3,1,6,36]{3,2,1,0:T(8,128)S(1)}, f32[3,1,6,36]{3,2,1,0:T(8,128)S(1)}, u32[]{:S(2)}, u32[]{:S(2)}) collective-permute-start(f32[3,1,6,36]{3,2,1,0:T(8,128)S(1)} %get-tuple-element.80), channel_id=1, source_target_pairs={{64,0},{128,64},{192,128},{256,192},{320,256},{384,320},{448,384},... | collective-permute-start | bytes 7784 | tf_op jit(solution)/shard_map/ppermute | solution.py:27
  39.1 12.4 %collective-permute-start.6 = (f32[3,1,6,36]{3,2,1,0:T(8,128)S(1)}, f32[3,1,6,36]{3,2,1,0:T(8,128)S(1)}, u32[]{:S(2)}, u32[]{:S(2)}) collective-permute-start(f32[3,1,6,36]{3,2,1,0:T(8,128)S(1)} %get-tuple-element.79), channel_id=1, source_target_pairs={{0,64},{64,128},{128,192},{192,256},{256,320},{320,384},{384,448},... | collective-permute-start | bytes 7784 | tf_op jit(solution)/shard_map/ppermute | solution.py:24
  44.8 11.0 %collective-permute-start.5 = (bf16[3,5,26,146]{3,2,1,0:T(8,128)(2,1)S(1)}, bf16[3,5,26,146]{3,2,1,0:T(8,128)(2,1)S(1)}, u32[]{:S(2)}, u32[]{:S(2)}) collective-permute-start(bf16[3,5,26,146]{3,2,1,0:T(8,128)(2,1)S(1)} %get-tuple-element.43), channel_id=1, source_target_pairs={{64,0},{128,64},{192,128},{256,192},{320,256},{384,320},{448,384},... | collective-permute-start | bytes 341648 | tf_op jit(solution)/shard_map/ppermute | solution.py:27
  46.8 10.1 %collective-permute-start.4 = (bf16[3,5,26,146]{3,2,1,0:T(8,128)(2,1)S(1)}, bf16[3,5,26,146]{3,2,1,0:T(8,128)(2,1)S(1)}, u32[]{:S(2)}, u32[]{:S(2)}) collective-permute-start(bf16[3,5,26,146]{3,2,1,0:T(8,128)(2,1)S(1)} %get-tuple-element.42), channel_id=1, source_target_pairs={{0,64},{64,128},{128,192},{192,256},{256,320},{320,384},{384,448},... | collective-permute-start | bytes 341648 | tf_op jit(solution)/shard_map/ppermute | solution.py:24
  63.1 8.4 %copy-start.2 = (f32[20,22,142]{2,1,0:T(8,128)S(1)}, f32[20,22,142]{2,1,0:T(8,128)}, u32[]{:S(2)}) copy-start(f32[20,22,142]{2,1,0:T(8,128)} %get-tuple-element.44) | copy-start | bytes 749764
  65.9 7.3 %copy-start = (f32[22,22,142]{2,1,0:T(8,128)S(1)}, f32[22,22,142]{2,1,0:T(8,128)}, u32[]{:S(2)}) copy-start(f32[22,22,142]{2,1,0:T(8,128)} %get-tuple-element.30) | copy-start | bytes 824740
  65.9 7.3 %copy-start.1 = (f32[22,22,142]{2,1,0:T(8,128)S(1)}, f32[22,22,142]{2,1,0:T(8,128)}, u32[]{:S(2)}) copy-start(f32[22,22,142]{2,1,0:T(8,128)} %get-tuple-element.31) | copy-start | bytes 824740
  71.5 2.3 %copy-start.13 = (bf16[1,400,140]{1,2,0:T(8,128)(2,1)S(1)}, bf16[1,400,140]{1,2,0:T(8,128)(2,1)}, u32[]{:S(2)}) copy-start(bf16[1,400,140]{1,2,0:T(8,128)(2,1)} %copy.70) | copy-start | bytes 336004
  73.0 1.0 copy-start.15
  73.0 1.0 copy-start.31
  73.0 0.9 copy-start.32
  73.0 0.9 copy-start.33
  73.0 0.9 copy-start.34
  73.6 1.3 %copy-start.16 = (f32[16,400,1]{1,0,2:T(8,128)S(1)}, f32[16,400,1]{1,0,2:T(8,128)}, u32[]{:S(2)}) copy-start(f32[16,400,1]{1,0,2:T(8,128)} %reshape.574) | copy-start | bytes 76804
  73.8 1.8 %copy-start.18 = (f32[36,140]{1,0:T(8,128)S(1)}, f32[36,140]{1,0:T(8,128)}, u32[]{:S(2)}) copy-start(f32[36,140]{1,0:T(8,128)} %select_add_fusion) | copy-start | bytes 60484
  73.9 2.6 %copy-start.14 = (f32[16,400,1]{1,0,2:T(8,128)S(1)}, f32[16,400,1]{1,0,2:T(8,128)}, u32[]{:S(2)}) copy-start(f32[16,400,1]{1,0,2:T(8,128)} %reshape.572) | copy-start | bytes 76804
  74.8 2.1 %copy-start.6 = (f32[3,4,4,32]{3,2,1,0:T(4,128)S(1)}, f32[3,4,4,32]{3,2,1,0:T(4,128)}, u32[]{:S(2)}) copy-start(f32[3,4,4,32]{3,2,1,0:T(4,128)} %copy-done.5) | copy-start | bytes 18436
  74.8 2.1 %copy-start.8 = (f32[3,4,4,32]{3,2,1,0:T(4,128)S(1)}, f32[3,4,4,32]{3,2,1,0:T(4,128)}, u32[]{:S(2)}) copy-start(f32[3,4,4,32]{3,2,1,0:T(4,128)} %copy-done.7) | copy-start | bytes 18436
  74.9 2.1 %copy-start.10 = (f32[3,4,4,2]{3,2,1,0:T(4,128)S(1)}, f32[3,4,4,2]{3,2,1,0:T(4,128)}, u32[]{:S(2)}) copy-start(f32[3,4,4,2]{3,2,1,0:T(4,128)} %copy-done.9) | copy-start | bytes 1156
  74.9 2.1 %copy-start.19 = (f32[1,4,4,34]{3,2,1,0:T(4,128)S(1)}, f32[1,4,4,34]{3,2,1,0:T(4,128)}, u32[]{:S(2)}) copy-start(f32[1,4,4,34]{3,2,1,0:T(4,128)} %fusion.147) | copy-start | bytes 6532
  74.9 2.1 %copy-start.35 = (pred[34]{0:T(512)(128)(4,1)S(1)}, pred[34]{0:T(512)(128)(4,1)}, u32[]{:S(2)}) copy-start(pred[34]{0:T(512)(128)(4,1)} %and_or_fusion) | copy-start | bytes 106
  74.9 15.8 %copy-start.30 = (f32[640]{0:T(1024)S(1)}, f32[640]{0:T(1024)}, u32[]{:S(2)}) copy-start(f32[640]{0:T(1024)} %copy-done.29) | copy-start | bytes 7684
  75.4 16.1 %copy-start.21 = (s32[140]{0:T(256)S(1)}, s32[140]{0:T(256)}, u32[]{:S(2)}) copy-start(s32[140]{0:T(256)} %copy-done.20) | copy-start | bytes 1684
  75.4 16.1 %copy-start.23 = (s32[140]{0:T(256)S(1)}, s32[140]{0:T(256)}, u32[]{:S(2)}) copy-start(s32[140]{0:T(256)} %copy-done.22) | copy-start | bytes 1684
  75.4 16.1 %copy-start.25 = (f32[140]{0:T(256)S(1)}, f32[140]{0:T(256)}, u32[]{:S(2)}) copy-start(f32[140]{0:T(256)} %copy-done.24) | copy-start | bytes 1684
  75.4 16.1 %copy-start.27 = (f32[140]{0:T(256)S(1)}, f32[140]{0:T(256)}, u32[]{:S(2)}) copy-start(f32[140]{0:T(256)} %copy-done.26) | copy-start | bytes 1684
  75.4 16.3 %copy-start.12 = (f32[400,36,1]{0,1,2:T(8,128)S(1)}, f32[400,36,1]{0,1,2:T(8,128)}, u32[]{:S(2)}) copy-start(f32[400,36,1]{0,1,2:T(8,128)} %copy-done.11) | copy-start | bytes 172804
  77.2 7.3 %collective-permute-start.9 = (f32[3,1,4,34]{3,2,1,0:T(4,128)S(1)}, f32[3,1,4,34]{3,2,1,0:T(4,128)S(1)}, u32[]{:S(2)}, u32[]{:S(2)}) collective-permute-start(f32[3,1,4,34]{3,2,1,0:T(4,128)S(1)} %get-tuple-element.90), channel_id=1, source_target_pairs={{64,0},{128,64},{192,128},{256,192},{320,256},{384,320},{448,384},... | collective-permute-start | bytes 4904 | tf_op jit(solution)/shard_map/ppermute | solution.py:27
  79.1 6.1 %collective-permute-start.8 = (f32[3,1,4,34]{3,2,1,0:T(4,128)S(1)}, f32[3,1,4,34]{3,2,1,0:T(4,128)S(1)}, u32[]{:S(2)}, u32[]{:S(2)}) collective-permute-start(f32[3,1,4,34]{3,2,1,0:T(4,128)S(1)} %get-tuple-element.89), channel_id=1, source_target_pairs={{0,64},{64,128},{128,192},{192,256},{256,320},{320,384},{384,448},... | collective-permute-start | bytes 4904 | tf_op jit(solution)/shard_map/ppermute | solution.py:24
  85.2 5.8 %collective-permute-start.11 = (f32[3,6,1,34]{3,2,1,0:T(1,128)S(1)}, f32[3,6,1,34]{3,2,1,0:T(1,128)S(1)}, u32[]{:S(2)}, u32[]{:S(2)}) collective-permute-start(f32[3,6,1,34]{3,2,1,0:T(1,128)S(1)} %get-tuple-element.88), channel_id=1, source_target_pairs={{8,0},{16,8},{24,16},{32,24},{40,32},{48,40},{56,48},{9,1},{17,9},... | collective-permute-start | bytes 7352 | tf_op jit(solution)/shard_map/ppermute | solution.py:27
  86.5 4.8 %collective-permute-start.10 = (f32[3,6,1,34]{3,2,1,0:T(1,128)S(1)}, f32[3,6,1,34]{3,2,1,0:T(1,128)S(1)}, u32[]{:S(2)}, u32[]{:S(2)}) collective-permute-start(f32[3,6,1,34]{3,2,1,0:T(1,128)S(1)} %get-tuple-element.87), channel_id=1, source_target_pairs={{0,8},{8,16},{16,24},{24,32},{32,40},{40,48},{48,56},{1,9},{9,17},... | collective-permute-start | bytes 7352 | tf_op jit(solution)/shard_map/ppermute | solution.py:24
  93.7 18.2 %copy-start.36 = (s32[64]{0:T(128)S(1)}, s32[64]{0:T(128)}, u32[]{:S(2)}) copy-start(s32[64]{0:T(128)} %get-tuple-element.39) | copy-start | bytes 772
  96.7 26.4 %all-to-all-start.1 = ((f32[3,64,16]{2,0,1:T(4,128)}), f32[3,64,16]{2,0,1:T(4,128)S(1)}, u32[]{:S(2)}, u32[]{:S(2)}) async-start(f32[3,64,16]{2,0,1:T(4,128)} %copy.78), calls=%async_computation.1 | async-start | bytes 262144 | tf_op jit(solution)/shard_map/all_to_all | solution.py:387

commit v9 on v8

--- a/solution.py
+++ b/solution.py
@@ -230,16 +230,25 @@
 
 def spread_plane(padded, plane, line):
     channels, nx, ny, nz = padded.shape
-    along = jnp.einsum(
-        "cij,jz->ciz", padded.reshape(channels, nx * ny, nz), line, precision=highest
-    )
-    return jnp.einsum("vi,ciz->cvz", plane, along, precision=highest)
-
-
-def collect_plane(volume, plane_back, line_back, nodes_x, nodes_y):
-    along = jnp.einsum("cvz,zk->cvk", volume, line_back, precision=highest)
-    summed = jnp.einsum("av,cvk->cak", plane_back, along, precision=highest)
-    return summed.reshape(volume.shape[0], nodes_x, nodes_y, line_back.shape[1])
+    return [
+        jnp.dot(
+            plane,
+            jnp.dot(padded[c].reshape(nx * ny, nz), line, precision=highest),
+            precision=highest,
+        )
+        for c in range(channels)
+    ]
+
+
+def collect_plane(volumes, plane_back, line_back, nodes_x, nodes_y):
+    return jnp.stack(
+        [
+            jnp.dot(
+                plane_back, jnp.dot(volume, line_back, precision=highest), precision=highest
+            ).reshape(nodes_x, nodes_y, line_back.shape[1])
+            for volume in volumes
+        ]
+    )
 
 
 NEIGHBOURS = [(0, 0)] + [(ry, rz) for ry in (-1, 0, 1) for rz in (-1, 0, 1) if (ry, rz) != (0, 0)]
@@ -356,11 +365,16 @@
     plane, plane_back = plane_tables(ex + 2, ey + 2, False)
     _, plane_square = plane_tables(ex + 2, ey + 2, True)
     wide_curvature = (
-        collect_plane(masked_slopes * slopes, plane_square, wide_square, ex, ey) + diagonal_shift
+        collect_plane(
+            [masked_slopes[c] * slopes[c] for c in range(3)], plane_square, wide_square, ex, ey
+        )
+        + diagonal_shift
     )
     moved = spread_plane(first_padded, plane, wide_table)
     residual = contrast + slopes[0] * moved[0] + slopes[1] * moved[1] + slopes[2] * moved[2]
-    image_part = collect_plane(masked_slopes * residual[None], plane_back, wide_back, ex, ey)
+    image_part = collect_plane(
+        [masked_slopes[c] * residual for c in range(3)], plane_back, wide_back, ex, ey
+    )
     force_total = image_part + elastic_weight * elastic_force(first_padded)
     wide_values = first_padded[:, 1:-1, 1:-1, 1:-1] - force_total / wide_curvature
     column = jnp.arange(ez + 2, dtype=jnp.int32)
@@ -372,7 +386,9 @@
     padded = jnp.pad(padded, ((0, 0), (0, 0), (0, 0), (1, 1)))
     moved = spread_plane(padded, plane, wide_table)
     residual = contrast + slopes[0] * moved[0] + slopes[1] * moved[1] + slopes[2] * moved[2]
-    image_part = collect_plane(masked_slopes * residual[None], plane_back, wide_back, ex, ey)
+    image_part = collect_plane(
+        [masked_slopes[c] * residual for c in range(3)], plane_back, wide_back, ex, ey
+    )
     force_total = image_part + elastic_weight * elastic_force(padded)
     tile_values = (wide_values - force_total / wide_curvature)[..., 1:-1]
     final_blocks = tile_values.reshape(3, blocks, block_nodes)

time: 125 us -> 136 us (1.088)
  the two profiles are of different devices: /device:TPU:193 before, /device:TPU:1 now
where the time goes in v9:
time: 136 us; the launch traced here: 135 us
  starting transfers between devices  60.1 us (44%)
  waiting for transfers between devices  19.9 us (15%)
  other arithmetic  19.2 us (14%)
  local copies, waits for them, and re-layouts  18.7 us (14%)
  matrix products  15 us (11%)
  between operations  1.79 us (1%)
    ppermute x6, starting transfers between devices, with_halo(): lax.ppermute(lax.slice_in_dim(block, block.shape[dim] - width, None, axis...  25.1 us
    all_to_all x1, starting transfers between devices, per_device(): lax.all_to_all(send_outgoing, ('gy', 'gz'), split_axis=1, concat_axis=1,...  13.3 us
    all_to_all x1, starting transfers between devices, per_device(): lax.all_to_all(outgoing, ('gy', 'gz'), split_axis=1, concat_axis=1, tiled...  12.8 us
    all_to_all x1, waiting for transfers between devices, per_device(): lax.all_to_all(outgoing, ('gy', 'gz'), split_axis=1, concat_axis=1, tiled...  10.4 us
    ppermute x6, waiting for transfers between devices, with_halo(): lax.ppermute(lax.slice_in_dim(block, 0, width, axis=dim), axis, backward)  9.43 us
    ppermute x6, starting transfers between devices, with_halo(): lax.ppermute(lax.slice_in_dim(block, 0, width, axis=dim), axis, backward)  8.78 us
    dot_general x9, matrix products, collect_plane(): jnp.dot(volume, line_back, precision=highest)  4.14 us
    another operation x6, local copies, waits for them, and re-layouts, derive_fields(): return jnp.stack([contrast] + slopes)  4.03 us
  transfers between devices with their start and end apart: 14, of which 4 were waited for; matrix products, arithmetic and copies ran while one was open for 16% of the time, Pallas kernels for 0%

profile of v9, /device:TPU:1, one launch (start us, length us, event | category | flops | bytes accessed | tf_op | source)
XLA Modules:
  0.0 134.6 jit_solution(14627536669345936901)
XLA Ops:
  0.0 0.9 convert_bitcast_fusion
  0.9 0.9 pad_maximum_fusion.8
  1.9 4.0 %collective-permute-start = (bf16[3,16,5,128]{3,2,1,0:T(8,128)(2,1)S(1)}, bf16[3,16,5,128]{3,2,1,0:T(8,128)(2,1)S(1)}, u32[]{:S(2)}, u32[]{:S(2)}) collective-permute-start(bf16[3,16,5,128]{3,2,1,0:T(8,128)(2,1)S(1)} %get-tuple-element.77), channel_id=1, source_target_pairs={{0,8},{8,16},{16,24},{24,32},{32,40},{40,48},{48,56},{1,9},{9,17},... | collective-permute-start | bytes 184328 | tf_op jit(solution)/shard_map/ppermute | solution.py:24
  5.9 1.3 collective-permute-start.1
  7.2 0.7 broadcast_add_fusion.2
  7.9 1.2 and_and_fusion
  9.7 1.1 concatenate.67
  10.8 0.7 fusion.10
  11.5 0.4 copy.80
  12.3 0.7 copy.81
  13.1 13.3 %all-to-all-start = ((f32[4,64,80]{2,0,1:T(4,128)}), f32[4,64,80]{2,0,1:T(4,128)S(1)}, u32[]{:S(2)}, u32[]{:S(2)}) async-start(f32[4,64,80]{2,0,1:T(4,128)} %copy.81), calls=%async_computation | async-start | bytes 262144 | tf_op jit(solution)/shard_map/all_to_all | solution.py:326
  26.5 0.6 fusion.206
  27.2 0.7 mul.943
  27.9 0.7 mul.940
  28.7 0.7 mul.1075
  29.4 0.7 mul.1072
  30.4 0.6 iota_compare_fusion.7
  31.0 0.5 and_or_fusion
  31.8 0.9 fusion.241
  32.7 3.5 %collective-permute-start.2 = (bf16[3,16,26,9]{3,2,1,0:T(8,128)(2,1)}, bf16[3,16,26,9]{3,2,1,0:T(8,128)(2,1)S(1)}, u32[]{:S(2)}, u32[]{:S(2)}) collective-permute-start(bf16[3,16,26,9]{3,2,1,0:T(8,128)(2,1)} %get-tuple-element.50), channel_id=1, source_target_pairs={{0,1},{1,2},{2,3},{3,4},{4,5},{5,6},{6,7},{8,9},{9,10},{10,11},{11... | collective-permute-start | bytes 67400 | tf_op jit(solution)/shard_map/ppermute | solution.py:24
  36.3 1.9 %collective-permute-start.3 = (bf16[3,16,26,9]{3,2,1,0:T(8,128)(2,1)S(1)}, bf16[3,16,26,9]{3,2,1,0:T(8,128)(2,1)S(1)}, u32[]{:S(2)}, u32[]{:S(2)}) collective-permute-start(bf16[3,16,26,9]{3,2,1,0:T(8,128)(2,1)S(1)} %get-tuple-element.51), channel_id=1, source_target_pairs={{1,0},{2,1},{3,2},{4,3},{5,4},{6,5},{7,6},{9,8},{10,9},{11,10},{12... | collective-permute-start | bytes 67400 | tf_op jit(solution)/shard_map/ppermute | solution.py:27
  39.4 0.8 fusion.11
  41.3 4.0 %collective-permute-start.6 = (f32[3,1,6,36]{3,2,1,0:T(8,128)S(1)}, f32[3,1,6,36]{3,2,1,0:T(8,128)S(1)}, u32[]{:S(2)}, u32[]{:S(2)}) collective-permute-start(f32[3,1,6,36]{3,2,1,0:T(8,128)S(1)} %get-tuple-element.79), channel_id=1, source_target_pairs={{0,64},{64,128},{128,192},{192,256},{256,320},{320,384},{384,448},... | collective-permute-start | bytes 7784 | tf_op jit(solution)/shard_map/ppermute | solution.py:24
  45.3 1.3 collective-permute-start.7
  46.6 0.5 pad_maximum_fusion.7
  47.1 4.6 %collective-permute-start.4 = (bf16[3,5,26,146]{3,2,1,0:T(8,128)(2,1)S(1)}, bf16[3,5,26,146]{3,2,1,0:T(8,128)(2,1)S(1)}, u32[]{:S(2)}, u32[]{:S(2)}) collective-permute-start(bf16[3,5,26,146]{3,2,1,0:T(8,128)(2,1)S(1)} %get-tuple-element.42), channel_id=1, source_target_pairs={{0,64},{64,128},{128,192},{192,256},{256,320},{320,384},{384,448},... | collective-permute-start | bytes 341648 | tf_op jit(solution)/shard_map/ppermute | solution.py:24
  51.7 1.5 %collective-permute-start.5 = (bf16[3,5,26,146]{3,2,1,0:T(8,128)(2,1)S(1)}, bf16[3,5,26,146]{3,2,1,0:T(8,128)(2,1)S(1)}, u32[]{:S(2)}, u32[]{:S(2)}) collective-permute-start(bf16[3,5,26,146]{3,2,1,0:T(8,128)(2,1)S(1)} %get-tuple-element.43), channel_id=1, source_target_pairs={{64,0},{128,64},{192,128},{256,192},{320,256},{384,320},{448,384},... | collective-permute-start | bytes 341648 | tf_op jit(solution)/shard_map/ppermute | solution.py:27
  53.7 0.8 fusion.148
  54.5 0.8 fusion.149
  55.3 0.8 fusion.150
  56.9 0.7 fusion.184
  57.6 0.7 fusion.178
  58.3 0.7 fusion.172
  59.0 2.9 %collective-permute-done.5 = bf16[3,5,26,146]{3,2,1,0:T(8,128)(2,1)S(1)} collective-permute-done((bf16[3,5,26,146]{3,2,1,0:T(8,128)(2,1)S(1)}, bf16[3,5,26,146]{3,2,1,0:T(8,128)(2,1)S(1)}, u32[]{:S(2)}, u32[]{:S(2)}) %collective-permute-start.5) | collective-permute-done | bytes 113912 | tf_op jit(solution)/shard_map/ppermute | solution.py:27
  61.8 0.7 maximum_convert_fusion
  63.0 0.6 fusion.31
  63.6 2.0 %add_multiply_fusion = (f32[22,22,142]{2,1,0:T(8,128)S(1)}, f32[22,22,142]{2,1,0:T(8,128)S(1)}, f32[22,22,142]{2,1,0:T(8,128)}) fusion(f32[22,22,146]{2,1,0:T(8,128)S(1)} %get-tuple-element.126, f32[22,22,146]{2,1,0:T(8,128)S(1)} %get-tuple-element.127), kind=kLoop, calls=%fused_computation.102 | loop fusion | flops 1374560 | bytes 3573856 | tf_op jit(solution)/shard_map/mul | solution.py:77
  65.6 1.0 fusion.238
  67.2 0.8 mul.986
  68.0 1.2 copy.92
  69.1 2.3 %fusion.49 = bf16[20,20,140]{2,1,0:T(8,128)(2,1)} fusion(f32[20,22,142]{2,1,0:T(8,128)} %get-tuple-element.45, f32[20,22,142]{2,1,0:T(8,128)} %get-tuple-element.44), kind=kLoop, calls=%fused_computation.113 | loop fusion | flops 168000 | bytes 560000 | tf_op jit(solution)/shard_map/convert.4
  71.4 1.7 %stack.62 = bf16[1,400,140]{2,1,0:T(8,128)(2,1)} reshape(bf16[20,20,140]{2,1,0:T(8,128)(2,1)} %fusion.49) | data formatting | bytes 224000 | tf_op jit(solution)/shard_map/stack | solution.py:91
  73.1 1.0 copy.89
  74.1 1.0 fusion.47
  75.2 1.0 stack.63
  77.0 1.0 convolution_bitcast_fusion.4
  78.0 1.0 convolution_bitcast_fusion.5
  79.9 0.4 fusion.9
  80.4 1.2 fusion.8
  81.8 0.5 fusion.7
  84.8 5.2 %collective-permute-start.8 = (f32[3,1,4,34]{3,2,1,0:T(4,128)S(1)}, f32[3,1,4,34]{3,2,1,0:T(4,128)S(1)}, u32[]{:S(2)}, u32[]{:S(2)}) collective-permute-start(f32[3,1,4,34]{3,2,1,0:T(4,128)S(1)} %get-tuple-element.95), channel_id=1, source_target_pairs={{0,64},{64,128},{128,192},{192,256},{256,320},{320,384},{384,448},... | collective-permute-start | bytes 4904 | tf_op jit(solution)/shard_map/ppermute | solution.py:24
  90.0 1.3 collective-permute-start.9
  91.3 4.0 %collective-permute-done.9 = f32[3,1,4,34]{3,2,1,0:T(4,128)S(1)} collective-permute-done((f32[3,1,4,34]{3,2,1,0:T(4,128)S(1)}, f32[3,1,4,34]{3,2,1,0:T(4,128)S(1)}, u32[]{:S(2)}, u32[]{:S(2)}) %collective-permute-start.9) | collective-permute-done | bytes 1664 | tf_op jit(solution)/shard_map/ppermute | solution.py:27
  95.3 3.7 %collective-permute-start.10 = (f32[3,6,1,34]{3,2,1,0:T(1,128)S(1)}, f32[3,6,1,34]{3,2,1,0:T(1,128)S(1)}, u32[]{:S(2)}, u32[]{:S(2)}) collective-permute-start(f32[3,6,1,34]{3,2,1,0:T(1,128)S(1)} %get-tuple-element.93), channel_id=1, source_target_pairs={{0,8},{8,16},{16,24},{24,32},{32,40},{40,48},{48,56},{1,9},{9,17},... | collective-permute-start | bytes 7352 | tf_op jit(solution)/shard_map/ppermute | solution.py:24
  99.0 1.5 %collective-permute-start.11 = (f32[3,6,1,34]{3,2,1,0:T(1,128)S(1)}, f32[3,6,1,34]{3,2,1,0:T(1,128)S(1)}, u32[]{:S(2)}, u32[]{:S(2)}) collective-permute-start(f32[3,6,1,34]{3,2,1,0:T(1,128)S(1)} %get-tuple-element.94), channel_id=1, source_target_pairs={{8,0},{16,8},{24,16},{32,24},{40,32},{48,40},{56,48},{9,1},{17,9},... | collective-permute-start | bytes 7352 | tf_op jit(solution)/shard_map/ppermute | solution.py:27
  100.8 2.6 %collective-permute-done.11 = f32[3,6,1,34]{3,2,1,0:T(1,128)S(1)} collective-permute-done((f32[3,6,1,34]{3,2,1,0:T(1,128)S(1)}, f32[3,6,1,34]{3,2,1,0:T(1,128)S(1)}, u32[]{:S(2)}, u32[]{:S(2)}) %collective-permute-start.11) | collective-permute-done | bytes 2480 | tf_op jit(solution)/shard_map/ppermute | solution.py:27
  104.2 0.5 fusion.6
  104.6 0.5 fusion.5
  105.1 0.5 fusion.4
  108.9 0.7 copy.103
  109.6 12.8 %all-to-all-start.1 = ((f32[3,64,16]{2,0,1:T(4,128)}), f32[3,64,16]{2,0,1:T(4,128)S(1)}, u32[]{:S(2)}, u32[]{:S(2)}) async-start(f32[3,64,16]{2,0,1:T(4,128)} %copy.103), calls=%async_computation.1 | async-start | bytes 262144 | tf_op jit(solution)/shard_map/all_to_all | solution.py:403
  122.5 0.7 slice_add_fusion.51
  123.2 10.4 %all-to-all-done.1 = f32[3,64,16]{2,0,1:T(4,128)S(1)} async-done(((f32[3,64,16]{2,0,1:T(4,128)}), f32[3,64,16]{2,0,1:T(4,128)S(1)}, u32[]{:S(2)}, u32[]{:S(2)}) %all-to-all-start.1) | async-done | bytes 12320 | tf_op jit(solution)/shard_map/all_to_all | solution.py:403
  133.8 0.9 convolution_bitcast_fusion.9
  (247 shorter events, 14.1 us)
Async XLA Ops:
  1.9 29.7 %collective-permute-start = (bf16[3,16,5,128]{3,2,1,0:T(8,128)(2,1)S(1)}, bf16[3,16,5,128]{3,2,1,0:T(8,128)(2,1)S(1)}, u32[]{:S(2)}, u32[]{:S(2)}) collective-permute-start(bf16[3,16,5,128]{3,2,1,0:T(8,128)(2,1)S(1)} %get-tuple-element.77), channel_id=1, source_target_pairs={{0,8},{8,16},{16,24},{24,32},{32,40},{40,48},{48,56},{1,9},{9,17},... | collective-permute-start | bytes 184328 | tf_op jit(solution)/shard_map/ppermute | solution.py:24
  5.9 25.7 %collective-permute-start.1 = (bf16[3,16,5,128]{3,2,1,0:T(8,128)(2,1)S(1)}, bf16[3,16,5,128]{3,2,1,0:T(8,128)(2,1)S(1)}, u32[]{:S(2)}, u32[]{:S(2)}) collective-permute-start(bf16[3,16,5,128]{3,2,1,0:T(8,128)(2,1)S(1)} %get-tuple-element.78), channel_id=1, source_target_pairs={{8,0},{16,8},{24,16},{32,24},{40,32},{48,40},{56,48},{9,1},{17,9},... | collective-permute-start | bytes 184328 | tf_op jit(solution)/shard_map/ppermute | solution.py:27
  9.7 1.2 copy-start.22
  11.5 20.1 %copy-start.1 = (bf16[16,16,128]{2,1,0:T(8,128)(2,1)S(1)}, bf16[16,16,128]{2,1,0:T(8,128)(2,1)}, u32[]{:S(2)}) copy-start(bf16[16,16,128]{2,1,0:T(8,128)(2,1)} %param.6) | copy-start | bytes 196612
  11.5 20.1 %copy-start.2 = (bf16[16,16,128]{2,1,0:T(8,128)(2,1)S(1)}, bf16[16,16,128]{2,1,0:T(8,128)(2,1)}, u32[]{:S(2)}) copy-start(bf16[16,16,128]{2,1,0:T(8,128)(2,1)} %param.5) | copy-start | bytes 196612
  13.1 25.1 %all-to-all-start = ((f32[4,64,80]{2,0,1:T(4,128)}), f32[4,64,80]{2,0,1:T(4,128)S(1)}, u32[]{:S(2)}, u32[]{:S(2)}) async-start(f32[4,64,80]{2,0,1:T(4,128)} %copy.81), calls=%async_computation | async-start | bytes 262144 | tf_op jit(solution)/shard_map/all_to_all | solution.py:326
  26.4 28.9 %copy-start.25 = (s32[140]{0:T(256)}, s32[140]{0:T(256)S(1)}, u32[]{:S(2)}) copy-start(s32[140]{0:T(256)S(1)} %broadcast_add_fusion) | copy-start | bytes 1684
  26.4 28.9 %copy-start.27 = (s32[140]{0:T(256)}, s32[140]{0:T(256)S(1)}, u32[]{:S(2)}) copy-start(s32[140]{0:T(256)S(1)} %and_select_fusion.1) | copy-start | bytes 1684
  27.1 28.2 %copy-start.29 = (f32[140]{0:T(256)}, f32[140]{0:T(256)S(1)}, u32[]{:S(2)}) copy-start(f32[140]{0:T(256)S(1)} %get-tuple-element.140) | copy-start | bytes 1684
  27.1 28.2 %copy-start.31 = (f32[140]{0:T(256)}, f32[140]{0:T(256)S(1)}, u32[]{:S(2)}) copy-start(f32[140]{0:T(256)S(1)} %get-tuple-element.141) | copy-start | bytes 1684
  32.7 13.8 %collective-permute-start.2 = (bf16[3,16,26,9]{3,2,1,0:T(8,128)(2,1)}, bf16[3,16,26,9]{3,2,1,0:T(8,128)(2,1)S(1)}, u32[]{:S(2)}, u32[]{:S(2)}) collective-permute-start(bf16[3,16,26,9]{3,2,1,0:T(8,128)(2,1)} %get-tuple-element.50), channel_id=1, source_target_pairs={{0,1},{1,2},{2,3},{3,4},{4,5},{5,6},{6,7},{8,9},{9,10},{10,11},{11... | collective-permute-start | bytes 67400 | tf_op jit(solution)/shard_map/ppermute | solution.py:24
  36.3 10.3 %collective-permute-start.3 = (bf16[3,16,26,9]{3,2,1,0:T(8,128)(2,1)S(1)}, bf16[3,16,26,9]{3,2,1,0:T(8,128)(2,1)S(1)}, u32[]{:S(2)}, u32[]{:S(2)}) collective-permute-start(bf16[3,16,26,9]{3,2,1,0:T(8,128)(2,1)S(1)} %get-tuple-element.51), channel_id=1, source_target_pairs={{1,0},{2,1},{3,2},{4,3},{5,4},{6,5},{7,6},{9,8},{10,9},{11,10},{12... | collective-permute-start | bytes 67400 | tf_op jit(solution)/shard_map/ppermute | solution.py:27
  39.4 1.1 copy-start.23
  40.8 15.9 %copy-start.3 = (f32[3,4,4,32]{3,2,1,0:T(4,128)}, f32[3,4,4,32]{3,2,1,0:T(4,128)S(1)}, u32[]{:S(2)}) copy-start(f32[3,4,4,32]{3,2,1,0:T(4,128)S(1)} %get-tuple-element.70) | copy-start | bytes 18436
  41.1 15.6 %copy-start.5 = (f32[3,4,4,2]{3,2,1,0:T(4,128)}, f32[3,4,4,2]{3,2,1,0:T(4,128)S(1)}, u32[]{:S(2)}) copy-start(f32[3,4,4,2]{3,2,1,0:T(4,128)S(1)} %slice.1068) | copy-start | bytes 1156
  41.3 11.9 %collective-permute-start.6 = (f32[3,1,6,36]{3,2,1,0:T(8,128)S(1)}, f32[3,1,6,36]{3,2,1,0:T(8,128)S(1)}, u32[]{:S(2)}, u32[]{:S(2)}) collective-permute-start(f32[3,1,6,36]{3,2,1,0:T(8,128)S(1)} %get-tuple-element.79), channel_id=1, source_target_pairs={{0,64},{64,128},{128,192},{192,256},{256,320},{320,384},{384,448},... | collective-permute-start | bytes 7784 | tf_op jit(solution)/shard_map/ppermute | solution.py:24
  45.3 7.9 %collective-permute-start.7 = (f32[3,1,6,36]{3,2,1,0:T(8,128)S(1)}, f32[3,1,6,36]{3,2,1,0:T(8,128)S(1)}, u32[]{:S(2)}, u32[]{:S(2)}) collective-permute-start(f32[3,1,6,36]{3,2,1,0:T(8,128)S(1)} %get-tuple-element.80), channel_id=1, source_target_pairs={{64,0},{128,64},{192,128},{256,192},{320,256},{384,320},{448,384},... | collective-permute-start | bytes 7784 | tf_op jit(solution)/shard_map/ppermute | solution.py:27
  47.1 11.9 %collective-permute-start.4 = (bf16[3,5,26,146]{3,2,1,0:T(8,128)(2,1)S(1)}, bf16[3,5,26,146]{3,2,1,0:T(8,128)(2,1)S(1)}, u32[]{:S(2)}, u32[]{:S(2)}) collective-permute-start(bf16[3,5,26,146]{3,2,1,0:T(8,128)(2,1)S(1)} %get-tuple-element.42), channel_id=1, source_target_pairs={{0,64},{64,128},{128,192},{192,256},{256,320},{320,384},{384,448},... | collective-permute-start | bytes 341648 | tf_op jit(solution)/shard_map/ppermute | solution.py:24
  51.7 10.1 %collective-permute-start.5 = (bf16[3,5,26,146]{3,2,1,0:T(8,128)(2,1)S(1)}, bf16[3,5,26,146]{3,2,1,0:T(8,128)(2,1)S(1)}, u32[]{:S(2)}, u32[]{:S(2)}) collective-permute-start(bf16[3,5,26,146]{3,2,1,0:T(8,128)(2,1)S(1)} %get-tuple-element.43), channel_id=1, source_target_pairs={{64,0},{128,64},{192,128},{256,192},{320,256},{384,320},{448,384},... | collective-permute-start | bytes 341648 | tf_op jit(solution)/shard_map/ppermute | solution.py:27
  76.3 0.7 copy-start.11
  76.3 0.7 copy-start.12
  76.3 0.7 copy-start.20
  76.3 0.7 copy-start.21
  76.7 2.7 %copy-start = (f32[22,22,142]{2,1,0:T(8,128)S(1)}, f32[22,22,142]{2,1,0:T(8,128)}, u32[]{:S(2)}) copy-start(f32[22,22,142]{2,1,0:T(8,128)} %get-tuple-element.31) | copy-start | bytes 824740
  77.0 2.9 %copy-start.16 = (f32[36,140]{1,0:T(8,128)S(1)}, f32[36,140]{1,0:T(8,128)}, u32[]{:S(2)}) copy-start(f32[36,140]{1,0:T(8,128)} %fusion.150) | copy-start | bytes 60484
  79.3 2.4 %copy-start.15 = (f32[36,140]{1,0:T(8,128)S(1)}, f32[36,140]{1,0:T(8,128)}, u32[]{:S(2)}) copy-start(f32[36,140]{1,0:T(8,128)} %fusion.148) | copy-start | bytes 60484
  79.9 3.3 %copy-start.10 = (f32[400,34,1]{0,1,2:T(8,128)S(1)}, f32[400,34,1]{0,1,2:T(8,128)}, u32[]{:S(2)}) copy-start(f32[400,34,1]{0,1,2:T(8,128)} %convolution_bitcast_fusion.4) | copy-start | bytes 163204
  79.9 3.3 %copy-start.13 = (f32[4,400]{1,0:T(4,128)S(1)}, f32[4,400]{1,0:T(4,128)}, u32[]{:S(2)}) copy-start(f32[4,400]{1,0:T(4,128)} %mul.1075) | copy-start | bytes 19204
  79.9 3.3 %copy-start.14 = (f32[4,400]{1,0:T(4,128)S(1)}, f32[4,400]{1,0:T(4,128)}, u32[]{:S(2)}) copy-start(f32[4,400]{1,0:T(4,128)} %mul.1072) | copy-start | bytes 19204
  79.9 3.5 %copy-start.9 = (f32[400,34,1]{0,1,2:T(8,128)S(1)}, f32[400,34,1]{0,1,2:T(8,128)}, u32[]{:S(2)}) copy-start(f32[400,34,1]{0,1,2:T(8,128)} %convolution_bitcast_fusion.5) | copy-start | bytes 163204
  79.9 4.0 %copy-start.7 = (f32[4,400]{1,0:T(4,128)S(1)}, f32[4,400]{1,0:T(4,128)}, u32[]{:S(2)}) copy-start(f32[4,400]{1,0:T(4,128)} %mul.943) | copy-start | bytes 19204
  79.9 4.0 %copy-start.8 = (f32[4,400]{1,0:T(4,128)S(1)}, f32[4,400]{1,0:T(4,128)}, u32[]{:S(2)}) copy-start(f32[4,400]{1,0:T(4,128)} %mul.940) | copy-start | bytes 19204
  80.4 4.2 %copy-start.4 = (f32[3,4,4,32]{3,2,1,0:T(4,128)S(1)}, f32[3,4,4,32]{3,2,1,0:T(4,128)}, u32[]{:S(2)}) copy-start(f32[3,4,4,32]{3,2,1,0:T(4,128)} %copy-done.3) | copy-start | bytes 18436
  80.4 4.2 %copy-start.6 = (f32[3,4,4,2]{3,2,1,0:T(4,128)S(1)}, f32[3,4,4,2]{3,2,1,0:T(4,128)}, u32[]{:S(2)}) copy-start(f32[3,4,4,2]{3,2,1,0:T(4,128)} %copy-done.5) | copy-start | bytes 1156
  80.4 4.2 %copy-start.17 = (f32[1,4,4,34]{3,2,1,0:T(4,128)S(1)}, f32[1,4,4,34]{3,2,1,0:T(4,128)}, u32[]{:S(2)}) copy-start(f32[1,4,4,34]{3,2,1,0:T(4,128)} %fusion.184) | copy-start | bytes 6532
  80.4 4.2 %copy-start.18 = (f32[1,4,4,34]{3,2,1,0:T(4,128)S(1)}, f32[1,4,4,34]{3,2,1,0:T(4,128)}, u32[]{:S(2)}) copy-start(f32[1,4,4,34]{3,2,1,0:T(4,128)} %fusion.178) | copy-start | bytes 6532
  80.4 4.2 %copy-start.19 = (f32[1,4,4,34]{3,2,1,0:T(4,128)S(1)}, f32[1,4,4,34]{3,2,1,0:T(4,128)}, u32[]{:S(2)}) copy-start(f32[1,4,4,34]{3,2,1,0:T(4,128)} %fusion.172) | copy-start | bytes 6532
  80.4 4.2 %copy-start.33 = (pred[34]{0:T(512)(128)(4,1)S(1)}, pred[34]{0:T(512)(128)(4,1)}, u32[]{:S(2)}) copy-start(pred[34]{0:T(512)(128)(4,1)} %and_or_fusion) | copy-start | bytes 106
  80.4 20.1 %copy-start.24 = (f32[640]{0:T(1024)S(1)}, f32[640]{0:T(1024)}, u32[]{:S(2)}) copy-start(f32[640]{0:T(1024)} %copy-done.23) | copy-start | bytes 7684
  81.7 21.9 %copy-start.26 = (s32[140]{0:T(256)S(1)}, s32[140]{0:T(256)}, u32[]{:S(2)}) copy-start(s32[140]{0:T(256)} %copy-done.25) | copy-start | bytes 1684
  81.7 21.9 %copy-start.28 = (s32[140]{0:T(256)S(1)}, s32[140]{0:T(256)}, u32[]{:S(2)}) copy-start(s32[140]{0:T(256)} %copy-done.27) | copy-start | bytes 1684
  81.7 21.9 %copy-start.30 = (f32[140]{0:T(256)S(1)}, f32[140]{0:T(256)}, u32[]{:S(2)}) copy-start(f32[140]{0:T(256)} %copy-done.29) | copy-start | bytes 1684
  81.7 21.9 %copy-start.32 = (f32[140]{0:T(256)S(1)}, f32[140]{0:T(256)}, u32[]{:S(2)}) copy-start(f32[140]{0:T(256)} %copy-done.31) | copy-start | bytes 1684
  84.8 6.5 %collective-permute-start.8 = (f32[3,1,4,34]{3,2,1,0:T(4,128)S(1)}, f32[3,1,4,34]{3,2,1,0:T(4,128)S(1)}, u32[]{:S(2)}, u32[]{:S(2)}) collective-permute-start(f32[3,1,4,34]{3,2,1,0:T(4,128)S(1)} %get-tuple-element.95), channel_id=1, source_target_pairs={{0,64},{64,128},{128,192},{192,256},{256,320},{320,384},{384,448},... | collective-permute-start | bytes 4904 | tf_op jit(solution)/shard_map/ppermute | solution.py:24
  90.0 5.3 %collective-permute-start.9 = (f32[3,1,4,34]{3,2,1,0:T(4,128)S(1)}, f32[3,1,4,34]{3,2,1,0:T(4,128)S(1)}, u32[]{:S(2)}, u32[]{:S(2)}) collective-permute-start(f32[3,1,4,34]{3,2,1,0:T(4,128)S(1)} %get-tuple-element.96), channel_id=1, source_target_pairs={{64,0},{128,64},{192,128},{256,192},{320,256},{384,320},{448,384},... | collective-permute-start | bytes 4904 | tf_op jit(solution)/shard_map/ppermute | solution.py:27
  95.3 5.5 %collective-permute-start.10 = (f32[3,6,1,34]{3,2,1,0:T(1,128)S(1)}, f32[3,6,1,34]{3,2,1,0:T(1,128)S(1)}, u32[]{:S(2)}, u32[]{:S(2)}) collective-permute-start(f32[3,6,1,34]{3,2,1,0:T(1,128)S(1)} %get-tuple-element.93), channel_id=1, source_target_pairs={{0,8},{8,16},{16,24},{24,32},{32,40},{40,48},{48,56},{1,9},{9,17},... | collective-permute-start | bytes 7352 | tf_op jit(solution)/shard_map/ppermute | solution.py:24
  99.0 4.4 %collective-permute-start.11 = (f32[3,6,1,34]{3,2,1,0:T(1,128)S(1)}, f32[3,6,1,34]{3,2,1,0:T(1,128)S(1)}, u32[]{:S(2)}, u32[]{:S(2)}) collective-permute-start(f32[3,6,1,34]{3,2,1,0:T(1,128)S(1)} %get-tuple-element.94), channel_id=1, source_target_pairs={{8,0},{16,8},{24,16},{32,24},{40,32},{48,40},{56,48},{9,1},{17,9},... | collective-permute-start | bytes 7352 | tf_op jit(solution)/shard_map/ppermute | solution.py:27
  106.5 15.9 %copy-start.34 = (s32[64]{0:T(128)S(1)}, s32[64]{0:T(128)}, u32[]{:S(2)}) copy-start(s32[64]{0:T(128)} %get-tuple-element.39) | copy-start | bytes 772
  109.6 23.9 %all-to-all-start.1 = ((f32[3,64,16]{2,0,1:T(4,128)}), f32[3,64,16]{2,0,1:T(4,128)S(1)}, u32[]{:S(2)}, u32[]{:S(2)}) async-start(f32[3,64,16]{2,0,1:T(4,128)} %copy.103), calls=%async_computation.1 | async-start | bytes 262144 | tf_op jit(solution)/shard_map/all_to_all | solution.py:403

commit v10 on v6

--- a/solution.py
+++ b/solution.py
@@ -222,6 +222,49 @@
     return collect_axis(reduced, 1, ELEM, squared)
 
 
+def split_exact(values):
+    high = lax.reduce_precision(values, exponent_bits=8, mantissa_bits=7)
+    rest = values - high
+    middle = lax.reduce_precision(rest, exponent_bits=8, mantissa_bits=7)
+    return jnp.stack([high, middle, rest - middle]).astype(jnp.bfloat16)
+
+
+def join_exact(pieces):
+    pieces = pieces.astype(jnp.float32)
+    return (pieces[0] + pieces[1]) + pieces[2]
+
+
+def x_round(images, nodes, image_width):
+    count = lax.axis_size("gx")
+    forward = [(i, i + 1) for i in range(count - 1)]
+    backward = [(target, source) for source, target in forward]
+    face_shape = (1, image_width) + images.shape[2:]
+    node_face = (nodes.shape[0], 1) + nodes.shape[2:]
+    used = 3 * nodes.shape[0] * node_face[2] * node_face[3]
+    room = image_width * images.shape[2] * images.shape[3]
+
+    def pack(image_face, node_slice):
+        coded = split_exact(node_slice).reshape(-1)
+        coded = jnp.pad(coded, (0, room - used)).reshape(face_shape)
+        return jnp.concatenate([image_face, coded])
+
+    low = lax.ppermute(
+        pack(images[:, images.shape[1] - image_width :], nodes[:, nodes.shape[1] - 1 :]),
+        "gx",
+        forward,
+    )
+    high = lax.ppermute(pack(images[:, :image_width], nodes[:, :1]), "gx", backward)
+    channels = images.shape[0]
+
+    def unpack(buffer):
+        coded = buffer[channels:].reshape(-1)[:used].reshape((3,) + node_face)
+        return join_exact(coded)
+
+    padded_images = jnp.concatenate([low[:channels], images, high[:channels]], axis=1)
+    padded_nodes = jnp.concatenate([unpack(low), nodes, unpack(high)], axis=1)
+    return padded_images, padded_nodes
+
+
 NEIGHBOURS = [(0, 0)] + [(ry, rz) for ry in (-1, 0, 1) for rz in (-1, 0, 1) if (ry, rz) != (0, 0)]
 HALO_CAP = 10
 
@@ -230,7 +273,6 @@
     stacked = jnp.stack([reference_image, deformed_image, roi_mask.astype(jnp.bfloat16)])
     stacked = with_halo(stacked, (("gy", 2),), 5)
     stacked = with_halo(stacked, (("gz", 3),), 5 + ELEM)
-    padded_images = with_halo(stacked, (("gx", 1),), 5).astype(jnp.float32)
     nodes_shape = (
         3,
         reference_image.shape[0] // ELEM,
@@ -325,7 +367,8 @@
         axis=3,
     )
     extended = jnp.concatenate([low_row, middle, high_row], axis=2)
-    first_padded = with_halo(extended, (("gx", 1),), 1)
+    padded_images, first_padded = x_round(stacked, extended, 5)
+    padded_images = padded_images.astype(jnp.float32)
     derived = derive_fields(padded_images[0], padded_images[1])
     region = padded_images[2][3:-3, 3:-3, 3:-3]
     contrast = derived[0].astype(jnp.float32)

time: 124 us -> 142 us (1.15)
  local copies, waits for them, and re-layouts: 12.4 us -> 22.3 us
  waiting for transfers between devices: 21.5 us -> 31.4 us
  starting transfers between devices: 60.6 us -> 51.7 us
  other arithmetic: 19.6 us -> 25.5 us
    ppermute x6 -> x4, starting transfers between devices: 24.7 us -> 14.6 us  [with_halo(): lax.ppermute(lax.slice_in_dim(block, block.shape[dim] - width, None, axis...]
    ppermute x0 -> x2, waiting for transfers between devices: none -> 10 us  [the longest x1 6.78 us: x_round(): lax.ppermute(pack(images[:, :image_width], nodes[:, :1]), 'gx', backward)]
    ppermute x0 -> x2, starting transfers between devices: none -> 5.48 us  [the longest x1 4.02 us: x_round(): lax.ppermute(pack(images[:, images.shape[1] - image_width:], nodes[:, nod...]
    add x43, other arithmetic: 0.71 us -> 6.06 us  [pair_op(): lax.slice_in_dim(volume, 1, length, axis=dimension)]
    ppermute x6 -> x4, starting transfers between devices: 8.77 us -> 5.8 us  [with_halo(): lax.ppermute(lax.slice_in_dim(block, 0, width, axis=dim), axis, backward)]
    unnamed x62 -> x128, local copies, waits for them, and re-layouts: 0.37 us -> 2.88 us
    all_to_all x1, waiting for transfers between devices: 0.77 us -> 2.77 us  [per_device(): lax.all_to_all(send_outgoing, ('gy', 'gz'), split_axis=1, concat_axis=1,...]
    squeeze x2, local copies, waits for them, and re-layouts: 0.28 us -> 2.08 us  [per_device(): moved[0]]
  transfers between devices with their start and end apart: 14 -> 12, of which waited for: 5 -> 7; matrix products, arithmetic and copies ran while one was open for 15% -> 11% of each run, Pallas kernels for 0% -> 0%
where the time goes in v10:
time: 142 us; the launch traced here: 140 us
  starting transfers between devices  51.7 us (36%)
  waiting for transfers between devices  31.4 us (22%)
  other arithmetic  25.5 us (18%)
  local copies, waits for them, and re-layouts  22.3 us (16%)
  matrix products  7.49 us (5%)
  between operations  2.02 us (1%)
    ppermute x4, starting transfers between devices, with_halo(): lax.ppermute(lax.slice_in_dim(block, block.shape[dim] - width, None, axis...  14.6 us
    all_to_all x1, starting transfers between devices, per_device(): lax.all_to_all(send_outgoing, ('gy', 'gz'), split_axis=1, concat_axis=1,...  13.3 us
    all_to_all x1, starting transfers between devices, per_device(): lax.all_to_all(outgoing, ('gy', 'gz'), split_axis=1, concat_axis=1, tiled...  12.5 us
    all_to_all x1, waiting for transfers between devices, per_device(): lax.all_to_all(outgoing, ('gy', 'gz'), split_axis=1, concat_axis=1, tiled...  10.4 us
    ppermute x4, waiting for transfers between devices, with_halo(): lax.ppermute(lax.slice_in_dim(block, 0, width, axis=dim), axis, backward)  8.24 us
    ppermute x1, waiting for transfers between devices, x_round(): lax.ppermute(pack(images[:, :image_width], nodes[:, :1]), 'gx', backward)  6.78 us
    add x43, other arithmetic, pair_op(): lax.slice_in_dim(volume, 1, length, axis=dimension)  6.06 us
    ppermute x4, starting transfers between devices, with_halo(): lax.ppermute(lax.slice_in_dim(block, 0, width, axis=dim), axis, backward)  5.8 us
  transfers between devices with their start and end apart: 12, of which 7 were waited for; matrix products, arithmetic and copies ran while one was open for 11% of the time, Pallas kernels for 0%

profile of v10, /device:TPU:1, one launch (start us, length us, event | category | flops | bytes accessed | tf_op | source)
XLA Modules:
  0.0 140.4 jit_solution(7492185032606363430)
XLA Ops:
  0.0 0.9 convert_bitcast_fusion
  0.9 0.9 pad_maximum_fusion.14
  1.9 4.0 %collective-permute-start = (bf16[3,16,5,128]{3,2,1,0:T(8,128)(2,1)S(1)}, bf16[3,16,5,128]{3,2,1,0:T(8,128)(2,1)S(1)}, u32[]{:S(2)}, u32[]{:S(2)}) collective-permute-start(bf16[3,16,5,128]{3,2,1,0:T(8,128)(2,1)S(1)} %get-tuple-element.107), channel_id=1, source_target_pairs={{0,8},{8,16},{16,24},{24,32},{32,40},{40,48},{48,56},{1,9},{9,17},... | collective-permute-start | bytes 184328 | tf_op jit(solution)/shard_map/ppermute | solution.py:24
  5.9 1.3 collective-permute-start.1
  7.2 0.7 broadcast_add_fusion.1
  7.9 1.3 and_and_fusion
  9.8 1.1 concatenate.80
  10.9 0.7 fusion.7
  12.4 0.7 copy.167
  13.1 13.3 %all-to-all-start = ((f32[4,64,80]{2,0,1:T(4,128)}), f32[4,64,80]{2,0,1:T(4,128)S(1)}, u32[]{:S(2)}, u32[]{:S(2)}) async-start(f32[4,64,80]{2,0,1:T(4,128)} %copy.167), calls=%async_computation | async-start | bytes 262144 | tf_op jit(solution)/shard_map/all_to_all | solution.py:339
  26.5 0.5 fusion.195
  27.1 0.6 iota_compare_fusion.8
  27.7 0.6 iota_compare_fusion.7
  28.3 0.6 select_add_fusion
  29.4 3.5 %collective-permute-start.2 = (bf16[3,16,26,9]{3,2,1,0:T(8,128)(2,1)S(1)}, bf16[3,16,26,9]{3,2,1,0:T(8,128)(2,1)S(1)}, u32[]{:S(2)}, u32[]{:S(2)}) collective-permute-start(bf16[3,16,26,9]{3,2,1,0:T(8,128)(2,1)S(1)} %get-tuple-element.80), channel_id=1, source_target_pairs={{0,1},{1,2},{2,3},{3,4},{4,5},{5,6},{6,7},{8,9},{9,10},{10,11},{11... | collective-permute-start | bytes 67400 | tf_op jit(solution)/shard_map/ppermute | solution.py:24
  32.9 1.9 %collective-permute-start.3 = (bf16[3,16,26,9]{3,2,1,0:T(8,128)(2,1)S(1)}, bf16[3,16,26,9]{3,2,1,0:T(8,128)(2,1)S(1)}, u32[]{:S(2)}, u32[]{:S(2)}) collective-permute-start(bf16[3,16,26,9]{3,2,1,0:T(8,128)(2,1)S(1)} %get-tuple-element.81), channel_id=1, source_target_pairs={{1,0},{2,1},{3,2},{4,3},{5,4},{6,5},{7,6},{9,8},{10,9},{11,10},{12... | collective-permute-start | bytes 67400 | tf_op jit(solution)/shard_map/ppermute | solution.py:27
  34.8 2.8 %all-to-all-done = f32[4,64,80]{2,0,1:T(4,128)S(1)} async-done(((f32[4,64,80]{2,0,1:T(4,128)}), f32[4,64,80]{2,0,1:T(4,128)S(1)}, u32[]{:S(2)}, u32[]{:S(2)}) %all-to-all-start) | async-done | bytes 81952 | tf_op jit(solution)/shard_map/all_to_all | solution.py:339
  38.8 0.8 fusion.8
  41.5 0.5 collective-permute-done.3
  42.0 0.5 fusion.57
  42.5 4.0 %collective-permute-start.4 = (bf16[4,5,26,146]{3,2,1,0:T(8,128)(2,1)S(1)}, bf16[4,5,26,146]{3,2,1,0:T(8,128)(2,1)S(1)}, u32[]{:S(2)}, u32[]{:S(2)}) collective-permute-start(bf16[4,5,26,146]{3,2,1,0:T(8,128)(2,1)S(1)} %get-tuple-element.68), channel_id=1, source_target_pairs={{0,64},{64,128},{128,192},{192,256},{256,320},{320,384},{384,448},... | collective-permute-start | bytes 455528 | tf_op jit(solution)/shard_map/ppermute | solution.py:251
  46.5 0.6 and_or_fusion
  47.1 0.6 mul.999
  47.7 0.7 mul.993
  48.4 0.6 fusion.190
  49.0 1.5 %collective-permute-start.5 = (bf16[4,5,26,146]{3,2,1,0:T(8,128)(2,1)S(1)}, bf16[4,5,26,146]{3,2,1,0:T(8,128)(2,1)S(1)}, u32[]{:S(2)}, u32[]{:S(2)}) collective-permute-start(bf16[4,5,26,146]{3,2,1,0:T(8,128)(2,1)S(1)} %get-tuple-element.69), channel_id=1, source_target_pairs={{64,0},{128,64},{192,128},{256,192},{320,256},{384,320},{448,384},... | collective-permute-start | bytes 455528 | tf_op jit(solution)/shard_map/ppermute | solution.py:256
  50.4 3.2 %collective-permute-done.4 = bf16[4,5,26,146]{3,2,1,0:T(8,128)(2,1)S(1)} collective-permute-done((bf16[4,5,26,146]{3,2,1,0:T(8,128)(2,1)S(1)}, bf16[4,5,26,146]{3,2,1,0:T(8,128)(2,1)S(1)}, u32[]{:S(2)}, u32[]{:S(2)}) %collective-permute-start.4) | collective-permute-done | bytes 151872 | tf_op jit(solution)/shard_map/ppermute | solution.py:251
  54.1 6.8 %collective-permute-done.5 = bf16[4,5,26,146]{3,2,1,0:T(8,128)(2,1)S(1)} collective-permute-done((bf16[4,5,26,146]{3,2,1,0:T(8,128)(2,1)S(1)}, bf16[4,5,26,146]{3,2,1,0:T(8,128)(2,1)S(1)}, u32[]{:S(2)}, u32[]{:S(2)}) %collective-permute-start.5) | collective-permute-done | bytes 151872 | tf_op jit(solution)/shard_map/ppermute | solution.py:256
  61.8 0.4 fusion.60
  62.2 0.8 maximum_convert_fusion
  64.1 2.0 %add_multiply_fusion = (f32[22,22,142]{2,1,0:T(8,128)S(1)}, f32[22,22,142]{2,1,0:T(8,128)S(1)}, f32[22,22,142]{2,1,0:T(8,128)}) fusion(f32[22,22,146]{2,1,0:T(8,128)S(1)} %fusion.33, f32[22,22,146]{2,1,0:T(8,128)S(1)} %fusion.41), kind=kLoop, calls=%fused_computation.95 | loop fusion | flops 1374560 | bytes 3573856 | tf_op jit(solution)/shard_map/mul | solution.py:77
  66.1 1.0 fusion.222
  67.8 0.6 slice_add_fusion.56
  68.4 0.6 slice_add_fusion.53
  69.0 0.6 fusion.172
  69.7 0.6 slice_add_fusion.49
  70.3 0.6 slice_add_fusion.52
  70.9 0.6 slice_add_fusion.48
  71.5 0.6 fusion.160
  72.1 0.6 fusion.166
  72.7 0.6 slice_add_fusion.45
  73.7 0.4 copy-done.37
  74.5 1.1 fusion.221
  75.6 1.9 %squeeze.121 = f32[20,20,140]{2,1,0:T(8,128)} reshape(f32[1,20,5,4,140]{4,3,2,1,0:T(4,128)} %get-tuple-element.65) | data formatting | bytes 448000 | tf_op jit(solution)/shard_map/squeeze | solution.py:379
  77.5 1.9 %squeeze.125 = f32[20,20,140]{2,1,0:T(8,128)} reshape(f32[1,20,5,4,140]{4,3,2,1,0:T(4,128)} %get-tuple-element.66) | data formatting | bytes 448000 | tf_op jit(solution)/shard_map/squeeze | solution.py:379
  79.5 1.9 %squeeze.123 = f32[20,20,140]{2,1,0:T(8,128)} reshape(f32[1,20,5,4,140]{4,3,2,1,0:T(4,128)} %get-tuple-element.67) | data formatting | bytes 448000 | tf_op jit(solution)/shard_map/squeeze | solution.py:379
  81.8 0.7 copy-done.4
  83.8 1.4 multiply_reduce_fusion.3
  85.7 0.6 copy-done
  86.7 1.1 fusion.46
  88.1 1.4 multiply_reduce_fusion.5
  90.3 4.2 %collective-permute-start.6 = (f32[3,1,4,34]{3,2,1,0:T(4,128)S(1)}, f32[3,1,4,34]{3,2,1,0:T(4,128)S(1)}, u32[]{:S(2)}, u32[]{:S(2)}) collective-permute-start(f32[3,1,4,34]{3,2,1,0:T(4,128)S(1)} %get-tuple-element.123), channel_id=1, source_target_pairs={{0,64},{64,128},{128,192},{192,256},{256,320},{320,384},{384,448},... | collective-permute-start | bytes 4904 | tf_op jit(solution)/shard_map/ppermute | solution.py:24
  94.5 1.3 collective-permute-start.7
  95.8 4.9 %collective-permute-done.7 = f32[3,1,4,34]{3,2,1,0:T(4,128)S(1)} collective-permute-done((f32[3,1,4,34]{3,2,1,0:T(4,128)S(1)}, f32[3,1,4,34]{3,2,1,0:T(4,128)S(1)}, u32[]{:S(2)}, u32[]{:S(2)}) %collective-permute-start.7) | collective-permute-done | bytes 1664 | tf_op jit(solution)/shard_map/ppermute | solution.py:27
  100.7 2.8 %collective-permute-start.8 = (f32[3,6,1,34]{3,2,1,0:T(1,128)S(1)}, f32[3,6,1,34]{3,2,1,0:T(1,128)S(1)}, u32[]{:S(2)}, u32[]{:S(2)}) collective-permute-start(f32[3,6,1,34]{3,2,1,0:T(1,128)S(1)} %get-tuple-element.121), channel_id=1, source_target_pairs={{0,8},{8,16},{16,24},{24,32},{32,40},{40,48},{48,56},{1,9},{9,17},... | collective-permute-start | bytes 7352 | tf_op jit(solution)/shard_map/ppermute | solution.py:24
  103.6 1.3 collective-permute-start.9
  105.2 2.8 %collective-permute-done.9 = f32[3,6,1,34]{3,2,1,0:T(1,128)S(1)} collective-permute-done((f32[3,6,1,34]{3,2,1,0:T(1,128)S(1)}, f32[3,6,1,34]{3,2,1,0:T(1,128)S(1)}, u32[]{:S(2)}, u32[]{:S(2)}) %collective-permute-start.9) | collective-permute-done | bytes 2480 | tf_op jit(solution)/shard_map/ppermute | solution.py:27
  110.9 1.2 fusion.48
  112.4 1.4 multiply_reduce_fusion.1
  115.1 0.7 copy.204
  115.8 12.5 %all-to-all-start.1 = ((f32[3,64,16]{2,0,1:T(4,128)}), f32[3,64,16]{2,0,1:T(4,128)S(1)}, u32[]{:S(2)}, u32[]{:S(2)}) async-start(f32[3,64,16]{2,0,1:T(4,128)} %copy.204), calls=%async_computation.1 | async-start | bytes 262144 | tf_op jit(solution)/shard_map/all_to_all | solution.py:404
  128.3 0.7 slice_add_fusion.61
  129.0 10.4 %all-to-all-done.1 = f32[3,64,16]{2,0,1:T(4,128)S(1)} async-done(((f32[3,64,16]{2,0,1:T(4,128)}), f32[3,64,16]{2,0,1:T(4,128)S(1)}, u32[]{:S(2)}, u32[]{:S(2)}) %all-to-all-start.1) | async-done | bytes 12320 | tf_op jit(solution)/shard_map/all_to_all | solution.py:404
  139.6 0.9 convolution_bitcast_fusion
  (308 shorter events, 16.1 us)
Async XLA Ops:
  1.9 27.1 %collective-permute-start = (bf16[3,16,5,128]{3,2,1,0:T(8,128)(2,1)S(1)}, bf16[3,16,5,128]{3,2,1,0:T(8,128)(2,1)S(1)}, u32[]{:S(2)}, u32[]{:S(2)}) collective-permute-start(bf16[3,16,5,128]{3,2,1,0:T(8,128)(2,1)S(1)} %get-tuple-element.107), channel_id=1, source_target_pairs={{0,8},{8,16},{16,24},{24,32},{32,40},{40,48},{48,56},{1,9},{9,17},... | collective-permute-start | bytes 184328 | tf_op jit(solution)/shard_map/ppermute | solution.py:24
  5.9 23.1 %collective-permute-start.1 = (bf16[3,16,5,128]{3,2,1,0:T(8,128)(2,1)S(1)}, bf16[3,16,5,128]{3,2,1,0:T(8,128)(2,1)S(1)}, u32[]{:S(2)}, u32[]{:S(2)}) collective-permute-start(bf16[3,16,5,128]{3,2,1,0:T(8,128)(2,1)S(1)} %get-tuple-element.108), channel_id=1, source_target_pairs={{8,0},{16,8},{24,16},{32,24},{40,32},{48,40},{56,48},{9,1},{17,9},... | collective-permute-start | bytes 184328 | tf_op jit(solution)/shard_map/ppermute | solution.py:27
  9.7 1.2 copy-start.33
  11.6 17.4 %copy-start.6 = (bf16[16,16,128]{2,1,0:T(8,128)(2,1)S(1)}, bf16[16,16,128]{2,1,0:T(8,128)(2,1)}, u32[]{:S(2)}) copy-start(bf16[16,16,128]{2,1,0:T(8,128)(2,1)} %param.6) | copy-start | bytes 196612
  11.6 17.4 %copy-start.7 = (bf16[16,16,128]{2,1,0:T(8,128)(2,1)S(1)}, bf16[16,16,128]{2,1,0:T(8,128)(2,1)}, u32[]{:S(2)}) copy-start(bf16[16,16,128]{2,1,0:T(8,128)(2,1)} %param.5) | copy-start | bytes 196612
  13.1 24.5 %all-to-all-start = ((f32[4,64,80]{2,0,1:T(4,128)}), f32[4,64,80]{2,0,1:T(4,128)S(1)}, u32[]{:S(2)}, u32[]{:S(2)}) async-start(f32[4,64,80]{2,0,1:T(4,128)} %copy.167), calls=%async_computation | async-start | bytes 262144 | tf_op jit(solution)/shard_map/all_to_all | solution.py:339
  27.1 34.7 %copy-start.54 = (f32[140]{0:T(256)}, f32[140]{0:T(256)S(1)}, u32[]{:S(2)}) copy-start(f32[140]{0:T(256)S(1)} %get-tuple-element.154) | copy-start | bytes 1684
  27.1 34.7 %copy-start.56 = (f32[140]{0:T(256)}, f32[140]{0:T(256)S(1)}, u32[]{:S(2)}) copy-start(f32[140]{0:T(256)S(1)} %get-tuple-element.155) | copy-start | bytes 1684
  27.1 34.7 %copy-start.46 = (s32[140]{0:T(256)}, s32[140]{0:T(256)S(1)}, u32[]{:S(2)}) copy-start(s32[140]{0:T(256)S(1)} %get-tuple-element.152) | copy-start | bytes 1684
  27.1 34.7 %copy-start.48 = (s32[140]{0:T(256)}, s32[140]{0:T(256)S(1)}, u32[]{:S(2)}) copy-start(s32[140]{0:T(256)S(1)} %get-tuple-element.153) | copy-start | bytes 1684
  29.0 18.1 %copy-start.36 = (f32[4]{0:T(128)}, f32[4]{0:T(128)S(1)}, u32[]{:S(2)}) copy-start(f32[4]{0:T(128)S(1)} %get-tuple-element.156) | copy-start | bytes 52
  29.0 18.7 %copy-start.40 = (f32[4]{0:T(128)}, f32[4]{0:T(128)S(1)}, u32[]{:S(2)}) copy-start(f32[4]{0:T(128)S(1)} %get-tuple-element.157) | copy-start | bytes 52
  29.4 12.1 %collective-permute-start.2 = (bf16[3,16,26,9]{3,2,1,0:T(8,128)(2,1)S(1)}, bf16[3,16,26,9]{3,2,1,0:T(8,128)(2,1)S(1)}, u32[]{:S(2)}, u32[]{:S(2)}) collective-permute-start(bf16[3,16,26,9]{3,2,1,0:T(8,128)(2,1)S(1)} %get-tuple-element.80), channel_id=1, source_target_pairs={{0,1},{1,2},{2,3},{3,4},{4,5},{5,6},{6,7},{8,9},{9,10},{10,11},{11... | collective-permute-start | bytes 67400 | tf_op jit(solution)/shard_map/ppermute | solution.py:24
  32.9 9.1 %collective-permute-start.3 = (bf16[3,16,26,9]{3,2,1,0:T(8,128)(2,1)S(1)}, bf16[3,16,26,9]{3,2,1,0:T(8,128)(2,1)S(1)}, u32[]{:S(2)}, u32[]{:S(2)}) collective-permute-start(bf16[3,16,26,9]{3,2,1,0:T(8,128)(2,1)S(1)} %get-tuple-element.81), channel_id=1, source_target_pairs={{1,0},{2,1},{3,2},{4,3},{5,4},{6,5},{7,6},{9,8},{10,9},{11,10},{12... | collective-permute-start | bytes 67400 | tf_op jit(solution)/shard_map/ppermute | solution.py:27
  38.8 1.6 %copy-start.34 = (f32[640]{0:T(1024)}, f32[640]{0:T(1024)S(1)}, u32[]{:S(2)}) copy-start(f32[640]{0:T(1024)S(1)} %slice_reduce_fusion) | copy-start | bytes 7684
  40.2 21.5 %copy-start.8 = (f32[3,4,4,32]{3,2,1,0:T(4,128)}, f32[3,4,4,32]{3,2,1,0:T(4,128)S(1)}, u32[]{:S(2)}) copy-start(f32[3,4,4,32]{3,2,1,0:T(4,128)S(1)} %get-tuple-element.99) | copy-start | bytes 18436
  40.3 21.5 %copy-start.10 = (f32[3,4,4,32]{3,2,1,0:T(4,128)}, f32[3,4,4,32]{3,2,1,0:T(4,128)S(1)}, u32[]{:S(2)}) copy-start(f32[3,4,4,32]{3,2,1,0:T(4,128)S(1)} %get-tuple-element.100) | copy-start | bytes 18436
  40.6 21.2 %copy-start.12 = (f32[3,4,4,2]{3,2,1,0:T(4,128)}, f32[3,4,4,2]{3,2,1,0:T(4,128)S(1)}, u32[]{:S(2)}) copy-start(f32[3,4,4,2]{3,2,1,0:T(4,128)S(1)} %slice.1146) | copy-start | bytes 1156
  42.5 11.2 %collective-permute-start.4 = (bf16[4,5,26,146]{3,2,1,0:T(8,128)(2,1)S(1)}, bf16[4,5,26,146]{3,2,1,0:T(8,128)(2,1)S(1)}, u32[]{:S(2)}, u32[]{:S(2)}) collective-permute-start(bf16[4,5,26,146]{3,2,1,0:T(8,128)(2,1)S(1)} %get-tuple-element.68), channel_id=1, source_target_pairs={{0,64},{64,128},{128,192},{192,256},{256,320},{320,384},{384,448},... | collective-permute-start | bytes 455528 | tf_op jit(solution)/shard_map/ppermute | solution.py:251
  49.0 11.9 %collective-permute-start.5 = (bf16[4,5,26,146]{3,2,1,0:T(8,128)(2,1)S(1)}, bf16[4,5,26,146]{3,2,1,0:T(8,128)(2,1)S(1)}, u32[]{:S(2)}, u32[]{:S(2)}) collective-permute-start(bf16[4,5,26,146]{3,2,1,0:T(8,128)(2,1)S(1)} %get-tuple-element.69), channel_id=1, source_target_pairs={{64,0},{128,64},{192,128},{256,192},{320,256},{384,320},{448,384},... | collective-permute-start | bytes 455528 | tf_op jit(solution)/shard_map/ppermute | solution.py:256
  67.7 5.7 %copy-start.50 = (f32[20]{0:T(128)S(1)}, f32[20]{0:T(128)}, u32[]{:S(2)}) copy-start(f32[20]{0:T(128)} %mul.999) | copy-start | bytes 244
  67.8 5.7 %copy-start.52 = (f32[20]{0:T(128)S(1)}, f32[20]{0:T(128)}, u32[]{:S(2)}) copy-start(f32[20]{0:T(128)} %mul.993) | copy-start | bytes 244
  81.4 1.2 copy-start.5
  81.7 6.1 %copy-start.14 = (f32[20,20,140]{2,0,1:T(8,128)}, f32[20,20,140]{2,0,1:T(8,128)S(1)}, u32[]{:S(2)}) copy-start(f32[20,20,140]{2,0,1:T(8,128)S(1)} %copy.213) | copy-start | bytes 672004
  83.0 4.9 %copy-start.16 = (bf16[20,20,140]{2,0,1:T(8,128)(2,1)}, bf16[20,20,140]{2,0,1:T(8,128)(2,1)S(1)}, u32[]{:S(2)}) copy-start(bf16[20,20,140]{2,0,1:T(8,128)(2,1)S(1)} %copy.210) | copy-start | bytes 336004
  83.4 4.5 %copy-start.18 = (bf16[20,20,140]{2,0,1:T(8,128)(2,1)}, bf16[20,20,140]{2,0,1:T(8,128)(2,1)S(1)}, u32[]{:S(2)}) copy-start(bf16[20,20,140]{2,0,1:T(8,128)(2,1)S(1)} %copy.211) | copy-start | bytes 336004
  83.6 4.3 %copy-start.20 = (bf16[20,20,140]{2,0,1:T(8,128)(2,1)}, bf16[20,20,140]{2,0,1:T(8,128)(2,1)S(1)}, u32[]{:S(2)}) copy-start(bf16[20,20,140]{2,0,1:T(8,128)(2,1)S(1)} %copy.212) | copy-start | bytes 336004
  85.2 1.2 copy-start.1
  85.2 1.3 copy-start.2
  85.2 1.5 %copy-start.3 = (f32[20,20,140]{2,1,0:T(8,128)S(1)}, f32[20,20,140]{2,1,0:T(8,128)}, u32[]{:S(2)}) copy-start(f32[20,20,140]{2,1,0:T(8,128)} %squeeze.123) | copy-start | bytes 672004
  86.7 1.3 copy-start.31
  86.7 1.3 copy-start.38
  86.7 1.3 copy-start.42
  88.0 1.8 %copy-start.22 = (f32[4,4,35]{2,1,0:T(4,128)S(1)}, f32[4,4,35]{2,1,0:T(4,128)}, u32[]{:S(2)}) copy-start(f32[4,4,35]{2,1,0:T(4,128)} %slice_add_fusion.56) | copy-start | bytes 6724
  88.0 1.8 %copy-start.23 = (f32[4,4,35]{2,1,0:T(4,128)S(1)}, f32[4,4,35]{2,1,0:T(4,128)}, u32[]{:S(2)}) copy-start(f32[4,4,35]{2,1,0:T(4,128)} %slice_add_fusion.53) | copy-start | bytes 6724
  88.0 1.8 %copy-start.24 = (f32[4,4,35]{2,1,0:T(4,128)S(1)}, f32[4,4,35]{2,1,0:T(4,128)}, u32[]{:S(2)}) copy-start(f32[4,4,35]{2,1,0:T(4,128)} %fusion.172) | copy-start | bytes 6724
  88.0 1.9 %copy-start.25 = (f32[4,4,35]{2,1,0:T(4,128)S(1)}, f32[4,4,35]{2,1,0:T(4,128)}, u32[]{:S(2)}) copy-start(f32[4,4,35]{2,1,0:T(4,128)} %slice_add_fusion.49) | copy-start | bytes 6724
  88.0 1.9 %copy-start.26 = (f32[4,4,35]{2,1,0:T(4,128)S(1)}, f32[4,4,35]{2,1,0:T(4,128)}, u32[]{:S(2)}) copy-start(f32[4,4,35]{2,1,0:T(4,128)} %slice_add_fusion.52) | copy-start | bytes 6724
  88.0 1.9 %copy-start.29 = (f32[4,4,35]{2,1,0:T(4,128)S(1)}, f32[4,4,35]{2,1,0:T(4,128)}, u32[]{:S(2)}) copy-start(f32[4,4,35]{2,1,0:T(4,128)} %fusion.166) | copy-start | bytes 6724
  88.0 2.0 %copy-start.27 = (f32[4,4,35]{2,1,0:T(4,128)S(1)}, f32[4,4,35]{2,1,0:T(4,128)}, u32[]{:S(2)}) copy-start(f32[4,4,35]{2,1,0:T(4,128)} %slice_add_fusion.48) | copy-start | bytes 6724
  88.0 2.0 %copy-start.28 = (f32[4,4,35]{2,1,0:T(4,128)S(1)}, f32[4,4,35]{2,1,0:T(4,128)}, u32[]{:S(2)}) copy-start(f32[4,4,35]{2,1,0:T(4,128)} %fusion.160) | copy-start | bytes 6724
  88.0 2.0 %copy-start.30 = (f32[4,4,35]{2,1,0:T(4,128)S(1)}, f32[4,4,35]{2,1,0:T(4,128)}, u32[]{:S(2)}) copy-start(f32[4,4,35]{2,1,0:T(4,128)} %slice_add_fusion.45) | copy-start | bytes 6724
  88.0 2.0 %copy-start.9 = (f32[3,4,4,32]{3,2,1,0:T(4,128)S(1)}, f32[3,4,4,32]{3,2,1,0:T(4,128)}, u32[]{:S(2)}) copy-start(f32[3,4,4,32]{3,2,1,0:T(4,128)} %copy-done.8) | copy-start | bytes 18436
  88.1 2.0 %copy-start.11 = (f32[3,4,4,32]{3,2,1,0:T(4,128)S(1)}, f32[3,4,4,32]{3,2,1,0:T(4,128)}, u32[]{:S(2)}) copy-start(f32[3,4,4,32]{3,2,1,0:T(4,128)} %copy-done.10) | copy-start | bytes 18436
  88.1 2.0 %copy-start.13 = (f32[3,4,4,2]{3,2,1,0:T(4,128)S(1)}, f32[3,4,4,2]{3,2,1,0:T(4,128)}, u32[]{:S(2)}) copy-start(f32[3,4,4,2]{3,2,1,0:T(4,128)} %copy-done.12) | copy-start | bytes 1156
  88.1 2.0 %copy-start.62 = (pred[34]{0:T(512)(128)(4,1)S(1)}, pred[34]{0:T(512)(128)(4,1)}, u32[]{:S(2)}) copy-start(pred[34]{0:T(512)(128)(4,1)} %and_or_fusion) | copy-start | bytes 106
  88.1 16.8 %copy-start.35 = (f32[640]{0:T(1024)S(1)}, f32[640]{0:T(1024)}, u32[]{:S(2)}) copy-start(f32[640]{0:T(1024)} %copy-done.34) | copy-start | bytes 7684
  89.5 18.7 %copy-start.47 = (s32[140]{0:T(256)S(1)}, s32[140]{0:T(256)}, u32[]{:S(2)}) copy-start(s32[140]{0:T(256)} %copy-done.46) | copy-start | bytes 1684
  89.5 18.7 %copy-start.49 = (s32[140]{0:T(256)S(1)}, s32[140]{0:T(256)}, u32[]{:S(2)}) copy-start(s32[140]{0:T(256)} %copy-done.48) | copy-start | bytes 1684
  89.5 18.7 %copy-start.55 = (f32[140]{0:T(256)S(1)}, f32[140]{0:T(256)}, u32[]{:S(2)}) copy-start(f32[140]{0:T(256)} %copy-done.54) | copy-start | bytes 1684
  89.5 18.7 %copy-start.57 = (f32[140]{0:T(256)S(1)}, f32[140]{0:T(256)}, u32[]{:S(2)}) copy-start(f32[140]{0:T(256)} %copy-done.56) | copy-start | bytes 1684
  90.3 5.5 %collective-permute-start.6 = (f32[3,1,4,34]{3,2,1,0:T(4,128)S(1)}, f32[3,1,4,34]{3,2,1,0:T(4,128)S(1)}, u32[]{:S(2)}, u32[]{:S(2)}) collective-permute-start(f32[3,1,4,34]{3,2,1,0:T(4,128)S(1)} %get-tuple-element.123), channel_id=1, source_target_pairs={{0,64},{64,128},{128,192},{192,256},{256,320},{320,384},{384,448},... | collective-permute-start | bytes 4904 | tf_op jit(solution)/shard_map/ppermute | solution.py:24
  94.5 6.2 %collective-permute-start.7 = (f32[3,1,4,34]{3,2,1,0:T(4,128)S(1)}, f32[3,1,4,34]{3,2,1,0:T(4,128)S(1)}, u32[]{:S(2)}, u32[]{:S(2)}) collective-permute-start(f32[3,1,4,34]{3,2,1,0:T(4,128)S(1)} %get-tuple-element.124), channel_id=1, source_target_pairs={{64,0},{128,64},{192,128},{256,192},{320,256},{384,320},{448,384},... | collective-permute-start | bytes 4904 | tf_op jit(solution)/shard_map/ppermute | solution.py:27
  100.7 4.4 %collective-permute-start.8 = (f32[3,6,1,34]{3,2,1,0:T(1,128)S(1)}, f32[3,6,1,34]{3,2,1,0:T(1,128)S(1)}, u32[]{:S(2)}, u32[]{:S(2)}) collective-permute-start(f32[3,6,1,34]{3,2,1,0:T(1,128)S(1)} %get-tuple-element.121), channel_id=1, source_target_pairs={{0,8},{8,16},{16,24},{24,32},{32,40},{40,48},{48,56},{1,9},{9,17},... | collective-permute-start | bytes 7352 | tf_op jit(solution)/shard_map/ppermute | solution.py:24
  103.6 4.4 %collective-permute-start.9 = (f32[3,6,1,34]{3,2,1,0:T(1,128)S(1)}, f32[3,6,1,34]{3,2,1,0:T(1,128)S(1)}, u32[]{:S(2)}, u32[]{:S(2)}) collective-permute-start(f32[3,6,1,34]{3,2,1,0:T(1,128)S(1)} %get-tuple-element.122), channel_id=1, source_target_pairs={{8,0},{16,8},{24,16},{32,24},{40,32},{48,40},{56,48},{9,1},{17,9},... | collective-permute-start | bytes 7352 | tf_op jit(solution)/shard_map/ppermute | solution.py:27
  110.9 1.5 %copy-start.15 = (f32[20,20,140]{2,0,1:T(8,128)S(1)}, f32[20,20,140]{2,0,1:T(8,128)}, u32[]{:S(2)}) copy-start(f32[20,20,140]{2,0,1:T(8,128)} %copy-done.14) | copy-start | bytes 672004
  110.9 1.5 %copy-start.17 = (bf16[20,20,140]{2,0,1:T(8,128)(2,1)S(1)}, bf16[20,20,140]{2,0,1:T(8,128)(2,1)}, u32[]{:S(2)}) copy-start(bf16[20,20,140]{2,0,1:T(8,128)(2,1)} %copy-done.16) | copy-start | bytes 336004
  110.9 1.5 %copy-start.19 = (bf16[20,20,140]{2,0,1:T(8,128)(2,1)S(1)}, bf16[20,20,140]{2,0,1:T(8,128)(2,1)}, u32[]{:S(2)}) copy-start(bf16[20,20,140]{2,0,1:T(8,128)(2,1)} %copy-done.18) | copy-start | bytes 336004
  110.9 1.5 %copy-start.21 = (bf16[20,20,140]{2,0,1:T(8,128)(2,1)S(1)}, bf16[20,20,140]{2,0,1:T(8,128)(2,1)}, u32[]{:S(2)}) copy-start(bf16[20,20,140]{2,0,1:T(8,128)(2,1)} %copy-done.20) | copy-start | bytes 336004
  110.9 1.5 %copy-start.32 = (f32[36,140]{1,0:T(8,128)S(1)}, f32[36,140]{1,0:T(8,128)}, u32[]{:S(2)}) copy-start(f32[36,140]{1,0:T(8,128)} %select_add_fusion) | copy-start | bytes 60484
  110.9 1.5 %copy-start.39 = (f32[4]{0:T(128)S(1)}, f32[4]{0:T(128)}, u32[]{:S(2)}) copy-start(f32[4]{0:T(128)} %copy-done.36) | copy-start | bytes 52
  110.9 1.5 %copy-start.43 = (f32[4]{0:T(128)S(1)}, f32[4]{0:T(128)}, u32[]{:S(2)}) copy-start(f32[4]{0:T(128)} %copy-done.40) | copy-start | bytes 52
  113.8 14.5 %copy-start.63 = (s32[64]{0:T(128)S(1)}, s32[64]{0:T(128)}, u32[]{:S(2)}) copy-start(s32[64]{0:T(128)} %get-tuple-element.59) | copy-start | bytes 772
  115.8 23.6 %all-to-all-start.1 = ((f32[3,64,16]{2,0,1:T(4,128)}), f32[3,64,16]{2,0,1:T(4,128)S(1)}, u32[]{:S(2)}, u32[]{:S(2)}) async-start(f32[3,64,16]{2,0,1:T(4,128)} %copy.204), calls=%async_computation.1 | async-start | bytes 262144 | tf_op jit(solution)/shard_map/all_to_all | solution.py:404
  (12 other events, 9.3 us)

commit v11 on v6

--- a/solution.py
+++ b/solution.py
@@ -284,16 +284,16 @@
     packing = (
         target_slot[:, None] == jnp.arange(members * HALO_CAP, dtype=jnp.int32)[None, :]
     ).astype(jnp.float32)
-    cand_data = jnp.concatenate(
-        [
-            jnp.concatenate([displacement] * len(NEIGHBOURS), axis=1),
-            jnp.broadcast_to(cand_label[None, :, None], (1, count, block_nodes)),
+    block_packing = jnp.sum(packing.reshape(len(NEIGHBOURS), blocks, -1), axis=0)
+    label_row = jnp.dot(cand_label, packing, precision=highest)
+    send_outgoing = jnp.concatenate(
+        [
+            jnp.einsum("cjn,jp->cpn", displacement, block_packing, precision=highest),
+            jnp.broadcast_to(label_row[None, :, None], (1, label_row.shape[0], block_nodes)),
         ]
     )
-    send_channels = cand_data.shape[0]
-    send_outgoing = jnp.einsum("cjn,jp->cpn", cand_data, packing, precision=highest).reshape(
-        send_channels, -1
-    )
+    send_channels = send_outgoing.shape[0]
+    send_outgoing = send_outgoing.reshape(send_channels, -1)
     send_incoming = lax.all_to_all(
         send_outgoing, ("gy", "gz"), split_axis=1, concat_axis=1, tiled=True
     ).reshape(send_channels, members * HALO_CAP, block_nodes)

time: 124 us -> 126 us (1.016)
  other arithmetic: 19.6 us -> 21.7 us
    ppermute x6, starting transfers between devices: 24.7 us -> 26.2 us  [with_halo(): lax.ppermute(lax.slice_in_dim(block, block.shape[dim] - width, None, axis...]
  transfers between devices with their start and end apart: 14 -> 14, of which waited for: 5 -> 4; matrix products, arithmetic and copies ran while one was open for 15% -> 16% of each run, Pallas kernels for 0% -> 0%
where the time goes in v11:
time: 126 us; the launch traced here: 125 us
  starting transfers between devices  61.2 us (49%)
  other arithmetic  21.7 us (17%)
  waiting for transfers between devices  20.9 us (17%)
  local copies, waits for them, and re-layouts  11.9 us (9%)
  matrix products  7.71 us (6%)
  between operations  1.91 us (2%)
    ppermute x6, starting transfers between devices, with_halo(): lax.ppermute(lax.slice_in_dim(block, block.shape[dim] - width, None, axis...  26.2 us
    all_to_all x1, starting transfers between devices, per_device(): lax.all_to_all(send_outgoing, ('gy', 'gz'), split_axis=1, concat_axis=1,...  13.3 us
    all_to_all x1, starting transfers between devices, per_device(): lax.all_to_all(outgoing, ('gy', 'gz'), split_axis=1, concat_axis=1, tiled...  12.8 us
    all_to_all x1, waiting for transfers between devices, per_device(): lax.all_to_all(outgoing, ('gy', 'gz'), split_axis=1, concat_axis=1, tiled...  11.1 us
    ppermute x6, waiting for transfers between devices, with_halo(): lax.ppermute(lax.slice_in_dim(block, 0, width, axis=dim), axis, backward)  9.71 us
    ppermute x6, starting transfers between devices, with_halo(): lax.ppermute(lax.slice_in_dim(block, 0, width, axis=dim), axis, backward)  8.77 us
    dot_general x3, matrix products, collect(): jnp.dot(volume.reshape(-1, shape_all[3]), table_back, precision=highest)  4.17 us
  transfers between devices with their start and end apart: 14, of which 4 were waited for; matrix products, arithmetic and copies ran while one was open for 16% of the time, Pallas kernels for 0%

profile of v11, /device:TPU:1, one launch (start us, length us, event | category | flops | bytes accessed | tf_op | source)
XLA Modules:
  0.0 125.2 jit_solution(13264743962131317779)
XLA Ops:
  0.0 0.9 convert_bitcast_fusion
  0.9 0.9 pad_maximum_fusion.9
  1.9 4.0 %collective-permute-start = (bf16[3,16,5,128]{3,2,1,0:T(8,128)(2,1)S(1)}, bf16[3,16,5,128]{3,2,1,0:T(8,128)(2,1)S(1)}, u32[]{:S(2)}, u32[]{:S(2)}) collective-permute-start(bf16[3,16,5,128]{3,2,1,0:T(8,128)(2,1)S(1)} %get-tuple-element.103), channel_id=1, source_target_pairs={{0,8},{8,16},{16,24},{24,32},{32,40},{40,48},{48,56},{1,9},{9,17},... | collective-permute-start | bytes 184328 | tf_op jit(solution)/shard_map/ppermute | solution.py:24
  5.9 1.3 %collective-permute-start.1 = (bf16[3,16,5,128]{3,2,1,0:T(8,128)(2,1)S(1)}, bf16[3,16,5,128]{3,2,1,0:T(8,128)(2,1)S(1)}, u32[]{:S(2)}, u32[]{:S(2)}) collective-permute-start(bf16[3,16,5,128]{3,2,1,0:T(8,128)(2,1)S(1)} %get-tuple-element.104), channel_id=1, source_target_pairs={{8,0},{16,8},{24,16},{32,24},{40,32},{48,40},{56,48},{9,1},{17,9},... | collective-permute-start | bytes 184328 | tf_op jit(solution)/shard_map/ppermute | solution.py:27
  7.2 0.7 broadcast_add_fusion.1
  7.9 1.2 and_and_fusion
  9.3 0.3 convert_reduce_fusion.1
  10.6 0.6 fusion.10
  11.3 0.4 copy.110
  11.7 0.4 all_to_all.12
  12.1 0.7 copy.111
  12.9 13.3 %all-to-all-start = ((f32[4,64,80]{2,0,1:T(4,128)}), f32[4,64,80]{2,0,1:T(4,128)S(1)}, u32[]{:S(2)}, u32[]{:S(2)}) async-start(f32[4,64,80]{2,0,1:T(4,128)} %copy.111), calls=%async_computation | async-start | bytes 262144 | tf_op jit(solution)/shard_map/all_to_all | solution.py:297
  26.2 0.6 fusion.180
  26.8 0.6 fusion.175
  27.5 0.6 iota_compare_fusion.8
  28.1 0.6 iota_compare_fusion.9
  28.7 0.7 mul.1004
  29.4 0.7 mul.1010
  30.0 0.6 select_add_fusion
  30.6 0.6 and_or_fusion
  31.4 0.9 fusion.210
  32.4 3.5 %collective-permute-start.2 = (bf16[3,16,26,9]{3,2,1,0:T(8,128)(2,1)}, bf16[3,16,26,9]{3,2,1,0:T(8,128)(2,1)S(1)}, u32[]{:S(2)}, u32[]{:S(2)}) collective-permute-start(bf16[3,16,26,9]{3,2,1,0:T(8,128)(2,1)} %get-tuple-element.76), channel_id=1, source_target_pairs={{0,1},{1,2},{2,3},{3,4},{4,5},{5,6},{6,7},{8,9},{9,10},{10,11},{11... | collective-permute-start | bytes 67400 | tf_op jit(solution)/shard_map/ppermute | solution.py:24
  35.9 1.9 %collective-permute-start.3 = (bf16[3,16,26,9]{3,2,1,0:T(8,128)(2,1)S(1)}, bf16[3,16,26,9]{3,2,1,0:T(8,128)(2,1)S(1)}, u32[]{:S(2)}, u32[]{:S(2)}) collective-permute-start(bf16[3,16,26,9]{3,2,1,0:T(8,128)(2,1)S(1)} %get-tuple-element.77), channel_id=1, source_target_pairs={{1,0},{2,1},{3,2},{4,3},{5,4},{6,5},{7,6},{9,8},{10,9},{11,10},{12... | collective-permute-start | bytes 67400 | tf_op jit(solution)/shard_map/ppermute | solution.py:27
  37.9 0.4 reshape.415
  38.5 0.3 slice.835
  38.8 0.3 copy.114
  39.1 0.8 fusion.7
  39.9 0.3 copy.115
  40.2 0.3 reshape.416
  40.9 4.0 %collective-permute-start.6 = (f32[3,1,6,36]{3,2,1,0:T(8,128)S(1)}, f32[3,1,6,36]{3,2,1,0:T(8,128)S(1)}, u32[]{:S(2)}, u32[]{:S(2)}) collective-permute-start(f32[3,1,6,36]{3,2,1,0:T(8,128)S(1)} %get-tuple-element.109), channel_id=1, source_target_pairs={{0,64},{64,128},{128,192},{192,256},{256,320},{320,384},{384,448},... | collective-permute-start | bytes 7784 | tf_op jit(solution)/shard_map/ppermute | solution.py:24
  44.9 1.3 %collective-permute-start.7 = (f32[3,1,6,36]{3,2,1,0:T(8,128)S(1)}, f32[3,1,6,36]{3,2,1,0:T(8,128)S(1)}, u32[]{:S(2)}, u32[]{:S(2)}) collective-permute-start(f32[3,1,6,36]{3,2,1,0:T(8,128)S(1)} %get-tuple-element.110), channel_id=1, source_target_pairs={{64,0},{128,64},{192,128},{256,192},{320,256},{384,320},{448,384},... | collective-permute-start | bytes 7784 | tf_op jit(solution)/shard_map/ppermute | solution.py:27
  46.3 1.2 pad_maximum_fusion.8
  47.4 5.3 %collective-permute-start.4 = (bf16[3,5,26,146]{3,2,1,0:T(8,128)(2,1)}, bf16[3,5,26,146]{3,2,1,0:T(8,128)(2,1)}, u32[]{:S(2)}, u32[]{:S(2)}) collective-permute-start(bf16[3,5,26,146]{3,2,1,0:T(8,128)(2,1)} %get-tuple-element.64), channel_id=1, source_target_pairs={{0,64},{64,128},{128,192},{192,256},{256,320},{320,384},{384,448},... | collective-permute-start | bytes 341648 | tf_op jit(solution)/shard_map/ppermute | solution.py:24
  52.8 1.5 %collective-permute-start.5 = (bf16[3,5,26,146]{3,2,1,0:T(8,128)(2,1)S(1)}, bf16[3,5,26,146]{3,2,1,0:T(8,128)(2,1)}, u32[]{:S(2)}, u32[]{:S(2)}) collective-permute-start(bf16[3,5,26,146]{3,2,1,0:T(8,128)(2,1)S(1)} %get-tuple-element.65), channel_id=1, source_target_pairs={{64,0},{128,64},{192,128},{256,192},{320,256},{384,320},{448,384},... | collective-permute-start | bytes 341648 | tf_op jit(solution)/shard_map/ppermute | solution.py:27
  55.4 0.4 fusion.56
  56.2 0.4 multiply_add_fusion.1
  57.6 4.3 %collective-permute-done.5 = bf16[3,5,26,146]{3,2,1,0:T(8,128)(2,1)} collective-permute-done((bf16[3,5,26,146]{3,2,1,0:T(8,128)(2,1)S(1)}, bf16[3,5,26,146]{3,2,1,0:T(8,128)(2,1)}, u32[]{:S(2)}, u32[]{:S(2)}) %collective-permute-start.5) | collective-permute-done | bytes 113912 | tf_op jit(solution)/shard_map/ppermute | solution.py:27
  61.8 1.8 %maximum_convert_fusion = f32[3,26,26,146]{3,2,1,0:T(8,128)S(1)} fusion(bf16[3,5,26,146]{3,2,1,0:T(8,128)(2,1)} %collective-permute-done.5, bf16[3,16,26,9]{3,2,1,0:T(8,128)(2,1)S(1)} %collective-permute-done.3, bf16[3,16,5,128]{3,2,1,0:T(8,128)(2,1)S(1)} %collective-permute-done.1, bf16[1,16,16,128]{3,2,1,0:T(8,128)(2,1)S(1)} %convert_bitcast_fusion, ...), kind=kLoop, calls=%fused_computation.15 | loop fusion | flops 5329584 | bytes 1776528 | tf_op jit(solution)/shard_map/convert_element_type | solution.py:233
  63.7 0.4 fusion.25
  64.0 0.6 fusion.33
  64.6 1.2 add_multiply_fusion
  66.3 0.3 fusion.55
  66.7 0.3 fusion.53
  67.9 1.4 %multiply_reduce_fusion.3 = (f32[3,20,5,34]{3,1,2,0:T(8,128)S(1)}, f32[3,20,5,34]{3,1,2,0:T(8,128)S(1)}) fusion(f32[4]{0:T(128)S(1)} %copy-done.44, f32[4]{0:T(128)S(1)} %copy-done.43, pred[36,140]{1,0:T(8,128)(4,1)S(1)} %copy-done.22, pred[36,140]{1,0:T(8,128)(4,1)S(1)} %copy-done.23, f32[140]{0:T(256)S(1)} %copy-done.40, f32[140]{0:T(256)S(1)} %copy-done.41, ...), kind=kOutput, calls=%fused_computation.30 | convolution fusion | flops 69541080 | bytes 652832 | tf_op jit(solution)/shard_map/dot_general | solution.py:219
  69.5 0.2 maximum_convert_fusion.1
  69.8 1.1 fusion.46
  71.1 1.4 %multiply_reduce_fusion.5 = (f32[3,20,5,34]{3,1,2,0:T(8,128)S(1)}, f32[3,20,5,34]{3,1,2,0:T(8,128)S(1)}) fusion(f32[4]{0:T(128)S(1)} %copy-done.20, f32[4]{0:T(128)S(1)} %copy-done.17, f32[36,140]{1,0:T(8,128)S(1)} %copy-done.12, f32[20,5,4,140]{3,0,2,1:T(8,128)S(1)} %bitcast.506, f32[20,5,4,140]{3,0,2,1:T(8,128)S(1)} %bitcast.503, ...), kind=kOutput, calls=%fused_computation.32 | convolution fusion | flops 69526800 | bytes 885792 | tf_op jit(solution)/shard_map/dot_general | solution.py:219
  72.9 5.5 %collective-permute-start.8 = (f32[3,1,4,34]{3,2,1,0:T(4,128)S(1)}, f32[3,1,4,34]{3,2,1,0:T(4,128)S(1)}, u32[]{:S(2)}, u32[]{:S(2)}) collective-permute-start(f32[3,1,4,34]{3,2,1,0:T(4,128)S(1)} %get-tuple-element.119), channel_id=1, source_target_pairs={{0,64},{64,128},{128,192},{192,256},{256,320},{320,384},{384,448},... | collective-permute-start | bytes 4904 | tf_op jit(solution)/shard_map/ppermute | solution.py:24
  78.4 1.3 %collective-permute-start.9 = (f32[3,1,4,34]{3,2,1,0:T(4,128)S(1)}, f32[3,1,4,34]{3,2,1,0:T(4,128)S(1)}, u32[]{:S(2)}, u32[]{:S(2)}) collective-permute-start(f32[3,1,4,34]{3,2,1,0:T(4,128)S(1)} %get-tuple-element.120), channel_id=1, source_target_pairs={{64,0},{128,64},{192,128},{256,192},{320,256},{384,320},{448,384},... | collective-permute-start | bytes 4904 | tf_op jit(solution)/shard_map/ppermute | solution.py:27
  79.7 4.0 %collective-permute-done.9 = f32[3,1,4,34]{3,2,1,0:T(4,128)S(1)} collective-permute-done((f32[3,1,4,34]{3,2,1,0:T(4,128)S(1)}, f32[3,1,4,34]{3,2,1,0:T(4,128)S(1)}, u32[]{:S(2)}, u32[]{:S(2)}) %collective-permute-start.9) | collective-permute-done | bytes 1664 | tf_op jit(solution)/shard_map/ppermute | solution.py:27
  83.7 3.9 %collective-permute-start.10 = (f32[3,6,1,34]{3,2,1,0:T(1,128)S(1)}, f32[3,6,1,34]{3,2,1,0:T(1,128)S(1)}, u32[]{:S(2)}, u32[]{:S(2)}) collective-permute-start(f32[3,6,1,34]{3,2,1,0:T(1,128)S(1)} %get-tuple-element.117), channel_id=1, source_target_pairs={{0,8},{8,16},{16,24},{24,32},{32,40},{40,48},{48,56},{1,9},{9,17},... | collective-permute-start | bytes 7352 | tf_op jit(solution)/shard_map/ppermute | solution.py:24
  87.5 1.5 %collective-permute-start.11 = (f32[3,6,1,34]{3,2,1,0:T(1,128)S(1)}, f32[3,6,1,34]{3,2,1,0:T(1,128)S(1)}, u32[]{:S(2)}, u32[]{:S(2)}) collective-permute-start(f32[3,6,1,34]{3,2,1,0:T(1,128)S(1)} %get-tuple-element.118), channel_id=1, source_target_pairs={{8,0},{16,8},{24,16},{32,24},{40,32},{48,40},{56,48},{9,1},{17,9},... | collective-permute-start | bytes 7352 | tf_op jit(solution)/shard_map/ppermute | solution.py:27
  89.1 0.6 add_convert_fusion
  89.8 0.7 eq.216
  90.5 1.5 %collective-permute-done.11 = f32[3,6,1,34]{3,2,1,0:T(1,128)S(1)} collective-permute-done((f32[3,6,1,34]{3,2,1,0:T(1,128)S(1)}, f32[3,6,1,34]{3,2,1,0:T(1,128)S(1)}, u32[]{:S(2)}, u32[]{:S(2)}) %collective-permute-start.11) | collective-permute-done | bytes 2480 | tf_op jit(solution)/shard_map/ppermute | solution.py:27
  92.8 0.6 slice_add_fusion.33
  93.5 0.4 fusion.89
  94.2 0.4 multiply_add_fusion
  95.3 1.3 %fusion.48 = f32[20,20,140]{2,1,0:T(8,128)S(1)} fusion(bf16[20,20,140]{2,1,0:T(8,128)(2,1)} %get-tuple-element.44, f32[20,20,140]{2,1,0:T(8,128)S(1)} %squeeze.128, f32[20,20,140]{2,1,0:T(8,128)S(1)} %squeeze.127, f32[20,20,140]{2,1,0:T(8,128)S(1)} %squeeze.126, f32[3,20,20,140]{3,2,1,0:T(8,128)S(1)} %maximum_convert_fusion.1), kind=kLoop, calls=%fused_computation.102 | loop fusion | flops 392000 | bytes 1680000 | tf_op jit(solution)/shard_map/add | solution.py:348
  96.8 1.4 %multiply_reduce_fusion.1 = (f32[3,20,5,34]{3,1,2,0:T(8,128)S(1)}, f32[3,20,5,34]{3,1,2,0:T(8,128)S(1)}) fusion(f32[4]{0:T(128)S(1)} %copy-done.21, f32[4]{0:T(128)S(1)} %copy-done.18, f32[36,140]{1,0:T(8,128)S(1)} %copy-done.13, f32[20,5,4,140]{3,0,2,1:T(8,128)S(1)} %bitcast.505, f32[20,5,4,140]{3,0,2,1:T(8,128)S(1)} %bitcast.504, ...), kind=kOutput, calls=%fused_computation.27 | convolution fusion | flops 69526800 | bytes 885792 | tf_op jit(solution)/shard_map/dot_general | solution.py:219
  99.5 0.7 copy.136
  100.2 12.8 %all-to-all-start.1 = ((f32[3,64,16]{2,0,1:T(4,128)}), f32[3,64,16]{2,0,1:T(4,128)S(1)}, u32[]{:S(2)}, u32[]{:S(2)}) async-start(f32[3,64,16]{2,0,1:T(4,128)} %copy.136), calls=%async_computation.1 | async-start | bytes 262144 | tf_op jit(solution)/shard_map/all_to_all | solution.py:361
  113.1 11.1 %all-to-all-done.1 = f32[3,64,16]{2,0,1:T(4,128)S(1)} async-done(((f32[3,64,16]{2,0,1:T(4,128)}), f32[3,64,16]{2,0,1:T(4,128)S(1)}, u32[]{:S(2)}, u32[]{:S(2)}) %all-to-all-start.1) | async-done | bytes 12320 | tf_op jit(solution)/shard_map/all_to_all | solution.py:361
  124.4 0.9 convolution_bitcast_fusion.1
  (266 shorter events, 9.4 us)
Async XLA Ops:
  0.0 10.4 %copy-start = (f32[3,64,8]{1,2,0:T(8,128)S(1)}, f32[3,64,8]{1,2,0:T(8,128)}, u32[]{:S(2)}) copy-start(f32[3,64,8]{1,2,0:T(8,128)} %param.8) | copy-start | bytes 18436
  1.9 29.4 %collective-permute-start = (bf16[3,16,5,128]{3,2,1,0:T(8,128)(2,1)S(1)}, bf16[3,16,5,128]{3,2,1,0:T(8,128)(2,1)S(1)}, u32[]{:S(2)}, u32[]{:S(2)}) collective-permute-start(bf16[3,16,5,128]{3,2,1,0:T(8,128)(2,1)S(1)} %get-tuple-element.103), channel_id=1, source_target_pairs={{0,8},{8,16},{16,24},{24,32},{32,40},{40,48},{48,56},{1,9},{9,17},... | collective-permute-start | bytes 184328 | tf_op jit(solution)/shard_map/ppermute | solution.py:24
  5.9 25.3 %collective-permute-start.1 = (bf16[3,16,5,128]{3,2,1,0:T(8,128)(2,1)S(1)}, bf16[3,16,5,128]{3,2,1,0:T(8,128)(2,1)S(1)}, u32[]{:S(2)}, u32[]{:S(2)}) collective-permute-start(bf16[3,16,5,128]{3,2,1,0:T(8,128)(2,1)S(1)} %get-tuple-element.104), channel_id=1, source_target_pairs={{8,0},{16,8},{24,16},{32,24},{40,32},{48,40},{56,48},{9,1},{17,9},... | collective-permute-start | bytes 184328 | tf_op jit(solution)/shard_map/ppermute | solution.py:27
  11.3 19.9 %copy-start.1 = (bf16[16,16,128]{2,1,0:T(8,128)(2,1)S(1)}, bf16[16,16,128]{2,1,0:T(8,128)(2,1)}, u32[]{:S(2)}) copy-start(bf16[16,16,128]{2,1,0:T(8,128)(2,1)} %param.6) | copy-start | bytes 196612
  11.3 19.9 %copy-start.2 = (bf16[16,16,128]{2,1,0:T(8,128)(2,1)S(1)}, bf16[16,16,128]{2,1,0:T(8,128)(2,1)}, u32[]{:S(2)}) copy-start(bf16[16,16,128]{2,1,0:T(8,128)(2,1)} %param.5) | copy-start | bytes 196612
  12.9 25.0 %all-to-all-start = ((f32[4,64,80]{2,0,1:T(4,128)}), f32[4,64,80]{2,0,1:T(4,128)S(1)}, u32[]{:S(2)}, u32[]{:S(2)}) async-start(f32[4,64,80]{2,0,1:T(4,128)} %copy.111), calls=%async_computation | async-start | bytes 262144 | tf_op jit(solution)/shard_map/all_to_all | solution.py:297
  26.2 12.0 %copy-start.24 = (s32[140]{0:T(256)}, s32[140]{0:T(256)S(1)}, u32[]{:S(2)}) copy-start(s32[140]{0:T(256)S(1)} %get-tuple-element.148) | copy-start | bytes 1684
  26.2 12.0 %copy-start.27 = (s32[140]{0:T(256)}, s32[140]{0:T(256)S(1)}, u32[]{:S(2)}) copy-start(s32[140]{0:T(256)S(1)} %get-tuple-element.149) | copy-start | bytes 1684
  27.4 10.8 %copy-start.34 = (f32[140]{0:T(256)}, f32[140]{0:T(256)S(1)}, u32[]{:S(2)}) copy-start(f32[140]{0:T(256)S(1)} %get-tuple-element.150) | copy-start | bytes 1684
  27.4 10.8 %copy-start.37 = (f32[140]{0:T(256)}, f32[140]{0:T(256)S(1)}, u32[]{:S(2)}) copy-start(f32[140]{0:T(256)S(1)} %get-tuple-element.151) | copy-start | bytes 1684
  27.5 28.7 %copy-start.16 = (f32[4]{0:T(128)}, f32[4]{0:T(128)S(1)}, u32[]{:S(2)}) copy-start(f32[4]{0:T(128)S(1)} %get-tuple-element.152) | copy-start | bytes 52
  27.5 28.7 %copy-start.19 = (f32[4]{0:T(128)}, f32[4]{0:T(128)S(1)}, u32[]{:S(2)}) copy-start(f32[4]{0:T(128)S(1)} %get-tuple-element.153) | copy-start | bytes 52
  32.4 13.9 %collective-permute-start.2 = (bf16[3,16,26,9]{3,2,1,0:T(8,128)(2,1)}, bf16[3,16,26,9]{3,2,1,0:T(8,128)(2,1)S(1)}, u32[]{:S(2)}, u32[]{:S(2)}) collective-permute-start(bf16[3,16,26,9]{3,2,1,0:T(8,128)(2,1)} %get-tuple-element.76), channel_id=1, source_target_pairs={{0,1},{1,2},{2,3},{3,4},{4,5},{5,6},{6,7},{8,9},{9,10},{10,11},{11... | collective-permute-start | bytes 67400 | tf_op jit(solution)/shard_map/ppermute | solution.py:24
  35.9 10.3 %collective-permute-start.3 = (bf16[3,16,26,9]{3,2,1,0:T(8,128)(2,1)S(1)}, bf16[3,16,26,9]{3,2,1,0:T(8,128)(2,1)S(1)}, u32[]{:S(2)}, u32[]{:S(2)}) collective-permute-start(bf16[3,16,26,9]{3,2,1,0:T(8,128)(2,1)S(1)} %get-tuple-element.77), channel_id=1, source_target_pairs={{1,0},{2,1},{3,2},{4,3},{5,4},{6,5},{7,6},{9,8},{10,9},{11,10},{12... | collective-permute-start | bytes 67400 | tf_op jit(solution)/shard_map/ppermute | solution.py:27
  38.5 1.8 %copy-start.14 = (f32[640]{0:T(1024)}, f32[640]{0:T(1024)S(1)}, u32[]{:S(2)}) copy-start(f32[640]{0:T(1024)S(1)} %slice_reduce_fusion) | copy-start | bytes 7684
  40.9 13.3 %collective-permute-start.6 = (f32[3,1,6,36]{3,2,1,0:T(8,128)S(1)}, f32[3,1,6,36]{3,2,1,0:T(8,128)S(1)}, u32[]{:S(2)}, u32[]{:S(2)}) collective-permute-start(f32[3,1,6,36]{3,2,1,0:T(8,128)S(1)} %get-tuple-element.109), channel_id=1, source_target_pairs={{0,64},{64,128},{128,192},{192,256},{256,320},{320,384},{384,448},... | collective-permute-start | bytes 7784 | tf_op jit(solution)/shard_map/ppermute | solution.py:24
  44.9 9.3 %collective-permute-start.7 = (f32[3,1,6,36]{3,2,1,0:T(8,128)S(1)}, f32[3,1,6,36]{3,2,1,0:T(8,128)S(1)}, u32[]{:S(2)}, u32[]{:S(2)}) collective-permute-start(f32[3,1,6,36]{3,2,1,0:T(8,128)S(1)} %get-tuple-element.110), channel_id=1, source_target_pairs={{64,0},{128,64},{192,128},{256,192},{320,256},{384,320},{448,384},... | collective-permute-start | bytes 7784 | tf_op jit(solution)/shard_map/ppermute | solution.py:27
  47.4 10.1 %collective-permute-start.4 = (bf16[3,5,26,146]{3,2,1,0:T(8,128)(2,1)}, bf16[3,5,26,146]{3,2,1,0:T(8,128)(2,1)}, u32[]{:S(2)}, u32[]{:S(2)}) collective-permute-start(bf16[3,5,26,146]{3,2,1,0:T(8,128)(2,1)} %get-tuple-element.64), channel_id=1, source_target_pairs={{0,64},{64,128},{128,192},{192,256},{256,320},{320,384},{384,448},... | collective-permute-start | bytes 341648 | tf_op jit(solution)/shard_map/ppermute | solution.py:24
  52.8 9.1 %collective-permute-start.5 = (bf16[3,5,26,146]{3,2,1,0:T(8,128)(2,1)S(1)}, bf16[3,5,26,146]{3,2,1,0:T(8,128)(2,1)}, u32[]{:S(2)}, u32[]{:S(2)}) collective-permute-start(bf16[3,5,26,146]{3,2,1,0:T(8,128)(2,1)S(1)} %get-tuple-element.65), channel_id=1, source_target_pairs={{64,0},{128,64},{192,128},{256,192},{320,256},{384,320},{448,384},... | collective-permute-start | bytes 341648 | tf_op jit(solution)/shard_map/ppermute | solution.py:27
  54.6 0.8 copy-start.25
  54.6 0.8 copy-start.28
  54.6 0.8 copy-start.35
  54.6 0.8 copy-start.38
  55.2 0.8 copy-start.30
  55.2 0.8 copy-start.32
  66.7 4.4 %copy-start.5 = (bf16[20,20,140]{2,0,1:T(8,128)(2,1)}, bf16[20,20,140]{2,0,1:T(8,128)(2,1)S(1)}, u32[]{:S(2)}) copy-start(bf16[20,20,140]{2,0,1:T(8,128)(2,1)S(1)} %copy.142) | copy-start | bytes 336004
  67.1 4.0 %copy-start.7 = (bf16[20,20,140]{2,0,1:T(8,128)(2,1)}, bf16[20,20,140]{2,0,1:T(8,128)(2,1)S(1)}, u32[]{:S(2)}) copy-start(bf16[20,20,140]{2,0,1:T(8,128)(2,1)S(1)} %copy.143) | copy-start | bytes 336004
  67.2 0.7 copy-start.22
  67.2 0.7 copy-start.23
  67.2 0.7 copy-start.40
  67.2 0.7 copy-start.41
  67.2 0.7 copy-start.43
  67.2 0.7 copy-start.44
  67.3 3.8 %copy-start.9 = (bf16[20,20,140]{2,0,1:T(8,128)(2,1)}, bf16[20,20,140]{2,0,1:T(8,128)(2,1)S(1)}, u32[]{:S(2)}) copy-start(bf16[20,20,140]{2,0,1:T(8,128)(2,1)S(1)} %copy.144) | copy-start | bytes 336004
  67.7 3.4 %copy-start.3 = (f32[20,20,140]{2,0,1:T(8,128)}, f32[20,20,140]{2,0,1:T(8,128)S(1)}, u32[]{:S(2)}) copy-start(f32[20,20,140]{2,0,1:T(8,128)S(1)} %copy.145) | copy-start | bytes 672004
  69.8 1.3 %copy-start.12 = (f32[36,140]{1,0:T(8,128)S(1)}, f32[36,140]{1,0:T(8,128)}, u32[]{:S(2)}) copy-start(f32[36,140]{1,0:T(8,128)} %select_add_fusion) | copy-start | bytes 60484
  69.8 1.3 %copy-start.17 = (f32[4]{0:T(128)S(1)}, f32[4]{0:T(128)}, u32[]{:S(2)}) copy-start(f32[4]{0:T(128)} %copy-done.16) | copy-start | bytes 52
  69.8 1.3 %copy-start.20 = (f32[4]{0:T(128)S(1)}, f32[4]{0:T(128)}, u32[]{:S(2)}) copy-start(f32[4]{0:T(128)} %copy-done.19) | copy-start | bytes 52
  71.1 1.6 %copy-start.42 = (pred[34]{0:T(512)(128)(4,1)S(1)}, pred[34]{0:T(512)(128)(4,1)}, u32[]{:S(2)}) copy-start(pred[34]{0:T(512)(128)(4,1)} %and_or_fusion) | copy-start | bytes 106
  71.1 18.5 %copy-start.15 = (f32[640]{0:T(1024)S(1)}, f32[640]{0:T(1024)}, u32[]{:S(2)}) copy-start(f32[640]{0:T(1024)} %copy-done.14) | copy-start | bytes 7684
  72.9 6.8 %collective-permute-start.8 = (f32[3,1,4,34]{3,2,1,0:T(4,128)S(1)}, f32[3,1,4,34]{3,2,1,0:T(4,128)S(1)}, u32[]{:S(2)}, u32[]{:S(2)}) collective-permute-start(f32[3,1,4,34]{3,2,1,0:T(4,128)S(1)} %get-tuple-element.119), channel_id=1, source_target_pairs={{0,64},{64,128},{128,192},{192,256},{256,320},{320,384},{384,448},... | collective-permute-start | bytes 4904 | tf_op jit(solution)/shard_map/ppermute | solution.py:24
  78.4 5.3 %collective-permute-start.9 = (f32[3,1,4,34]{3,2,1,0:T(4,128)S(1)}, f32[3,1,4,34]{3,2,1,0:T(4,128)S(1)}, u32[]{:S(2)}, u32[]{:S(2)}) collective-permute-start(f32[3,1,4,34]{3,2,1,0:T(4,128)S(1)} %get-tuple-element.120), channel_id=1, source_target_pairs={{64,0},{128,64},{192,128},{256,192},{320,256},{384,320},{448,384},... | collective-permute-start | bytes 4904 | tf_op jit(solution)/shard_map/ppermute | solution.py:27
  83.7 6.8 %collective-permute-start.10 = (f32[3,6,1,34]{3,2,1,0:T(1,128)S(1)}, f32[3,6,1,34]{3,2,1,0:T(1,128)S(1)}, u32[]{:S(2)}, u32[]{:S(2)}) collective-permute-start(f32[3,6,1,34]{3,2,1,0:T(1,128)S(1)} %get-tuple-element.117), channel_id=1, source_target_pairs={{0,8},{8,16},{16,24},{24,32},{32,40},{40,48},{48,56},{1,9},{9,17},... | collective-permute-start | bytes 7352 | tf_op jit(solution)/shard_map/ppermute | solution.py:24
  87.5 4.4 %collective-permute-start.11 = (f32[3,6,1,34]{3,2,1,0:T(1,128)S(1)}, f32[3,6,1,34]{3,2,1,0:T(1,128)S(1)}, u32[]{:S(2)}, u32[]{:S(2)}) collective-permute-start(f32[3,6,1,34]{3,2,1,0:T(1,128)S(1)} %get-tuple-element.118), channel_id=1, source_target_pairs={{8,0},{16,8},{24,16},{32,24},{40,32},{48,40},{56,48},{9,1},{17,9},... | collective-permute-start | bytes 7352 | tf_op jit(solution)/shard_map/ppermute | solution.py:27
  92.1 1.4 %copy-start.26 = (s32[140]{0:T(256)S(1)}, s32[140]{0:T(256)}, u32[]{:S(2)}) copy-start(s32[140]{0:T(256)} %copy-done.24) | copy-start | bytes 1684
  92.1 1.3 %copy-start.29 = (s32[140]{0:T(256)S(1)}, s32[140]{0:T(256)}, u32[]{:S(2)}) copy-start(s32[140]{0:T(256)} %copy-done.27) | copy-start | bytes 1684
  92.1 1.3 %copy-start.36 = (f32[140]{0:T(256)S(1)}, f32[140]{0:T(256)}, u32[]{:S(2)}) copy-start(f32[140]{0:T(256)} %copy-done.34) | copy-start | bytes 1684
  92.1 1.3 %copy-start.39 = (f32[140]{0:T(256)S(1)}, f32[140]{0:T(256)}, u32[]{:S(2)}) copy-start(f32[140]{0:T(256)} %copy-done.37) | copy-start | bytes 1684
  92.7 1.3 %copy-start.31 = (f32[20]{0:T(128)S(1)}, f32[20]{0:T(128)}, u32[]{:S(2)}) copy-start(f32[20]{0:T(128)} %mul.1004) | copy-start | bytes 244
  92.7 1.3 %copy-start.33 = (f32[20]{0:T(128)S(1)}, f32[20]{0:T(128)}, u32[]{:S(2)}) copy-start(f32[20]{0:T(128)} %mul.1010) | copy-start | bytes 244
  95.2 1.5 %copy-start.4 = (f32[20,20,140]{2,0,1:T(8,128)S(1)}, f32[20,20,140]{2,0,1:T(8,128)}, u32[]{:S(2)}) copy-start(f32[20,20,140]{2,0,1:T(8,128)} %copy-done.3) | copy-start | bytes 672004
  95.3 1.5 %copy-start.6 = (bf16[20,20,140]{2,0,1:T(8,128)(2,1)S(1)}, bf16[20,20,140]{2,0,1:T(8,128)(2,1)}, u32[]{:S(2)}) copy-start(bf16[20,20,140]{2,0,1:T(8,128)(2,1)} %copy-done.5) | copy-start | bytes 336004
  95.3 1.5 %copy-start.8 = (bf16[20,20,140]{2,0,1:T(8,128)(2,1)S(1)}, bf16[20,20,140]{2,0,1:T(8,128)(2,1)}, u32[]{:S(2)}) copy-start(bf16[20,20,140]{2,0,1:T(8,128)(2,1)} %copy-done.7) | copy-start | bytes 336004
  95.3 1.5 %copy-start.10 = (bf16[20,20,140]{2,0,1:T(8,128)(2,1)S(1)}, bf16[20,20,140]{2,0,1:T(8,128)(2,1)}, u32[]{:S(2)}) copy-start(bf16[20,20,140]{2,0,1:T(8,128)(2,1)} %copy-done.9) | copy-start | bytes 336004
  95.3 1.5 %copy-start.13 = (f32[36,140]{1,0:T(8,128)S(1)}, f32[36,140]{1,0:T(8,128)}, u32[]{:S(2)}) copy-start(f32[36,140]{1,0:T(8,128)} %select_add_fusion) | copy-start | bytes 60484
  95.3 1.5 %copy-start.18 = (f32[4]{0:T(128)S(1)}, f32[4]{0:T(128)}, u32[]{:S(2)}) copy-start(f32[4]{0:T(128)} %copy-done.16) | copy-start | bytes 52
  95.3 1.5 %copy-start.21 = (f32[4]{0:T(128)S(1)}, f32[4]{0:T(128)}, u32[]{:S(2)}) copy-start(f32[4]{0:T(128)} %copy-done.19) | copy-start | bytes 52
  96.8 1.9 %copy-start.11 = (f32[4,4,35]{2,1,0:T(4,128)S(1)}, f32[4,4,35]{2,1,0:T(4,128)}, u32[]{:S(2)}) copy-start(f32[4,4,35]{2,1,0:T(4,128)} %slice_add_fusion.33) | copy-start | bytes 6724
  98.2 0.8 copy-start.45
  98.2 0.8 copy-start.47
  98.2 14.9 %copy-start.46 = (s32[64]{0:T(128)S(1)}, s32[64]{0:T(128)}, u32[]{:S(2)}) copy-start(s32[64]{0:T(128)} %get-tuple-element.55) | copy-start | bytes 772
  100.2 24.0 %all-to-all-start.1 = ((f32[3,64,16]{2,0,1:T(4,128)}), f32[3,64,16]{2,0,1:T(4,128)S(1)}, u32[]{:S(2)}, u32[]{:S(2)}) async-start(f32[3,64,16]{2,0,1:T(4,128)} %copy.136), calls=%async_computation.1 | async-start | bytes 262144 | tf_op jit(solution)/shard_map/all_to_all | solution.py:361

commit v12 on v6

--- a/solution.py
+++ b/solution.py
@@ -68,10 +68,10 @@
     return summed
 
 
-def derive_fields(first_padded, second_padded):
+def derive_fields(first_padded, second_padded, dimensions=(0, 1, 2)):
     first_smooth = first_padded
     second_smooth = second_padded
-    for dimension in range(3):
+    for dimension in dimensions:
         first_smooth = smooth_axis(first_smooth, dimension)
         second_smooth = smooth_axis(second_smooth, dimension)
     average = (first_smooth + second_smooth) * 0.5
@@ -230,7 +230,19 @@
     stacked = jnp.stack([reference_image, deformed_image, roi_mask.astype(jnp.bfloat16)])
     stacked = with_halo(stacked, (("gy", 2),), 5)
     stacked = with_halo(stacked, (("gz", 3),), 5 + ELEM)
-    padded_images = with_halo(stacked, (("gx", 1),), 5).astype(jnp.float32)
+    count_x = lax.axis_size("gx")
+    forward_x = [(i, i + 1) for i in range(count_x - 1)]
+    backward_x = [(target, source) for source, target in forward_x]
+    low_face = lax.ppermute(stacked[:, stacked.shape[1] - 5 :], "gx", forward_x)
+    high_face = lax.ppermute(stacked[:, :5], "gx", backward_x)
+
+    def smooth_yz(volume):
+        return smooth_axis(smooth_axis(volume.astype(jnp.float32), 2), 3)
+
+    smoothed = jnp.concatenate(
+        [smooth_yz(low_face[:2]), smooth_yz(stacked[:2]), smooth_yz(high_face[:2])], axis=1
+    )
+    mask_padded = jnp.concatenate([low_face[2], stacked[2], high_face[2]], axis=0)
     nodes_shape = (
         3,
         reference_image.shape[0] // ELEM,
@@ -326,8 +338,8 @@
     )
     extended = jnp.concatenate([low_row, middle, high_row], axis=2)
     first_padded = with_halo(extended, (("gx", 1),), 1)
-    derived = derive_fields(padded_images[0], padded_images[1])
-    region = padded_images[2][3:-3, 3:-3, 3:-3]
+    derived = derive_fields(smoothed[0], smoothed[1], (0,))
+    region = mask_padded[3:-3, 3:-3, 3:-3].astype(jnp.float32)
     contrast = derived[0].astype(jnp.float32)
     slopes = derived[1:].astype(jnp.float32)
     masked_slopes = slopes * region[None]

time: 124 us -> 131 us (1.056)
  waiting for transfers between devices: 21.5 us -> 26.1 us
  local copies, waits for them, and re-layouts: 12.4 us -> 15.7 us
    ppermute x0 -> x2, starting transfers between devices: none -> 6.61 us  [the longest x1 5.32 us: per_device(): low_face = lax.ppermute(stacked[:, stacked.shape[1] - 5:], 'gx', forward_x)]
    ppermute x6 -> x5, starting transfers between devices: 24.7 us -> 19.2 us  [with_halo(): lax.ppermute(lax.slice_in_dim(block, block.shape[dim] - width, None, axis...]
    ppermute x6 -> x5, waiting for transfers between devices: 9.66 us -> 13.6 us  [with_halo(): lax.ppermute(lax.slice_in_dim(block, 0, width, axis=dim), axis, backward)]
    ppermute x6 -> x5, waiting for transfers between devices: 0.02 us -> 2.03 us  [with_halo(): lax.ppermute(lax.slice_in_dim(block, block.shape[dim] - width, None, axis...]
    squeeze x1 -> x3, local copies, waits for them, and re-layouts: 0.07 us -> 1.88 us  [the longest x1 0.97 us: per_device(): high_face[2]]
    add x2, other arithmetic: 2.33 us -> 0.6 us  [per_device(): contrast + slopes[0] * moved[0] + slopes[1] * moved[1]]
    unnamed x62 -> x76, local copies, waits for them, and re-layouts: 0.37 us -> 1.7 us
    ppermute x6 -> x5, starting transfers between devices: 8.77 us -> 7.49 us  [with_halo(): lax.ppermute(lax.slice_in_dim(block, 0, width, axis=dim), axis, backward)]
  transfers between devices with their start and end apart: 14 -> 14, of which waited for: 5 -> 6; matrix products, arithmetic and copies ran while one was open for 15% -> 16% of each run, Pallas kernels for 0% -> 0%
where the time goes in v12:
time: 131 us; the launch traced here: 130 us
  starting transfers between devices  59.8 us (46%)
  waiting for transfers between devices  26.1 us (20%)
  other arithmetic  19.3 us (15%)
  local copies, waits for them, and re-layouts  15.7 us (12%)
  matrix products  7.51 us (6%)
  between operations  1.81 us (1%)
    ppermute x5, starting transfers between devices, with_halo(): lax.ppermute(lax.slice_in_dim(block, block.shape[dim] - width, None, axis...  19.2 us
    ppermute x5, waiting for transfers between devices, with_halo(): lax.ppermute(lax.slice_in_dim(block, 0, width, axis=dim), axis, backward)  13.6 us
    all_to_all x1, starting transfers between devices, per_device(): lax.all_to_all(send_outgoing, ('gy', 'gz'), split_axis=1, concat_axis=1,...  13.3 us
    all_to_all x1, starting transfers between devices, per_device(): lax.all_to_all(outgoing, ('gy', 'gz'), split_axis=1, concat_axis=1, tiled...  13.2 us
    all_to_all x1, waiting for transfers between devices, per_device(): lax.all_to_all(outgoing, ('gy', 'gz'), split_axis=1, concat_axis=1, tiled...  10.4 us
    ppermute x5, starting transfers between devices, with_halo(): lax.ppermute(lax.slice_in_dim(block, 0, width, axis=dim), axis, backward)  7.49 us
    ppermute x1, starting transfers between devices, per_device(): low_face = lax.ppermute(stacked[:, stacked.shape[1] - 5:], 'gx', forward_x)  5.32 us
    dot_general x3, matrix products, collect(): jnp.dot(volume.reshape(-1, shape_all[3]), table_back, precision=highest)  4.16 us
  transfers between devices with their start and end apart: 14, of which 6 were waited for; matrix products, arithmetic and copies ran while one was open for 16% of the time, Pallas kernels for 0%

profile of v12, /device:TPU:1, one launch (start us, length us, event | category | flops | bytes accessed | tf_op | source)
XLA Modules:
  0.0 130.2 jit_solution(12313199345198799329)
XLA Ops:
  0.0 0.9 convert_bitcast_fusion
  0.9 0.9 pad_maximum_fusion.6
  1.9 4.0 %collective-permute-start = (bf16[3,16,5,128]{3,2,1,0:T(8,128)(2,1)S(1)}, bf16[3,16,5,128]{3,2,1,0:T(8,128)(2,1)S(1)}, u32[]{:S(2)}, u32[]{:S(2)}) collective-permute-start(bf16[3,16,5,128]{3,2,1,0:T(8,128)(2,1)S(1)} %get-tuple-element.99), channel_id=1, source_target_pairs={{0,8},{8,16},{16,24},{24,32},{32,40},{40,48},{48,56},{1,9},{9,17},... | collective-permute-start | bytes 184328 | tf_op jit(solution)/shard_map/ppermute | solution.py:24
  5.9 1.3 collective-permute-start.1
  7.2 0.7 broadcast_add_fusion.1
  7.9 1.2 and_and_fusion
  9.3 0.3 convert_reduce_fusion
  9.8 0.5 copy-done.11
  10.3 1.1 concatenate.71
  11.4 0.7 fusion.7
  12.1 0.4 copy.110
  12.5 0.4 all_to_all.12
  12.9 0.7 copy.111
  13.6 13.3 %all-to-all-start = ((f32[4,64,80]{2,0,1:T(4,128)}), f32[4,64,80]{2,0,1:T(4,128)S(1)}, u32[]{:S(2)}, u32[]{:S(2)}) async-start(f32[4,64,80]{2,0,1:T(4,128)} %copy.111), calls=%async_computation | async-start | bytes 262144 | tf_op jit(solution)/shard_map/all_to_all | solution.py:309
  27.0 0.6 fusion.189
  27.6 0.6 fusion.184
  28.2 0.6 iota_compare_fusion.7
  28.8 0.6 iota_compare_fusion.8
  29.4 0.6 select_add_fusion
  30.5 3.5 %collective-permute-start.2 = (bf16[3,16,26,9]{3,2,1,0:T(8,128)(2,1)S(1)}, bf16[3,16,26,9]{3,2,1,0:T(8,128)(2,1)S(1)}, u32[]{:S(2)}, u32[]{:S(2)}) collective-permute-start(bf16[3,16,26,9]{3,2,1,0:T(8,128)(2,1)S(1)} %get-tuple-element.70), channel_id=1, source_target_pairs={{0,1},{1,2},{2,3},{3,4},{4,5},{5,6},{6,7},{8,9},{9,10},{10,11},{11... | collective-permute-start | bytes 67400 | tf_op jit(solution)/shard_map/ppermute | solution.py:24
  34.0 1.9 %collective-permute-start.3 = (bf16[3,16,26,9]{3,2,1,0:T(8,128)(2,1)S(1)}, bf16[3,16,26,9]{3,2,1,0:T(8,128)(2,1)S(1)}, u32[]{:S(2)}, u32[]{:S(2)}) collective-permute-start(bf16[3,16,26,9]{3,2,1,0:T(8,128)(2,1)S(1)} %get-tuple-element.71), channel_id=1, source_target_pairs={{1,0},{2,1},{3,2},{4,3},{5,4},{6,5},{7,6},{9,8},{10,9},{11,10},{12... | collective-permute-start | bytes 67400 | tf_op jit(solution)/shard_map/ppermute | solution.py:27
  35.9 0.6 and_or_fusion
  36.7 2.0 %collective-permute-done.2 = bf16[3,16,26,9]{3,2,1,0:T(8,128)(2,1)S(1)} collective-permute-done((bf16[3,16,26,9]{3,2,1,0:T(8,128)(2,1)S(1)}, bf16[3,16,26,9]{3,2,1,0:T(8,128)(2,1)S(1)}, u32[]{:S(2)}, u32[]{:S(2)}) %collective-permute-start.2) | collective-permute-done | bytes 22496 | tf_op jit(solution)/shard_map/ppermute | solution.py:24
  38.7 4.4 %collective-permute-done.3 = bf16[3,16,26,9]{3,2,1,0:T(8,128)(2,1)S(1)} collective-permute-done((bf16[3,16,26,9]{3,2,1,0:T(8,128)(2,1)S(1)}, bf16[3,16,26,9]{3,2,1,0:T(8,128)(2,1)S(1)}, u32[]{:S(2)}, u32[]{:S(2)}) %collective-permute-start.3) | collective-permute-done | bytes 22496 | tf_op jit(solution)/shard_map/ppermute | solution.py:27
  43.1 0.7 pad_maximum_fusion.1
  43.9 0.9 fusion.214
  44.8 1.3 collective-permute-start.5
  46.1 5.3 %collective-permute-start.4 = (bf16[3,5,26,146]{3,2,1,0:T(8,128)(2,1)}, bf16[3,5,26,146]{3,2,1,0:T(8,128)(2,1)}, u32[]{:S(2)}, u32[]{:S(2)}) collective-permute-start(bf16[3,5,26,146]{3,2,1,0:T(8,128)(2,1)} %get-tuple-element.60), channel_id=1, source_target_pairs={{0,64},{64,128},{128,192},{192,256},{256,320},{320,384},{384,448},... | collective-permute-start | bytes 341648 | tf_op jit(solution)/shard_map/ppermute | solution.py:236
  51.5 0.4 fusion.15
  51.9 0.9 fusion.11
  52.8 0.4 reshape.465
  54.0 0.8 fusion.8
  54.8 0.3 copy.115
  55.8 3.3 %collective-permute-start.6 = (f32[3,1,6,36]{3,2,1,0:T(8,128)S(1)}, f32[3,1,6,36]{3,2,1,0:T(8,128)S(1)}, u32[]{:S(2)}, u32[]{:S(2)}) collective-permute-start(f32[3,1,6,36]{3,2,1,0:T(8,128)S(1)} %get-tuple-element.105), channel_id=1, source_target_pairs={{0,64},{64,128},{128,192},{192,256},{256,320},{320,384},{384,448},... | collective-permute-start | bytes 7784 | tf_op jit(solution)/shard_map/ppermute | solution.py:24
  59.2 1.5 %collective-permute-start.7 = (f32[3,1,6,36]{3,2,1,0:T(8,128)S(1)}, f32[3,1,6,36]{3,2,1,0:T(8,128)S(1)}, u32[]{:S(2)}, u32[]{:S(2)}) collective-permute-start(f32[3,1,6,36]{3,2,1,0:T(8,128)S(1)} %get-tuple-element.106), channel_id=1, source_target_pairs={{64,0},{128,64},{192,128},{256,192},{320,256},{384,320},{448,384},... | collective-permute-start | bytes 7784 | tf_op jit(solution)/shard_map/ppermute | solution.py:27
  60.7 3.6 %collective-permute-done.7 = f32[3,1,6,36]{3,2,1,0:T(8,128)S(1)} collective-permute-done((f32[3,1,6,36]{3,2,1,0:T(8,128)S(1)}, f32[3,1,6,36]{3,2,1,0:T(8,128)S(1)}, u32[]{:S(2)}, u32[]{:S(2)}) %collective-permute-start.7) | collective-permute-done | bytes 2624 | tf_op jit(solution)/shard_map/ppermute | solution.py:27
  65.4 0.4 fusion.66
  66.1 0.4 multiply_add_fusion.1
  67.5 0.9 slice_convert_fusion.1
  68.6 0.9 slice_convert_fusion.2
  69.7 0.6 fusion.48
  70.3 0.3 fusion.45
  71.1 0.3 fusion.42
  72.0 1.0 slice_bitcast_fusion.4
  72.9 0.9 slice_bitcast_fusion.5
  74.2 1.4 %multiply_reduce_fusion.3 = (f32[3,20,5,34]{3,1,2,0:T(8,128)S(1)}, f32[3,20,5,34]{3,1,2,0:T(8,128)S(1)}) fusion(f32[4]{0:T(128)S(1)} %copy-done.35, f32[4]{0:T(128)S(1)} %copy-done.34, pred[36,140]{1,0:T(8,128)(4,1)S(1)} %copy-done.18, pred[36,140]{1,0:T(8,128)(4,1)S(1)} %copy-done.19, f32[140]{0:T(256)S(1)} %copy-done.32, f32[140]{0:T(256)S(1)} %copy-done.33, ...), kind=kOutput, calls=%fused_computation.45 | convolution fusion | flops 69541080 | bytes 652832 | tf_op jit(solution)/shard_map/dot_general | solution.py:219
  76.9 1.4 %multiply_reduce_fusion.5 = (f32[3,20,5,34]{3,1,2,0:T(8,128)S(1)}, f32[3,20,5,34]{3,1,2,0:T(8,128)S(1)}) fusion(f32[4]{0:T(128)S(1)} %copy-done.17, f32[4]{0:T(128)S(1)} %copy-done.15, f32[36,140]{1,0:T(8,128)S(1)} %copy-done.10, f32[20,5,4,140]{3,0,2,1:T(8,128)S(1)} %bitcast.491, f32[20,5,4,140]{3,0,2,1:T(8,128)S(1)} %bitcast.488, ...), kind=kOutput, calls=%fused_computation.47 | convolution fusion | flops 69526800 | bytes 885792 | tf_op jit(solution)/shard_map/dot_general | solution.py:219
  78.6 5.2 %collective-permute-start.8 = (f32[3,1,4,34]{3,2,1,0:T(4,128)S(1)}, f32[3,1,4,34]{3,2,1,0:T(4,128)S(1)}, u32[]{:S(2)}, u32[]{:S(2)}) collective-permute-start(f32[3,1,4,34]{3,2,1,0:T(4,128)S(1)} %get-tuple-element.115), channel_id=1, source_target_pairs={{0,64},{64,128},{128,192},{192,256},{256,320},{320,384},{384,448},... | collective-permute-start | bytes 4904 | tf_op jit(solution)/shard_map/ppermute | solution.py:24
  83.8 1.3 collective-permute-start.9
  85.1 3.1 %collective-permute-done.9 = f32[3,1,4,34]{3,2,1,0:T(4,128)S(1)} collective-permute-done((f32[3,1,4,34]{3,2,1,0:T(4,128)S(1)}, f32[3,1,4,34]{3,2,1,0:T(4,128)S(1)}, u32[]{:S(2)}, u32[]{:S(2)}) %collective-permute-start.9) | collective-permute-done | bytes 1664 | tf_op jit(solution)/shard_map/ppermute | solution.py:27
  88.2 3.1 %collective-permute-start.10 = (f32[3,6,1,34]{3,2,1,0:T(1,128)S(1)}, f32[3,6,1,34]{3,2,1,0:T(1,128)S(1)}, u32[]{:S(2)}, u32[]{:S(2)}) collective-permute-start(f32[3,6,1,34]{3,2,1,0:T(1,128)S(1)} %get-tuple-element.113), channel_id=1, source_target_pairs={{0,8},{8,16},{16,24},{24,32},{32,40},{40,48},{48,56},{1,9},{9,17},... | collective-permute-start | bytes 7352 | tf_op jit(solution)/shard_map/ppermute | solution.py:24
  91.3 1.5 %collective-permute-start.11 = (f32[3,6,1,34]{3,2,1,0:T(1,128)S(1)}, f32[3,6,1,34]{3,2,1,0:T(1,128)S(1)}, u32[]{:S(2)}, u32[]{:S(2)}) collective-permute-start(f32[3,6,1,34]{3,2,1,0:T(1,128)S(1)} %get-tuple-element.114), channel_id=1, source_target_pairs={{8,0},{16,8},{24,16},{32,24},{40,32},{48,40},{56,48},{9,1},{17,9},... | collective-permute-start | bytes 7352 | tf_op jit(solution)/shard_map/ppermute | solution.py:27
  93.2 2.6 %collective-permute-done.11 = f32[3,6,1,34]{3,2,1,0:T(1,128)S(1)} collective-permute-done((f32[3,6,1,34]{3,2,1,0:T(1,128)S(1)}, f32[3,6,1,34]{3,2,1,0:T(1,128)S(1)}, u32[]{:S(2)}, u32[]{:S(2)}) %collective-permute-start.11) | collective-permute-done | bytes 2480 | tf_op jit(solution)/shard_map/ppermute | solution.py:27
  96.7 0.4 fusion.99
  97.4 0.4 multiply_add_fusion
  97.8 1.0 fusion.212
  99.1 1.1 squeeze.136
  100.7 0.5 copy-done.3
  101.5 1.4 %multiply_reduce_fusion.1 = (f32[3,20,5,34]{3,1,2,0:T(8,128)S(1)}, f32[3,20,5,34]{3,1,2,0:T(8,128)S(1)}) fusion(f32[4]{0:T(128)S(1)} %copy-done.17, f32[4]{0:T(128)S(1)} %copy-done.15, f32[36,140]{1,0:T(8,128)S(1)} %copy-done.10, f32[20,5,4,140]{3,0,2,1:T(8,128)S(1)} %bitcast.490, f32[20,5,4,140]{3,0,2,1:T(8,128)S(1)} %bitcast.489, ...), kind=kOutput, calls=%fused_computation.42 | convolution fusion | flops 69526800 | bytes 885792 | tf_op jit(solution)/shard_map/dot_general | solution.py:219
  104.2 0.7 copy.136
  104.9 13.2 %all-to-all-start.1 = ((f32[3,64,16]{2,0,1:T(4,128)}), f32[3,64,16]{2,0,1:T(4,128)S(1)}, u32[]{:S(2)}, u32[]{:S(2)}) async-start(f32[3,64,16]{2,0,1:T(4,128)} %copy.136), calls=%async_computation.1 | async-start | bytes 262144 | tf_op jit(solution)/shard_map/all_to_all | solution.py:373
  118.1 0.7 slice_add_fusion.57
  118.7 10.4 %all-to-all-done.1 = f32[3,64,16]{2,0,1:T(4,128)S(1)} async-done(((f32[3,64,16]{2,0,1:T(4,128)}), f32[3,64,16]{2,0,1:T(4,128)S(1)}, u32[]{:S(2)}, u32[]{:S(2)}) %all-to-all-start.1) | async-done | bytes 12320 | tf_op jit(solution)/shard_map/all_to_all | solution.py:373
  129.3 0.9 convolution_bitcast_fusion
  (245 shorter events, 11.2 us)
Async XLA Ops:
  1.9 28.2 %collective-permute-start = (bf16[3,16,5,128]{3,2,1,0:T(8,128)(2,1)S(1)}, bf16[3,16,5,128]{3,2,1,0:T(8,128)(2,1)S(1)}, u32[]{:S(2)}, u32[]{:S(2)}) collective-permute-start(bf16[3,16,5,128]{3,2,1,0:T(8,128)(2,1)S(1)} %get-tuple-element.99), channel_id=1, source_target_pairs={{0,8},{8,16},{16,24},{24,32},{32,40},{40,48},{48,56},{1,9},{9,17},... | collective-permute-start | bytes 184328 | tf_op jit(solution)/shard_map/ppermute | solution.py:24
  5.9 24.2 %collective-permute-start.1 = (bf16[3,16,5,128]{3,2,1,0:T(8,128)(2,1)S(1)}, bf16[3,16,5,128]{3,2,1,0:T(8,128)(2,1)S(1)}, u32[]{:S(2)}, u32[]{:S(2)}) collective-permute-start(bf16[3,16,5,128]{3,2,1,0:T(8,128)(2,1)S(1)} %get-tuple-element.100), channel_id=1, source_target_pairs={{8,0},{16,8},{24,16},{32,24},{40,32},{48,40},{56,48},{9,1},{17,9},... | collective-permute-start | bytes 184328 | tf_op jit(solution)/shard_map/ppermute | solution.py:27
  9.7 0.6 copy-start.11
  12.1 18.0 %copy-start = (bf16[16,16,128]{2,1,0:T(8,128)(2,1)S(1)}, bf16[16,16,128]{2,1,0:T(8,128)(2,1)}, u32[]{:S(2)}) copy-start(bf16[16,16,128]{2,1,0:T(8,128)(2,1)} %param.6) | copy-start | bytes 196612
  12.1 18.0 %copy-start.1 = (bf16[16,16,128]{2,1,0:T(8,128)(2,1)S(1)}, bf16[16,16,128]{2,1,0:T(8,128)(2,1)}, u32[]{:S(2)}) copy-start(bf16[16,16,128]{2,1,0:T(8,128)(2,1)} %param.5) | copy-start | bytes 196612
  13.6 39.2 %all-to-all-start = ((f32[4,64,80]{2,0,1:T(4,128)}), f32[4,64,80]{2,0,1:T(4,128)S(1)}, u32[]{:S(2)}, u32[]{:S(2)}) async-start(f32[4,64,80]{2,0,1:T(4,128)} %copy.111), calls=%async_computation | async-start | bytes 262144 | tf_op jit(solution)/shard_map/all_to_all | solution.py:309
  27.0 38.4 %copy-start.20 = (s32[140]{0:T(256)}, s32[140]{0:T(256)S(1)}, u32[]{:S(2)}) copy-start(s32[140]{0:T(256)S(1)} %get-tuple-element.144) | copy-start | bytes 1684
  27.0 38.4 %copy-start.22 = (s32[140]{0:T(256)}, s32[140]{0:T(256)S(1)}, u32[]{:S(2)}) copy-start(s32[140]{0:T(256)S(1)} %get-tuple-element.145) | copy-start | bytes 1684
  28.2 37.2 %copy-start.28 = (f32[140]{0:T(256)}, f32[140]{0:T(256)S(1)}, u32[]{:S(2)}) copy-start(f32[140]{0:T(256)S(1)} %get-tuple-element.146) | copy-start | bytes 1684
  28.2 37.2 %copy-start.30 = (f32[140]{0:T(256)}, f32[140]{0:T(256)S(1)}, u32[]{:S(2)}) copy-start(f32[140]{0:T(256)S(1)} %get-tuple-element.147) | copy-start | bytes 1684
  30.1 36.1 %copy-start.14 = (f32[4]{0:T(128)}, f32[4]{0:T(128)S(1)}, u32[]{:S(2)}) copy-start(f32[4]{0:T(128)S(1)} %get-tuple-element.148) | copy-start | bytes 52
  30.1 36.1 %copy-start.16 = (f32[4]{0:T(128)}, f32[4]{0:T(128)S(1)}, u32[]{:S(2)}) copy-start(f32[4]{0:T(128)S(1)} %get-tuple-element.149) | copy-start | bytes 52
  30.5 8.2 %collective-permute-start.2 = (bf16[3,16,26,9]{3,2,1,0:T(8,128)(2,1)S(1)}, bf16[3,16,26,9]{3,2,1,0:T(8,128)(2,1)S(1)}, u32[]{:S(2)}, u32[]{:S(2)}) collective-permute-start(bf16[3,16,26,9]{3,2,1,0:T(8,128)(2,1)S(1)} %get-tuple-element.70), channel_id=1, source_target_pairs={{0,1},{1,2},{2,3},{3,4},{4,5},{5,6},{6,7},{8,9},{9,10},{10,11},{11... | collective-permute-start | bytes 67400 | tf_op jit(solution)/shard_map/ppermute | solution.py:24
  34.0 9.1 %collective-permute-start.3 = (bf16[3,16,26,9]{3,2,1,0:T(8,128)(2,1)S(1)}, bf16[3,16,26,9]{3,2,1,0:T(8,128)(2,1)S(1)}, u32[]{:S(2)}, u32[]{:S(2)}) collective-permute-start(bf16[3,16,26,9]{3,2,1,0:T(8,128)(2,1)S(1)} %get-tuple-element.71), channel_id=1, source_target_pairs={{1,0},{2,1},{3,2},{4,3},{5,4},{6,5},{7,6},{9,8},{10,9},{11,10},{12... | collective-permute-start | bytes 67400 | tf_op jit(solution)/shard_map/ppermute | solution.py:27
  36.6 29.3 %copy-start.24 = (f32[20]{0:T(128)}, f32[20]{0:T(128)S(1)}, u32[]{:S(2)}) copy-start(f32[20]{0:T(128)S(1)} %mul.1044) | copy-start | bytes 244
  36.7 29.2 %copy-start.26 = (f32[20]{0:T(128)}, f32[20]{0:T(128)S(1)}, u32[]{:S(2)}) copy-start(f32[20]{0:T(128)S(1)} %mul.1050) | copy-start | bytes 244
  44.8 22.6 %collective-permute-start.5 = (bf16[3,5,26,146]{3,2,1,0:T(8,128)(2,1)}, bf16[3,5,26,146]{3,2,1,0:T(8,128)(2,1)}, u32[]{:S(2)}, u32[]{:S(2)}) collective-permute-start(bf16[3,5,26,146]{3,2,1,0:T(8,128)(2,1)} %get-tuple-element.61), channel_id=1, source_target_pairs={{64,0},{128,64},{192,128},{256,192},{320,256},{384,320},{448,384},... | collective-permute-start | bytes 341648 | tf_op jit(solution)/shard_map/ppermute | solution.py:237
  46.1 22.4 %collective-permute-start.4 = (bf16[3,5,26,146]{3,2,1,0:T(8,128)(2,1)}, bf16[3,5,26,146]{3,2,1,0:T(8,128)(2,1)}, u32[]{:S(2)}, u32[]{:S(2)}) collective-permute-start(bf16[3,5,26,146]{3,2,1,0:T(8,128)(2,1)} %get-tuple-element.60), channel_id=1, source_target_pairs={{0,64},{64,128},{128,192},{192,256},{256,320},{320,384},{384,448},... | collective-permute-start | bytes 341648 | tf_op jit(solution)/shard_map/ppermute | solution.py:236
  53.3 1.8 %copy-start.12 = (f32[640]{0:T(1024)}, f32[640]{0:T(1024)S(1)}, u32[]{:S(2)}) copy-start(f32[640]{0:T(1024)S(1)} %slice_reduce_fusion) | copy-start | bytes 7684
  55.8 4.8 %collective-permute-start.6 = (f32[3,1,6,36]{3,2,1,0:T(8,128)S(1)}, f32[3,1,6,36]{3,2,1,0:T(8,128)S(1)}, u32[]{:S(2)}, u32[]{:S(2)}) collective-permute-start(f32[3,1,6,36]{3,2,1,0:T(8,128)S(1)} %get-tuple-element.105), channel_id=1, source_target_pairs={{0,64},{64,128},{128,192},{192,256},{256,320},{320,384},{384,448},... | collective-permute-start | bytes 7784 | tf_op jit(solution)/shard_map/ppermute | solution.py:24
  59.2 5.1 %collective-permute-start.7 = (f32[3,1,6,36]{3,2,1,0:T(8,128)S(1)}, f32[3,1,6,36]{3,2,1,0:T(8,128)S(1)}, u32[]{:S(2)}, u32[]{:S(2)}) collective-permute-start(f32[3,1,6,36]{3,2,1,0:T(8,128)S(1)} %get-tuple-element.106), channel_id=1, source_target_pairs={{64,0},{128,64},{192,128},{256,192},{320,256},{384,320},{448,384},... | collective-permute-start | bytes 7784 | tf_op jit(solution)/shard_map/ppermute | solution.py:27
  71.5 5.1 %copy-start.4 = (bf16[20,20,140]{2,0,1:T(8,128)(2,1)}, bf16[20,20,140]{2,0,1:T(8,128)(2,1)S(1)}, u32[]{:S(2)}) copy-start(bf16[20,20,140]{2,0,1:T(8,128)(2,1)S(1)} %copy.143) | copy-start | bytes 336004
  71.6 4.9 %copy-start.6 = (bf16[20,20,140]{2,0,1:T(8,128)(2,1)}, bf16[20,20,140]{2,0,1:T(8,128)(2,1)S(1)}, u32[]{:S(2)}) copy-start(bf16[20,20,140]{2,0,1:T(8,128)(2,1)S(1)} %copy.144) | copy-start | bytes 336004
  71.8 2.3 %copy-start.18 = (pred[36,140]{1,0:T(8,128)(4,1)S(1)}, pred[36,140]{1,0:T(8,128)(4,1)}, u32[]{:S(2)}) copy-start(pred[36,140]{1,0:T(8,128)(4,1)} %iota_compare_fusion.7) | copy-start | bytes 15124
  71.9 2.3 %copy-start.19 = (pred[36,140]{1,0:T(8,128)(4,1)S(1)}, pred[36,140]{1,0:T(8,128)(4,1)}, u32[]{:S(2)}) copy-start(pred[36,140]{1,0:T(8,128)(4,1)} %iota_compare_fusion.8) | copy-start | bytes 15124
  71.9 2.3 %copy-start.32 = (f32[140]{0:T(256)S(1)}, f32[140]{0:T(256)}, u32[]{:S(2)}) copy-start(f32[140]{0:T(256)} %get-tuple-element.152) | copy-start | bytes 1684
  71.9 2.3 %copy-start.33 = (f32[140]{0:T(256)S(1)}, f32[140]{0:T(256)}, u32[]{:S(2)}) copy-start(f32[140]{0:T(256)} %get-tuple-element.153) | copy-start | bytes 1684
  71.9 2.3 %copy-start.34 = (f32[4]{0:T(128)S(1)}, f32[4]{0:T(128)}, u32[]{:S(2)}) copy-start(f32[4]{0:T(128)} %get-tuple-element.154) | copy-start | bytes 52
  71.9 2.3 %copy-start.35 = (f32[4]{0:T(128)S(1)}, f32[4]{0:T(128)}, u32[]{:S(2)}) copy-start(f32[4]{0:T(128)} %get-tuple-element.155) | copy-start | bytes 52
  72.0 4.6 %copy-start.8 = (bf16[20,20,140]{2,0,1:T(8,128)(2,1)}, bf16[20,20,140]{2,0,1:T(8,128)(2,1)S(1)}, u32[]{:S(2)}) copy-start(bf16[20,20,140]{2,0,1:T(8,128)(2,1)S(1)} %copy.142) | copy-start | bytes 336004
  74.2 2.4 %copy-start.2 = (f32[20,20,140]{2,0,1:T(8,128)}, f32[20,20,140]{2,0,1:T(8,128)S(1)}, u32[]{:S(2)}) copy-start(f32[20,20,140]{2,0,1:T(8,128)S(1)} %copy.145) | copy-start | bytes 672004
  76.1 0.8 copy-start.10
  76.1 0.8 copy-start.15
  76.1 0.8 copy-start.17
  76.9 1.6 %copy-start.36 = (pred[34]{0:T(512)(128)(4,1)S(1)}, pred[34]{0:T(512)(128)(4,1)}, u32[]{:S(2)}) copy-start(pred[34]{0:T(512)(128)(4,1)} %and_or_fusion) | copy-start | bytes 106
  76.9 16.0 %copy-start.13 = (f32[640]{0:T(1024)S(1)}, f32[640]{0:T(1024)}, u32[]{:S(2)}) copy-start(f32[640]{0:T(1024)} %copy-done.12) | copy-start | bytes 7684
  78.6 6.5 %collective-permute-start.8 = (f32[3,1,4,34]{3,2,1,0:T(4,128)S(1)}, f32[3,1,4,34]{3,2,1,0:T(4,128)S(1)}, u32[]{:S(2)}, u32[]{:S(2)}) collective-permute-start(f32[3,1,4,34]{3,2,1,0:T(4,128)S(1)} %get-tuple-element.115), channel_id=1, source_target_pairs={{0,64},{64,128},{128,192},{192,256},{256,320},{320,384},{384,448},... | collective-permute-start | bytes 4904 | tf_op jit(solution)/shard_map/ppermute | solution.py:24
  83.8 4.4 %collective-permute-start.9 = (f32[3,1,4,34]{3,2,1,0:T(4,128)S(1)}, f32[3,1,4,34]{3,2,1,0:T(4,128)S(1)}, u32[]{:S(2)}, u32[]{:S(2)}) collective-permute-start(f32[3,1,4,34]{3,2,1,0:T(4,128)S(1)} %get-tuple-element.116), channel_id=1, source_target_pairs={{64,0},{128,64},{192,128},{256,192},{320,256},{384,320},{448,384},... | collective-permute-start | bytes 4904 | tf_op jit(solution)/shard_map/ppermute | solution.py:27
  88.2 4.9 %collective-permute-start.10 = (f32[3,6,1,34]{3,2,1,0:T(1,128)S(1)}, f32[3,6,1,34]{3,2,1,0:T(1,128)S(1)}, u32[]{:S(2)}, u32[]{:S(2)}) collective-permute-start(f32[3,6,1,34]{3,2,1,0:T(1,128)S(1)} %get-tuple-element.113), channel_id=1, source_target_pairs={{0,8},{8,16},{16,24},{24,32},{32,40},{40,48},{48,56},{1,9},{9,17},... | collective-permute-start | bytes 7352 | tf_op jit(solution)/shard_map/ppermute | solution.py:24
  91.3 4.4 %collective-permute-start.11 = (f32[3,6,1,34]{3,2,1,0:T(1,128)S(1)}, f32[3,6,1,34]{3,2,1,0:T(1,128)S(1)}, u32[]{:S(2)}, u32[]{:S(2)}) collective-permute-start(f32[3,6,1,34]{3,2,1,0:T(1,128)S(1)} %get-tuple-element.114), channel_id=1, source_target_pairs={{8,0},{16,8},{24,16},{32,24},{40,32},{48,40},{56,48},{9,1},{17,9},... | collective-permute-start | bytes 7352 | tf_op jit(solution)/shard_map/ppermute | solution.py:27
  95.9 0.8 copy-start.21
  95.9 0.8 copy-start.23
  95.9 0.8 copy-start.29
  95.9 0.8 copy-start.31
  96.4 0.7 copy-start.25
  96.5 0.7 copy-start.27
  100.2 1.0 copy-start.3
  100.2 1.1 copy-start.5
  100.2 1.2 copy-start.7
  100.2 1.3 copy-start.9
  102.9 15.2 %copy-start.37 = (s32[64]{0:T(128)S(1)}, s32[64]{0:T(128)}, u32[]{:S(2)}) copy-start(s32[64]{0:T(128)} %get-tuple-element.53) | copy-start | bytes 772
  104.9 24.3 %all-to-all-start.1 = ((f32[3,64,16]{2,0,1:T(4,128)}), f32[3,64,16]{2,0,1:T(4,128)S(1)}, u32[]{:S(2)}, u32[]{:S(2)}) async-start(f32[3,64,16]{2,0,1:T(4,128)} %copy.136), calls=%async_computation.1 | async-start | bytes 262144 | tf_op jit(solution)/shard_map/all_to_all | solution.py:373

commit v13 on v6

--- a/solution.py
+++ b/solution.py
@@ -342,7 +342,7 @@
         (column == ez + 1) & (lax.axis_index("gz") == size_z - 1)
     )
     wide_values = jnp.where(ghost, 0.0, wide_values)
-    padded = with_halo(wide_values, (("gx", 1), ("gy", 2)), 1)
+    padded = with_halo(wide_values, (("gy", 2), ("gx", 1)), 1)
     padded = jnp.pad(padded, ((0, 0), (0, 0), (0, 0), (1, 1)))
     moved = spread(padded, wide_table)
     residual = contrast + slopes[0] * moved[0] + slopes[1] * moved[1] + slopes[2] * moved[2]

time: 124 us -> 124 us (level)
  no operation moved by 1% of the time
where the time goes in v13:
time: 124 us; the launch traced here: 123 us
  starting transfers between devices  60.6 us (49%)
  waiting for transfers between devices  21.6 us (17%)
  other arithmetic  19.6 us (16%)
  local copies, waits for them, and re-layouts  12.4 us (10%)
  matrix products  7.49 us (6%)
  between operations  1.7 us (1%)
    ppermute x6, starting transfers between devices, with_halo(): lax.ppermute(lax.slice_in_dim(block, block.shape[dim] - width, None, axis...  24.7 us
    all_to_all x1, starting transfers between devices, per_device(): lax.all_to_all(outgoing, ('gy', 'gz'), split_axis=1, concat_axis=1, tiled...  13.8 us
    all_to_all x1, starting transfers between devices, per_device(): lax.all_to_all(send_outgoing, ('gy', 'gz'), split_axis=1, concat_axis=1,...  13.3 us
    all_to_all x1, waiting for transfers between devices, per_device(): lax.all_to_all(outgoing, ('gy', 'gz'), split_axis=1, concat_axis=1, tiled...  11.1 us
    ppermute x6, waiting for transfers between devices, with_halo(): lax.ppermute(lax.slice_in_dim(block, 0, width, axis=dim), axis, backward)  9.7 us
    ppermute x6, starting transfers between devices, with_halo(): lax.ppermute(lax.slice_in_dim(block, 0, width, axis=dim), axis, backward)  8.77 us
    dot_general x3, matrix products, collect(): jnp.dot(volume.reshape(-1, shape_all[3]), table_back, precision=highest)  4.16 us
    unnamed x4, matrix products  2.57 us
  transfers between devices with their start and end apart: 14, of which 5 were waited for; matrix products, arithmetic and copies ran while one was open for 15% of the time, Pallas kernels for 0%

profile of v13, /device:TPU:1, one launch (start us, length us, event | category | flops | bytes accessed | tf_op | source)
XLA Modules:
  0.0 123.3 jit_solution(1488054077380853890)
XLA Ops:
  0.0 0.9 convert_bitcast_fusion
  0.9 0.9 pad_maximum_fusion.9
  1.9 4.0 %collective-permute-start = (bf16[3,16,5,128]{3,2,1,0:T(8,128)(2,1)S(1)}, bf16[3,16,5,128]{3,2,1,0:T(8,128)(2,1)S(1)}, u32[]{:S(2)}, u32[]{:S(2)}) collective-permute-start(bf16[3,16,5,128]{3,2,1,0:T(8,128)(2,1)S(1)} %get-tuple-element.103), channel_id=1, source_target_pairs={{0,8},{8,16},{16,24},{24,32},{32,40},{40,48},{48,56},{1,9},{9,17},... | collective-permute-start | bytes 184328 | tf_op jit(solution)/shard_map/ppermute | solution.py:24
  5.9 1.3 %collective-permute-start.1 = (bf16[3,16,5,128]{3,2,1,0:T(8,128)(2,1)S(1)}, bf16[3,16,5,128]{3,2,1,0:T(8,128)(2,1)S(1)}, u32[]{:S(2)}, u32[]{:S(2)}) collective-permute-start(bf16[3,16,5,128]{3,2,1,0:T(8,128)(2,1)S(1)} %get-tuple-element.104), channel_id=1, source_target_pairs={{8,0},{16,8},{24,16},{32,24},{40,32},{48,40},{56,48},{9,1},{17,9},... | collective-permute-start | bytes 184328 | tf_op jit(solution)/shard_map/ppermute | solution.py:27
  7.2 0.7 broadcast_add_fusion.1
  7.9 1.2 %and_and_fusion = (pred[64]{0:T(512)(128)(4,1)S(1)}, s32[64]{0:T(128)S(1)}, s32[64]{0:T(128)S(1)}, s32[64]{0:T(128)S(1)}, s32[64]{0:T(128)S(1)}, /*index=5*/s32[64]{0:T(128)}) fusion(s32[64]{0:T(128)S(1)} %get-tuple-element.49, s32[64]{0:T(128)} %param.9), kind=kLoop, calls=%fused_computation.423 | loop fusion | flops 4928 | bytes 1856 | tf_op jit(solution)/shard_map/and | solution.py:268
  9.3 0.3 convert_reduce_fusion
  9.8 1.1 concatenate.68
  10.9 0.7 fusion.7
  11.6 0.4 copy.110
  12.0 0.4 all_to_all.12
  12.4 0.7 copy.111
  13.1 13.3 %all-to-all-start = ((f32[4,64,80]{2,0,1:T(4,128)}), f32[4,64,80]{2,0,1:T(4,128)S(1)}, u32[]{:S(2)}, u32[]{:S(2)}) async-start(f32[4,64,80]{2,0,1:T(4,128)} %copy.111), calls=%async_computation | async-start | bytes 262144 | tf_op jit(solution)/shard_map/all_to_all | solution.py:297
  26.5 0.6 fusion.181
  27.1 0.6 fusion.176
  27.7 0.6 iota_compare_fusion.8
  28.3 0.6 mul.993
  29.0 0.6 mul.999
  29.6 0.6 and_or_fusion
  30.4 1.0 fusion.212
  31.3 3.5 %collective-permute-start.2 = (bf16[3,16,26,9]{3,2,1,0:T(8,128)(2,1)}, bf16[3,16,26,9]{3,2,1,0:T(8,128)(2,1)S(1)}, u32[]{:S(2)}, u32[]{:S(2)}) collective-permute-start(bf16[3,16,26,9]{3,2,1,0:T(8,128)(2,1)} %get-tuple-element.76), channel_id=1, source_target_pairs={{0,1},{1,2},{2,3},{3,4},{4,5},{5,6},{6,7},{8,9},{9,10},{10,11},{11... | collective-permute-start | bytes 67400 | tf_op jit(solution)/shard_map/ppermute | solution.py:24
  34.9 1.9 %collective-permute-start.3 = (bf16[3,16,26,9]{3,2,1,0:T(8,128)(2,1)S(1)}, bf16[3,16,26,9]{3,2,1,0:T(8,128)(2,1)S(1)}, u32[]{:S(2)}, u32[]{:S(2)}) collective-permute-start(bf16[3,16,26,9]{3,2,1,0:T(8,128)(2,1)S(1)} %get-tuple-element.77), channel_id=1, source_target_pairs={{1,0},{2,1},{3,2},{4,3},{5,4},{6,5},{7,6},{9,8},{10,9},{11,10},{12... | collective-permute-start | bytes 67400 | tf_op jit(solution)/shard_map/ppermute | solution.py:27
  36.8 0.8 all-to-all-done
  37.6 0.4 reshape.464
  38.2 0.3 slice.835
  38.5 0.3 copy.114
  38.8 0.8 fusion.8
  39.6 0.3 copy.115
  39.9 0.3 reshape.465
  40.6 4.0 %collective-permute-start.6 = (f32[3,1,6,36]{3,2,1,0:T(8,128)S(1)}, f32[3,1,6,36]{3,2,1,0:T(8,128)S(1)}, u32[]{:S(2)}, u32[]{:S(2)}) collective-permute-start(f32[3,1,6,36]{3,2,1,0:T(8,128)S(1)} %get-tuple-element.109), channel_id=1, source_target_pairs={{0,64},{64,128},{128,192},{192,256},{256,320},{320,384},{384,448},... | collective-permute-start | bytes 7784 | tf_op jit(solution)/shard_map/ppermute | solution.py:24
  44.6 1.3 %collective-permute-start.7 = (f32[3,1,6,36]{3,2,1,0:T(8,128)S(1)}, f32[3,1,6,36]{3,2,1,0:T(8,128)S(1)}, u32[]{:S(2)}, u32[]{:S(2)}) collective-permute-start(f32[3,1,6,36]{3,2,1,0:T(8,128)S(1)} %get-tuple-element.110), channel_id=1, source_target_pairs={{64,0},{128,64},{192,128},{256,192},{320,256},{384,320},{448,384},... | collective-permute-start | bytes 7784 | tf_op jit(solution)/shard_map/ppermute | solution.py:27
  45.9 1.1 pad_maximum_fusion.8
  47.1 5.3 %collective-permute-start.4 = (bf16[3,5,26,146]{3,2,1,0:T(8,128)(2,1)}, bf16[3,5,26,146]{3,2,1,0:T(8,128)(2,1)}, u32[]{:S(2)}, u32[]{:S(2)}) collective-permute-start(bf16[3,5,26,146]{3,2,1,0:T(8,128)(2,1)} %get-tuple-element.64), channel_id=1, source_target_pairs={{0,64},{64,128},{128,192},{192,256},{256,320},{320,384},{384,448},... | collective-permute-start | bytes 341648 | tf_op jit(solution)/shard_map/ppermute | solution.py:24
  52.4 1.5 %collective-permute-start.5 = (bf16[3,5,26,146]{3,2,1,0:T(8,128)(2,1)S(1)}, bf16[3,5,26,146]{3,2,1,0:T(8,128)(2,1)}, u32[]{:S(2)}, u32[]{:S(2)}) collective-permute-start(bf16[3,5,26,146]{3,2,1,0:T(8,128)(2,1)S(1)} %get-tuple-element.65), channel_id=1, source_target_pairs={{64,0},{128,64},{192,128},{256,192},{320,256},{384,320},{448,384},... | collective-permute-start | bytes 341648 | tf_op jit(solution)/shard_map/ppermute | solution.py:27
  55.1 0.4 fusion.58
  55.8 0.4 multiply_add_fusion.1
  57.1 3.8 %collective-permute-done.5 = bf16[3,5,26,146]{3,2,1,0:T(8,128)(2,1)} collective-permute-done((bf16[3,5,26,146]{3,2,1,0:T(8,128)(2,1)S(1)}, bf16[3,5,26,146]{3,2,1,0:T(8,128)(2,1)}, u32[]{:S(2)}, u32[]{:S(2)}) %collective-permute-start.5) | collective-permute-done | bytes 113912 | tf_op jit(solution)/shard_map/ppermute | solution.py:27
  60.9 1.8 %maximum_convert_fusion = f32[3,26,26,146]{3,2,1,0:T(8,128)S(1)} fusion(bf16[3,5,26,146]{3,2,1,0:T(8,128)(2,1)} %collective-permute-done.5, bf16[3,16,26,9]{3,2,1,0:T(8,128)(2,1)S(1)} %collective-permute-done.3, bf16[3,16,5,128]{3,2,1,0:T(8,128)(2,1)S(1)} %collective-permute-done.1, bf16[1,16,16,128]{3,2,1,0:T(8,128)(2,1)S(1)} %convert_bitcast_fusion, ...), kind=kLoop, calls=%fused_computation.13 | loop fusion | flops 5329584 | bytes 1776528 | tf_op jit(solution)/shard_map/convert_element_type | solution.py:233
  62.7 0.4 fusion.25
  63.1 0.6 fusion.33
  63.7 1.2 add_multiply_fusion
  65.3 0.3 fusion.55
  65.7 0.3 fusion.53
  66.7 0.2 copy-done.10
  67.0 1.4 %multiply_reduce_fusion.3 = (f32[3,20,5,34]{3,1,2,0:T(8,128)S(1)}, f32[3,20,5,34]{3,1,2,0:T(8,128)S(1)}) fusion(f32[4]{0:T(128)S(1)} %copy-done.27, f32[4]{0:T(128)S(1)} %copy-done.26, pred[36,140]{1,0:T(8,128)(4,1)S(1)} %iota_compare_fusion.7, pred[36,140]{1,0:T(8,128)(4,1)S(1)} %copy-done.10, f32[140]{0:T(256)S(1)} %copy-done.23, f32[140]{0:T(256)S(1)} %copy-done.24, ...), kind=kOutput, calls=%fused_computation.27 | convolution fusion | flops 69541080 | bytes 652832 | tf_op jit(solution)/shard_map/dot_general | solution.py:219
  68.6 0.2 maximum_convert_fusion.1
  68.8 1.1 fusion.46
  70.1 1.4 %multiply_reduce_fusion.5 = (f32[3,20,5,34]{3,1,2,0:T(8,128)S(1)}, f32[3,20,5,34]{3,1,2,0:T(8,128)S(1)}) fusion(f32[4]{0:T(128)S(1)} %get-tuple-element.153, f32[4]{0:T(128)S(1)} %get-tuple-element.152, f32[36,140]{1,0:T(8,128)S(1)} %select_add_fusion, f32[20,5,4,140]{3,0,2,1:T(8,128)S(1)} %bitcast.486, f32[20,5,4,140]{3,0,2,1:T(8,128)S(1)} %bitcast.483, ...), kind=kOutput, calls=%fused_computation.29 | convolution fusion | flops 69526800 | bytes 885792 | tf_op jit(solution)/shard_map/dot_general | solution.py:219
  71.8 2.3 %collective-permute-start.8 = (f32[3,4,1,34]{3,2,1,0:T(1,128)S(1)}, f32[3,4,1,34]{3,2,1,0:T(1,128)S(1)}, u32[]{:S(2)}, u32[]{:S(2)}) collective-permute-start(f32[3,4,1,34]{3,2,1,0:T(1,128)S(1)} %get-tuple-element.119), channel_id=1, source_target_pairs={{0,8},{8,16},{16,24},{24,32},{32,40},{40,48},{48,56},{1,9},{9,17},... | collective-permute-start | bytes 4904 | tf_op jit(solution)/shard_map/ppermute | solution.py:24
  74.2 1.3 %collective-permute-start.9 = (f32[3,4,1,34]{3,2,1,0:T(1,128)S(1)}, f32[3,4,1,34]{3,2,1,0:T(1,128)S(1)}, u32[]{:S(2)}, u32[]{:S(2)}) collective-permute-start(f32[3,4,1,34]{3,2,1,0:T(1,128)S(1)} %get-tuple-element.120), channel_id=1, source_target_pairs={{8,0},{16,8},{24,16},{32,24},{40,32},{48,40},{56,48},{9,1},{17,9},... | collective-permute-start | bytes 4904 | tf_op jit(solution)/shard_map/ppermute | solution.py:27
  75.5 3.5 %collective-permute-done.9 = f32[3,4,1,34]{3,2,1,0:T(1,128)S(1)} collective-permute-done((f32[3,4,1,34]{3,2,1,0:T(1,128)S(1)}, f32[3,4,1,34]{3,2,1,0:T(1,128)S(1)}, u32[]{:S(2)}, u32[]{:S(2)}) %collective-permute-start.9) | collective-permute-done | bytes 1664 | tf_op jit(solution)/shard_map/ppermute | solution.py:27
  79.0 5.5 %collective-permute-start.10 = (f32[3,1,6,34]{3,2,1,0:T(8,128)S(1)}, f32[3,1,6,34]{3,2,1,0:T(8,128)S(1)}, u32[]{:S(2)}, u32[]{:S(2)}) collective-permute-start(f32[3,1,6,34]{3,2,1,0:T(8,128)S(1)} %get-tuple-element.117), channel_id=1, source_target_pairs={{0,64},{64,128},{128,192},{192,256},{256,320},{320,384},{384,448},... | collective-permute-start | bytes 7352 | tf_op jit(solution)/shard_map/ppermute | solution.py:24
  84.5 1.5 %collective-permute-start.11 = (f32[3,1,6,34]{3,2,1,0:T(8,128)S(1)}, f32[3,1,6,34]{3,2,1,0:T(8,128)S(1)}, u32[]{:S(2)}, u32[]{:S(2)}) collective-permute-start(f32[3,1,6,34]{3,2,1,0:T(8,128)S(1)} %get-tuple-element.118), channel_id=1, source_target_pairs={{64,0},{128,64},{192,128},{256,192},{320,256},{384,320},{448,384},... | collective-permute-start | bytes 7352 | tf_op jit(solution)/shard_map/ppermute | solution.py:27
  86.0 0.6 add_convert_fusion
  86.7 0.7 eq.206
  87.4 2.4 %collective-permute-done.11 = f32[3,1,6,34]{3,2,1,0:T(8,128)S(1)} collective-permute-done((f32[3,1,6,34]{3,2,1,0:T(8,128)S(1)}, f32[3,1,6,34]{3,2,1,0:T(8,128)S(1)}, u32[]{:S(2)}, u32[]{:S(2)}) %collective-permute-start.11) | collective-permute-done | bytes 2480 | tf_op jit(solution)/shard_map/ppermute | solution.py:27
  90.8 0.4 fusion.91
  91.5 0.4 multiply_add_fusion
  92.6 1.2 %fusion.48 = f32[20,20,140]{2,1,0:T(8,128)S(1)} fusion(bf16[20,20,140]{2,1,0:T(8,128)(2,1)} %get-tuple-element.44, f32[20,20,140]{2,1,0:T(8,128)S(1)} %squeeze.128, f32[20,20,140]{2,1,0:T(8,128)S(1)} %squeeze.127, f32[20,20,140]{2,1,0:T(8,128)S(1)} %squeeze.126, f32[3,20,20,140]{3,2,1,0:T(8,128)S(1)} %maximum_convert_fusion.1), kind=kLoop, calls=%fused_computation.99 | loop fusion | flops 392000 | bytes 1680000 | tf_op jit(solution)/shard_map/add | solution.py:348
  94.0 1.4 %multiply_reduce_fusion.1 = (f32[3,20,5,34]{3,1,2,0:T(8,128)S(1)}, f32[3,20,5,34]{3,1,2,0:T(8,128)S(1)}) fusion(f32[4]{0:T(128)S(1)} %get-tuple-element.153, f32[4]{0:T(128)S(1)} %get-tuple-element.152, f32[36,140]{1,0:T(8,128)S(1)} %select_add_fusion, f32[20,5,4,140]{3,0,2,1:T(8,128)S(1)} %bitcast.485, f32[20,5,4,140]{3,0,2,1:T(8,128)S(1)} %bitcast.484, ...), kind=kOutput, calls=%fused_computation.24 | convolution fusion | flops 69526800 | bytes 885792 | tf_op jit(solution)/shard_map/dot_general | solution.py:219
  96.7 0.7 copy.136
  97.4 13.8 %all-to-all-start.1 = ((f32[3,64,16]{2,0,1:T(4,128)}), f32[3,64,16]{2,0,1:T(4,128)S(1)}, u32[]{:S(2)}, u32[]{:S(2)}) async-start(f32[3,64,16]{2,0,1:T(4,128)} %copy.136), calls=%async_computation.1 | async-start | bytes 262144 | tf_op jit(solution)/shard_map/all_to_all | solution.py:361
  111.2 11.1 %all-to-all-done.1 = f32[3,64,16]{2,0,1:T(4,128)S(1)} async-done(((f32[3,64,16]{2,0,1:T(4,128)}), f32[3,64,16]{2,0,1:T(4,128)S(1)}, u32[]{:S(2)}, u32[]{:S(2)}) %all-to-all-start.1) | async-done | bytes 12320 | tf_op jit(solution)/shard_map/all_to_all | solution.py:361
  122.5 0.9 convolution_bitcast_fusion
  (221 shorter events, 8.2 us)
Async XLA Ops:
  1.9 28.3 %collective-permute-start = (bf16[3,16,5,128]{3,2,1,0:T(8,128)(2,1)S(1)}, bf16[3,16,5,128]{3,2,1,0:T(8,128)(2,1)S(1)}, u32[]{:S(2)}, u32[]{:S(2)}) collective-permute-start(bf16[3,16,5,128]{3,2,1,0:T(8,128)(2,1)S(1)} %get-tuple-element.103), channel_id=1, source_target_pairs={{0,8},{8,16},{16,24},{24,32},{32,40},{40,48},{48,56},{1,9},{9,17},... | collective-permute-start | bytes 184328 | tf_op jit(solution)/shard_map/ppermute | solution.py:24
  5.9 24.3 %collective-permute-start.1 = (bf16[3,16,5,128]{3,2,1,0:T(8,128)(2,1)S(1)}, bf16[3,16,5,128]{3,2,1,0:T(8,128)(2,1)S(1)}, u32[]{:S(2)}, u32[]{:S(2)}) collective-permute-start(bf16[3,16,5,128]{3,2,1,0:T(8,128)(2,1)S(1)} %get-tuple-element.104), channel_id=1, source_target_pairs={{8,0},{16,8},{24,16},{32,24},{40,32},{48,40},{56,48},{9,1},{17,9},... | collective-permute-start | bytes 184328 | tf_op jit(solution)/shard_map/ppermute | solution.py:27
  11.6 18.6 %copy-start = (bf16[16,16,128]{2,1,0:T(8,128)(2,1)S(1)}, bf16[16,16,128]{2,1,0:T(8,128)(2,1)}, u32[]{:S(2)}) copy-start(bf16[16,16,128]{2,1,0:T(8,128)(2,1)} %param.6) | copy-start | bytes 196612
  11.6 18.6 %copy-start.1 = (bf16[16,16,128]{2,1,0:T(8,128)(2,1)S(1)}, bf16[16,16,128]{2,1,0:T(8,128)(2,1)}, u32[]{:S(2)}) copy-start(bf16[16,16,128]{2,1,0:T(8,128)(2,1)} %param.5) | copy-start | bytes 196612
  13.1 24.5 %all-to-all-start = ((f32[4,64,80]{2,0,1:T(4,128)}), f32[4,64,80]{2,0,1:T(4,128)S(1)}, u32[]{:S(2)}, u32[]{:S(2)}) async-start(f32[4,64,80]{2,0,1:T(4,128)} %copy.111), calls=%async_computation | async-start | bytes 262144 | tf_op jit(solution)/shard_map/all_to_all | solution.py:297
  26.5 28.6 %copy-start.11 = (s32[140]{0:T(256)}, s32[140]{0:T(256)S(1)}, u32[]{:S(2)}) copy-start(s32[140]{0:T(256)S(1)} %get-tuple-element.149) | copy-start | bytes 1684
  27.7 9.9 %copy-start.17 = (f32[140]{0:T(256)}, f32[140]{0:T(256)S(1)}, u32[]{:S(2)}) copy-start(f32[140]{0:T(256)S(1)} %get-tuple-element.150) | copy-start | bytes 1684
  27.7 10.3 %copy-start.20 = (f32[140]{0:T(256)}, f32[140]{0:T(256)S(1)}, u32[]{:S(2)}) copy-start(f32[140]{0:T(256)S(1)} %get-tuple-element.151) | copy-start | bytes 1684
  31.3 14.6 %collective-permute-start.2 = (bf16[3,16,26,9]{3,2,1,0:T(8,128)(2,1)}, bf16[3,16,26,9]{3,2,1,0:T(8,128)(2,1)S(1)}, u32[]{:S(2)}, u32[]{:S(2)}) collective-permute-start(bf16[3,16,26,9]{3,2,1,0:T(8,128)(2,1)} %get-tuple-element.76), channel_id=1, source_target_pairs={{0,1},{1,2},{2,3},{3,4},{4,5},{5,6},{6,7},{8,9},{9,10},{10,11},{11... | collective-permute-start | bytes 67400 | tf_op jit(solution)/shard_map/ppermute | solution.py:24
  34.9 11.1 %collective-permute-start.3 = (bf16[3,16,26,9]{3,2,1,0:T(8,128)(2,1)S(1)}, bf16[3,16,26,9]{3,2,1,0:T(8,128)(2,1)S(1)}, u32[]{:S(2)}, u32[]{:S(2)}) collective-permute-start(bf16[3,16,26,9]{3,2,1,0:T(8,128)(2,1)S(1)} %get-tuple-element.77), channel_id=1, source_target_pairs={{1,0},{2,1},{3,2},{4,3},{5,4},{6,5},{7,6},{9,8},{10,9},{11,10},{12... | collective-permute-start | bytes 67400 | tf_op jit(solution)/shard_map/ppermute | solution.py:27
  40.6 13.3 %collective-permute-start.6 = (f32[3,1,6,36]{3,2,1,0:T(8,128)S(1)}, f32[3,1,6,36]{3,2,1,0:T(8,128)S(1)}, u32[]{:S(2)}, u32[]{:S(2)}) collective-permute-start(f32[3,1,6,36]{3,2,1,0:T(8,128)S(1)} %get-tuple-element.109), channel_id=1, source_target_pairs={{0,64},{64,128},{128,192},{192,256},{256,320},{320,384},{384,448},... | collective-permute-start | bytes 7784 | tf_op jit(solution)/shard_map/ppermute | solution.py:24
  44.6 9.3 %collective-permute-start.7 = (f32[3,1,6,36]{3,2,1,0:T(8,128)S(1)}, f32[3,1,6,36]{3,2,1,0:T(8,128)S(1)}, u32[]{:S(2)}, u32[]{:S(2)}) collective-permute-start(f32[3,1,6,36]{3,2,1,0:T(8,128)S(1)} %get-tuple-element.110), channel_id=1, source_target_pairs={{64,0},{128,64},{192,128},{256,192},{320,256},{384,320},{448,384},... | collective-permute-start | bytes 7784 | tf_op jit(solution)/shard_map/ppermute | solution.py:27
  47.1 10.0 %collective-permute-start.4 = (bf16[3,5,26,146]{3,2,1,0:T(8,128)(2,1)}, bf16[3,5,26,146]{3,2,1,0:T(8,128)(2,1)}, u32[]{:S(2)}, u32[]{:S(2)}) collective-permute-start(bf16[3,5,26,146]{3,2,1,0:T(8,128)(2,1)} %get-tuple-element.64), channel_id=1, source_target_pairs={{0,64},{64,128},{128,192},{192,256},{256,320},{320,384},{384,448},... | collective-permute-start | bytes 341648 | tf_op jit(solution)/shard_map/ppermute | solution.py:24
  52.4 8.5 %collective-permute-start.5 = (bf16[3,5,26,146]{3,2,1,0:T(8,128)(2,1)S(1)}, bf16[3,5,26,146]{3,2,1,0:T(8,128)(2,1)}, u32[]{:S(2)}, u32[]{:S(2)}) collective-permute-start(bf16[3,5,26,146]{3,2,1,0:T(8,128)(2,1)S(1)} %get-tuple-element.65), channel_id=1, source_target_pairs={{64,0},{128,64},{192,128},{256,192},{320,256},{384,320},{448,384},... | collective-permute-start | bytes 341648 | tf_op jit(solution)/shard_map/ppermute | solution.py:27
  54.2 0.8 copy-start.18
  54.3 0.8 copy-start.21
  54.8 0.7 copy-start.13
  54.9 0.7 copy-start.15
  65.7 4.3 %copy-start.4 = (bf16[20,20,140]{2,0,1:T(8,128)(2,1)}, bf16[20,20,140]{2,0,1:T(8,128)(2,1)S(1)}, u32[]{:S(2)}) copy-start(bf16[20,20,140]{2,0,1:T(8,128)(2,1)S(1)} %copy.142) | copy-start | bytes 336004
  66.1 3.9 %copy-start.6 = (bf16[20,20,140]{2,0,1:T(8,128)(2,1)}, bf16[20,20,140]{2,0,1:T(8,128)(2,1)S(1)}, u32[]{:S(2)}) copy-start(bf16[20,20,140]{2,0,1:T(8,128)(2,1)S(1)} %copy.143) | copy-start | bytes 336004
  66.2 0.7 copy-start.10
  66.3 0.7 copy-start.23
  66.3 0.7 copy-start.24
  66.3 0.7 copy-start.26
  66.3 0.7 copy-start.27
  66.3 3.7 %copy-start.8 = (bf16[20,20,140]{2,0,1:T(8,128)(2,1)}, bf16[20,20,140]{2,0,1:T(8,128)(2,1)S(1)}, u32[]{:S(2)}) copy-start(bf16[20,20,140]{2,0,1:T(8,128)(2,1)S(1)} %copy.144) | copy-start | bytes 336004
  66.7 3.4 %copy-start.2 = (f32[20,20,140]{2,0,1:T(8,128)}, f32[20,20,140]{2,0,1:T(8,128)S(1)}, u32[]{:S(2)}) copy-start(f32[20,20,140]{2,0,1:T(8,128)S(1)} %copy.145) | copy-start | bytes 672004
  70.1 1.6 %copy-start.25 = (pred[34]{0:T(512)(128)(4,1)S(1)}, pred[34]{0:T(512)(128)(4,1)}, u32[]{:S(2)}) copy-start(pred[34]{0:T(512)(128)(4,1)} %and_or_fusion) | copy-start | bytes 106
  71.8 3.7 %collective-permute-start.8 = (f32[3,4,1,34]{3,2,1,0:T(1,128)S(1)}, f32[3,4,1,34]{3,2,1,0:T(1,128)S(1)}, u32[]{:S(2)}, u32[]{:S(2)}) collective-permute-start(f32[3,4,1,34]{3,2,1,0:T(1,128)S(1)} %get-tuple-element.119), channel_id=1, source_target_pairs={{0,8},{8,16},{16,24},{24,32},{32,40},{40,48},{48,56},{1,9},{9,17},... | collective-permute-start | bytes 4904 | tf_op jit(solution)/shard_map/ppermute | solution.py:24
  74.2 4.8 %collective-permute-start.9 = (f32[3,4,1,34]{3,2,1,0:T(1,128)S(1)}, f32[3,4,1,34]{3,2,1,0:T(1,128)S(1)}, u32[]{:S(2)}, u32[]{:S(2)}) collective-permute-start(f32[3,4,1,34]{3,2,1,0:T(1,128)S(1)} %get-tuple-element.120), channel_id=1, source_target_pairs={{8,0},{16,8},{24,16},{32,24},{40,32},{48,40},{56,48},{9,1},{17,9},... | collective-permute-start | bytes 4904 | tf_op jit(solution)/shard_map/ppermute | solution.py:27
  79.0 8.4 %collective-permute-start.10 = (f32[3,1,6,34]{3,2,1,0:T(8,128)S(1)}, f32[3,1,6,34]{3,2,1,0:T(8,128)S(1)}, u32[]{:S(2)}, u32[]{:S(2)}) collective-permute-start(f32[3,1,6,34]{3,2,1,0:T(8,128)S(1)} %get-tuple-element.117), channel_id=1, source_target_pairs={{0,64},{64,128},{128,192},{192,256},{256,320},{320,384},{384,448},... | collective-permute-start | bytes 7352 | tf_op jit(solution)/shard_map/ppermute | solution.py:24
  84.5 5.3 %collective-permute-start.11 = (f32[3,1,6,34]{3,2,1,0:T(8,128)S(1)}, f32[3,1,6,34]{3,2,1,0:T(8,128)S(1)}, u32[]{:S(2)}, u32[]{:S(2)}) collective-permute-start(f32[3,1,6,34]{3,2,1,0:T(8,128)S(1)} %get-tuple-element.118), channel_id=1, source_target_pairs={{64,0},{128,64},{192,128},{256,192},{320,256},{384,320},{448,384},... | collective-permute-start | bytes 7352 | tf_op jit(solution)/shard_map/ppermute | solution.py:27
  90.0 0.8 copy-start.12
  90.0 0.8 copy-start.19
  90.0 0.8 copy-start.22
  90.5 0.7 copy-start.14
  90.5 0.7 copy-start.16
  92.5 1.4 %copy-start.3 = (f32[20,20,140]{2,0,1:T(8,128)S(1)}, f32[20,20,140]{2,0,1:T(8,128)}, u32[]{:S(2)}) copy-start(f32[20,20,140]{2,0,1:T(8,128)} %copy-done.2) | copy-start | bytes 672004
  92.5 1.4 %copy-start.5 = (bf16[20,20,140]{2,0,1:T(8,128)(2,1)S(1)}, bf16[20,20,140]{2,0,1:T(8,128)(2,1)}, u32[]{:S(2)}) copy-start(bf16[20,20,140]{2,0,1:T(8,128)(2,1)} %copy-done.4) | copy-start | bytes 336004
  92.5 1.4 %copy-start.7 = (bf16[20,20,140]{2,0,1:T(8,128)(2,1)S(1)}, bf16[20,20,140]{2,0,1:T(8,128)(2,1)}, u32[]{:S(2)}) copy-start(bf16[20,20,140]{2,0,1:T(8,128)(2,1)} %copy-done.6) | copy-start | bytes 336004
  92.6 1.4 %copy-start.9 = (bf16[20,20,140]{2,0,1:T(8,128)(2,1)S(1)}, bf16[20,20,140]{2,0,1:T(8,128)(2,1)}, u32[]{:S(2)}) copy-start(bf16[20,20,140]{2,0,1:T(8,128)(2,1)} %copy-done.8) | copy-start | bytes 336004
  95.4 0.8 copy-start.28
  95.4 0.8 copy-start.30
  95.4 15.8 %copy-start.29 = (s32[64]{0:T(128)S(1)}, s32[64]{0:T(128)}, u32[]{:S(2)}) copy-start(s32[64]{0:T(128)} %get-tuple-element.55) | copy-start | bytes 772
  97.4 24.9 %all-to-all-start.1 = ((f32[3,64,16]{2,0,1:T(4,128)}), f32[3,64,16]{2,0,1:T(4,128)S(1)}, u32[]{:S(2)}, u32[]{:S(2)}) async-start(f32[3,64,16]{2,0,1:T(4,128)} %copy.136), calls=%async_computation.1 | async-start | bytes 262144 | tf_op jit(solution)/shard_map/all_to_all | solution.py:361

commit v14 on v6

--- a/solution.py
+++ b/solution.py
@@ -230,7 +230,7 @@
     stacked = jnp.stack([reference_image, deformed_image, roi_mask.astype(jnp.bfloat16)])
     stacked = with_halo(stacked, (("gy", 2),), 5)
     stacked = with_halo(stacked, (("gz", 3),), 5 + ELEM)
-    padded_images = with_halo(stacked, (("gx", 1),), 5).astype(jnp.float32)
+    padded_images = with_halo(stacked, (("gx", 1),), 5)
     nodes_shape = (
         3,
         reference_image.shape[0] // ELEM,
@@ -326,8 +326,10 @@
     )
     extended = jnp.concatenate([low_row, middle, high_row], axis=2)
     first_padded = with_halo(extended, (("gx", 1),), 1)
-    derived = derive_fields(padded_images[0], padded_images[1])
-    region = padded_images[2][3:-3, 3:-3, 3:-3]
+    derived = derive_fields(
+        padded_images[0].astype(jnp.float32), padded_images[1].astype(jnp.float32)
+    )
+    region = padded_images[2][3:-3, 3:-3, 3:-3].astype(jnp.float32)
     contrast = derived[0].astype(jnp.float32)
     slopes = derived[1:].astype(jnp.float32)
     masked_slopes = slopes * region[None]

time: 124 us -> 119 us (0.960)
  the two profiles are of different devices: /device:TPU:1 before, /device:TPU:193 now
where the time goes in v14:
time: 119 us
  starting transfers between devices  62.7 us (53%)
  other arithmetic  20.2 us (17%)
  waiting for transfers between devices  13.2 us (11%)
  local copies, waits for them, and re-layouts  12.9 us (11%)
  matrix products  7.52 us (6%)
  between operations  2.02 us (2%)
    ppermute x6, starting transfers between devices, with_halo(): lax.ppermute(lax.slice_in_dim(block, block.shape[dim] - width, None, axis...  26.7 us
    all_to_all x1, starting transfers between devices, per_device(): lax.all_to_all(outgoing, ('gy', 'gz'), split_axis=1, concat_axis=1, tiled...  14 us
    ppermute x6, starting transfers between devices, with_halo(): lax.ppermute(lax.slice_in_dim(block, 0, width, axis=dim), axis, backward)  11.3 us
    all_to_all x1, starting transfers between devices, per_device(): lax.all_to_all(send_outgoing, ('gy', 'gz'), split_axis=1, concat_axis=1,...  10.8 us
    all_to_all x1, waiting for transfers between devices, per_device(): lax.all_to_all(outgoing, ('gy', 'gz'), split_axis=1, concat_axis=1, tiled...  10.4 us
    dot_general x3, matrix products, collect(): jnp.dot(volume.reshape(-1, shape_all[3]), table_back, precision=highest)  4.17 us
    concatenate x3, other arithmetic, with_halo(): block = jnp.concatenate([low, block, high], axis=dim)  3.02 us
    unnamed x4, matrix products  2.57 us
  transfers between devices with their start and end apart: 14, of which 4 were waited for; matrix products, arithmetic and copies ran while one was open for 11% of the time, Pallas kernels for 0%

profile of v14, /device:TPU:193, one launch (start us, length us, event | category | flops | bytes accessed | tf_op | source)
XLA Modules:
  0.0 118.5 jit_solution(9821048744570057544)
XLA Ops:
  0.0 0.7 broadcast_add_fusion.1
  0.7 1.2 %and_and_fusion = (pred[64]{0:T(512)(128)(4,1)S(1)}, s32[64]{0:T(128)S(1)}, s32[64]{0:T(128)S(1)}, s32[64]{0:T(128)S(1)}, s32[64]{0:T(128)S(1)}, /*index=5*/s32[64]{0:T(128)}) fusion(s32[64]{0:T(128)S(1)} %get-tuple-element.49, s32[64]{0:T(128)} %param.9), kind=kLoop, calls=%fused_computation.426 | loop fusion | flops 4928 | bytes 1856 | tf_op jit(solution)/shard_map/and | solution.py:268
  2.1 0.3 convert_reduce_fusion
  2.5 0.6 copy-done.21
  3.1 1.1 concatenate.68
  4.3 0.7 fusion.7
  5.0 0.4 copy.110
  5.4 0.4 all_to_all.12
  5.7 0.7 copy.111
  6.5 10.8 %all-to-all-start = ((f32[4,64,80]{2,0,1:T(4,128)}), f32[4,64,80]{2,0,1:T(4,128)S(1)}, u32[]{:S(2)}, u32[]{:S(2)}) async-start(f32[4,64,80]{2,0,1:T(4,128)} %copy.111), calls=%async_computation | async-start | bytes 262144 | tf_op jit(solution)/shard_map/all_to_all | solution.py:297
  17.4 1.3 %collective-permute-start.1 = (bf16[3,16,5,128]{3,2,1,0:T(8,128)(2,1)S(1)}, bf16[3,16,5,128]{3,2,1,0:T(8,128)(2,1)S(1)}, u32[]{:S(2)}, u32[]{:S(2)}) collective-permute-start(bf16[3,16,5,128]{3,2,1,0:T(8,128)(2,1)S(1)} %get-tuple-element.105), channel_id=1, source_target_pairs={{8,0},{16,8},{24,16},{32,24},{40,32},{48,40},{56,48},{9,1},{17,9},... | collective-permute-start | bytes 184328 | tf_op jit(solution)/shard_map/ppermute | solution.py:27
  18.7 4.0 %collective-permute-start = (bf16[3,16,5,128]{3,2,1,0:T(8,128)(2,1)S(1)}, bf16[3,16,5,128]{3,2,1,0:T(8,128)(2,1)S(1)}, u32[]{:S(2)}, u32[]{:S(2)}) collective-permute-start(bf16[3,16,5,128]{3,2,1,0:T(8,128)(2,1)S(1)} %get-tuple-element.104), channel_id=1, source_target_pairs={{0,8},{8,16},{16,24},{24,32},{32,40},{40,48},{48,56},{1,9},{9,17},... | collective-permute-start | bytes 184328 | tf_op jit(solution)/shard_map/ppermute | solution.py:24
  22.8 0.5 fusion.181
  23.4 0.6 fusion.176
  24.1 0.6 iota_compare_fusion.7
  24.7 0.6 iota_compare_fusion.8
  25.3 0.6 select_add_fusion
  26.0 0.6 and_or_fusion
  26.7 0.9 fusion.212
  27.6 2.9 %collective-permute-start.3 = (bf16[3,16,26,9]{3,2,1,0:T(8,128)(2,1)}, bf16[3,16,26,9]{3,2,1,0:T(8,128)(2,1)S(1)}, u32[]{:S(2)}, u32[]{:S(2)}) collective-permute-start(bf16[3,16,26,9]{3,2,1,0:T(8,128)(2,1)} %get-tuple-element.78), channel_id=1, source_target_pairs={{1,0},{2,1},{3,2},{4,3},{5,4},{6,5},{7,6},{9,8},{10,9},{11,10},{12... | collective-permute-start | bytes 67400 | tf_op jit(solution)/shard_map/ppermute | solution.py:27
  30.6 3.1 %collective-permute-start.2 = (bf16[3,16,26,9]{3,2,1,0:T(8,128)(2,1)S(1)}, bf16[3,16,26,9]{3,2,1,0:T(8,128)(2,1)S(1)}, u32[]{:S(2)}, u32[]{:S(2)}) collective-permute-start(bf16[3,16,26,9]{3,2,1,0:T(8,128)(2,1)S(1)} %get-tuple-element.77), channel_id=1, source_target_pairs={{0,1},{1,2},{2,3},{3,4},{4,5},{5,6},{6,7},{8,9},{9,10},{10,11},{11... | collective-permute-start | bytes 67400 | tf_op jit(solution)/shard_map/ppermute | solution.py:24
  33.7 0.4 reshape.465
  34.3 0.3 slice.829
  34.6 0.3 copy.114
  34.9 0.8 fusion.8
  35.7 0.3 copy.115
  36.8 1.9 %collective-permute-start.7 = (f32[3,1,6,36]{3,2,1,0:T(8,128)S(1)}, f32[3,1,6,36]{3,2,1,0:T(8,128)S(1)}, u32[]{:S(2)}, u32[]{:S(2)}) collective-permute-start(f32[3,1,6,36]{3,2,1,0:T(8,128)S(1)} %get-tuple-element.111), channel_id=1, source_target_pairs={{64,0},{128,64},{192,128},{256,192},{320,256},{384,320},{448,384},... | collective-permute-start | bytes 7784 | tf_op jit(solution)/shard_map/ppermute | solution.py:27
  38.7 5.2 %collective-permute-start.6 = (f32[3,1,6,36]{3,2,1,0:T(8,128)S(1)}, f32[3,1,6,36]{3,2,1,0:T(8,128)S(1)}, u32[]{:S(2)}, u32[]{:S(2)}) collective-permute-start(f32[3,1,6,36]{3,2,1,0:T(8,128)S(1)} %get-tuple-element.110), channel_id=1, source_target_pairs={{0,64},{64,128},{128,192},{192,256},{256,320},{320,384},{384,448},... | collective-permute-start | bytes 7784 | tf_op jit(solution)/shard_map/ppermute | solution.py:24
  44.0 0.5 pad_maximum_fusion.9
  44.4 1.9 %collective-permute-start.5 = (bf16[3,5,26,146]{3,2,1,0:T(8,128)(2,1)S(1)}, bf16[3,5,26,146]{3,2,1,0:T(8,128)(2,1)S(1)}, u32[]{:S(2)}, u32[]{:S(2)}) collective-permute-start(bf16[3,5,26,146]{3,2,1,0:T(8,128)(2,1)S(1)} %get-tuple-element.66), channel_id=1, source_target_pairs={{64,0},{128,64},{192,128},{256,192},{320,256},{384,320},{448,384},... | collective-permute-start | bytes 341648 | tf_op jit(solution)/shard_map/ppermute | solution.py:27
  46.4 4.8 %collective-permute-start.4 = (bf16[3,5,26,146]{3,2,1,0:T(8,128)(2,1)S(1)}, bf16[3,5,26,146]{3,2,1,0:T(8,128)(2,1)}, u32[]{:S(2)}, u32[]{:S(2)}) collective-permute-start(bf16[3,5,26,146]{3,2,1,0:T(8,128)(2,1)S(1)} %get-tuple-element.65), channel_id=1, source_target_pairs={{0,64},{64,128},{128,192},{192,256},{256,320},{320,384},{384,448},... | collective-permute-start | bytes 341648 | tf_op jit(solution)/shard_map/ppermute | solution.py:24
  51.2 0.4 fusion.58
  52.0 0.4 multiply_add_fusion.1
  54.4 1.0 collective-permute-done.5
  55.4 1.0 collective-permute-done.4
  56.4 2.7 %pad_maximum_fusion = bf16[3,26,26,146]{3,2,1,0:T(8,128)(2,1)S(1)} fusion(bf16[3,5,26,146]{3,2,1,0:T(8,128)(2,1)S(1)} %collective-permute-done.5, bf16[3,16,26,9]{3,2,1,0:T(8,128)(2,1)S(1)} %collective-permute-done.3, bf16[3,16,5,128]{3,2,1,0:T(8,128)(2,1)S(1)} %collective-permute-done.1, bf16[1,16,16,128]{3,2,1,0:T(8,128)(2,1)S(1)} %convert_bitcast_fusion, ...), kind=kLoop, calls=%fused_computation.13 | loop fusion | flops 5329584 | bytes 1184352 | tf_op jit(solution)/shard_map/concatenate | solution.py:28
  59.3 0.4 fusion.20
  59.7 0.3 fusion.33
  60.0 0.3 fusion.41
  60.3 1.2 add_multiply_fusion
  62.1 0.3 fusion.53
  62.5 0.3 fusion.55
  63.1 1.1 fusion.46
  64.7 0.3 copy-done.19
  65.0 1.4 %multiply_reduce_fusion.5 = (f32[3,20,5,34]{3,1,2,0:T(8,128)S(1)}, f32[3,20,5,34]{3,1,2,0:T(8,128)S(1)}) fusion(f32[4]{0:T(128)S(1)} %copy-done.27, f32[4]{0:T(128)S(1)} %copy-done.25, f32[36,140]{1,0:T(8,128)S(1)} %copy-done.19, f32[20,5,4,140]{3,0,2,1:T(8,128)S(1)} %bitcast.485, f32[20,5,4,140]{3,0,2,1:T(8,128)S(1)} %bitcast.482, ...), kind=kOutput, calls=%fused_computation.28 | convolution fusion | flops 69526800 | bytes 885792 | tf_op jit(solution)/shard_map/dot_general | solution.py:219
  66.8 1.4 %multiply_reduce_fusion.3 = (f32[3,20,5,34]{3,1,2,0:T(8,128)S(1)}, f32[3,20,5,34]{3,1,2,0:T(8,128)S(1)}) fusion(f32[4]{0:T(128)S(1)} %copy-done.51, f32[4]{0:T(128)S(1)} %copy-done.50, pred[36,140]{1,0:T(8,128)(4,1)S(1)} %copy-done.28, pred[36,140]{1,0:T(8,128)(4,1)S(1)} %copy-done.29, f32[140]{0:T(256)S(1)} %copy-done.48, f32[140]{0:T(256)S(1)} %copy-done.49, ...), kind=kOutput, calls=%fused_computation.26 | convolution fusion | flops 69541080 | bytes 652832 | tf_op jit(solution)/shard_map/dot_general | solution.py:219
  68.6 1.9 %collective-permute-start.9 = (f32[3,1,4,34]{3,2,1,0:T(4,128)S(1)}, f32[3,1,4,34]{3,2,1,0:T(4,128)S(1)}, u32[]{:S(2)}, u32[]{:S(2)}) collective-permute-start(f32[3,1,4,34]{3,2,1,0:T(4,128)S(1)} %get-tuple-element.121), channel_id=1, source_target_pairs={{64,0},{128,64},{192,128},{256,192},{320,256},{384,320},{448,384},... | collective-permute-start | bytes 4904 | tf_op jit(solution)/shard_map/ppermute | solution.py:27
  70.6 5.4 %collective-permute-start.8 = (f32[3,1,4,34]{3,2,1,0:T(4,128)S(1)}, f32[3,1,4,34]{3,2,1,0:T(4,128)S(1)}, u32[]{:S(2)}, u32[]{:S(2)}) collective-permute-start(f32[3,1,4,34]{3,2,1,0:T(4,128)S(1)} %get-tuple-element.120), channel_id=1, source_target_pairs={{0,64},{64,128},{128,192},{192,256},{256,320},{320,384},{384,448},... | collective-permute-start | bytes 4904 | tf_op jit(solution)/shard_map/ppermute | solution.py:24
  76.0 0.7 collective-permute-done.8
  76.8 1.3 %collective-permute-start.11 = (f32[3,6,1,34]{3,2,1,0:T(1,128)S(1)}, f32[3,6,1,34]{3,2,1,0:T(1,128)S(1)}, u32[]{:S(2)}, u32[]{:S(2)}) collective-permute-start(f32[3,6,1,34]{3,2,1,0:T(1,128)S(1)} %get-tuple-element.119), channel_id=1, source_target_pairs={{8,0},{16,8},{24,16},{32,24},{40,32},{48,40},{56,48},{9,1},{17,9},... | collective-permute-start | bytes 7352 | tf_op jit(solution)/shard_map/ppermute | solution.py:27
  78.1 4.2 %collective-permute-start.10 = (f32[3,6,1,34]{3,2,1,0:T(1,128)S(1)}, f32[3,6,1,34]{3,2,1,0:T(1,128)S(1)}, u32[]{:S(2)}, u32[]{:S(2)}) collective-permute-start(f32[3,6,1,34]{3,2,1,0:T(1,128)S(1)} %get-tuple-element.118), channel_id=1, source_target_pairs={{0,8},{8,16},{16,24},{24,32},{32,40},{40,48},{48,56},{1,9},{9,17},... | collective-permute-start | bytes 7352 | tf_op jit(solution)/shard_map/ppermute | solution.py:24
  82.3 0.5 add_convert_fusion
  82.9 0.7 eq.206
  83.6 0.6 copy-done.30
  84.2 0.6 copy-done.32
  84.8 0.4 fusion.91
  85.5 0.4 multiply_add_fusion
  86.7 1.2 %fusion.48 = f32[20,20,140]{2,1,0:T(8,128)S(1)} fusion(bf16[20,20,140]{2,1,0:T(8,128)(2,1)} %get-tuple-element.44, f32[20,20,140]{2,1,0:T(8,128)S(1)} %squeeze.128, f32[20,20,140]{2,1,0:T(8,128)S(1)} %squeeze.127, f32[20,20,140]{2,1,0:T(8,128)S(1)} %squeeze.126, f32[3,20,20,140]{3,2,1,0:T(8,128)S(1)} %maximum_convert_fusion), kind=kLoop, calls=%fused_computation.98 | loop fusion | flops 392000 | bytes 1680000 | tf_op jit(solution)/shard_map/add | solution.py:350
  88.1 1.4 %multiply_reduce_fusion.1 = (f32[3,20,5,34]{3,1,2,0:T(8,128)S(1)}, f32[3,20,5,34]{3,1,2,0:T(8,128)S(1)}) fusion(f32[4]{0:T(128)S(1)} %copy-done.27, f32[4]{0:T(128)S(1)} %copy-done.25, f32[36,140]{1,0:T(8,128)S(1)} %copy-done.20, f32[20,5,4,140]{3,0,2,1:T(8,128)S(1)} %bitcast.486, f32[20,5,4,140]{3,0,2,1:T(8,128)S(1)} %bitcast.484, ...), kind=kOutput, calls=%fused_computation.23 | convolution fusion | flops 69526800 | bytes 885792 | tf_op jit(solution)/shard_map/dot_general | solution.py:219
  91.7 0.7 copy.136
  92.4 14.0 %all-to-all-start.1 = ((f32[3,64,16]{2,0,1:T(4,128)}), f32[3,64,16]{2,0,1:T(4,128)S(1)}, u32[]{:S(2)}, u32[]{:S(2)}) async-start(f32[3,64,16]{2,0,1:T(4,128)} %copy.136), calls=%async_computation.1 | async-start | bytes 262144 | tf_op jit(solution)/shard_map/all_to_all | solution.py:363
  106.4 0.7 slice_add_fusion.57
  107.0 10.4 %all-to-all-done.1 = f32[3,64,16]{2,0,1:T(4,128)S(1)} async-done(((f32[3,64,16]{2,0,1:T(4,128)}), f32[3,64,16]{2,0,1:T(4,128)S(1)}, u32[]{:S(2)}, u32[]{:S(2)}) %all-to-all-start.1) | async-done | bytes 12320 | tf_op jit(solution)/shard_map/all_to_all | solution.py:363
  117.7 0.9 convolution_bitcast_fusion
  (272 shorter events, 9.1 us)
Async XLA Ops:
  4.9 12.4 %copy-start.18 = (s32[16,16,128]{2,1,0:T(8,128)S(1)}, s32[16,16,128]{2,1,0:T(8,128)}, u32[]{:S(2)}) copy-start(s32[16,16,128]{2,1,0:T(8,128)} %param.7) | copy-start | bytes 393220
  4.9 12.4 %copy-start.2 = (bf16[16,16,128]{2,1,0:T(8,128)(2,1)S(1)}, bf16[16,16,128]{2,1,0:T(8,128)(2,1)}, u32[]{:S(2)}) copy-start(bf16[16,16,128]{2,1,0:T(8,128)(2,1)} %param.6) | copy-start | bytes 196612
  5.0 12.4 %copy-start.3 = (bf16[16,16,128]{2,1,0:T(8,128)(2,1)S(1)}, bf16[16,16,128]{2,1,0:T(8,128)(2,1)}, u32[]{:S(2)}) copy-start(bf16[16,16,128]{2,1,0:T(8,128)(2,1)} %param.5) | copy-start | bytes 196612
  6.5 27.2 %all-to-all-start = ((f32[4,64,80]{2,0,1:T(4,128)}), f32[4,64,80]{2,0,1:T(4,128)S(1)}, u32[]{:S(2)}, u32[]{:S(2)}) async-start(f32[4,64,80]{2,0,1:T(4,128)} %copy.111), calls=%async_computation | async-start | bytes 262144 | tf_op jit(solution)/shard_map/all_to_all | solution.py:297
  17.4 9.1 %collective-permute-start.1 = (bf16[3,16,5,128]{3,2,1,0:T(8,128)(2,1)S(1)}, bf16[3,16,5,128]{3,2,1,0:T(8,128)(2,1)S(1)}, u32[]{:S(2)}, u32[]{:S(2)}) collective-permute-start(bf16[3,16,5,128]{3,2,1,0:T(8,128)(2,1)S(1)} %get-tuple-element.105), channel_id=1, source_target_pairs={{8,0},{16,8},{24,16},{32,24},{40,32},{48,40},{56,48},{9,1},{17,9},... | collective-permute-start | bytes 184328 | tf_op jit(solution)/shard_map/ppermute | solution.py:27
  18.7 7.8 %collective-permute-start = (bf16[3,16,5,128]{3,2,1,0:T(8,128)(2,1)S(1)}, bf16[3,16,5,128]{3,2,1,0:T(8,128)(2,1)S(1)}, u32[]{:S(2)}, u32[]{:S(2)}) collective-permute-start(bf16[3,16,5,128]{3,2,1,0:T(8,128)(2,1)S(1)} %get-tuple-element.104), channel_id=1, source_target_pairs={{0,8},{8,16},{16,24},{24,32},{32,40},{40,48},{48,56},{1,9},{9,17},... | collective-permute-start | bytes 184328 | tf_op jit(solution)/shard_map/ppermute | solution.py:24
  22.7 29.2 %copy-start.24 = (f32[4]{0:T(128)}, f32[4]{0:T(128)S(1)}, u32[]{:S(2)}) copy-start(f32[4]{0:T(128)S(1)} %get-tuple-element.153) | copy-start | bytes 52
  22.8 29.2 %copy-start.26 = (f32[4]{0:T(128)}, f32[4]{0:T(128)S(1)}, u32[]{:S(2)}) copy-start(f32[4]{0:T(128)S(1)} %get-tuple-element.154) | copy-start | bytes 52
  22.8 11.3 %copy-start.42 = (f32[140]{0:T(256)}, f32[140]{0:T(256)S(1)}, u32[]{:S(2)}) copy-start(f32[140]{0:T(256)S(1)} %get-tuple-element.151) | copy-start | bytes 1684
  22.8 11.3 %copy-start.45 = (f32[140]{0:T(256)}, f32[140]{0:T(256)S(1)}, u32[]{:S(2)}) copy-start(f32[140]{0:T(256)S(1)} %get-tuple-element.152) | copy-start | bytes 1684
  22.8 28.3 %copy-start.34 = (s32[140]{0:T(256)}, s32[140]{0:T(256)S(1)}, u32[]{:S(2)}) copy-start(s32[140]{0:T(256)S(1)} %get-tuple-element.149) | copy-start | bytes 1684
  22.8 28.3 %copy-start.36 = (s32[140]{0:T(256)}, s32[140]{0:T(256)S(1)}, u32[]{:S(2)}) copy-start(s32[140]{0:T(256)S(1)} %get-tuple-element.150) | copy-start | bytes 1684
  24.0 27.7 %copy-start.38 = (f32[20]{0:T(128)}, f32[20]{0:T(128)S(1)}, u32[]{:S(2)}) copy-start(f32[20]{0:T(128)S(1)} %mul.1008) | copy-start | bytes 244
  24.1 27.6 %copy-start.40 = (f32[20]{0:T(128)}, f32[20]{0:T(128)S(1)}, u32[]{:S(2)}) copy-start(f32[20]{0:T(128)S(1)} %mul.1002) | copy-start | bytes 244
  27.6 16.3 %collective-permute-start.3 = (bf16[3,16,26,9]{3,2,1,0:T(8,128)(2,1)}, bf16[3,16,26,9]{3,2,1,0:T(8,128)(2,1)S(1)}, u32[]{:S(2)}, u32[]{:S(2)}) collective-permute-start(bf16[3,16,26,9]{3,2,1,0:T(8,128)(2,1)} %get-tuple-element.78), channel_id=1, source_target_pairs={{1,0},{2,1},{3,2},{4,3},{5,4},{6,5},{7,6},{9,8},{10,9},{11,10},{12... | collective-permute-start | bytes 67400 | tf_op jit(solution)/shard_map/ppermute | solution.py:27
  30.6 13.4 %collective-permute-start.2 = (bf16[3,16,26,9]{3,2,1,0:T(8,128)(2,1)S(1)}, bf16[3,16,26,9]{3,2,1,0:T(8,128)(2,1)S(1)}, u32[]{:S(2)}, u32[]{:S(2)}) collective-permute-start(bf16[3,16,26,9]{3,2,1,0:T(8,128)(2,1)S(1)} %get-tuple-element.77), channel_id=1, source_target_pairs={{0,1},{1,2},{2,3},{3,4},{4,5},{5,6},{6,7},{8,9},{9,10},{10,11},{11... | collective-permute-start | bytes 67400 | tf_op jit(solution)/shard_map/ppermute | solution.py:24
  34.3 1.8 %copy-start.22 = (f32[640]{0:T(1024)}, f32[640]{0:T(1024)S(1)}, u32[]{:S(2)}) copy-start(f32[640]{0:T(1024)S(1)} %slice_reduce_fusion) | copy-start | bytes 7684
  36.3 14.9 %copy-start.43 = (f32[140]{0:T(256)S(1)}, f32[140]{0:T(256)}, u32[]{:S(2)}) copy-start(f32[140]{0:T(256)} %copy-done.42) | copy-start | bytes 1684
  36.3 14.9 %copy-start.46 = (f32[140]{0:T(256)S(1)}, f32[140]{0:T(256)}, u32[]{:S(2)}) copy-start(f32[140]{0:T(256)} %copy-done.45) | copy-start | bytes 1684
  36.3 16.9 %copy-start.4 = (f32[3,4,4,32]{3,2,1,0:T(4,128)}, f32[3,4,4,32]{3,2,1,0:T(4,128)S(1)}, u32[]{:S(2)}) copy-start(f32[3,4,4,32]{3,2,1,0:T(4,128)S(1)} %get-tuple-element.96) | copy-start | bytes 18436
  36.4 16.9 %copy-start.6 = (f32[3,4,4,32]{3,2,1,0:T(4,128)}, f32[3,4,4,32]{3,2,1,0:T(4,128)S(1)}, u32[]{:S(2)}) copy-start(f32[3,4,4,32]{3,2,1,0:T(4,128)S(1)} %get-tuple-element.97) | copy-start | bytes 18436
  36.4 16.9 %copy-start.8 = (f32[3,4,4,2]{3,2,1,0:T(4,128)}, f32[3,4,4,2]{3,2,1,0:T(4,128)S(1)}, u32[]{:S(2)}) copy-start(f32[3,4,4,2]{3,2,1,0:T(4,128)S(1)} %slice.1088) | copy-start | bytes 1156
  36.8 14.3 %collective-permute-start.7 = (f32[3,1,6,36]{3,2,1,0:T(8,128)S(1)}, f32[3,1,6,36]{3,2,1,0:T(8,128)S(1)}, u32[]{:S(2)}, u32[]{:S(2)}) collective-permute-start(f32[3,1,6,36]{3,2,1,0:T(8,128)S(1)} %get-tuple-element.111), channel_id=1, source_target_pairs={{64,0},{128,64},{192,128},{256,192},{320,256},{384,320},{448,384},... | collective-permute-start | bytes 7784 | tf_op jit(solution)/shard_map/ppermute | solution.py:27
  38.7 12.4 %collective-permute-start.6 = (f32[3,1,6,36]{3,2,1,0:T(8,128)S(1)}, f32[3,1,6,36]{3,2,1,0:T(8,128)S(1)}, u32[]{:S(2)}, u32[]{:S(2)}) collective-permute-start(f32[3,1,6,36]{3,2,1,0:T(8,128)S(1)} %get-tuple-element.110), channel_id=1, source_target_pairs={{0,64},{64,128},{128,192},{192,256},{256,320},{320,384},{384,448},... | collective-permute-start | bytes 7784 | tf_op jit(solution)/shard_map/ppermute | solution.py:24
  43.9 7.7 %copy-start = (bf16[3,16,26,9]{3,2,1,0:T(8,128)(2,1)}, bf16[3,16,26,9]{3,2,1,0:T(8,128)(2,1)S(1)}, u32[]{:S(2)}) copy-start(bf16[3,16,26,9]{3,2,1,0:T(8,128)(2,1)S(1)} %collective-permute-done.2) | copy-start | bytes 67396
  44.4 11.0 %collective-permute-start.5 = (bf16[3,5,26,146]{3,2,1,0:T(8,128)(2,1)S(1)}, bf16[3,5,26,146]{3,2,1,0:T(8,128)(2,1)S(1)}, u32[]{:S(2)}, u32[]{:S(2)}) collective-permute-start(bf16[3,5,26,146]{3,2,1,0:T(8,128)(2,1)S(1)} %get-tuple-element.66), channel_id=1, source_target_pairs={{64,0},{128,64},{192,128},{256,192},{320,256},{384,320},{448,384},... | collective-permute-start | bytes 341648 | tf_op jit(solution)/shard_map/ppermute | solution.py:27
  46.4 10.1 %collective-permute-start.4 = (bf16[3,5,26,146]{3,2,1,0:T(8,128)(2,1)S(1)}, bf16[3,5,26,146]{3,2,1,0:T(8,128)(2,1)}, u32[]{:S(2)}, u32[]{:S(2)}) collective-permute-start(bf16[3,5,26,146]{3,2,1,0:T(8,128)(2,1)S(1)} %get-tuple-element.65), channel_id=1, source_target_pairs={{0,64},{64,128},{128,192},{192,256},{256,320},{320,384},{384,448},... | collective-permute-start | bytes 341648 | tf_op jit(solution)/shard_map/ppermute | solution.py:24
  53.5 2.9 %copy-start.1 = (bf16[3,16,26,9]{3,2,1,0:T(8,128)(2,1)S(1)}, bf16[3,16,26,9]{3,2,1,0:T(8,128)(2,1)}, u32[]{:S(2)}) copy-start(bf16[3,16,26,9]{3,2,1,0:T(8,128)(2,1)} %copy-done) | copy-start | bytes 67396
  62.1 4.6 %copy-start.12 = (bf16[20,20,140]{2,0,1:T(8,128)(2,1)}, bf16[20,20,140]{2,0,1:T(8,128)(2,1)S(1)}, u32[]{:S(2)}) copy-start(bf16[20,20,140]{2,0,1:T(8,128)(2,1)S(1)} %copy.144) | copy-start | bytes 336004
  62.5 4.2 %copy-start.14 = (bf16[20,20,140]{2,0,1:T(8,128)(2,1)}, bf16[20,20,140]{2,0,1:T(8,128)(2,1)S(1)}, u32[]{:S(2)}) copy-start(bf16[20,20,140]{2,0,1:T(8,128)(2,1)S(1)} %copy.143) | copy-start | bytes 336004
  62.9 3.8 %copy-start.16 = (bf16[20,20,140]{2,0,1:T(8,128)(2,1)}, bf16[20,20,140]{2,0,1:T(8,128)(2,1)S(1)}, u32[]{:S(2)}) copy-start(bf16[20,20,140]{2,0,1:T(8,128)(2,1)S(1)} %copy.142) | copy-start | bytes 336004
  64.7 2.0 %copy-start.10 = (f32[20,20,140]{2,0,1:T(8,128)}, f32[20,20,140]{2,0,1:T(8,128)S(1)}, u32[]{:S(2)}) copy-start(f32[20,20,140]{2,0,1:T(8,128)S(1)} %copy.145) | copy-start | bytes 672004
  65.0 1.7 %copy-start.28 = (pred[36,140]{1,0:T(8,128)(4,1)S(1)}, pred[36,140]{1,0:T(8,128)(4,1)}, u32[]{:S(2)}) copy-start(pred[36,140]{1,0:T(8,128)(4,1)} %iota_compare_fusion.7) | copy-start | bytes 15124
  65.0 1.7 %copy-start.29 = (pred[36,140]{1,0:T(8,128)(4,1)S(1)}, pred[36,140]{1,0:T(8,128)(4,1)}, u32[]{:S(2)}) copy-start(pred[36,140]{1,0:T(8,128)(4,1)} %iota_compare_fusion.8) | copy-start | bytes 15124
  65.0 1.7 %copy-start.48 = (f32[140]{0:T(256)S(1)}, f32[140]{0:T(256)}, u32[]{:S(2)}) copy-start(f32[140]{0:T(256)} %get-tuple-element.157) | copy-start | bytes 1684
  65.0 1.7 %copy-start.49 = (f32[140]{0:T(256)S(1)}, f32[140]{0:T(256)}, u32[]{:S(2)}) copy-start(f32[140]{0:T(256)} %get-tuple-element.158) | copy-start | bytes 1684
  65.0 1.7 %copy-start.50 = (f32[4]{0:T(128)S(1)}, f32[4]{0:T(128)}, u32[]{:S(2)}) copy-start(f32[4]{0:T(128)} %get-tuple-element.159) | copy-start | bytes 52
  65.0 1.7 %copy-start.51 = (f32[4]{0:T(128)S(1)}, f32[4]{0:T(128)}, u32[]{:S(2)}) copy-start(f32[4]{0:T(128)} %get-tuple-element.160) | copy-start | bytes 52
  66.7 1.7 %copy-start.5 = (f32[3,4,4,32]{3,2,1,0:T(4,128)S(1)}, f32[3,4,4,32]{3,2,1,0:T(4,128)}, u32[]{:S(2)}) copy-start(f32[3,4,4,32]{3,2,1,0:T(4,128)} %copy-done.4) | copy-start | bytes 18436
  66.8 1.7 %copy-start.7 = (f32[3,4,4,32]{3,2,1,0:T(4,128)S(1)}, f32[3,4,4,32]{3,2,1,0:T(4,128)}, u32[]{:S(2)}) copy-start(f32[3,4,4,32]{3,2,1,0:T(4,128)} %copy-done.6) | copy-start | bytes 18436
  66.8 1.7 %copy-start.9 = (f32[3,4,4,2]{3,2,1,0:T(4,128)S(1)}, f32[3,4,4,2]{3,2,1,0:T(4,128)}, u32[]{:S(2)}) copy-start(f32[3,4,4,2]{3,2,1,0:T(4,128)} %copy-done.8) | copy-start | bytes 1156
  66.8 1.7 %copy-start.52 = (pred[34]{0:T(512)(128)(4,1)S(1)}, pred[34]{0:T(512)(128)(4,1)}, u32[]{:S(2)}) copy-start(pred[34]{0:T(512)(128)(4,1)} %and_or_fusion) | copy-start | bytes 106
  66.8 16.0 %copy-start.23 = (f32[640]{0:T(1024)S(1)}, f32[640]{0:T(1024)}, u32[]{:S(2)}) copy-start(f32[640]{0:T(1024)} %copy-done.22) | copy-start | bytes 7684
  66.8 18.0 %copy-start.35 = (s32[140]{0:T(256)S(1)}, s32[140]{0:T(256)}, u32[]{:S(2)}) copy-start(s32[140]{0:T(256)} %copy-done.34) | copy-start | bytes 1684
  66.8 18.0 %copy-start.37 = (s32[140]{0:T(256)S(1)}, s32[140]{0:T(256)}, u32[]{:S(2)}) copy-start(s32[140]{0:T(256)} %copy-done.36) | copy-start | bytes 1684
  66.8 18.0 %copy-start.44 = (f32[140]{0:T(256)S(1)}, f32[140]{0:T(256)}, u32[]{:S(2)}) copy-start(f32[140]{0:T(256)} %copy-done.42) | copy-start | bytes 1684
  66.8 18.0 %copy-start.47 = (f32[140]{0:T(256)S(1)}, f32[140]{0:T(256)}, u32[]{:S(2)}) copy-start(f32[140]{0:T(256)} %copy-done.45) | copy-start | bytes 1684
  68.3 17.1 %copy-start.39 = (f32[20]{0:T(128)S(1)}, f32[20]{0:T(128)}, u32[]{:S(2)}) copy-start(f32[20]{0:T(128)} %copy-done.38) | copy-start | bytes 244
  68.3 17.1 %copy-start.41 = (f32[20]{0:T(128)S(1)}, f32[20]{0:T(128)}, u32[]{:S(2)}) copy-start(f32[20]{0:T(128)} %copy-done.40) | copy-start | bytes 244
  68.6 7.4 %collective-permute-start.9 = (f32[3,1,4,34]{3,2,1,0:T(4,128)S(1)}, f32[3,1,4,34]{3,2,1,0:T(4,128)S(1)}, u32[]{:S(2)}, u32[]{:S(2)}) collective-permute-start(f32[3,1,4,34]{3,2,1,0:T(4,128)S(1)} %get-tuple-element.121), channel_id=1, source_target_pairs={{64,0},{128,64},{192,128},{256,192},{320,256},{384,320},{448,384},... | collective-permute-start | bytes 4904 | tf_op jit(solution)/shard_map/ppermute | solution.py:27
  70.6 6.2 %collective-permute-start.8 = (f32[3,1,4,34]{3,2,1,0:T(4,128)S(1)}, f32[3,1,4,34]{3,2,1,0:T(4,128)S(1)}, u32[]{:S(2)}, u32[]{:S(2)}) collective-permute-start(f32[3,1,4,34]{3,2,1,0:T(4,128)S(1)} %get-tuple-element.120), channel_id=1, source_target_pairs={{0,64},{64,128},{128,192},{192,256},{256,320},{320,384},{384,448},... | collective-permute-start | bytes 4904 | tf_op jit(solution)/shard_map/ppermute | solution.py:24
  76.8 6.8 %collective-permute-start.11 = (f32[3,6,1,34]{3,2,1,0:T(1,128)S(1)}, f32[3,6,1,34]{3,2,1,0:T(1,128)S(1)}, u32[]{:S(2)}, u32[]{:S(2)}) collective-permute-start(f32[3,6,1,34]{3,2,1,0:T(1,128)S(1)} %get-tuple-element.119), channel_id=1, source_target_pairs={{8,0},{16,8},{24,16},{32,24},{40,32},{48,40},{56,48},{9,1},{17,9},... | collective-permute-start | bytes 7352 | tf_op jit(solution)/shard_map/ppermute | solution.py:27
  78.1 5.5 %collective-permute-start.10 = (f32[3,6,1,34]{3,2,1,0:T(1,128)S(1)}, f32[3,6,1,34]{3,2,1,0:T(1,128)S(1)}, u32[]{:S(2)}, u32[]{:S(2)}) collective-permute-start(f32[3,6,1,34]{3,2,1,0:T(1,128)S(1)} %get-tuple-element.118), channel_id=1, source_target_pairs={{0,8},{8,16},{16,24},{24,32},{32,40},{40,48},{48,56},{1,9},{9,17},... | collective-permute-start | bytes 7352 | tf_op jit(solution)/shard_map/ppermute | solution.py:24
  86.6 1.4 %copy-start.11 = (f32[20,20,140]{2,0,1:T(8,128)S(1)}, f32[20,20,140]{2,0,1:T(8,128)}, u32[]{:S(2)}) copy-start(f32[20,20,140]{2,0,1:T(8,128)} %copy-done.10) | copy-start | bytes 672004
  86.6 1.4 %copy-start.13 = (bf16[20,20,140]{2,0,1:T(8,128)(2,1)S(1)}, bf16[20,20,140]{2,0,1:T(8,128)(2,1)}, u32[]{:S(2)}) copy-start(bf16[20,20,140]{2,0,1:T(8,128)(2,1)} %copy-done.12) | copy-start | bytes 336004
  86.6 1.4 %copy-start.15 = (bf16[20,20,140]{2,0,1:T(8,128)(2,1)S(1)}, bf16[20,20,140]{2,0,1:T(8,128)(2,1)}, u32[]{:S(2)}) copy-start(bf16[20,20,140]{2,0,1:T(8,128)(2,1)} %copy-done.14) | copy-start | bytes 336004
  86.6 1.4 %copy-start.17 = (bf16[20,20,140]{2,0,1:T(8,128)(2,1)S(1)}, bf16[20,20,140]{2,0,1:T(8,128)(2,1)}, u32[]{:S(2)}) copy-start(bf16[20,20,140]{2,0,1:T(8,128)(2,1)} %copy-done.16) | copy-start | bytes 336004
  86.6 1.4 %copy-start.20 = (f32[36,140]{1,0:T(8,128)S(1)}, f32[36,140]{1,0:T(8,128)}, u32[]{:S(2)}) copy-start(f32[36,140]{1,0:T(8,128)} %select_add_fusion) | copy-start | bytes 60484
  88.1 1.7 %copy-start.31 = (f32[3,6,1,34]{3,2,1,0:T(1,128)S(1)}, f32[3,6,1,34]{3,2,1,0:T(1,128)}, u32[]{:S(2)}) copy-start(f32[3,6,1,34]{3,2,1,0:T(1,128)} %copy-done.30) | copy-start | bytes 7348
  88.1 1.7 %copy-start.33 = (f32[3,6,1,34]{3,2,1,0:T(1,128)S(1)}, f32[3,6,1,34]{3,2,1,0:T(1,128)}, u32[]{:S(2)}) copy-start(f32[3,6,1,34]{3,2,1,0:T(1,128)} %copy-done.32) | copy-start | bytes 7348
  90.1 1.1 copy-start.53
  90.1 1.1 copy-start.55
  90.3 16.0 %copy-start.54 = (s32[64]{0:T(128)S(1)}, s32[64]{0:T(128)}, u32[]{:S(2)}) copy-start(s32[64]{0:T(128)} %get-tuple-element.55) | copy-start | bytes 772
  92.4 25.1 %all-to-all-start.1 = ((f32[3,64,16]{2,0,1:T(4,128)}), f32[3,64,16]{2,0,1:T(4,128)S(1)}, u32[]{:S(2)}, u32[]{:S(2)}) async-start(f32[3,64,16]{2,0,1:T(4,128)} %copy.136), calls=%async_computation.1 | async-start | bytes 262144 | tf_op jit(solution)/shard_map/all_to_all | solution.py:363
  (6 other events, 4.1 us)

commit v15 on v14

--- a/solution.py
+++ b/solution.py
@@ -344,7 +344,7 @@
         (column == ez + 1) & (lax.axis_index("gz") == size_z - 1)
     )
     wide_values = jnp.where(ghost, 0.0, wide_values)
-    padded = with_halo(wide_values, (("gx", 1), ("gy", 2)), 1)
+    padded = with_halo(wide_values, (("gy", 2), ("gx", 1)), 1)
     padded = jnp.pad(padded, ((0, 0), (0, 0), (0, 0), (1, 1)))
     moved = spread(padded, wide_table)
     residual = contrast + slopes[0] * moved[0] + slopes[1] * moved[1] + slopes[2] * moved[2]

time: 119 us -> 120 us (level)
  no operation moved by 1% of the time
where the time goes in v15:
time: 120 us; the launch traced here: 119 us
  starting transfers between devices  63.5 us (53%)
  other arithmetic  20.2 us (17%)
  waiting for transfers between devices  13.2 us (11%)
  local copies, waits for them, and re-layouts  12.9 us (11%)
  matrix products  7.5 us (6%)
  between operations  2.02 us (2%)
    ppermute x6, starting transfers between devices, with_halo(): lax.ppermute(lax.slice_in_dim(block, block.shape[dim] - width, None, axis...  26.7 us
    all_to_all x1, starting transfers between devices, per_device(): lax.all_to_all(outgoing, ('gy', 'gz'), split_axis=1, concat_axis=1, tiled...  14.7 us
    ppermute x6, starting transfers between devices, with_halo(): lax.ppermute(lax.slice_in_dim(block, 0, width, axis=dim), axis, backward)  11.3 us
    all_to_all x1, starting transfers between devices, per_device(): lax.all_to_all(send_outgoing, ('gy', 'gz'), split_axis=1, concat_axis=1,...  10.8 us
    all_to_all x1, waiting for transfers between devices, per_device(): lax.all_to_all(outgoing, ('gy', 'gz'), split_axis=1, concat_axis=1, tiled...  10.4 us
    dot_general x3, matrix products, collect(): jnp.dot(volume.reshape(-1, shape_all[3]), table_back, precision=highest)  4.17 us
    concatenate x3, other arithmetic, with_halo(): block = jnp.concatenate([low, block, high], axis=dim)  3.01 us
    unnamed x4, matrix products  2.57 us
  transfers between devices with their start and end apart: 14, of which 4 were waited for; matrix products, arithmetic and copies ran while one was open for 11% of the time, Pallas kernels for 0%

profile of v15, /device:TPU:193, one launch (start us, length us, event | category | flops | bytes accessed | tf_op | source)
XLA Modules:
  0.0 119.3 jit_solution(1406393957562362241)
XLA Ops:
  0.0 0.7 broadcast_add_fusion.1
  0.7 1.2 %and_and_fusion = (pred[64]{0:T(512)(128)(4,1)S(1)}, s32[64]{0:T(128)S(1)}, s32[64]{0:T(128)S(1)}, s32[64]{0:T(128)S(1)}, s32[64]{0:T(128)S(1)}, /*index=5*/s32[64]{0:T(128)}) fusion(s32[64]{0:T(128)S(1)} %get-tuple-element.49, s32[64]{0:T(128)} %param.9), kind=kLoop, calls=%fused_computation.426 | loop fusion | flops 4928 | bytes 1856 | tf_op jit(solution)/shard_map/and | solution.py:268
  2.1 0.3 convert_reduce_fusion
  2.5 0.6 copy-done.21
  3.1 1.1 concatenate.68
  4.3 0.7 fusion.7
  5.0 0.4 copy.110
  5.4 0.4 all_to_all.12
  5.7 0.7 copy.111
  6.5 10.8 %all-to-all-start = ((f32[4,64,80]{2,0,1:T(4,128)}), f32[4,64,80]{2,0,1:T(4,128)S(1)}, u32[]{:S(2)}, u32[]{:S(2)}) async-start(f32[4,64,80]{2,0,1:T(4,128)} %copy.111), calls=%async_computation | async-start | bytes 262144 | tf_op jit(solution)/shard_map/all_to_all | solution.py:297
  17.4 1.3 %collective-permute-start.1 = (bf16[3,16,5,128]{3,2,1,0:T(8,128)(2,1)S(1)}, bf16[3,16,5,128]{3,2,1,0:T(8,128)(2,1)S(1)}, u32[]{:S(2)}, u32[]{:S(2)}) collective-permute-start(bf16[3,16,5,128]{3,2,1,0:T(8,128)(2,1)S(1)} %get-tuple-element.105), channel_id=1, source_target_pairs={{8,0},{16,8},{24,16},{32,24},{40,32},{48,40},{56,48},{9,1},{17,9},... | collective-permute-start | bytes 184328 | tf_op jit(solution)/shard_map/ppermute | solution.py:27
  18.7 4.0 %collective-permute-start = (bf16[3,16,5,128]{3,2,1,0:T(8,128)(2,1)S(1)}, bf16[3,16,5,128]{3,2,1,0:T(8,128)(2,1)S(1)}, u32[]{:S(2)}, u32[]{:S(2)}) collective-permute-start(bf16[3,16,5,128]{3,2,1,0:T(8,128)(2,1)S(1)} %get-tuple-element.104), channel_id=1, source_target_pairs={{0,8},{8,16},{16,24},{24,32},{32,40},{40,48},{48,56},{1,9},{9,17},... | collective-permute-start | bytes 184328 | tf_op jit(solution)/shard_map/ppermute | solution.py:24
  22.8 0.5 fusion.181
  23.4 0.6 fusion.176
  24.1 0.6 iota_compare_fusion.7
  24.7 0.6 iota_compare_fusion.8
  25.3 0.6 select_add_fusion
  26.0 0.6 and_or_fusion
  26.7 0.9 fusion.212
  27.6 2.9 %collective-permute-start.3 = (bf16[3,16,26,9]{3,2,1,0:T(8,128)(2,1)}, bf16[3,16,26,9]{3,2,1,0:T(8,128)(2,1)S(1)}, u32[]{:S(2)}, u32[]{:S(2)}) collective-permute-start(bf16[3,16,26,9]{3,2,1,0:T(8,128)(2,1)} %get-tuple-element.78), channel_id=1, source_target_pairs={{1,0},{2,1},{3,2},{4,3},{5,4},{6,5},{7,6},{9,8},{10,9},{11,10},{12... | collective-permute-start | bytes 67400 | tf_op jit(solution)/shard_map/ppermute | solution.py:27
  30.6 3.1 %collective-permute-start.2 = (bf16[3,16,26,9]{3,2,1,0:T(8,128)(2,1)S(1)}, bf16[3,16,26,9]{3,2,1,0:T(8,128)(2,1)S(1)}, u32[]{:S(2)}, u32[]{:S(2)}) collective-permute-start(bf16[3,16,26,9]{3,2,1,0:T(8,128)(2,1)S(1)} %get-tuple-element.77), channel_id=1, source_target_pairs={{0,1},{1,2},{2,3},{3,4},{4,5},{5,6},{6,7},{8,9},{9,10},{10,11},{11... | collective-permute-start | bytes 67400 | tf_op jit(solution)/shard_map/ppermute | solution.py:24
  33.7 0.4 reshape.465
  34.3 0.3 slice.829
  34.6 0.3 copy.114
  34.9 0.8 fusion.8
  35.7 0.3 copy.115
  36.8 1.9 %collective-permute-start.7 = (f32[3,1,6,36]{3,2,1,0:T(8,128)S(1)}, f32[3,1,6,36]{3,2,1,0:T(8,128)S(1)}, u32[]{:S(2)}, u32[]{:S(2)}) collective-permute-start(f32[3,1,6,36]{3,2,1,0:T(8,128)S(1)} %get-tuple-element.111), channel_id=1, source_target_pairs={{64,0},{128,64},{192,128},{256,192},{320,256},{384,320},{448,384},... | collective-permute-start | bytes 7784 | tf_op jit(solution)/shard_map/ppermute | solution.py:27
  38.7 5.2 %collective-permute-start.6 = (f32[3,1,6,36]{3,2,1,0:T(8,128)S(1)}, f32[3,1,6,36]{3,2,1,0:T(8,128)S(1)}, u32[]{:S(2)}, u32[]{:S(2)}) collective-permute-start(f32[3,1,6,36]{3,2,1,0:T(8,128)S(1)} %get-tuple-element.110), channel_id=1, source_target_pairs={{0,64},{64,128},{128,192},{192,256},{256,320},{320,384},{384,448},... | collective-permute-start | bytes 7784 | tf_op jit(solution)/shard_map/ppermute | solution.py:24
  44.0 0.5 pad_maximum_fusion.9
  44.4 1.9 %collective-permute-start.5 = (bf16[3,5,26,146]{3,2,1,0:T(8,128)(2,1)S(1)}, bf16[3,5,26,146]{3,2,1,0:T(8,128)(2,1)S(1)}, u32[]{:S(2)}, u32[]{:S(2)}) collective-permute-start(bf16[3,5,26,146]{3,2,1,0:T(8,128)(2,1)S(1)} %get-tuple-element.66), channel_id=1, source_target_pairs={{64,0},{128,64},{192,128},{256,192},{320,256},{384,320},{448,384},... | collective-permute-start | bytes 341648 | tf_op jit(solution)/shard_map/ppermute | solution.py:27
  46.4 4.8 %collective-permute-start.4 = (bf16[3,5,26,146]{3,2,1,0:T(8,128)(2,1)S(1)}, bf16[3,5,26,146]{3,2,1,0:T(8,128)(2,1)}, u32[]{:S(2)}, u32[]{:S(2)}) collective-permute-start(bf16[3,5,26,146]{3,2,1,0:T(8,128)(2,1)S(1)} %get-tuple-element.65), channel_id=1, source_target_pairs={{0,64},{64,128},{128,192},{192,256},{256,320},{320,384},{384,448},... | collective-permute-start | bytes 341648 | tf_op jit(solution)/shard_map/ppermute | solution.py:24
  51.2 0.4 fusion.58
  52.0 0.4 multiply_add_fusion.1
  54.4 1.0 collective-permute-done.5
  55.4 1.0 collective-permute-done.4
  56.4 2.7 %pad_maximum_fusion = bf16[3,26,26,146]{3,2,1,0:T(8,128)(2,1)S(1)} fusion(bf16[3,5,26,146]{3,2,1,0:T(8,128)(2,1)S(1)} %collective-permute-done.5, bf16[3,16,26,9]{3,2,1,0:T(8,128)(2,1)S(1)} %collective-permute-done.3, bf16[3,16,5,128]{3,2,1,0:T(8,128)(2,1)S(1)} %collective-permute-done.1, bf16[1,16,16,128]{3,2,1,0:T(8,128)(2,1)S(1)} %convert_bitcast_fusion, ...), kind=kLoop, calls=%fused_computation.13 | loop fusion | flops 5329584 | bytes 1184352 | tf_op jit(solution)/shard_map/concatenate | solution.py:28
  59.3 0.4 fusion.20
  59.7 0.3 fusion.33
  60.0 0.3 fusion.41
  60.3 1.2 add_multiply_fusion
  62.1 0.3 fusion.53
  62.5 0.3 fusion.55
  63.1 1.1 fusion.46
  64.7 0.3 copy-done.19
  65.0 1.4 %multiply_reduce_fusion.5 = (f32[3,20,5,34]{3,1,2,0:T(8,128)S(1)}, f32[3,20,5,34]{3,1,2,0:T(8,128)S(1)}) fusion(f32[4]{0:T(128)S(1)} %copy-done.27, f32[4]{0:T(128)S(1)} %copy-done.25, f32[36,140]{1,0:T(8,128)S(1)} %copy-done.19, f32[20,5,4,140]{3,0,2,1:T(8,128)S(1)} %bitcast.485, f32[20,5,4,140]{3,0,2,1:T(8,128)S(1)} %bitcast.482, ...), kind=kOutput, calls=%fused_computation.28 | convolution fusion | flops 69526800 | bytes 885792 | tf_op jit(solution)/shard_map/dot_general | solution.py:219
  66.8 1.4 %multiply_reduce_fusion.3 = (f32[3,20,5,34]{3,1,2,0:T(8,128)S(1)}, f32[3,20,5,34]{3,1,2,0:T(8,128)S(1)}) fusion(f32[4]{0:T(128)S(1)} %copy-done.51, f32[4]{0:T(128)S(1)} %copy-done.50, pred[36,140]{1,0:T(8,128)(4,1)S(1)} %copy-done.32, pred[36,140]{1,0:T(8,128)(4,1)S(1)} %copy-done.33, f32[140]{0:T(256)S(1)} %copy-done.48, f32[140]{0:T(256)S(1)} %copy-done.49, ...), kind=kOutput, calls=%fused_computation.26 | convolution fusion | flops 69541080 | bytes 652832 | tf_op jit(solution)/shard_map/dot_general | solution.py:219
  68.6 1.3 %collective-permute-start.9 = (f32[3,4,1,34]{3,2,1,0:T(1,128)S(1)}, f32[3,4,1,34]{3,2,1,0:T(1,128)S(1)}, u32[]{:S(2)}, u32[]{:S(2)}) collective-permute-start(f32[3,4,1,34]{3,2,1,0:T(1,128)S(1)} %get-tuple-element.121), channel_id=1, source_target_pairs={{8,0},{16,8},{24,16},{32,24},{40,32},{48,40},{56,48},{9,1},{17,9},... | collective-permute-start | bytes 4904 | tf_op jit(solution)/shard_map/ppermute | solution.py:27
  69.9 4.0 %collective-permute-start.8 = (f32[3,4,1,34]{3,2,1,0:T(1,128)S(1)}, f32[3,4,1,34]{3,2,1,0:T(1,128)S(1)}, u32[]{:S(2)}, u32[]{:S(2)}) collective-permute-start(f32[3,4,1,34]{3,2,1,0:T(1,128)S(1)} %get-tuple-element.120), channel_id=1, source_target_pairs={{0,8},{8,16},{16,24},{24,32},{32,40},{40,48},{48,56},{1,9},{9,17},... | collective-permute-start | bytes 4904 | tf_op jit(solution)/shard_map/ppermute | solution.py:24
  74.0 0.7 collective-permute-done.8
  74.7 1.9 %collective-permute-start.11 = (f32[3,1,6,34]{3,2,1,0:T(8,128)S(1)}, f32[3,1,6,34]{3,2,1,0:T(8,128)S(1)}, u32[]{:S(2)}, u32[]{:S(2)}) collective-permute-start(f32[3,1,6,34]{3,2,1,0:T(8,128)S(1)} %get-tuple-element.119), channel_id=1, source_target_pairs={{64,0},{128,64},{192,128},{256,192},{320,256},{384,320},{448,384},... | collective-permute-start | bytes 7352 | tf_op jit(solution)/shard_map/ppermute | solution.py:27
  76.6 5.6 %collective-permute-start.10 = (f32[3,1,6,34]{3,2,1,0:T(8,128)S(1)}, f32[3,1,6,34]{3,2,1,0:T(8,128)S(1)}, u32[]{:S(2)}, u32[]{:S(2)}) collective-permute-start(f32[3,1,6,34]{3,2,1,0:T(8,128)S(1)} %get-tuple-element.118), channel_id=1, source_target_pairs={{0,64},{64,128},{128,192},{192,256},{256,320},{320,384},{384,448},... | collective-permute-start | bytes 7352 | tf_op jit(solution)/shard_map/ppermute | solution.py:24
  82.3 0.5 add_convert_fusion
  82.9 0.7 eq.206
  83.6 0.6 copy-done.28
  84.2 0.6 copy-done.30
  84.8 0.4 fusion.91
  85.5 0.4 multiply_add_fusion
  86.6 1.2 %fusion.48 = f32[20,20,140]{2,1,0:T(8,128)S(1)} fusion(bf16[20,20,140]{2,1,0:T(8,128)(2,1)} %get-tuple-element.44, f32[20,20,140]{2,1,0:T(8,128)S(1)} %squeeze.128, f32[20,20,140]{2,1,0:T(8,128)S(1)} %squeeze.127, f32[20,20,140]{2,1,0:T(8,128)S(1)} %squeeze.126, f32[3,20,20,140]{3,2,1,0:T(8,128)S(1)} %maximum_convert_fusion), kind=kLoop, calls=%fused_computation.98 | loop fusion | flops 392000 | bytes 1680000 | tf_op jit(solution)/shard_map/add | solution.py:350
  88.1 1.4 %multiply_reduce_fusion.1 = (f32[3,20,5,34]{3,1,2,0:T(8,128)S(1)}, f32[3,20,5,34]{3,1,2,0:T(8,128)S(1)}) fusion(f32[4]{0:T(128)S(1)} %copy-done.27, f32[4]{0:T(128)S(1)} %copy-done.25, f32[36,140]{1,0:T(8,128)S(1)} %copy-done.20, f32[20,5,4,140]{3,0,2,1:T(8,128)S(1)} %bitcast.486, f32[20,5,4,140]{3,0,2,1:T(8,128)S(1)} %bitcast.484, ...), kind=kOutput, calls=%fused_computation.23 | convolution fusion | flops 69526800 | bytes 885792 | tf_op jit(solution)/shard_map/dot_general | solution.py:219
  91.7 0.7 copy.136
  92.4 14.7 %all-to-all-start.1 = ((f32[3,64,16]{2,0,1:T(4,128)}), f32[3,64,16]{2,0,1:T(4,128)S(1)}, u32[]{:S(2)}, u32[]{:S(2)}) async-start(f32[3,64,16]{2,0,1:T(4,128)} %copy.136), calls=%async_computation.1 | async-start | bytes 262144 | tf_op jit(solution)/shard_map/all_to_all | solution.py:363
  107.1 0.7 slice_add_fusion.57
  107.8 10.4 %all-to-all-done.1 = f32[3,64,16]{2,0,1:T(4,128)S(1)} async-done(((f32[3,64,16]{2,0,1:T(4,128)}), f32[3,64,16]{2,0,1:T(4,128)S(1)}, u32[]{:S(2)}, u32[]{:S(2)}) %all-to-all-start.1) | async-done | bytes 12320 | tf_op jit(solution)/shard_map/all_to_all | solution.py:363
  118.4 0.9 convolution_bitcast_fusion
  (272 shorter events, 9.1 us)
Async XLA Ops:
  4.9 12.4 %copy-start.18 = (s32[16,16,128]{2,1,0:T(8,128)S(1)}, s32[16,16,128]{2,1,0:T(8,128)}, u32[]{:S(2)}) copy-start(s32[16,16,128]{2,1,0:T(8,128)} %param.7) | copy-start | bytes 393220
  4.9 12.4 %copy-start.2 = (bf16[16,16,128]{2,1,0:T(8,128)(2,1)S(1)}, bf16[16,16,128]{2,1,0:T(8,128)(2,1)}, u32[]{:S(2)}) copy-start(bf16[16,16,128]{2,1,0:T(8,128)(2,1)} %param.6) | copy-start | bytes 196612
  5.0 12.4 %copy-start.3 = (bf16[16,16,128]{2,1,0:T(8,128)(2,1)S(1)}, bf16[16,16,128]{2,1,0:T(8,128)(2,1)}, u32[]{:S(2)}) copy-start(bf16[16,16,128]{2,1,0:T(8,128)(2,1)} %param.5) | copy-start | bytes 196612
  6.5 27.2 %all-to-all-start = ((f32[4,64,80]{2,0,1:T(4,128)}), f32[4,64,80]{2,0,1:T(4,128)S(1)}, u32[]{:S(2)}, u32[]{:S(2)}) async-start(f32[4,64,80]{2,0,1:T(4,128)} %copy.111), calls=%async_computation | async-start | bytes 262144 | tf_op jit(solution)/shard_map/all_to_all | solution.py:297
  17.4 9.1 %collective-permute-start.1 = (bf16[3,16,5,128]{3,2,1,0:T(8,128)(2,1)S(1)}, bf16[3,16,5,128]{3,2,1,0:T(8,128)(2,1)S(1)}, u32[]{:S(2)}, u32[]{:S(2)}) collective-permute-start(bf16[3,16,5,128]{3,2,1,0:T(8,128)(2,1)S(1)} %get-tuple-element.105), channel_id=1, source_target_pairs={{8,0},{16,8},{24,16},{32,24},{40,32},{48,40},{56,48},{9,1},{17,9},... | collective-permute-start | bytes 184328 | tf_op jit(solution)/shard_map/ppermute | solution.py:27
  18.7 7.8 %collective-permute-start = (bf16[3,16,5,128]{3,2,1,0:T(8,128)(2,1)S(1)}, bf16[3,16,5,128]{3,2,1,0:T(8,128)(2,1)S(1)}, u32[]{:S(2)}, u32[]{:S(2)}) collective-permute-start(bf16[3,16,5,128]{3,2,1,0:T(8,128)(2,1)S(1)} %get-tuple-element.104), channel_id=1, source_target_pairs={{0,8},{8,16},{16,24},{24,32},{32,40},{40,48},{48,56},{1,9},{9,17},... | collective-permute-start | bytes 184328 | tf_op jit(solution)/shard_map/ppermute | solution.py:24
  22.7 29.2 %copy-start.24 = (f32[4]{0:T(128)}, f32[4]{0:T(128)S(1)}, u32[]{:S(2)}) copy-start(f32[4]{0:T(128)S(1)} %get-tuple-element.153) | copy-start | bytes 52
  22.8 29.2 %copy-start.26 = (f32[4]{0:T(128)}, f32[4]{0:T(128)S(1)}, u32[]{:S(2)}) copy-start(f32[4]{0:T(128)S(1)} %get-tuple-element.154) | copy-start | bytes 52
  22.8 11.3 %copy-start.42 = (f32[140]{0:T(256)}, f32[140]{0:T(256)S(1)}, u32[]{:S(2)}) copy-start(f32[140]{0:T(256)S(1)} %get-tuple-element.151) | copy-start | bytes 1684
  22.8 11.3 %copy-start.45 = (f32[140]{0:T(256)}, f32[140]{0:T(256)S(1)}, u32[]{:S(2)}) copy-start(f32[140]{0:T(256)S(1)} %get-tuple-element.152) | copy-start | bytes 1684
  22.8 28.3 %copy-start.34 = (s32[140]{0:T(256)}, s32[140]{0:T(256)S(1)}, u32[]{:S(2)}) copy-start(s32[140]{0:T(256)S(1)} %get-tuple-element.149) | copy-start | bytes 1684
  22.8 28.3 %copy-start.36 = (s32[140]{0:T(256)}, s32[140]{0:T(256)S(1)}, u32[]{:S(2)}) copy-start(s32[140]{0:T(256)S(1)} %get-tuple-element.150) | copy-start | bytes 1684
  24.0 27.7 %copy-start.38 = (f32[20]{0:T(128)}, f32[20]{0:T(128)S(1)}, u32[]{:S(2)}) copy-start(f32[20]{0:T(128)S(1)} %mul.1008) | copy-start | bytes 244
  24.1 27.6 %copy-start.40 = (f32[20]{0:T(128)}, f32[20]{0:T(128)S(1)}, u32[]{:S(2)}) copy-start(f32[20]{0:T(128)S(1)} %mul.1002) | copy-start | bytes 244
  27.6 16.3 %collective-permute-start.3 = (bf16[3,16,26,9]{3,2,1,0:T(8,128)(2,1)}, bf16[3,16,26,9]{3,2,1,0:T(8,128)(2,1)S(1)}, u32[]{:S(2)}, u32[]{:S(2)}) collective-permute-start(bf16[3,16,26,9]{3,2,1,0:T(8,128)(2,1)} %get-tuple-element.78), channel_id=1, source_target_pairs={{1,0},{2,1},{3,2},{4,3},{5,4},{6,5},{7,6},{9,8},{10,9},{11,10},{12... | collective-permute-start | bytes 67400 | tf_op jit(solution)/shard_map/ppermute | solution.py:27
  30.6 13.4 %collective-permute-start.2 = (bf16[3,16,26,9]{3,2,1,0:T(8,128)(2,1)S(1)}, bf16[3,16,26,9]{3,2,1,0:T(8,128)(2,1)S(1)}, u32[]{:S(2)}, u32[]{:S(2)}) collective-permute-start(bf16[3,16,26,9]{3,2,1,0:T(8,128)(2,1)S(1)} %get-tuple-element.77), channel_id=1, source_target_pairs={{0,1},{1,2},{2,3},{3,4},{4,5},{5,6},{6,7},{8,9},{9,10},{10,11},{11... | collective-permute-start | bytes 67400 | tf_op jit(solution)/shard_map/ppermute | solution.py:24
  34.3 1.8 %copy-start.22 = (f32[640]{0:T(1024)}, f32[640]{0:T(1024)S(1)}, u32[]{:S(2)}) copy-start(f32[640]{0:T(1024)S(1)} %slice_reduce_fusion) | copy-start | bytes 7684
  36.3 14.9 %copy-start.43 = (f32[140]{0:T(256)S(1)}, f32[140]{0:T(256)}, u32[]{:S(2)}) copy-start(f32[140]{0:T(256)} %copy-done.42) | copy-start | bytes 1684
  36.3 14.9 %copy-start.46 = (f32[140]{0:T(256)S(1)}, f32[140]{0:T(256)}, u32[]{:S(2)}) copy-start(f32[140]{0:T(256)} %copy-done.45) | copy-start | bytes 1684
  36.3 16.9 %copy-start.4 = (f32[3,4,4,32]{3,2,1,0:T(4,128)}, f32[3,4,4,32]{3,2,1,0:T(4,128)S(1)}, u32[]{:S(2)}) copy-start(f32[3,4,4,32]{3,2,1,0:T(4,128)S(1)} %get-tuple-element.96) | copy-start | bytes 18436
  36.4 16.9 %copy-start.6 = (f32[3,4,4,32]{3,2,1,0:T(4,128)}, f32[3,4,4,32]{3,2,1,0:T(4,128)S(1)}, u32[]{:S(2)}) copy-start(f32[3,4,4,32]{3,2,1,0:T(4,128)S(1)} %get-tuple-element.97) | copy-start | bytes 18436
  36.4 16.9 %copy-start.8 = (f32[3,4,4,2]{3,2,1,0:T(4,128)}, f32[3,4,4,2]{3,2,1,0:T(4,128)S(1)}, u32[]{:S(2)}) copy-start(f32[3,4,4,2]{3,2,1,0:T(4,128)S(1)} %slice.1088) | copy-start | bytes 1156
  36.8 14.3 %collective-permute-start.7 = (f32[3,1,6,36]{3,2,1,0:T(8,128)S(1)}, f32[3,1,6,36]{3,2,1,0:T(8,128)S(1)}, u32[]{:S(2)}, u32[]{:S(2)}) collective-permute-start(f32[3,1,6,36]{3,2,1,0:T(8,128)S(1)} %get-tuple-element.111), channel_id=1, source_target_pairs={{64,0},{128,64},{192,128},{256,192},{320,256},{384,320},{448,384},... | collective-permute-start | bytes 7784 | tf_op jit(solution)/shard_map/ppermute | solution.py:27
  38.7 12.4 %collective-permute-start.6 = (f32[3,1,6,36]{3,2,1,0:T(8,128)S(1)}, f32[3,1,6,36]{3,2,1,0:T(8,128)S(1)}, u32[]{:S(2)}, u32[]{:S(2)}) collective-permute-start(f32[3,1,6,36]{3,2,1,0:T(8,128)S(1)} %get-tuple-element.110), channel_id=1, source_target_pairs={{0,64},{64,128},{128,192},{192,256},{256,320},{320,384},{384,448},... | collective-permute-start | bytes 7784 | tf_op jit(solution)/shard_map/ppermute | solution.py:24
  43.9 7.7 %copy-start = (bf16[3,16,26,9]{3,2,1,0:T(8,128)(2,1)}, bf16[3,16,26,9]{3,2,1,0:T(8,128)(2,1)S(1)}, u32[]{:S(2)}) copy-start(bf16[3,16,26,9]{3,2,1,0:T(8,128)(2,1)S(1)} %collective-permute-done.2) | copy-start | bytes 67396
  44.4 11.0 %collective-permute-start.5 = (bf16[3,5,26,146]{3,2,1,0:T(8,128)(2,1)S(1)}, bf16[3,5,26,146]{3,2,1,0:T(8,128)(2,1)S(1)}, u32[]{:S(2)}, u32[]{:S(2)}) collective-permute-start(bf16[3,5,26,146]{3,2,1,0:T(8,128)(2,1)S(1)} %get-tuple-element.66), channel_id=1, source_target_pairs={{64,0},{128,64},{192,128},{256,192},{320,256},{384,320},{448,384},... | collective-permute-start | bytes 341648 | tf_op jit(solution)/shard_map/ppermute | solution.py:27
  46.4 10.1 %collective-permute-start.4 = (bf16[3,5,26,146]{3,2,1,0:T(8,128)(2,1)S(1)}, bf16[3,5,26,146]{3,2,1,0:T(8,128)(2,1)}, u32[]{:S(2)}, u32[]{:S(2)}) collective-permute-start(bf16[3,5,26,146]{3,2,1,0:T(8,128)(2,1)S(1)} %get-tuple-element.65), channel_id=1, source_target_pairs={{0,64},{64,128},{128,192},{192,256},{256,320},{320,384},{384,448},... | collective-permute-start | bytes 341648 | tf_op jit(solution)/shard_map/ppermute | solution.py:24
  53.5 2.9 %copy-start.1 = (bf16[3,16,26,9]{3,2,1,0:T(8,128)(2,1)S(1)}, bf16[3,16,26,9]{3,2,1,0:T(8,128)(2,1)}, u32[]{:S(2)}) copy-start(bf16[3,16,26,9]{3,2,1,0:T(8,128)(2,1)} %copy-done) | copy-start | bytes 67396
  62.1 4.6 %copy-start.12 = (bf16[20,20,140]{2,0,1:T(8,128)(2,1)}, bf16[20,20,140]{2,0,1:T(8,128)(2,1)S(1)}, u32[]{:S(2)}) copy-start(bf16[20,20,140]{2,0,1:T(8,128)(2,1)S(1)} %copy.144) | copy-start | bytes 336004
  62.5 4.2 %copy-start.14 = (bf16[20,20,140]{2,0,1:T(8,128)(2,1)}, bf16[20,20,140]{2,0,1:T(8,128)(2,1)S(1)}, u32[]{:S(2)}) copy-start(bf16[20,20,140]{2,0,1:T(8,128)(2,1)S(1)} %copy.143) | copy-start | bytes 336004
  62.9 3.8 %copy-start.16 = (bf16[20,20,140]{2,0,1:T(8,128)(2,1)}, bf16[20,20,140]{2,0,1:T(8,128)(2,1)S(1)}, u32[]{:S(2)}) copy-start(bf16[20,20,140]{2,0,1:T(8,128)(2,1)S(1)} %copy.142) | copy-start | bytes 336004
  64.7 2.0 %copy-start.10 = (f32[20,20,140]{2,0,1:T(8,128)}, f32[20,20,140]{2,0,1:T(8,128)S(1)}, u32[]{:S(2)}) copy-start(f32[20,20,140]{2,0,1:T(8,128)S(1)} %copy.145) | copy-start | bytes 672004
  65.0 1.7 %copy-start.32 = (pred[36,140]{1,0:T(8,128)(4,1)S(1)}, pred[36,140]{1,0:T(8,128)(4,1)}, u32[]{:S(2)}) copy-start(pred[36,140]{1,0:T(8,128)(4,1)} %iota_compare_fusion.7) | copy-start | bytes 15124
  65.0 1.7 %copy-start.33 = (pred[36,140]{1,0:T(8,128)(4,1)S(1)}, pred[36,140]{1,0:T(8,128)(4,1)}, u32[]{:S(2)}) copy-start(pred[36,140]{1,0:T(8,128)(4,1)} %iota_compare_fusion.8) | copy-start | bytes 15124
  65.0 1.7 %copy-start.48 = (f32[140]{0:T(256)S(1)}, f32[140]{0:T(256)}, u32[]{:S(2)}) copy-start(f32[140]{0:T(256)} %get-tuple-element.157) | copy-start | bytes 1684
  65.0 1.7 %copy-start.49 = (f32[140]{0:T(256)S(1)}, f32[140]{0:T(256)}, u32[]{:S(2)}) copy-start(f32[140]{0:T(256)} %get-tuple-element.158) | copy-start | bytes 1684
  65.0 1.7 %copy-start.50 = (f32[4]{0:T(128)S(1)}, f32[4]{0:T(128)}, u32[]{:S(2)}) copy-start(f32[4]{0:T(128)} %get-tuple-element.159) | copy-start | bytes 52
  65.0 1.7 %copy-start.51 = (f32[4]{0:T(128)S(1)}, f32[4]{0:T(128)}, u32[]{:S(2)}) copy-start(f32[4]{0:T(128)} %get-tuple-element.160) | copy-start | bytes 52
  66.7 1.7 %copy-start.5 = (f32[3,4,4,32]{3,2,1,0:T(4,128)S(1)}, f32[3,4,4,32]{3,2,1,0:T(4,128)}, u32[]{:S(2)}) copy-start(f32[3,4,4,32]{3,2,1,0:T(4,128)} %copy-done.4) | copy-start | bytes 18436
  66.8 1.7 %copy-start.7 = (f32[3,4,4,32]{3,2,1,0:T(4,128)S(1)}, f32[3,4,4,32]{3,2,1,0:T(4,128)}, u32[]{:S(2)}) copy-start(f32[3,4,4,32]{3,2,1,0:T(4,128)} %copy-done.6) | copy-start | bytes 18436
  66.8 1.7 %copy-start.9 = (f32[3,4,4,2]{3,2,1,0:T(4,128)S(1)}, f32[3,4,4,2]{3,2,1,0:T(4,128)}, u32[]{:S(2)}) copy-start(f32[3,4,4,2]{3,2,1,0:T(4,128)} %copy-done.8) | copy-start | bytes 1156
  66.8 1.7 %copy-start.52 = (pred[34]{0:T(512)(128)(4,1)S(1)}, pred[34]{0:T(512)(128)(4,1)}, u32[]{:S(2)}) copy-start(pred[34]{0:T(512)(128)(4,1)} %and_or_fusion) | copy-start | bytes 106
  66.8 16.0 %copy-start.23 = (f32[640]{0:T(1024)S(1)}, f32[640]{0:T(1024)}, u32[]{:S(2)}) copy-start(f32[640]{0:T(1024)} %copy-done.22) | copy-start | bytes 7684
  66.8 18.0 %copy-start.35 = (s32[140]{0:T(256)S(1)}, s32[140]{0:T(256)}, u32[]{:S(2)}) copy-start(s32[140]{0:T(256)} %copy-done.34) | copy-start | bytes 1684
  66.8 18.0 %copy-start.37 = (s32[140]{0:T(256)S(1)}, s32[140]{0:T(256)}, u32[]{:S(2)}) copy-start(s32[140]{0:T(256)} %copy-done.36) | copy-start | bytes 1684
  66.8 18.0 %copy-start.44 = (f32[140]{0:T(256)S(1)}, f32[140]{0:T(256)}, u32[]{:S(2)}) copy-start(f32[140]{0:T(256)} %copy-done.42) | copy-start | bytes 1684
  66.8 18.0 %copy-start.47 = (f32[140]{0:T(256)S(1)}, f32[140]{0:T(256)}, u32[]{:S(2)}) copy-start(f32[140]{0:T(256)} %copy-done.45) | copy-start | bytes 1684
  68.3 17.0 %copy-start.39 = (f32[20]{0:T(128)S(1)}, f32[20]{0:T(128)}, u32[]{:S(2)}) copy-start(f32[20]{0:T(128)} %copy-done.38) | copy-start | bytes 244
  68.3 17.0 %copy-start.41 = (f32[20]{0:T(128)S(1)}, f32[20]{0:T(128)}, u32[]{:S(2)}) copy-start(f32[20]{0:T(128)} %copy-done.40) | copy-start | bytes 244
  68.6 5.3 %collective-permute-start.9 = (f32[3,4,1,34]{3,2,1,0:T(1,128)S(1)}, f32[3,4,1,34]{3,2,1,0:T(1,128)S(1)}, u32[]{:S(2)}, u32[]{:S(2)}) collective-permute-start(f32[3,4,1,34]{3,2,1,0:T(1,128)S(1)} %get-tuple-element.121), channel_id=1, source_target_pairs={{8,0},{16,8},{24,16},{32,24},{40,32},{48,40},{56,48},{9,1},{17,9},... | collective-permute-start | bytes 4904 | tf_op jit(solution)/shard_map/ppermute | solution.py:27
  69.9 4.8 %collective-permute-start.8 = (f32[3,4,1,34]{3,2,1,0:T(1,128)S(1)}, f32[3,4,1,34]{3,2,1,0:T(1,128)S(1)}, u32[]{:S(2)}, u32[]{:S(2)}) collective-permute-start(f32[3,4,1,34]{3,2,1,0:T(1,128)S(1)} %get-tuple-element.120), channel_id=1, source_target_pairs={{0,8},{8,16},{16,24},{24,32},{32,40},{40,48},{48,56},{1,9},{9,17},... | collective-permute-start | bytes 4904 | tf_op jit(solution)/shard_map/ppermute | solution.py:24
  74.7 8.9 %collective-permute-start.11 = (f32[3,1,6,34]{3,2,1,0:T(8,128)S(1)}, f32[3,1,6,34]{3,2,1,0:T(8,128)S(1)}, u32[]{:S(2)}, u32[]{:S(2)}) collective-permute-start(f32[3,1,6,34]{3,2,1,0:T(8,128)S(1)} %get-tuple-element.119), channel_id=1, source_target_pairs={{64,0},{128,64},{192,128},{256,192},{320,256},{384,320},{448,384},... | collective-permute-start | bytes 7352 | tf_op jit(solution)/shard_map/ppermute | solution.py:27
  76.6 7.0 %collective-permute-start.10 = (f32[3,1,6,34]{3,2,1,0:T(8,128)S(1)}, f32[3,1,6,34]{3,2,1,0:T(8,128)S(1)}, u32[]{:S(2)}, u32[]{:S(2)}) collective-permute-start(f32[3,1,6,34]{3,2,1,0:T(8,128)S(1)} %get-tuple-element.118), channel_id=1, source_target_pairs={{0,64},{64,128},{128,192},{192,256},{256,320},{320,384},{384,448},... | collective-permute-start | bytes 7352 | tf_op jit(solution)/shard_map/ppermute | solution.py:24
  86.6 1.4 %copy-start.11 = (f32[20,20,140]{2,0,1:T(8,128)S(1)}, f32[20,20,140]{2,0,1:T(8,128)}, u32[]{:S(2)}) copy-start(f32[20,20,140]{2,0,1:T(8,128)} %copy-done.10) | copy-start | bytes 672004
  86.6 1.4 %copy-start.13 = (bf16[20,20,140]{2,0,1:T(8,128)(2,1)S(1)}, bf16[20,20,140]{2,0,1:T(8,128)(2,1)}, u32[]{:S(2)}) copy-start(bf16[20,20,140]{2,0,1:T(8,128)(2,1)} %copy-done.12) | copy-start | bytes 336004
  86.6 1.4 %copy-start.15 = (bf16[20,20,140]{2,0,1:T(8,128)(2,1)S(1)}, bf16[20,20,140]{2,0,1:T(8,128)(2,1)}, u32[]{:S(2)}) copy-start(bf16[20,20,140]{2,0,1:T(8,128)(2,1)} %copy-done.14) | copy-start | bytes 336004
  86.6 1.4 %copy-start.17 = (bf16[20,20,140]{2,0,1:T(8,128)(2,1)S(1)}, bf16[20,20,140]{2,0,1:T(8,128)(2,1)}, u32[]{:S(2)}) copy-start(bf16[20,20,140]{2,0,1:T(8,128)(2,1)} %copy-done.16) | copy-start | bytes 336004
  86.6 1.4 %copy-start.20 = (f32[36,140]{1,0:T(8,128)S(1)}, f32[36,140]{1,0:T(8,128)}, u32[]{:S(2)}) copy-start(f32[36,140]{1,0:T(8,128)} %select_add_fusion) | copy-start | bytes 60484
  88.1 1.7 %copy-start.29 = (f32[3,1,6,34]{3,2,1,0:T(8,128)S(1)}, f32[3,1,6,34]{3,2,1,0:T(8,128)}, u32[]{:S(2)}) copy-start(f32[3,1,6,34]{3,2,1,0:T(8,128)} %copy-done.28) | copy-start | bytes 7348
  88.1 1.7 %copy-start.31 = (f32[3,1,6,34]{3,2,1,0:T(8,128)S(1)}, f32[3,1,6,34]{3,2,1,0:T(8,128)}, u32[]{:S(2)}) copy-start(f32[3,1,6,34]{3,2,1,0:T(8,128)} %copy-done.30) | copy-start | bytes 7348
  90.1 1.1 copy-start.53
  90.1 1.1 copy-start.55
  90.3 16.8 %copy-start.54 = (s32[64]{0:T(128)S(1)}, s32[64]{0:T(128)}, u32[]{:S(2)}) copy-start(s32[64]{0:T(128)} %get-tuple-element.55) | copy-start | bytes 772
  92.4 25.9 %all-to-all-start.1 = ((f32[3,64,16]{2,0,1:T(4,128)}), f32[3,64,16]{2,0,1:T(4,128)S(1)}, u32[]{:S(2)}, u32[]{:S(2)}) async-start(f32[3,64,16]{2,0,1:T(4,128)} %copy.136), calls=%async_computation.1 | async-start | bytes 262144 | tf_op jit(solution)/shard_map/all_to_all | solution.py:363
  (6 other events, 4.1 us)

commit v16 on v14

--- a/solution.py
+++ b/solution.py
@@ -326,9 +326,8 @@
     )
     extended = jnp.concatenate([low_row, middle, high_row], axis=2)
     first_padded = with_halo(extended, (("gx", 1),), 1)
-    derived = derive_fields(
-        padded_images[0].astype(jnp.float32), padded_images[1].astype(jnp.float32)
-    )
+    image_pair = padded_images[:2].astype(jnp.float32)
+    derived = derive_fields(image_pair[0], image_pair[1])
     region = padded_images[2][3:-3, 3:-3, 3:-3].astype(jnp.float32)
     contrast = derived[0].astype(jnp.float32)
     slopes = derived[1:].astype(jnp.float32)

time: 119 us -> 125 us (1.050)
  the two profiles are of different devices: /device:TPU:193 before, /device:TPU:1 now
where the time goes in v16:
time: 125 us; the launch traced here: 124 us
  starting transfers between devices  60.6 us (48%)
  waiting for transfers between devices  21.5 us (17%)
  other arithmetic  21 us (17%)
  local copies, waits for them, and re-layouts  12.1 us (10%)
  matrix products  7.5 us (6%)
  between operations  1.71 us (1%)
    ppermute x6, starting transfers between devices, with_halo(): lax.ppermute(lax.slice_in_dim(block, block.shape[dim] - width, None, axis...  24.7 us
    all_to_all x1, starting transfers between devices, per_device(): lax.all_to_all(outgoing, ('gy', 'gz'), split_axis=1, concat_axis=1, tiled...  13.8 us
    all_to_all x1, starting transfers between devices, per_device(): lax.all_to_all(send_outgoing, ('gy', 'gz'), split_axis=1, concat_axis=1,...  13.3 us
    all_to_all x1, waiting for transfers between devices, per_device(): lax.all_to_all(outgoing, ('gy', 'gz'), split_axis=1, concat_axis=1, tiled...  11.1 us
    ppermute x6, waiting for transfers between devices, with_halo(): lax.ppermute(lax.slice_in_dim(block, 0, width, axis=dim), axis, backward)  9.67 us
    ppermute x6, starting transfers between devices, with_halo(): lax.ppermute(lax.slice_in_dim(block, 0, width, axis=dim), axis, backward)  8.77 us
    dot_general x3, matrix products, collect(): jnp.dot(volume.reshape(-1, shape_all[3]), table_back, precision=highest)  4.16 us
    concatenate x3, other arithmetic, with_halo(): block = jnp.concatenate([low, block, high], axis=dim)  3.07 us
  transfers between devices with their start and end apart: 14, of which 5 were waited for; matrix products, arithmetic and copies ran while one was open for 15% of the time, Pallas kernels for 0%

profile of v16, /device:TPU:1, one launch (start us, length us, event | category | flops | bytes accessed | tf_op | source)
XLA Modules:
  0.0 124.4 jit_solution(4911876827170339861)
XLA Ops:
  0.0 0.9 convert_bitcast_fusion
  0.9 0.9 pad_maximum_fusion.10
  1.9 4.0 %collective-permute-start = (bf16[3,16,5,128]{3,2,1,0:T(8,128)(2,1)S(1)}, bf16[3,16,5,128]{3,2,1,0:T(8,128)(2,1)S(1)}, u32[]{:S(2)}, u32[]{:S(2)}) collective-permute-start(bf16[3,16,5,128]{3,2,1,0:T(8,128)(2,1)S(1)} %get-tuple-element.103), channel_id=1, source_target_pairs={{0,8},{8,16},{16,24},{24,32},{32,40},{40,48},{48,56},{1,9},{9,17},... | collective-permute-start | bytes 184328 | tf_op jit(solution)/shard_map/ppermute | solution.py:24
  5.9 1.3 %collective-permute-start.1 = (bf16[3,16,5,128]{3,2,1,0:T(8,128)(2,1)S(1)}, bf16[3,16,5,128]{3,2,1,0:T(8,128)(2,1)S(1)}, u32[]{:S(2)}, u32[]{:S(2)}) collective-permute-start(bf16[3,16,5,128]{3,2,1,0:T(8,128)(2,1)S(1)} %get-tuple-element.104), channel_id=1, source_target_pairs={{8,0},{16,8},{24,16},{32,24},{40,32},{48,40},{56,48},{9,1},{17,9},... | collective-permute-start | bytes 184328 | tf_op jit(solution)/shard_map/ppermute | solution.py:27
  7.2 0.7 broadcast_add_fusion.1
  7.9 1.2 and_and_fusion
  9.3 0.3 convert_reduce_fusion
  9.8 1.1 concatenate.68
  10.9 0.7 fusion.7
  11.6 0.4 copy.110
  12.0 0.4 all_to_all.12
  12.4 0.7 copy.111
  13.1 13.3 %all-to-all-start = ((f32[4,64,80]{2,0,1:T(4,128)}), f32[4,64,80]{2,0,1:T(4,128)S(1)}, u32[]{:S(2)}, u32[]{:S(2)}) async-start(f32[4,64,80]{2,0,1:T(4,128)} %copy.111), calls=%async_computation | async-start | bytes 262144 | tf_op jit(solution)/shard_map/all_to_all | solution.py:297
  26.5 0.6 fusion.181
  27.1 0.6 fusion.176
  27.7 0.6 iota_compare_fusion.8
  28.3 0.6 mul.1002
  28.9 0.6 mul.996
  29.6 0.6 and_or_fusion
  30.4 1.0 fusion.212
  31.3 3.5 %collective-permute-start.2 = (bf16[3,16,26,9]{3,2,1,0:T(8,128)(2,1)}, bf16[3,16,26,9]{3,2,1,0:T(8,128)(2,1)S(1)}, u32[]{:S(2)}, u32[]{:S(2)}) collective-permute-start(bf16[3,16,26,9]{3,2,1,0:T(8,128)(2,1)} %get-tuple-element.76), channel_id=1, source_target_pairs={{0,1},{1,2},{2,3},{3,4},{4,5},{5,6},{6,7},{8,9},{9,10},{10,11},{11... | collective-permute-start | bytes 67400 | tf_op jit(solution)/shard_map/ppermute | solution.py:24
  34.9 1.9 %collective-permute-start.3 = (bf16[3,16,26,9]{3,2,1,0:T(8,128)(2,1)S(1)}, bf16[3,16,26,9]{3,2,1,0:T(8,128)(2,1)S(1)}, u32[]{:S(2)}, u32[]{:S(2)}) collective-permute-start(bf16[3,16,26,9]{3,2,1,0:T(8,128)(2,1)S(1)} %get-tuple-element.77), channel_id=1, source_target_pairs={{1,0},{2,1},{3,2},{4,3},{5,4},{6,5},{7,6},{9,8},{10,9},{11,10},{12... | collective-permute-start | bytes 67400 | tf_op jit(solution)/shard_map/ppermute | solution.py:27
  36.8 0.8 all-to-all-done
  37.6 0.4 reshape.465
  38.2 0.3 slice.838
  38.5 0.3 copy.114
  38.8 0.8 fusion.8
  39.6 0.3 copy.115
  39.9 0.3 reshape.466
  40.6 4.0 %collective-permute-start.6 = (f32[3,1,6,36]{3,2,1,0:T(8,128)S(1)}, f32[3,1,6,36]{3,2,1,0:T(8,128)S(1)}, u32[]{:S(2)}, u32[]{:S(2)}) collective-permute-start(f32[3,1,6,36]{3,2,1,0:T(8,128)S(1)} %get-tuple-element.109), channel_id=1, source_target_pairs={{0,64},{64,128},{128,192},{192,256},{256,320},{320,384},{384,448},... | collective-permute-start | bytes 7784 | tf_op jit(solution)/shard_map/ppermute | solution.py:24
  44.6 1.3 %collective-permute-start.7 = (f32[3,1,6,36]{3,2,1,0:T(8,128)S(1)}, f32[3,1,6,36]{3,2,1,0:T(8,128)S(1)}, u32[]{:S(2)}, u32[]{:S(2)}) collective-permute-start(f32[3,1,6,36]{3,2,1,0:T(8,128)S(1)} %get-tuple-element.110), channel_id=1, source_target_pairs={{64,0},{128,64},{192,128},{256,192},{320,256},{384,320},{448,384},... | collective-permute-start | bytes 7784 | tf_op jit(solution)/shard_map/ppermute | solution.py:27
  45.9 1.1 pad_maximum_fusion.9
  47.1 5.3 %collective-permute-start.4 = (bf16[3,5,26,146]{3,2,1,0:T(8,128)(2,1)}, bf16[3,5,26,146]{3,2,1,0:T(8,128)(2,1)}, u32[]{:S(2)}, u32[]{:S(2)}) collective-permute-start(bf16[3,5,26,146]{3,2,1,0:T(8,128)(2,1)} %get-tuple-element.64), channel_id=1, source_target_pairs={{0,64},{64,128},{128,192},{192,256},{256,320},{320,384},{384,448},... | collective-permute-start | bytes 341648 | tf_op jit(solution)/shard_map/ppermute | solution.py:24
  52.4 1.5 %collective-permute-start.5 = (bf16[3,5,26,146]{3,2,1,0:T(8,128)(2,1)S(1)}, bf16[3,5,26,146]{3,2,1,0:T(8,128)(2,1)}, u32[]{:S(2)}, u32[]{:S(2)}) collective-permute-start(bf16[3,5,26,146]{3,2,1,0:T(8,128)(2,1)S(1)} %get-tuple-element.65), channel_id=1, source_target_pairs={{64,0},{128,64},{192,128},{256,192},{320,256},{384,320},{448,384},... | collective-permute-start | bytes 341648 | tf_op jit(solution)/shard_map/ppermute | solution.py:27
  54.3 0.2 fusion.194
  55.1 0.4 fusion.58
  55.8 0.4 multiply_add_fusion.1
  57.1 3.8 %collective-permute-done.5 = bf16[3,5,26,146]{3,2,1,0:T(8,128)(2,1)} collective-permute-done((bf16[3,5,26,146]{3,2,1,0:T(8,128)(2,1)S(1)}, bf16[3,5,26,146]{3,2,1,0:T(8,128)(2,1)}, u32[]{:S(2)}, u32[]{:S(2)}) %collective-permute-start.5) | collective-permute-done | bytes 113912 | tf_op jit(solution)/shard_map/ppermute | solution.py:27
  60.9 2.8 %pad_maximum_fusion = bf16[3,26,26,146]{3,2,1,0:T(8,128)(2,1)S(1)} fusion(bf16[3,5,26,146]{3,2,1,0:T(8,128)(2,1)} %collective-permute-done.5, bf16[3,16,26,9]{3,2,1,0:T(8,128)(2,1)S(1)} %collective-permute-done.3, bf16[3,16,5,128]{3,2,1,0:T(8,128)(2,1)S(1)} %collective-permute-done.1, bf16[1,16,16,128]{3,2,1,0:T(8,128)(2,1)S(1)} %convert_bitcast_fusion, ...), kind=kLoop, calls=%fused_computation.13 | loop fusion | flops 5329584 | bytes 1184352 | tf_op jit(solution)/shard_map/concatenate | solution.py:28
  63.9 0.4 fusion.25
  64.3 0.6 fusion.33
  64.9 1.2 add_multiply_fusion
  66.4 0.3 fusion.55
  66.9 0.3 fusion.53
  68.0 1.4 %multiply_reduce_fusion.3 = (f32[3,20,5,34]{3,1,2,0:T(8,128)S(1)}, f32[3,20,5,34]{3,1,2,0:T(8,128)S(1)}) fusion(f32[4]{0:T(128)S(1)} %copy-done.27, f32[4]{0:T(128)S(1)} %copy-done.26, pred[36,140]{1,0:T(8,128)(4,1)S(1)} %iota_compare_fusion.7, pred[36,140]{1,0:T(8,128)(4,1)S(1)} %copy-done.10, f32[140]{0:T(256)S(1)} %copy-done.23, f32[140]{0:T(256)S(1)} %copy-done.24, ...), kind=kOutput, calls=%fused_computation.27 | convolution fusion | flops 69541080 | bytes 652832 | tf_op jit(solution)/shard_map/dot_general | solution.py:219
  69.6 0.2 maximum_convert_fusion
  69.8 1.1 fusion.46
  71.1 1.4 %multiply_reduce_fusion.5 = (f32[3,20,5,34]{3,1,2,0:T(8,128)S(1)}, f32[3,20,5,34]{3,1,2,0:T(8,128)S(1)}) fusion(f32[4]{0:T(128)S(1)} %get-tuple-element.153, f32[4]{0:T(128)S(1)} %get-tuple-element.152, f32[36,140]{1,0:T(8,128)S(1)} %select_add_fusion, f32[20,5,4,140]{3,0,2,1:T(8,128)S(1)} %bitcast.486, f32[20,5,4,140]{3,0,2,1:T(8,128)S(1)} %bitcast.483, ...), kind=kOutput, calls=%fused_computation.29 | convolution fusion | flops 69526800 | bytes 885792 | tf_op jit(solution)/shard_map/dot_general | solution.py:219
  72.9 5.5 %collective-permute-start.8 = (f32[3,1,4,34]{3,2,1,0:T(4,128)S(1)}, f32[3,1,4,34]{3,2,1,0:T(4,128)S(1)}, u32[]{:S(2)}, u32[]{:S(2)}) collective-permute-start(f32[3,1,4,34]{3,2,1,0:T(4,128)S(1)} %get-tuple-element.119), channel_id=1, source_target_pairs={{0,64},{64,128},{128,192},{192,256},{256,320},{320,384},{384,448},... | collective-permute-start | bytes 4904 | tf_op jit(solution)/shard_map/ppermute | solution.py:24
  78.4 1.3 %collective-permute-start.9 = (f32[3,1,4,34]{3,2,1,0:T(4,128)S(1)}, f32[3,1,4,34]{3,2,1,0:T(4,128)S(1)}, u32[]{:S(2)}, u32[]{:S(2)}) collective-permute-start(f32[3,1,4,34]{3,2,1,0:T(4,128)S(1)} %get-tuple-element.120), channel_id=1, source_target_pairs={{64,0},{128,64},{192,128},{256,192},{320,256},{384,320},{448,384},... | collective-permute-start | bytes 4904 | tf_op jit(solution)/shard_map/ppermute | solution.py:27
  79.7 4.0 %collective-permute-done.9 = f32[3,1,4,34]{3,2,1,0:T(4,128)S(1)} collective-permute-done((f32[3,1,4,34]{3,2,1,0:T(4,128)S(1)}, f32[3,1,4,34]{3,2,1,0:T(4,128)S(1)}, u32[]{:S(2)}, u32[]{:S(2)}) %collective-permute-start.9) | collective-permute-done | bytes 1664 | tf_op jit(solution)/shard_map/ppermute | solution.py:27
  83.7 2.3 %collective-permute-start.10 = (f32[3,6,1,34]{3,2,1,0:T(1,128)S(1)}, f32[3,6,1,34]{3,2,1,0:T(1,128)S(1)}, u32[]{:S(2)}, u32[]{:S(2)}) collective-permute-start(f32[3,6,1,34]{3,2,1,0:T(1,128)S(1)} %get-tuple-element.117), channel_id=1, source_target_pairs={{0,8},{8,16},{16,24},{24,32},{32,40},{40,48},{48,56},{1,9},{9,17},... | collective-permute-start | bytes 7352 | tf_op jit(solution)/shard_map/ppermute | solution.py:24
  86.0 1.5 %collective-permute-start.11 = (f32[3,6,1,34]{3,2,1,0:T(1,128)S(1)}, f32[3,6,1,34]{3,2,1,0:T(1,128)S(1)}, u32[]{:S(2)}, u32[]{:S(2)}) collective-permute-start(f32[3,6,1,34]{3,2,1,0:T(1,128)S(1)} %get-tuple-element.118), channel_id=1, source_target_pairs={{8,0},{16,8},{24,16},{32,24},{40,32},{48,40},{56,48},{9,1},{17,9},... | collective-permute-start | bytes 7352 | tf_op jit(solution)/shard_map/ppermute | solution.py:27
  87.5 0.6 add_convert_fusion
  88.3 0.7 eq.206
  88.9 1.9 %collective-permute-done.11 = f32[3,6,1,34]{3,2,1,0:T(1,128)S(1)} collective-permute-done((f32[3,6,1,34]{3,2,1,0:T(1,128)S(1)}, f32[3,6,1,34]{3,2,1,0:T(1,128)S(1)}, u32[]{:S(2)}, u32[]{:S(2)}) %collective-permute-start.11) | collective-permute-done | bytes 2480 | tf_op jit(solution)/shard_map/ppermute | solution.py:27
  91.8 0.4 fusion.91
  92.5 0.4 multiply_add_fusion
  93.6 1.2 fusion.48
  95.0 1.4 %multiply_reduce_fusion.1 = (f32[3,20,5,34]{3,1,2,0:T(8,128)S(1)}, f32[3,20,5,34]{3,1,2,0:T(8,128)S(1)}) fusion(f32[4]{0:T(128)S(1)} %get-tuple-element.153, f32[4]{0:T(128)S(1)} %get-tuple-element.152, f32[36,140]{1,0:T(8,128)S(1)} %select_add_fusion, f32[20,5,4,140]{3,0,2,1:T(8,128)S(1)} %bitcast.485, f32[20,5,4,140]{3,0,2,1:T(8,128)S(1)} %bitcast.484, ...), kind=kOutput, calls=%fused_computation.24 | convolution fusion | flops 69526800 | bytes 885792 | tf_op jit(solution)/shard_map/dot_general | solution.py:219
  97.7 0.7 copy.136
  98.5 13.8 %all-to-all-start.1 = ((f32[3,64,16]{2,0,1:T(4,128)}), f32[3,64,16]{2,0,1:T(4,128)S(1)}, u32[]{:S(2)}, u32[]{:S(2)}) async-start(f32[3,64,16]{2,0,1:T(4,128)} %copy.136), calls=%async_computation.1 | async-start | bytes 262144 | tf_op jit(solution)/shard_map/all_to_all | solution.py:362
  112.2 11.1 %all-to-all-done.1 = f32[3,64,16]{2,0,1:T(4,128)S(1)} async-done(((f32[3,64,16]{2,0,1:T(4,128)}), f32[3,64,16]{2,0,1:T(4,128)S(1)}, u32[]{:S(2)}, u32[]{:S(2)}) %all-to-all-start.1) | async-done | bytes 12320 | tf_op jit(solution)/shard_map/all_to_all | solution.py:362
  123.5 0.9 convolution_bitcast_fusion
  (222 shorter events, 8.3 us)
Async XLA Ops:
  1.9 28.3 %collective-permute-start = (bf16[3,16,5,128]{3,2,1,0:T(8,128)(2,1)S(1)}, bf16[3,16,5,128]{3,2,1,0:T(8,128)(2,1)S(1)}, u32[]{:S(2)}, u32[]{:S(2)}) collective-permute-start(bf16[3,16,5,128]{3,2,1,0:T(8,128)(2,1)S(1)} %get-tuple-element.103), channel_id=1, source_target_pairs={{0,8},{8,16},{16,24},{24,32},{32,40},{40,48},{48,56},{1,9},{9,17},... | collective-permute-start | bytes 184328 | tf_op jit(solution)/shard_map/ppermute | solution.py:24
  5.9 24.3 %collective-permute-start.1 = (bf16[3,16,5,128]{3,2,1,0:T(8,128)(2,1)S(1)}, bf16[3,16,5,128]{3,2,1,0:T(8,128)(2,1)S(1)}, u32[]{:S(2)}, u32[]{:S(2)}) collective-permute-start(bf16[3,16,5,128]{3,2,1,0:T(8,128)(2,1)S(1)} %get-tuple-element.104), channel_id=1, source_target_pairs={{8,0},{16,8},{24,16},{32,24},{40,32},{48,40},{56,48},{9,1},{17,9},... | collective-permute-start | bytes 184328 | tf_op jit(solution)/shard_map/ppermute | solution.py:27
  11.6 18.6 %copy-start = (bf16[16,16,128]{2,1,0:T(8,128)(2,1)S(1)}, bf16[16,16,128]{2,1,0:T(8,128)(2,1)}, u32[]{:S(2)}) copy-start(bf16[16,16,128]{2,1,0:T(8,128)(2,1)} %param.6) | copy-start | bytes 196612
  11.6 18.6 %copy-start.1 = (bf16[16,16,128]{2,1,0:T(8,128)(2,1)S(1)}, bf16[16,16,128]{2,1,0:T(8,128)(2,1)}, u32[]{:S(2)}) copy-start(bf16[16,16,128]{2,1,0:T(8,128)(2,1)} %param.5) | copy-start | bytes 196612
  13.1 24.5 %all-to-all-start = ((f32[4,64,80]{2,0,1:T(4,128)}), f32[4,64,80]{2,0,1:T(4,128)S(1)}, u32[]{:S(2)}, u32[]{:S(2)}) async-start(f32[4,64,80]{2,0,1:T(4,128)} %copy.111), calls=%async_computation | async-start | bytes 262144 | tf_op jit(solution)/shard_map/all_to_all | solution.py:297
  26.5 28.6 %copy-start.11 = (s32[140]{0:T(256)}, s32[140]{0:T(256)S(1)}, u32[]{:S(2)}) copy-start(s32[140]{0:T(256)S(1)} %get-tuple-element.149) | copy-start | bytes 1684
  27.7 9.9 %copy-start.17 = (f32[140]{0:T(256)}, f32[140]{0:T(256)S(1)}, u32[]{:S(2)}) copy-start(f32[140]{0:T(256)S(1)} %get-tuple-element.150) | copy-start | bytes 1684
  27.7 10.3 %copy-start.20 = (f32[140]{0:T(256)}, f32[140]{0:T(256)S(1)}, u32[]{:S(2)}) copy-start(f32[140]{0:T(256)S(1)} %get-tuple-element.151) | copy-start | bytes 1684
  31.3 14.6 %collective-permute-start.2 = (bf16[3,16,26,9]{3,2,1,0:T(8,128)(2,1)}, bf16[3,16,26,9]{3,2,1,0:T(8,128)(2,1)S(1)}, u32[]{:S(2)}, u32[]{:S(2)}) collective-permute-start(bf16[3,16,26,9]{3,2,1,0:T(8,128)(2,1)} %get-tuple-element.76), channel_id=1, source_target_pairs={{0,1},{1,2},{2,3},{3,4},{4,5},{5,6},{6,7},{8,9},{9,10},{10,11},{11... | collective-permute-start | bytes 67400 | tf_op jit(solution)/shard_map/ppermute | solution.py:24
  34.9 11.1 %collective-permute-start.3 = (bf16[3,16,26,9]{3,2,1,0:T(8,128)(2,1)S(1)}, bf16[3,16,26,9]{3,2,1,0:T(8,128)(2,1)S(1)}, u32[]{:S(2)}, u32[]{:S(2)}) collective-permute-start(bf16[3,16,26,9]{3,2,1,0:T(8,128)(2,1)S(1)} %get-tuple-element.77), channel_id=1, source_target_pairs={{1,0},{2,1},{3,2},{4,3},{5,4},{6,5},{7,6},{9,8},{10,9},{11,10},{12... | collective-permute-start | bytes 67400 | tf_op jit(solution)/shard_map/ppermute | solution.py:27
  40.6 13.3 %collective-permute-start.6 = (f32[3,1,6,36]{3,2,1,0:T(8,128)S(1)}, f32[3,1,6,36]{3,2,1,0:T(8,128)S(1)}, u32[]{:S(2)}, u32[]{:S(2)}) collective-permute-start(f32[3,1,6,36]{3,2,1,0:T(8,128)S(1)} %get-tuple-element.109), channel_id=1, source_target_pairs={{0,64},{64,128},{128,192},{192,256},{256,320},{320,384},{384,448},... | collective-permute-start | bytes 7784 | tf_op jit(solution)/shard_map/ppermute | solution.py:24
  44.6 9.3 %collective-permute-start.7 = (f32[3,1,6,36]{3,2,1,0:T(8,128)S(1)}, f32[3,1,6,36]{3,2,1,0:T(8,128)S(1)}, u32[]{:S(2)}, u32[]{:S(2)}) collective-permute-start(f32[3,1,6,36]{3,2,1,0:T(8,128)S(1)} %get-tuple-element.110), channel_id=1, source_target_pairs={{64,0},{128,64},{192,128},{256,192},{320,256},{384,320},{448,384},... | collective-permute-start | bytes 7784 | tf_op jit(solution)/shard_map/ppermute | solution.py:27
  47.1 10.0 %collective-permute-start.4 = (bf16[3,5,26,146]{3,2,1,0:T(8,128)(2,1)}, bf16[3,5,26,146]{3,2,1,0:T(8,128)(2,1)}, u32[]{:S(2)}, u32[]{:S(2)}) collective-permute-start(bf16[3,5,26,146]{3,2,1,0:T(8,128)(2,1)} %get-tuple-element.64), channel_id=1, source_target_pairs={{0,64},{64,128},{128,192},{192,256},{256,320},{320,384},{384,448},... | collective-permute-start | bytes 341648 | tf_op jit(solution)/shard_map/ppermute | solution.py:24
  52.4 8.5 %collective-permute-start.5 = (bf16[3,5,26,146]{3,2,1,0:T(8,128)(2,1)S(1)}, bf16[3,5,26,146]{3,2,1,0:T(8,128)(2,1)}, u32[]{:S(2)}, u32[]{:S(2)}) collective-permute-start(bf16[3,5,26,146]{3,2,1,0:T(8,128)(2,1)S(1)} %get-tuple-element.65), channel_id=1, source_target_pairs={{64,0},{128,64},{192,128},{256,192},{320,256},{384,320},{448,384},... | collective-permute-start | bytes 341648 | tf_op jit(solution)/shard_map/ppermute | solution.py:27
  54.2 0.8 copy-start.18
  54.3 0.8 copy-start.21
  54.8 0.7 copy-start.13
  54.9 0.7 copy-start.15
  66.8 4.2 %copy-start.4 = (bf16[20,20,140]{2,0,1:T(8,128)(2,1)}, bf16[20,20,140]{2,0,1:T(8,128)(2,1)S(1)}, u32[]{:S(2)}) copy-start(bf16[20,20,140]{2,0,1:T(8,128)(2,1)S(1)} %copy.142) | copy-start | bytes 336004
  67.2 3.9 %copy-start.6 = (bf16[20,20,140]{2,0,1:T(8,128)(2,1)}, bf16[20,20,140]{2,0,1:T(8,128)(2,1)S(1)}, u32[]{:S(2)}) copy-start(bf16[20,20,140]{2,0,1:T(8,128)(2,1)S(1)} %copy.143) | copy-start | bytes 336004
  67.2 0.7 copy-start.10
  67.3 0.7 copy-start.23
  67.3 0.7 copy-start.24
  67.3 0.7 copy-start.26
  67.3 0.7 copy-start.27
  67.5 3.6 %copy-start.8 = (bf16[20,20,140]{2,0,1:T(8,128)(2,1)}, bf16[20,20,140]{2,0,1:T(8,128)(2,1)S(1)}, u32[]{:S(2)}) copy-start(bf16[20,20,140]{2,0,1:T(8,128)(2,1)S(1)} %copy.144) | copy-start | bytes 336004
  67.8 3.3 %copy-start.2 = (f32[20,20,140]{2,0,1:T(8,128)}, f32[20,20,140]{2,0,1:T(8,128)S(1)}, u32[]{:S(2)}) copy-start(f32[20,20,140]{2,0,1:T(8,128)S(1)} %copy.145) | copy-start | bytes 672004
  71.1 1.6 %copy-start.25 = (pred[34]{0:T(512)(128)(4,1)S(1)}, pred[34]{0:T(512)(128)(4,1)}, u32[]{:S(2)}) copy-start(pred[34]{0:T(512)(128)(4,1)} %and_or_fusion) | copy-start | bytes 106
  72.9 6.8 %collective-permute-start.8 = (f32[3,1,4,34]{3,2,1,0:T(4,128)S(1)}, f32[3,1,4,34]{3,2,1,0:T(4,128)S(1)}, u32[]{:S(2)}, u32[]{:S(2)}) collective-permute-start(f32[3,1,4,34]{3,2,1,0:T(4,128)S(1)} %get-tuple-element.119), channel_id=1, source_target_pairs={{0,64},{64,128},{128,192},{192,256},{256,320},{320,384},{384,448},... | collective-permute-start | bytes 4904 | tf_op jit(solution)/shard_map/ppermute | solution.py:24
  78.4 5.3 %collective-permute-start.9 = (f32[3,1,4,34]{3,2,1,0:T(4,128)S(1)}, f32[3,1,4,34]{3,2,1,0:T(4,128)S(1)}, u32[]{:S(2)}, u32[]{:S(2)}) collective-permute-start(f32[3,1,4,34]{3,2,1,0:T(4,128)S(1)} %get-tuple-element.120), channel_id=1, source_target_pairs={{64,0},{128,64},{192,128},{256,192},{320,256},{384,320},{448,384},... | collective-permute-start | bytes 4904 | tf_op jit(solution)/shard_map/ppermute | solution.py:27
  83.7 5.3 %collective-permute-start.10 = (f32[3,6,1,34]{3,2,1,0:T(1,128)S(1)}, f32[3,6,1,34]{3,2,1,0:T(1,128)S(1)}, u32[]{:S(2)}, u32[]{:S(2)}) collective-permute-start(f32[3,6,1,34]{3,2,1,0:T(1,128)S(1)} %get-tuple-element.117), channel_id=1, source_target_pairs={{0,8},{8,16},{16,24},{24,32},{32,40},{40,48},{48,56},{1,9},{9,17},... | collective-permute-start | bytes 7352 | tf_op jit(solution)/shard_map/ppermute | solution.py:24
  86.0 4.8 %collective-permute-start.11 = (f32[3,6,1,34]{3,2,1,0:T(1,128)S(1)}, f32[3,6,1,34]{3,2,1,0:T(1,128)S(1)}, u32[]{:S(2)}, u32[]{:S(2)}) collective-permute-start(f32[3,6,1,34]{3,2,1,0:T(1,128)S(1)} %get-tuple-element.118), channel_id=1, source_target_pairs={{8,0},{16,8},{24,16},{32,24},{40,32},{48,40},{56,48},{9,1},{17,9},... | collective-permute-start | bytes 7352 | tf_op jit(solution)/shard_map/ppermute | solution.py:27
  91.0 0.8 copy-start.12
  91.0 0.8 copy-start.19
  91.0 0.8 copy-start.22
  91.5 0.7 copy-start.14
  91.6 0.7 copy-start.16
  93.6 1.4 %copy-start.3 = (f32[20,20,140]{2,0,1:T(8,128)S(1)}, f32[20,20,140]{2,0,1:T(8,128)}, u32[]{:S(2)}) copy-start(f32[20,20,140]{2,0,1:T(8,128)} %copy-done.2) | copy-start | bytes 672004
  93.6 1.4 %copy-start.5 = (bf16[20,20,140]{2,0,1:T(8,128)(2,1)S(1)}, bf16[20,20,140]{2,0,1:T(8,128)(2,1)}, u32[]{:S(2)}) copy-start(bf16[20,20,140]{2,0,1:T(8,128)(2,1)} %copy-done.4) | copy-start | bytes 336004
  93.6 1.4 %copy-start.7 = (bf16[20,20,140]{2,0,1:T(8,128)(2,1)S(1)}, bf16[20,20,140]{2,0,1:T(8,128)(2,1)}, u32[]{:S(2)}) copy-start(bf16[20,20,140]{2,0,1:T(8,128)(2,1)} %copy-done.6) | copy-start | bytes 336004
  93.6 1.4 %copy-start.9 = (bf16[20,20,140]{2,0,1:T(8,128)(2,1)S(1)}, bf16[20,20,140]{2,0,1:T(8,128)(2,1)}, u32[]{:S(2)}) copy-start(bf16[20,20,140]{2,0,1:T(8,128)(2,1)} %copy-done.8) | copy-start | bytes 336004
  96.4 0.8 copy-start.28
  96.4 0.8 copy-start.30
  96.5 15.8 %copy-start.29 = (s32[64]{0:T(128)S(1)}, s32[64]{0:T(128)}, u32[]{:S(2)}) copy-start(s32[64]{0:T(128)} %get-tuple-element.55) | copy-start | bytes 772
  98.5 24.9 %all-to-all-start.1 = ((f32[3,64,16]{2,0,1:T(4,128)}), f32[3,64,16]{2,0,1:T(4,128)S(1)}, u32[]{:S(2)}, u32[]{:S(2)}) async-start(f32[3,64,16]{2,0,1:T(4,128)} %copy.136), calls=%async_computation.1 | async-start | bytes 262144 | tf_op jit(solution)/shard_map/all_to_all | solution.py:362
